TPU v7x, 128 devices: a whole 4x4x4 slice. The times are simulated.
128 devices in a mesh: feed: 8 (over y, core), chan: 16 (over z, x).
Axes of the slice: x: 4, y: 4, z: 4, core: 2. Of those that a mesh axis runs over, the one named last changes fastest.
Arguments:
- voltages: bfloat16 [2, 2, 16, 8192, 1024], P(None, None, 'chan', None, 'feed'), may hold values from -6 to 6
- history: bfloat16 [2, 2, 16, 48, 1024], P(None, None, 'chan', None, 'feed'), may hold values from -6 to 6
- gains: float32 [2, 2, 16, 1024], P(None, None, 'chan', 'feed'), may hold values from -4 to 4
- weights: bfloat16 [2, 16, 1024, 1024], P(None, 'chan'), may hold values from -0.09375 to 0.09375
- beam_lists: int32 [16, 128], replicated, may hold values from 0 to 1023, as said below
- beam_counts: int32 [16], replicated, may hold values from 1 to 128, as said below
Outputs:
- power_blocks: bfloat16 [256, 256, 2048], P('feed', None, 'chan')
Inputs may be any that keep to these rules, and one draw needn't show every extreme that they name: `beam_lists`: row n holds in its first beam_counts[n] entries, in increasing order, the beams that node n owns, and 0 in the others; every beam is owned by exactly one node. `beam_counts`: the counts sum to 1024; some node owns exactly 128 beams.
All inputs are finite; a program needn't handle non-finite values.
Results may differ from a plain program's by a relative error of at most 0.013.
Values may be sent and summed in bfloat16 or wider, within the bound.
No kernel may reach another device: no remote copies, remote signals or barrier semaphores. Data moves between devices by JAX's collectives and lax.ppermute only.
A program may use at most 192 MiB of HBM per device.

v0:
```python
import math

import jax
import jax.numpy as jnp
from jax import lax
from jax.sharding import PartitionSpec as P

U = 16
TAPS = 4
TINT = 2


def window_taps():
    length = TAPS * U
    positions = jnp.arange(length, dtype=jnp.float32)
    offsets = (positions - (length - 1) / 2.0) / U
    hann_taper = 0.5 - 0.5 * jnp.cos(2.0 * math.pi * (positions + 0.5) / length)
    taps_window = jnp.sinc(offsets) * hann_taper
    return taps_window / jnp.sqrt(jnp.sum(taps_window * taps_window) / U)


def dft_table():
    index_n = jnp.arange(U, dtype=jnp.int32)
    products = index_n[:, None] * index_n[None, :] % U
    phases = 2.0 * math.pi * products.astype(jnp.float32) / U
    cosine = jnp.cos(phases) / math.sqrt(U)
    sine = jnp.sin(phases) / math.sqrt(U)
    return jnp.stack([jnp.stack([cosine, -sine]), jnp.stack([sine, cosine])])


def filterbank(stream, frames, gains):
    shape_in = stream.shape
    taps_window = window_taps().reshape(TAPS, U)
    table = dft_table()
    frames_data = stream.reshape(
        shape_in[0], shape_in[1], shape_in[2], frames + TAPS - 1, U, shape_in[4]
    )
    filtered = taps_window[0][:, None] * frames_data[:, :, :, 0:frames].astype(jnp.float32)
    for tap_index in range(1, TAPS):
        filtered = filtered + taps_window[tap_index][:, None] * frames_data[
            :, :, :, tap_index : tap_index + frames
        ].astype(jnp.float32)
    spec_parts = []
    for part_out in range(2):
        total = None
        for part_in in range(2):
            for index_n in range(U):
                term = (
                    filtered[part_in, :, :, :, index_n : index_n + 1, :]
                    * table[part_in, part_out, index_n][:, None]
                )
                total = term if total is None else total + term
        spec_parts.append(total)
    gain_cols = gains[:, :, :, None, None, :]
    real_part = gain_cols[0] * spec_parts[0] - gain_cols[1] * spec_parts[1]
    imag_part = gain_cols[0] * spec_parts[1] + gain_cols[1] * spec_parts[0]
    return jnp.stack([real_part, imag_part]).astype(jnp.bfloat16)


def detect(calibrated, weights):
    spectra_here = calibrated.shape[3]
    fine_items = calibrated.shape[4]
    beam_total = weights.shape[3]
    rows_real = calibrated[0, :, 0].reshape(-1, calibrated.shape[5])
    rows_imag = calibrated[1, :, 0].reshape(-1, calibrated.shape[5])
    weight_real = weights[0, 0]
    weight_imag = weights[1, 0]
    upper_block = jnp.concatenate([weight_real, weight_imag], axis=1)
    lower_block = jnp.concatenate([-weight_imag, weight_real], axis=1)
    joined = jnp.dot(rows_real, upper_block, preferred_element_type=jnp.float32) + jnp.dot(
        rows_imag, lower_block, preferred_element_type=jnp.float32
    )
    real_part = joined[:, :beam_total]
    imag_part = joined[:, beam_total:]
    power_sum = (real_part * real_part + imag_part * imag_part).reshape(
        2, spectra_here, fine_items, beam_total
    )
    power_sum = jnp.sum(power_sum, axis=0).reshape(
        spectra_here // TINT, TINT, fine_items, beam_total
    )
    power_sum = jnp.sum(power_sum, axis=1) * (1.0 / (4.0 * TINT))
    outputs = [power_sum.astype(jnp.bfloat16)]
    return jnp.stack(outputs, axis=1)


def on_device(voltages, history, gains, weights, beam_lists, beam_counts):
    capacity = beam_lists.shape[1]
    flat_ids = beam_lists.reshape(-1)
    live_slots = (jnp.arange(capacity, dtype=jnp.int32)[None, :] < beam_counts[:, None]).reshape(-1)
    stream = jnp.concatenate([history, voltages], axis=3)
    calibrated = filterbank(stream, voltages.shape[3] // U, gains)
    beam_calibrated = lax.all_to_all(calibrated, "feed", split_axis=3, concat_axis=5, tiled=True)
    detected = detect(beam_calibrated, weights)
    bins_local, coarse_local, fine_items, beam_total = detected.shape
    picked = jnp.take(
        detected.reshape(bins_local, coarse_local * fine_items, beam_total), flat_ids, axis=2
    )
    return lax.all_to_all(
        jnp.where(live_slots, picked, jnp.zeros((), jnp.bfloat16)),
        "chan",
        split_axis=2,
        concat_axis=1,
        tiled=True,
    )


def solution(mesh):
    in_specs = (
        P(None, None, "chan", None, "feed"),
        P(None, None, "chan", None, "feed"),
        P(None, None, "chan", "feed"),
        P(None, "chan", None, None),
        P(),
        P(),
    )
    out_specs = P("feed", None, "chan")
    return jax.shard_map(
        on_device, mesh=mesh, in_specs=in_specs, out_specs=out_specs, check_vma=False
    )
```

profile of v0, /device:TPU:0, one launch (start us, length us, event | category | flops | bytes accessed | tf_op | source)
XLA Modules:
  0.0 429.2 jit_solution(4782768966015367416)
XLA Ops:
  0.0 0.7 multiply_reduce_fusion
  0.7 4.3 pad_maximum_fusion
  5.0 11.6 %fusion.35 = (bf16[2,2,1,512,16,128]{5,4,3,1,0,2:T(8,128)(2,1)}, bf16[2,2,1,512,16,128]{5,4,3,1,0,2:T(8,128)(2,1)}, bf16[2,2,1,512,16,128]{5,4,3,1,0,2:T(8,128)(2,1)}, bf16[2,2,1,512,16,128]{5,4,3,1,0,2:T(8,128)(2,1)}) fusion(bf16[2,2,1,515,16,128]{5,4,3,1,0,2:T(8,128)(2,1)S(1)} %bitcast.249), kind=kLoop, calls=%fused_computation.172 | loop fusion | bytes 67108864 | tf_op jit(solution)/shard_map/slice | solution.py:38
  17.2 0.1 broadcast_divide_fusion
  17.3 0.1 fusion.38
  17.4 56.0 %multiply_add_fusion = f32[2,2,1,512,16,128]{5,1,3,4,2,0:T(2,128)} fusion(f32[16]{0:T(128)S(1)} %get-tuple-element.117, f32[16]{0:T(128)S(1)} %get-tuple-element.118, f32[16]{0:T(128)S(1)} %get-tuple-element.119, f32[16]{0:T(128)S(1)} %get-tuple-element.116, bf16[2,2,1,512,16,128]{5,4,3,1,0,2:T(8,128)(2,1)} %get-tuple-element.43, ...), kind=kLoop, calls=%fused_computation.1 | loop fusion | flops 46137344 | bytes 50331904 | tf_op jit(solution)/shard_map/add | solution.py:40
  73.3 6.9 %slice_bitcast_fusion.33 = (f32[2,512,128]{2,0,1:T(2,128)S(1)}, f32[2,512,128]{2,0,1:T(2,128)S(1)}, f32[2,512,128]{2,0,1:T(2,128)S(1)}, f32[2,512,128]{2,0,1:T(2...) fusion(f32[2,2,1,512,16,128]{5,1,3,4,2,0:T(2,128)} %multiply_ad, ...), kind=kLoop, calls=%fused_computation.61 | loop fusion | bytes 19922944 | tf_op jit(solution)/shard_map/mul | solution.py:49
  80.2 0.0 copy-start.3
  80.2 4.9 %slice_bitcast_fusion.32 = (f32[2,512,128]{2,0,1:T(2,128)}, f32[2,512,128]{2,0,1:T(2,128)}, f32[2,512,128]{2,0,1:T(2,128)}, f32[2,512,128]{2,0,1:T(2,128)}, f32[...) fusion(f32[2,2,1,512,16,128]{5,1,3,4,2,0:T(2,128)} %multiply_ad, ...), kind=kLoop, calls=%fused_computation.60 | loop fusion | bytes 13631488 | tf_op jit(solution)/shard_map/mul | solution.py:49
  85.2 0.1 sine_multiply_fusion
  85.2 0.1 fusion.21
  85.4 0.0 copy-done.3
  85.4 49.3 %fusion.1 = (bf16[1,2,1,512,16,128]{5,4,1,0,2,3:T(8,128)(2,1)}, f32[1,2,512,16,128]{4,3,1,2,0:T(8,128)}, f32[1,2,512,16,128]{4,3,1,2,0:T(8,128)}) fusion(f32[2,128]{1,0:T(2,128)S(1)} %bitcast.259, f32[2,128]{1,0:T(2,128)S(1)} %bitcast.257, f32[16]{0:T(128)S(1)} %get-tuple-element.81, f32[2,512,128]{2,0,1:T(2,128)S(1)} %get-tuple-element.9, ...), kind=kLoop, calls=%fused_computation.13 | loop fusion | flops 272629760 | bytes 37754880 | tf_op jit(solution)/shard_map/stack | solution.py:57
  134.7 7.9 %fusion.2 = bf16[1,2,1,512,16,128]{5,4,1,0,2,3:T(8,128)(2,1)S(1)} fusion(f32[1,2,512,16,128]{4,3,1,2,0:T(8,128)} %get-tuple-element.7, f32[1,2,512,16,128]{4,3,1,2,0:T(8,128)} %get-tuple-element.6, f32[2,128]{1,0:T(2,128)S(1)} %bitcast.260, f32[2,128]{1,0:T(2,128)S(1)} %bitcast.258), kind=kLoop, calls=%fused_computation.14 | loop fusion | flops 8388608 | bytes 20973568 | tf_op jit(solution)/shard_map/stack | solution.py:57
  142.6 6.5 %pad_maximum_fusion.1 = bf16[2,2,1,512,16,128]{5,4,1,0,2,3:T(8,128)(2,1)} fusion(bf16[1,2,1,512,16,128]{5,4,1,0,2,3:T(8,128)(2,1)S(1)} %fusion.2, bf16[1,2,1,512,16,128]{5,4,1,0,2,3:T(8,128)(2,1)} %get-tuple-element.5), kind=kLoop, calls=%fused_computation.6 | loop fusion | flops 4194304 | bytes 16777216 | tf_op jit(solution)/shard_map/stack | solution.py:57
  149.1 0.0 copy-start.4
  149.1 0.0 copy-start.2
  149.1 5.1 %all-to-all-start = ((bf16[2,2,1,512,16,128]{5,4,1,0,2,3:T(8,128)(2,1)}), bf16[2,2,1,512,16,128]{5,4,1,0,2,3:T(8,128)(2,1)}, u32[]{:S(2)}, u32[]{:S(2)}) async-start(bf16[2,2,1,512,16,128]{5,4,1,0,2,3:T(8,128)(2,1)} %pad_maximum_fusion.1), calls=%async_computation | async-start | bytes 16777216 | tf_op jit(solution)/shard_map/all_to_all | solution.py:92
  154.2 0.0 copy-done.4
  154.2 0.1 fusion.20
  154.2 0.0 copy-done.2
  154.3 1.7 fusion.34
  156.0 4.7 %slice_bitcast_fusion.1 = (bf16[1024,1024]{1,0:T(8,128)(2,1)}, bf16[1024,1024]{1,0:T(8,128)(2,1)}) fusion(bf16[2,1,1024,1024]{3,2,1,0:T(8,128)(2,1)} %param.9), kind=kLoop, calls=%fused_computation.29 | loop fusion | bytes 8388608 | tf_op jit(solution)/shard_map/squeeze | solution.py:66
  160.7 88.1 %all-to-all-done = bf16[2,2,1,512,16,128]{5,4,1,0,2,3:T(8,128)(2,1)} async-done(((bf16[2,2,1,512,16,128]{5,4,1,0,2,3:T(8,128)(2,1)}), bf16[2,2,1,512,16,128]{5,4,1,0,2,3:T(8,128)(2,1)}, u32[]{:S(2)}, u32[]{:S(2)}) %all-to-all-start) | async-done | bytes 8388640 | tf_op jit(solution)/shard_map/all_to_all | solution.py:92
  248.8 8.1 %copy.43 = bf16[2,2,1,512,16,128]{5,4,3,1,0,2:T(8,128)(2,1)} copy(bf16[2,2,1,512,16,128]{5,4,1,0,2,3:T(8,128)(2,1)} %all-to-all-done) | data formatting | bytes 16777216 | tf_op jit(solution)/shard_map/all_to_all | solution.py:92
  256.8 4.4 %fusion.36 = (bf16[1,2,1,64,16,8,128]{6,4,3,5,1,0,2:T(8,128)(2,1)S(1)}, bf16[1,2,1,64,16,8,128]{6,4,3,5,1,0,2:T(8,128)(2,1)S(1)}) fusion(bf16[2,2,1,64,16,8,128]{6,4,3,5,1,0,2:T(8,128)(2,1)} %bitcast.252), kind=kLoop, calls=%fused_computation.173 | loop fusion | bytes 16777216 | tf_op jit(solution)/shard_map/slice | solution.py:65
  261.2 0.0 copy-start
  261.2 0.0 copy-start.1
  261.2 4.9 %copy.44 = bf16[1,2,1,64,16,8,128]{6,5,4,3,1,2,0:T(8,128)(2,1)S(1)} copy(bf16[1,2,1,64,16,8,128]{6,4,3,5,1,0,2:T(8,128)(2,1)S(1)} %get-tuple-element.45) | data formatting | bytes 8388608 | tf_op jit(solution)/shard_map/slice | solution.py:64
  266.1 4.9 %copy.45 = bf16[1,2,1,64,16,8,128]{6,5,4,3,1,2,0:T(8,128)(2,1)S(1)} copy(bf16[1,2,1,64,16,8,128]{6,4,3,5,1,0,2:T(8,128)(2,1)S(1)} %get-tuple-element.44) | data formatting | bytes 8388608 | tf_op jit(solution)/shard_map/slice | solution.py:65
  271.0 0.0 copy-done
  271.0 0.0 copy-done.1
  271.0 12.0 %fusion.5 = f32[2048,2048]{1,0:T(8,128)} fusion(bf16[256,8,8,128]{3,2,1,0:T(8,128)(2,1)S(1)} %bitcast.254, bf16[1024,1024]{1,0:T(8,128)(2,1)S(1)} %copy-done.1, bf16[1024,1024]{1,0:T(8,128)(2,1)S(1)} %copy-done), kind=kOutput, calls=%fused_computation.17 | convolution fusion | flops 8598323200 | bytes 25165824 | tf_op jit(solution)/shard_map/dot_general | solution.py:70
  282.9 17.8 %convolution_add_fusion = f32[2048,2048]{1,0:T(8,128)} fusion(f32[2048,2048]{1,0:T(8,128)} %fusion.5, bf16[256,8,8,128]{3,2,1,0:T(8,128)(2,1)S(1)} %bitcast.253, bf16[1024,1024]{1,0:T(8,128)(2,1)} %get-tuple-element.46, bf16[1024,1024]{1,0:T(8,128)(2,1)S(1)} %fusion.34), kind=kOutput, calls=%fused_computation.12 | convolution fusion | flops 8602517504 | bytes 41943040 | tf_op jit(solution)/shard_map/dot_general | solution.py:70
  300.7 9.3 %fusion = f32[2048,1024]{1,0:T(8,128)} fusion(f32[2048,2048]{1,0:T(8,128)} %convolution_add_fusion), kind=kLoop, calls=%fused_computation.4 | loop fusion | flops 6291456 | bytes 25165824 | tf_op jit(solution)/shard_map/add | solution.py:75
  310.0 6.7 %reduce_sum.28 = f32[64,16,1024]{2,1,0:T(8,128)} reduce(f32[2,64,16,1024]{3,2,1,0:T(8,128)} %bitcast.250, f32[]{:T(128)} %constant.78.clone.1), dimensions={0}, to_apply=%region_1.2 | reduce | flops 1048576 | bytes 12582916 | tf_op jit(solution)/shard_map/reduce_sum | solution.py:78
  316.6 2.8 bitcast_reduce_fusion
  319.4 0.2 multiply_convert_fusion
  319.7 5.1 %copy.46 = bf16[32,16,1024]{0,1,2:T(8,128)(2,1)} copy(bf16[32,16,1024]{2,1,0:T(8,128)(2,1)S(1)} %multiply_convert_fusion) | data formatting | bytes 2097152 | tf_op jit(solution)/shard_map/convert_element_type | solution.py:82
  324.8 18.4 %gather_fusion = bf16[2048,32,16]{1,2,0:T(8,128)(2,1)} fusion(bf16[32,16,1024]{0,1,2:T(8,128)(2,1)} %copy.46, s32[2048]{0:T(1024)S(1)} %broadcast_clamp_fusion), kind=kCustom, calls=%fused_computation | custom fusion | bytes 4202496 | tf_op jit(solution)/shard_map/jit(_take)/gather | solution.py:95
  343.3 12.1 %fusion.39 = bf16[2048,16,32]{2,1,0:T(8,128)(2,1)} fusion(bf16[2048,32,16]{1,2,0:T(8,128)(2,1)} %gather_fusion, pred[2048]{0:T(1024)(128)(4,1)S(1)} %compare_and_fusion, pred[2048]{0:T(1024)(128)(4,1)S(1)} %fusion.20), kind=kLoop, calls=%fused_computation.176 | loop fusion | flops 2097152 | bytes 4198400
  355.4 13.4 %reshape.1023 = bf16[16,2,32768]{2,1,0:T(2,128)(2,1)S(1)} reshape(bf16[2048,16,32]{2,1,0:T(8,128)(2,1)} %fusion.39) | data formatting | bytes 4194304
  368.8 36.1 %all_to_all.33 = bf16[16,2,32768]{2,1,0:T(2,128)(2,1)} all-to-all(bf16[16,2,32768]{2,1,0:T(2,128)(2,1)S(1)} %reshape.1023), channel_id=1, replica_groups=mesh['feed'=8,'chan'=16] {'chan'}, dimensions={0} | all-to-all | bytes 4194304 | tf_op jit(solution)/shard_map/all_to_all | solution.py:98
  404.8 12.9 %reshape.1024 = bf16[2048,16,32]{2,1,0:T(8,128)(2,1)} reshape(bf16[16,2,32768]{2,1,0:T(2,128)(2,1)} %all_to_all.33) | data formatting | bytes 4194304
  417.8 11.2 %copy.48 = bf16[32,16,16,128]{3,2,1,0:T(8,128)(2,1)} copy(bf16[32,16,16,128]{0,2,3,1:T(8,128)(2,1)} %bitcast.251) | data formatting | bytes 4194304 | tf_op jit(solution)/shard_map/all_to_all | solution.py:98
  (9 shorter events, 0.1 us)
Async XLA Ops:
  80.2 5.2 %copy-start.3 = (f32[2,2,1,128]{3,2,1,0:T(1,128)S(1)}, f32[2,2,1,128]{3,2,1,0:T(1,128)}, u32[]{:S(2)}) copy-start(f32[2,2,1,128]{3,2,1,0:T(1,128)} %param.8) | copy-start | bytes 6148
  149.1 5.1 %copy-start.4 = (s32[16]{0:T(128)S(1)}, s32[16]{0:T(128)}, u32[]{:S(2)}) copy-start(s32[16]{0:T(128)} %param.11) | copy-start | bytes 196
  149.1 5.2 %copy-start.2 = (s32[16,128]{1,0:T(8,128)S(1)}, s32[16,128]{1,0:T(8,128)}, u32[]{:S(2)}) copy-start(s32[16,128]{1,0:T(8,128)} %param.10) | copy-start | bytes 24580
  149.1 99.7 %all-to-all-start = ((bf16[2,2,1,512,16,128]{5,4,1,0,2,3:T(8,128)(2,1)}), bf16[2,2,1,512,16,128]{5,4,1,0,2,3:T(8,128)(2,1)}, u32[]{:S(2)}, u32[]{:S(2)}) async-start(bf16[2,2,1,512,16,128]{5,4,1,0,2,3:T(8,128)(2,1)} %pad_maximum_fusion.1), calls=%async_computation | async-start | bytes 16777216 | tf_op jit(solution)/shard_map/all_to_all | solution.py:92
  261.2 9.8 %copy-start = (bf16[1024,1024]{1,0:T(8,128)(2,1)S(1)}, bf16[1024,1024]{1,0:T(8,128)(2,1)}, u32[]{:S(2)}) copy-start(bf16[1024,1024]{1,0:T(8,128)(2,1)} %get-tuple-element.46) | copy-start | bytes 6291460
  261.2 9.7 %copy-start.1 = (bf16[1024,1024]{1,0:T(8,128)(2,1)S(1)}, bf16[1024,1024]{1,0:T(8,128)(2,1)}, u32[]{:S(2)}) copy-start(bf16[1024,1024]{1,0:T(8,128)(2,1)} %get-tuple-element.47) | copy-start | bytes 6291460
where the time goes:
time: 438 us; the launch traced here: 429 us
  other arithmetic  158 us (36%)
  local copies, waits for them, and re-layouts  111 us (25%)
  waiting for transfers between devices  88.1 us (20%)
  blocking collectives  36.1 us (8%)
  matrix products  29.7 us (7%)
  starting transfers between devices  5.08 us (1%)
    all_to_all x1, waiting for transfers between devices, on_device(): lax.all_to_all(calibrated, 'feed', split_axis=3, concat_axis=5, tiled=True)  88.1 us
    another operation x3, other arithmetic, filterbank(): return jnp.stack([real_part, imag_part]).astype(jnp.bfloat16)  63.7 us
    add x1, other arithmetic, filterbank(): filtered + taps_window[tap_index][:, None] * frames_data[:, :, :, tap_ind...  56 us
    all_to_all x1, blocking collectives, on_device(): lax.all_to_all(jnp.where(live_slots, picked, jnp.zeros((), jnp.bfloat16))...  36.1 us
    unnamed x12, local copies, waits for them, and re-layouts  26.4 us
    gather x1, local copies, waits for them, and re-layouts, on_device(): jnp.take(detected.reshape(bins_local, coarse_local * fine_items, beam_tot...  18.4 us
    dot_general x1, matrix products, detect(): jnp.dot(rows_imag, lower_block, preferred_element_type=jnp.float32)  17.8 us
    unnamed x1, other arithmetic  12.1 us
  transfers between devices with their start and end apart: 1, of which 1 were waited for; matrix products, arithmetic and copies ran while one was open for 2% of the time, Pallas kernels for 0%

commit v1 on v0

v1 whole, which is shorter than its diff:
```python
import math

import numpy as np
import jax
import jax.numpy as jnp
from jax import lax
from jax.experimental import pallas as pl
from jax.experimental.pallas import tpu as pltpu
from jax.sharding import PartitionSpec as P

U = 16
TAPS = 4
TINT = 2
IB = 4


def window_taps_np():
    length = TAPS * U
    positions = np.arange(length, dtype=np.float64)
    offsets = (positions - (length - 1) / 2.0) / U
    hann_taper = 0.5 - 0.5 * np.cos(2.0 * math.pi * (positions + 0.5) / length)
    taps_window = np.sinc(offsets) * hann_taper
    taps_window = taps_window / np.sqrt(np.sum(taps_window * taps_window) / U)
    return taps_window.astype(np.float32)


def _cmul_const(re, im, wr, wi):
    if wi == 0.0:
        if wr == 1.0:
            return re, im
        if wr == -1.0:
            return -re, -im
        return re * wr, im * wr
    if wr == 0.0:
        if wi == 1.0:
            return -im, re
        if wi == -1.0:
            return im, -re
        return -im * wi, re * wi
    return re * wr - im * wi, im * wr + re * wi


def _fft(xs):
    count = len(xs)
    if count == 1:
        return xs
    even = _fft(xs[0::2])
    odd = _fft(xs[1::2])
    out = [None] * count
    for k in range(count // 2):
        angle = -2.0 * math.pi * k / count
        wr, wi = math.cos(angle), math.sin(angle)
        wr = float(np.round(wr)) if abs(wr - np.round(wr)) < 1e-12 else wr
        wi = float(np.round(wi)) if abs(wi - np.round(wi)) < 1e-12 else wi
        tr, ti = _cmul_const(odd[k][0], odd[k][1], wr, wi)
        er, ei = even[k]
        out[k] = (er + tr, ei + ti)
        out[k + count // 2] = (er - tr, ei - ti)
    return out


def _filter_kernel(main_ref, pre0_ref, pre1_ref, pre2_ref, hist_ref, gain_ref, out_ref, xs_ref, sc_ref):
    tdev = pl.program_id(1)
    taps = (window_taps_np() * np.float32(0.25)).astype(np.float32)
    rows_main = main_ref.shape[3]
    for r in range(2):
        xs_ref[r, pl.ds(48, rows_main), :] = main_ref[r, 0, 0].astype(jnp.float32)

    @pl.when(tdev == 0)
    def _():
        for r in range(2):
            xs_ref[r, pl.ds(0, 48), :] = hist_ref[r, 0, 0].astype(jnp.float32)

    @pl.when(tdev != 0)
    def _():
        for r in range(2):
            for m, pre in enumerate((pre0_ref, pre1_ref, pre2_ref)):
                xs_ref[r, pl.ds(16 * m, 16), :] = pre[r, 0, 0].astype(jnp.float32)

    g_re = gain_ref[0, 0]
    g_im = gain_ref[1, 0]
    frames = rows_main // (U * TINT)
    for j in range(TINT):
        filt = []
        for n in range(U):
            parts = []
            for r in range(2):
                acc = None
                for q in range(TAPS):
                    x = xs_ref[r, pl.ds((j + q) * U + n, frames, stride=U * TINT), :]
                    term = np.float32(taps[q * U + n]) * x
                    acc = term if acc is None else acc + term
                parts.append(acc)
            filt.append((parts[0], parts[1]))
        spec = _fft(filt)
        for k in range(U):
            s_re, s_im = spec[k]
            c_re = g_re * s_re - g_im * s_im
            c_im = g_re * s_im + g_im * s_re
            sc_ref[0, j, pl.ds(k, frames, stride=U), :] = c_re
            sc_ref[1, j, pl.ds(k, frames, stride=U), :] = c_im
    nb = out_ref.shape[1]
    for s in range(2):
        for j in range(TINT):
            val = sc_ref[s, j].astype(jnp.bfloat16)
            out_ref[0, :, s, 0, j] = val.reshape(nb, IB, U, 128)


def filterbank(voltages, history, gains):
    _, pols, _, samples, feeds = voltages.shape
    nblk = 8
    rows_main = samples // nblk
    frames_blk = rows_main // U
    nb = frames_blk // TINT // IB

    def pre_map(m):
        def index(p, t):
            return (0, p, 0, jnp.maximum(t * (rows_main // 16) - 3 + m, 0), 0)

        return index

    return pl.pallas_call(
        _filter_kernel,
        grid=(pols, nblk),
        in_specs=[
            pl.BlockSpec((2, 1, 1, rows_main, feeds), lambda p, t: (0, p, 0, t, 0)),
            pl.BlockSpec((2, 1, 1, 16, feeds), pre_map(0)),
            pl.BlockSpec((2, 1, 1, 16, feeds), pre_map(1)),
            pl.BlockSpec((2, 1, 1, 16, feeds), pre_map(2)),
            pl.BlockSpec((2, 1, 1, 48, feeds), lambda p, t: (0, p, 0, 0, 0)),
            pl.BlockSpec((2, 1, 1, feeds), lambda p, t: (0, p, 0, 0)),
        ],
        out_specs=pl.BlockSpec((1, nb, 2, 1, 2, IB, U, feeds), lambda p, t: (t, 0, 0, p, 0, 0, 0, 0)),
        out_shape=jax.ShapeDtypeStruct((nblk, nb, 2, pols, 2, IB, U, feeds), jnp.bfloat16),
        scratch_shapes=[
            pltpu.VMEM((2, rows_main + 48, feeds), jnp.float32),
            pltpu.VMEM((2, TINT, frames_blk // TINT * U, feeds), jnp.float32),
        ],
        cost_estimate=pl.CostEstimate(
            flops=2 * 2 * pols * samples * feeds * 20,
            bytes_accessed=2 * voltages.size * 2,
            transcendentals=0,
        ),
    )(voltages, voltages, voltages, voltages, history, gains)


def _beam_kernel(cal_ref, w_ref, sel_ref, out_ref):
    nsrc = cal_ref.shape[0]
    rows = 2 * 2 * IB * U
    halves = []
    for s in range(2):
        pieces = [cal_ref[d, 0, s].reshape(rows, 128) for d in range(nsrc)]
        halves.append(jnp.concatenate(pieces, axis=1))
    lhs = jnp.concatenate(halves, axis=0)
    prod_re = jnp.dot(lhs, w_ref[0, 0], preferred_element_type=jnp.float32)
    prod_im = jnp.dot(lhs, w_ref[1, 0], preferred_element_type=jnp.float32)
    real_part = prod_re[:rows] - prod_im[rows:]
    imag_part = prod_im[:rows] + prod_re[rows:]
    power = real_part * real_part + imag_part * imag_part
    quarter = rows // 2
    power = power[:quarter] + power[quarter:]
    eighth = quarter // 2
    power = power[:eighth] + power[eighth:]
    detected = (power * (1.0 / (4.0 * TINT))).astype(jnp.bfloat16)
    picked = jnp.dot(detected, sel_ref[...], preferred_element_type=jnp.float32).astype(jnp.bfloat16)
    nodes = out_ref.shape[1]
    for n in range(nodes):
        out_ref[:, n] = picked[:, n * 128 : (n + 1) * 128].reshape(IB, U, 128)


def beamform(cal, weights, select):
    nsrc, nb = cal.shape[0], cal.shape[1]
    feeds, beams = weights.shape[2], weights.shape[3]
    slots = select.shape[1]
    nodes = slots // 128
    return pl.pallas_call(
        _beam_kernel,
        grid=(nb,),
        in_specs=[
            pl.BlockSpec((nsrc, 1, 2, 2, 2, IB, U, 128), lambda i: (0, i, 0, 0, 0, 0, 0, 0)),
            pl.BlockSpec((2, 1, feeds, beams), lambda i: (0, 0, 0, 0)),
            pl.BlockSpec((beams, slots), lambda i: (0, 0)),
        ],
        out_specs=pl.BlockSpec((IB, nodes, U, 128), lambda i: (i, 0, 0, 0)),
        out_shape=jax.ShapeDtypeStruct((nb * IB, nodes, U, 128), jnp.bfloat16),
        cost_estimate=pl.CostEstimate(
            flops=2 * 2 * (4 * nb * IB * U * TINT) * feeds * beams + 2 * nb * IB * U * beams * slots,
            bytes_accessed=cal.size * 2 + weights.size * 2 + select.size * 2 + nb * IB * U * slots * 2,
            transcendentals=0,
        ),
        compiler_params=pltpu.CompilerParams(vmem_limit_bytes=60 * 1024 * 1024),
    )(cal, weights, select)


def on_device(voltages, history, gains, weights, beam_lists, beam_counts):
    capacity = beam_lists.shape[1]
    beams = weights.shape[3]
    flat_ids = beam_lists.reshape(-1)
    live_slots = (jnp.arange(capacity, dtype=jnp.int32)[None, :] < beam_counts[:, None]).reshape(-1)
    select = (
        (jnp.arange(beams, dtype=jnp.int32)[:, None] == flat_ids[None, :]) & live_slots[None, :]
    ).astype(jnp.bfloat16)
    calibrated = filterbank(voltages, history, gains)
    gathered = lax.all_to_all(calibrated, "feed", split_axis=0, concat_axis=0, tiled=True)
    picked = beamform(gathered, weights, select)
    exchanged = lax.all_to_all(picked, "chan", split_axis=1, concat_axis=1, tiled=True)
    bins, nodes, fine, width = exchanged.shape
    return exchanged.reshape(bins, nodes * fine, width)


def solution(mesh):
    in_specs = (
        P(None, None, "chan", None, "feed"),
        P(None, None, "chan", None, "feed"),
        P(None, None, "chan", "feed"),
        P(None, "chan", None, None),
        P(),
        P(),
    )
    out_specs = P("feed", None, "chan")
    return jax.shard_map(
        on_device, mesh=mesh, in_specs=in_specs, out_specs=out_specs, check_vma=False
    )
```

time: 438 us -> 231 us (0.53)
  the two profiles are of different devices: /device:TPU:0 before, /device:TPU:1 now
where the time goes in v1:
time: 231 us; the launch traced here: 230 us
  Pallas kernels  90.8 us (39%)
  waiting for transfers between devices  90.1 us (39%)
  blocking collectives  34.8 us (15%)
  starting transfers between devices  6.34 us (3%)
  local copies, waits for them, and re-layouts  4.04 us (2%)
  other arithmetic  3.72 us (2%)
    all_to_all x1, waiting for transfers between devices, on_device(): lax.all_to_all(calibrated, 'feed', split_axis=0, concat_axis=0, tiled=True)  90.1 us
    pallas_call x1, Pallas kernels, filterbank(): pl.pallas_call(_filter_kernel, grid=(pols, nblk), in_specs=[pl.BlockSpec(...  61.3 us
    all_to_all x1, blocking collectives, on_device(): lax.all_to_all(picked, 'chan', split_axis=1, concat_axis=1, tiled=True)  34.8 us
    pallas_call x1, Pallas kernels, beamform(): pl.pallas_call(_beam_kernel, grid=(nb,), in_specs=[pl.BlockSpec((nsrc, 1,...  29.5 us
    all_to_all x1, starting transfers between devices, on_device(): lax.all_to_all(calibrated, 'feed', split_axis=0, concat_axis=0, tiled=True)  6.34 us
  transfers between devices with their start and end apart: 1, of which 1 were waited for; matrix products, arithmetic and copies ran while one was open for 2% of the time, Pallas kernels for 0%

profile of v1, /device:TPU:1, one launch (start us, length us, event | category | flops | bytes accessed | tf_op | source)
XLA Modules:
  0.0 229.9 jit_solution(15458765733508747938)
XLA Ops:
  0.0 61.3 %shard_map.64 = bf16[8,8,2,2,2,4,16,128]{7,6,5,4,3,2,1,0:T(8,128)(2,1)} custom-call(bf16[2,2,1,8192,128]{4,3,2,1,0:T(8,128)(2,1)} %pre2_ref.1, bf16[2,2,1,8192,128]{4,3,2,1,0:T(8,128)(2,1)} %pre2_ref.1, bf16[2,2,1,8192,128]{4,3,2,1,0:T(8,128)(2,1)} %pre2_ref.1, bf16[2,2,1,8192,128]{4,3,2,1,0:T(8,128)(2,1)} %pre2_ref.1, bf16[2,2,1,48,128]{4,3,2,1,0:T(8,128)(2,1)} %hist_ref.1, ...), custom_call_target="tpu_custom_call" | custom-call | flops 167772160 | bytes 16777216 | tf_op jit(solution)/shard_map/pallas_call | solution.py:122
  61.3 0.0 copy-start.1
  61.3 0.0 copy-start
  61.3 6.3 %all-to-all-start = ((bf16[8,8,2,2,2,4,16,128]{7,6,5,4,3,2,1,0:T(8,128)(2,1)}), bf16[8,8,2,2,2,4,16,128]{7,6,5,4,3,2,1,0:T(8,128)(2,1)}, u32[]{:S(2)}, u32[]{:S(2)}) async-start(bf16[8,8,2,2,2,4,16,128]{7,6,5,4,3,2,1,0:T(8,128)(2,1)} %shard_map.64), calls=%async_computation | async-start | bytes 16777216 | tf_op jit(solution)/shard_map/all_to_all | solution.py:204
  67.6 0.0 copy-done.1
  67.6 0.1 fusion.2
  67.7 0.0 copy-done
  67.7 3.7 %fusion.1.sel_ref = bf16[1024,2048]{1,0:T(8,128)(2,1)} fusion(s32[2048]{0:T(1024)S(1)} %bitcast.4, pred[2048]{0:T(1024)(128)(4,1)S(1)} %fusion.2), kind=kLoop, calls=%fused_computation.2 | loop fusion | flops 6291456 | bytes 4204544 | tf_op jit(solution)/shard_map/convert_element_type | solution.py:202
  71.4 90.1 %all-to-all-done.cal_ref = bf16[8,8,2,2,2,4,16,128]{7,6,5,4,3,2,1,0:T(8,128)(2,1)} async-done(((bf16[8,8,2,2,2,4,16,128]{7,6,5,4,3,2,1,0:T(8,128)(2,1)}), bf16[8,8,2,2,2,4,16,128]{7,6,5,4,3,2,1,0:T(8,128)(2,1)}, u32[]{:S(2)}, u32[]{:S(2)}) %all-to-all-start) | async-done | bytes 8388640 | tf_op jit(solution)/shard_map/all_to_all | solution.py:204
  161.5 29.5 %shard_map.65 = bf16[32,16,16,128]{3,2,1,0:T(8,128)(2,1)} custom-call(bf16[8,8,2,2,2,4,16,128]{7,6,5,4,3,2,1,0:T(8,128)(2,1)} %all-to-all-done.cal_ref, bf16[2,1,1024,1024]{3,2,1,0:T(8,128)(2,1)} %w_ref.1, bf16[1024,2048]{1,0:T(8,128)(2,1)} %fusion.1.sel_ref), custom_call_target="tpu_custom_call" | custom-call | flops 19327352832 | bytes 18874368 | tf_op jit(solution)/shard_map/pallas_call | solution.py:176
  191.0 2.1 copy.8
  193.1 34.8 %all_to_all.10 = bf16[32,16,16,128]{3,2,0,1:T(8,128)(2,1)S(1)} all-to-all(bf16[32,16,16,128]{3,2,0,1:T(8,128)(2,1)S(1)} %copy.8), channel_id=1, replica_groups=mesh['feed'=8,'chan'=16] {'chan'}, dimensions={1} | all-to-all | bytes 4194304 | tf_op jit(solution)/shard_map/all_to_all | solution.py:206
  228.0 1.9 copy.9
Async XLA Ops:
  61.3 6.3 %copy-start.1 = (s32[16]{0:T(128)S(1)}, s32[16]{0:T(128)}, u32[]{:S(2)}) copy-start(s32[16]{0:T(128)} %param.11) | copy-start | bytes 196
  61.3 6.4 %copy-start = (s32[16,128]{1,0:T(8,128)S(1)}, s32[16,128]{1,0:T(8,128)}, u32[]{:S(2)}) copy-start(s32[16,128]{1,0:T(8,128)} %param.10) | copy-start | bytes 24580
  61.3 100.2 %all-to-all-start = ((bf16[8,8,2,2,2,4,16,128]{7,6,5,4,3,2,1,0:T(8,128)(2,1)}), bf16[8,8,2,2,2,4,16,128]{7,6,5,4,3,2,1,0:T(8,128)(2,1)}, u32[]{:S(2)}, u32[]{:S(2)}) async-start(bf16[8,8,2,2,2,4,16,128]{7,6,5,4,3,2,1,0:T(8,128)(2,1)} %shard_map.64), calls=%async_computation | async-start | bytes 16777216 | tf_op jit(solution)/shard_map/all_to_all | solution.py:204

commit v2 on v1

--- a/solution.py
+++ b/solution.py
@@ -12,6 +12,7 @@
 TAPS = 4
 TINT = 2
 IB = 4
+CHUNKS = 4
 
 
 def window_taps_np():
@@ -59,89 +60,101 @@
     return out
 
 
-def _filter_kernel(main_ref, pre0_ref, pre1_ref, pre2_ref, hist_ref, gain_ref, out_ref, xs_ref, sc_ref):
-    tdev = pl.program_id(1)
+def _filter_kernel(chunk, main_ref, pre0_ref, pre1_ref, pre2_ref, hist_ref, gain_ref, out_ref, xs_ref, sc_ref):
     taps = (window_taps_np() * np.float32(0.25)).astype(np.float32)
-    rows_main = main_ref.shape[3]
-    for r in range(2):
-        xs_ref[r, pl.ds(48, rows_main), :] = main_ref[r, 0, 0].astype(jnp.float32)
-
-    @pl.when(tdev == 0)
-    def _():
-        for r in range(2):
-            xs_ref[r, pl.ds(0, 48), :] = hist_ref[r, 0, 0].astype(jnp.float32)
-
-    @pl.when(tdev != 0)
-    def _():
-        for r in range(2):
-            for m, pre in enumerate((pre0_ref, pre1_ref, pre2_ref)):
-                xs_ref[r, pl.ds(16 * m, 16), :] = pre[r, 0, 0].astype(jnp.float32)
-
+    rows_main = main_ref.shape[4]
+    frames = rows_main // (U * TINT)
+    nblk = main_ref.shape[2]
+    nb = out_ref.shape[1]
     g_re = gain_ref[0, 0]
     g_im = gain_ref[1, 0]
-    frames = rows_main // (U * TINT)
-    for j in range(TINT):
-        filt = []
-        for n in range(U):
-            parts = []
+
+    def block(tdev, carry):
+        for r in range(2):
+            xs_ref[r, pl.ds(48, rows_main), :] = main_ref[r, 0, tdev, 0].astype(jnp.float32)
+        if chunk == 0:
+            prev = jnp.maximum(tdev - 1, 0)
             for r in range(2):
-                acc = None
-                for q in range(TAPS):
-                    x = xs_ref[r, pl.ds((j + q) * U + n, frames, stride=U * TINT), :]
-                    term = np.float32(taps[q * U + n]) * x
-                    acc = term if acc is None else acc + term
-                parts.append(acc)
-            filt.append((parts[0], parts[1]))
-        spec = _fft(filt)
-        for k in range(U):
-            s_re, s_im = spec[k]
-            c_re = g_re * s_re - g_im * s_im
-            c_im = g_re * s_im + g_im * s_re
-            sc_ref[0, j, pl.ds(k, frames, stride=U), :] = c_re
-            sc_ref[1, j, pl.ds(k, frames, stride=U), :] = c_im
-    nb = out_ref.shape[1]
-    for s in range(2):
+                for m, pre in enumerate((pre0_ref, pre1_ref, pre2_ref)):
+                    xs_ref[r, pl.ds(16 * m, 16), :] = pre[r, 0, prev, 0].astype(jnp.float32)
+
+            @pl.when(tdev == 0)
+            def _():
+                for r in range(2):
+                    xs_ref[r, pl.ds(0, 48), :] = hist_ref[r, 0, 0].astype(jnp.float32)
+        else:
+            for r in range(2):
+                for m, pre in enumerate((pre0_ref, pre1_ref, pre2_ref)):
+                    xs_ref[r, pl.ds(16 * m, 16), :] = pre[r, 0, tdev, 0].astype(jnp.float32)
+
         for j in range(TINT):
-            val = sc_ref[s, j].astype(jnp.bfloat16)
-            out_ref[0, :, s, 0, j] = val.reshape(nb, IB, U, 128)
-
-
-def filterbank(voltages, history, gains):
+            filt = []
+            for n in range(U):
+                parts = []
+                for r in range(2):
+                    acc = None
+                    for q in range(TAPS):
+                        x = xs_ref[r, pl.ds((j + q) * U + n, frames, stride=U * TINT), :]
+                        term = np.float32(taps[q * U + n]) * x
+                        acc = term if acc is None else acc + term
+                    parts.append(acc)
+                filt.append((parts[0], parts[1]))
+            spec = _fft(filt)
+            for k in range(U):
+                s_re, s_im = spec[k]
+                c_re = g_re * s_re - g_im * s_im
+                c_im = g_re * s_im + g_im * s_re
+                sc_ref[0, j, pl.ds(k, frames, stride=U), :] = c_re
+                sc_ref[1, j, pl.ds(k, frames, stride=U), :] = c_im
+        for s in range(2):
+            for j in range(TINT):
+                val = sc_ref[s, j].astype(jnp.bfloat16)
+                out_ref[tdev, :, s, 0, j] = val.reshape(nb, IB, U, 128)
+        return carry
+
+    lax.fori_loop(0, nblk, block, 0)
+
+
+def filterbank(voltages, history, gains, chunk, chunks):
     _, pols, _, samples, feeds = voltages.shape
     nblk = 8
-    rows_main = samples // nblk
-    frames_blk = rows_main // U
-    nb = frames_blk // TINT // IB
+    rows_blk = samples // nblk
+    rows_main = rows_blk // chunks
+    frames = rows_main // U
+    nb = frames // TINT // IB
+    main = voltages.reshape(2, pols, nblk, chunks, rows_main, feeds)
+    units = voltages.reshape(2, pols, nblk, rows_blk // 16, 16, feeds)
+    if chunk == 0:
+        first = rows_blk // 16 - 3
+    else:
+        first = chunk * rows_main // 16 - 3
 
     def pre_map(m):
-        def index(p, t):
-            return (0, p, 0, jnp.maximum(t * (rows_main // 16) - 3 + m, 0), 0)
-
-        return index
+        return lambda p: (0, p, 0, first + m, 0, 0)
 
     return pl.pallas_call(
-        _filter_kernel,
-        grid=(pols, nblk),
+        lambda *refs: _filter_kernel(chunk, *refs),
+        grid=(pols,),
         in_specs=[
-            pl.BlockSpec((2, 1, 1, rows_main, feeds), lambda p, t: (0, p, 0, t, 0)),
-            pl.BlockSpec((2, 1, 1, 16, feeds), pre_map(0)),
-            pl.BlockSpec((2, 1, 1, 16, feeds), pre_map(1)),
-            pl.BlockSpec((2, 1, 1, 16, feeds), pre_map(2)),
-            pl.BlockSpec((2, 1, 1, 48, feeds), lambda p, t: (0, p, 0, 0, 0)),
-            pl.BlockSpec((2, 1, 1, feeds), lambda p, t: (0, p, 0, 0)),
+            pl.BlockSpec((2, 1, nblk, 1, rows_main, feeds), lambda p: (0, p, 0, chunk, 0, 0)),
+            pl.BlockSpec((2, 1, nblk, 1, 16, feeds), pre_map(0)),
+            pl.BlockSpec((2, 1, nblk, 1, 16, feeds), pre_map(1)),
+            pl.BlockSpec((2, 1, nblk, 1, 16, feeds), pre_map(2)),
+            pl.BlockSpec((2, 1, 1, 48, feeds), lambda p: (0, p, 0, 0, 0)),
+            pl.BlockSpec((2, 1, 1, feeds), lambda p: (0, p, 0, 0)),
         ],
-        out_specs=pl.BlockSpec((1, nb, 2, 1, 2, IB, U, feeds), lambda p, t: (t, 0, 0, p, 0, 0, 0, 0)),
+        out_specs=pl.BlockSpec((nblk, nb, 2, 1, 2, IB, U, feeds), lambda p: (0, 0, 0, p, 0, 0, 0, 0)),
         out_shape=jax.ShapeDtypeStruct((nblk, nb, 2, pols, 2, IB, U, feeds), jnp.bfloat16),
         scratch_shapes=[
             pltpu.VMEM((2, rows_main + 48, feeds), jnp.float32),
-            pltpu.VMEM((2, TINT, frames_blk // TINT * U, feeds), jnp.float32),
+            pltpu.VMEM((2, TINT, frames // TINT * U, feeds), jnp.float32),
         ],
         cost_estimate=pl.CostEstimate(
-            flops=2 * 2 * pols * samples * feeds * 20,
-            bytes_accessed=2 * voltages.size * 2,
+            flops=2 * 2 * pols * samples * feeds * 20 // chunks,
+            bytes_accessed=2 * voltages.size * 2 // chunks,
             transcendentals=0,
         ),
-    )(voltages, voltages, voltages, voltages, history, gains)
+    )(main, units, units, units, history, gains)
 
 
 def _beam_kernel(cal_ref, w_ref, sel_ref, out_ref):
@@ -200,10 +213,13 @@
     select = (
         (jnp.arange(beams, dtype=jnp.int32)[:, None] == flat_ids[None, :]) & live_slots[None, :]
     ).astype(jnp.bfloat16)
-    calibrated = filterbank(voltages, history, gains)
-    gathered = lax.all_to_all(calibrated, "feed", split_axis=0, concat_axis=0, tiled=True)
-    picked = beamform(gathered, weights, select)
-    exchanged = lax.all_to_all(picked, "chan", split_axis=1, concat_axis=1, tiled=True)
+    outs = []
+    for chunk in range(CHUNKS):
+        calibrated = filterbank(voltages, history, gains, chunk, CHUNKS)
+        gathered = lax.all_to_all(calibrated, "feed", split_axis=0, concat_axis=0, tiled=True)
+        picked = beamform(gathered, weights, select)
+        outs.append(lax.all_to_all(picked, "chan", split_axis=1, concat_axis=1, tiled=True))
+    exchanged = jnp.concatenate(outs, axis=0)
     bins, nodes, fine, width = exchanged.shape
     return exchanged.reshape(bins, nodes * fine, width)
 

time: 231 us -> 222 us (0.961)
  waiting for transfers between devices: 90.1 us -> 45.2 us
  starting transfers between devices: 6.34 us -> 40 us
  blocking collectives: 34.8 us -> 15.5 us
  Pallas kernels: 90.8 us -> 101 us
  local copies, waits for them, and re-layouts: 4.04 us -> 12.8 us
    all_to_all x1 -> x4, waiting for transfers between devices: 90.1 us -> 45.2 us  [on_device(): lax.all_to_all(calibrated, 'feed', split_axis=0, concat_axis=0, tiled=True)]
    all_to_all x0 -> x3, starting transfers between devices: none -> 20.9 us  [on_device(): lax.all_to_all(picked, 'chan', split_axis=1, concat_axis=1, tiled=True)]
    all_to_all x1, blocking collectives: 34.8 us -> 15.5 us  [on_device(): lax.all_to_all(picked, 'chan', split_axis=1, concat_axis=1, tiled=True)]
    pallas_call x1 -> x4, Pallas kernels: 29.5 us -> 42.9 us  [beamform(): pl.pallas_call(_beam_kernel, grid=(nb,), in_specs=[pl.BlockSpec((nsrc, 1,...]
    all_to_all x1 -> x4, starting transfers between devices: 6.34 us -> 19.1 us  [on_device(): lax.all_to_all(calibrated, 'feed', split_axis=0, concat_axis=0, tiled=True)]
    pallas_call x1 -> x4, local copies, waits for them, and re-layouts: 2.13 us -> 6.8 us  [beamform(): pl.pallas_call(_beam_kernel, grid=(nb,), in_specs=[pl.BlockSpec((nsrc, 1,...]
    unnamed x4 -> x12, local copies, waits for them, and re-layouts: 0.01 us -> 4.12 us
    pallas_call x1 -> x4, Pallas kernels: 61.3 us -> 58.5 us  [filterbank(): pl.pallas_call(lambda *refs: _filter_kernel(chunk, *refs), grid=(pols,),...]
  transfers between devices with their start and end apart: 1 -> 7, of which waited for: 1 -> 4; matrix products, arithmetic and copies ran while one was open for 2% -> 5% of each run, Pallas kernels for 0% -> 40%
where the time goes in v2:
time: 222 us; the launch traced here: 219 us
  Pallas kernels  101 us (45%)
  waiting for transfers between devices  45.2 us (20%)
  starting transfers between devices  40 us (18%)
  blocking collectives  15.5 us (7%)
  local copies, waits for them, and re-layouts  12.8 us (6%)
  other arithmetic  3.99 us (2%)
    pallas_call x4, Pallas kernels, filterbank(): pl.pallas_call(lambda *refs: _filter_kernel(chunk, *refs), grid=(pols,),...  58.5 us
    all_to_all x4, waiting for transfers between devices, on_device(): lax.all_to_all(calibrated, 'feed', split_axis=0, concat_axis=0, tiled=True)  45.2 us
    pallas_call x4, Pallas kernels, beamform(): pl.pallas_call(_beam_kernel, grid=(nb,), in_specs=[pl.BlockSpec((nsrc, 1,...  42.9 us
    all_to_all x3, starting transfers between devices, on_device(): lax.all_to_all(picked, 'chan', split_axis=1, concat_axis=1, tiled=True)  20.9 us
    all_to_all x4, starting transfers between devices, on_device(): lax.all_to_all(calibrated, 'feed', split_axis=0, concat_axis=0, tiled=True)  19.1 us
    all_to_all x1, blocking collectives, on_device(): lax.all_to_all(picked, 'chan', split_axis=1, concat_axis=1, tiled=True)  15.5 us
    pallas_call x4, local copies, waits for them, and re-layouts, beamform(): pl.pallas_call(_beam_kernel, grid=(nb,), in_specs=[pl.BlockSpec((nsrc, 1,...  6.8 us
  transfers between devices with their start and end apart: 7, of which 4 were waited for; matrix products, arithmetic and copies ran while one was open for 5% of the time, Pallas kernels for 40%

profile of v2, /device:TPU:1, one launch (start us, length us, event | category | flops | bytes accessed | tf_op | source)
XLA Modules:
  0.0 218.9 jit_solution(3473530605760148896)
XLA Ops:
  0.0 14.7 %shard_map.64 = bf16[8,2,2,2,2,4,16,128]{7,6,5,4,3,2,1,0:T(8,128)(2,1)} custom-call(bf16[2,2,8,4,256,128]{5,4,3,2,1,0:T(8,128)(2,1)} %bitcast.6, bf16[2,2,8,64,16,128]{5,4,3,2,1,0:T(8,128)(2,1)} %bitcast.7, bf16[2,2,8,64,16,128]{5,4,3,2,1,0:T(8,128)(2,1)} %bitcast.8, bf16[2,2,8,64,16,128]{5,4,3,2,1,0:T(8,128)(2,1)} %bitcast.9, ...), custom_call_target="tpu_custom_call" | custom-call | flops 41943040 | bytes 4194304 | tf_op jit(solution)/shard_map/pallas_call | solution.py:135
  14.7 6.0 %all-to-all-start = ((bf16[8,2,2,2,2,4,16,128]{7,6,5,4,3,2,1,0:T(8,128)(2,1)}), bf16[8,2,2,2,2,4,16,128]{7,6,5,4,3,2,1,0:T(8,128)(2,1)S(1)}, u32[]{:S(2)}, u32[]{:S(2)}) async-start(bf16[8,2,2,2,2,4,16,128]{7,6,5,4,3,2,1,0:T(8,128)(2,1)} %shard_map.64), calls=%async_computation | async-start | bytes 4194304 | tf_op jit(solution)/shard_map/all_to_all | solution.py:219
  20.6 14.6 %shard_map.66 = bf16[8,2,2,2,2,4,16,128]{7,6,5,4,3,2,1,0:T(8,128)(2,1)} custom-call(bf16[2,2,8,4,256,128]{5,4,3,2,1,0:T(8,128)(2,1)} %bitcast.10, bf16[2,2,8,64,16,128]{5,4,3,2,1,0:T(8,128)(2,1)} %bitcast.11, bf16[2,2,8,64,16,128]{5,4,3,2,1,0:T(8,128)(2,1)} %bitcast.12, bf16[2,2,8,64,16,128]{5,4,3,2,1,0:T(8,128)(2,1)} %bitcast.13, ...), custom_call_target="tpu_custom_call" | custom-call | flops 41943040 | bytes 4194304 | tf_op jit(solution)/shard_map/pallas_call | solution.py:135
  35.2 11.8 %all-to-all-done.cal_ref = bf16[8,2,2,2,2,4,16,128]{7,6,5,4,3,2,1,0:T(8,128)(2,1)S(1)} async-done(((bf16[8,2,2,2,2,4,16,128]{7,6,5,4,3,2,1,0:T(8,128)(2,1)}), bf16[8,2,2,2,2,4,16,128]{7,6,5,4,3,2,1,0:T(8,128)(2,1)S(1)}, u32[]{:S(2)}, u32[]{:S(2)}) %all-to-all-start) | async-done | bytes 2097184 | tf_op jit(solution)/shard_map/all_to_all | solution.py:219
  47.0 0.0 copy-start.3
  47.0 1.4 copy-done.3
  48.4 4.4 %all-to-all-start.2 = ((bf16[8,2,2,2,2,4,16,128]{7,6,5,4,3,2,1,0:T(8,128)(2,1)}), bf16[8,2,2,2,2,4,16,128]{7,6,5,4,3,2,1,0:T(8,128)(2,1)S(1)}, u32[]{:S(2)}, u32[]{:S(2)}) async-start(bf16[8,2,2,2,2,4,16,128]{7,6,5,4,3,2,1,0:T(8,128)(2,1)} %shard_map.66), calls=%async_computation.2 | async-start | bytes 4194304 | tf_op jit(solution)/shard_map/all_to_all | solution.py:219
  52.7 14.6 %shard_map.68 = bf16[8,2,2,2,2,4,16,128]{7,6,5,4,3,2,1,0:T(8,128)(2,1)} custom-call(bf16[2,2,8,4,256,128]{5,4,3,2,1,0:T(8,128)(2,1)} %bitcast.14, bf16[2,2,8,64,16,128]{5,4,3,2,1,0:T(8,128)(2,1)} %bitcast.15, bf16[2,2,8,64,16,128]{5,4,3,2,1,0:T(8,128)(2,1)} %bitcast.16, bf16[2,2,8,64,16,128]{5,4,3,2,1,0:T(8,128)(2,1)} %bitcast.17, ...), custom_call_target="tpu_custom_call" | custom-call | flops 41943040 | bytes 4194304 | tf_op jit(solution)/shard_map/pallas_call | solution.py:135
  67.4 11.7 %all-to-all-done.2.cal_ref = bf16[8,2,2,2,2,4,16,128]{7,6,5,4,3,2,1,0:T(8,128)(2,1)S(1)} async-done(((bf16[8,2,2,2,2,4,16,128]{7,6,5,4,3,2,1,0:T(8,128)(2,1)}), bf16[8,2,2,2,2,4,16,128]{7,6,5,4,3,2,1,0:T(8,128)(2,1)S(1)}, u32[]{:S(2)}, u32[]{:S(2)}) %all-to-all-start.2) | async-done | bytes 2097184 | tf_op jit(solution)/shard_map/all_to_all | solution.py:219
  79.1 0.0 copy-start.2
  79.1 1.4 copy-done.2
  80.5 4.4 %all-to-all-start.4 = ((bf16[8,2,2,2,2,4,16,128]{7,6,5,4,3,2,1,0:T(8,128)(2,1)}), bf16[8,2,2,2,2,4,16,128]{7,6,5,4,3,2,1,0:T(8,128)(2,1)S(1)}, u32[]{:S(2)}, u32[]{:S(2)}) async-start(bf16[8,2,2,2,2,4,16,128]{7,6,5,4,3,2,1,0:T(8,128)(2,1)} %shard_map.68), calls=%async_computation.4 | async-start | bytes 4194304 | tf_op jit(solution)/shard_map/all_to_all | solution.py:219
  84.8 14.6 %shard_map.70 = bf16[8,2,2,2,2,4,16,128]{7,6,5,4,3,2,1,0:T(8,128)(2,1)} custom-call(bf16[2,2,8,4,256,128]{5,4,3,2,1,0:T(8,128)(2,1)} %bitcast.18, bf16[2,2,8,64,16,128]{5,4,3,2,1,0:T(8,128)(2,1)} %bitcast.19, bf16[2,2,8,64,16,128]{5,4,3,2,1,0:T(8,128)(2,1)} %bitcast.20, bf16[2,2,8,64,16,128]{5,4,3,2,1,0:T(8,128)(2,1)} %bitcast.21, ...), custom_call_target="tpu_custom_call" | custom-call | flops 41943040 | bytes 4194304 | tf_op jit(solution)/shard_map/pallas_call | solution.py:135
  99.4 0.0 copy-start.5
  99.4 0.0 copy-start.4
  99.4 11.8 %all-to-all-done.4.cal_ref = bf16[8,2,2,2,2,4,16,128]{7,6,5,4,3,2,1,0:T(8,128)(2,1)S(1)} async-done(((bf16[8,2,2,2,2,4,16,128]{7,6,5,4,3,2,1,0:T(8,128)(2,1)}), bf16[8,2,2,2,2,4,16,128]{7,6,5,4,3,2,1,0:T(8,128)(2,1)S(1)}, u32[]{:S(2)}, u32[]{:S(2)}) %all-to-all-start.4) | async-done | bytes 2097184 | tf_op jit(solution)/shard_map/all_to_all | solution.py:219
  111.2 0.0 copy-start.1
  111.2 1.4 copy-done.1
  112.6 4.4 %all-to-all-start.6 = ((bf16[8,2,2,2,2,4,16,128]{7,6,5,4,3,2,1,0:T(8,128)(2,1)}), bf16[8,2,2,2,2,4,16,128]{7,6,5,4,3,2,1,0:T(8,128)(2,1)S(1)}, u32[]{:S(2)}, u32[]{:S(2)}) async-start(bf16[8,2,2,2,2,4,16,128]{7,6,5,4,3,2,1,0:T(8,128)(2,1)} %shard_map.70), calls=%async_computation.6 | async-start | bytes 4194304 | tf_op jit(solution)/shard_map/all_to_all | solution.py:219
  116.9 0.0 copy-done.5
  116.9 0.1 fusion.2
  117.0 0.0 copy-done.4
  117.0 3.7 %fusion.1.sel_ref = bf16[1024,2048]{1,0:T(8,128)(2,1)} fusion(s32[2048]{0:T(1024)S(1)} %bitcast.22, pred[2048]{0:T(1024)(128)(4,1)S(1)} %fusion.2), kind=kLoop, calls=%fused_computation.2 | loop fusion | flops 6291456 | bytes 4204544 | tf_op jit(solution)/shard_map/convert_element_type | solution.py:215
  120.7 10.7 %shard_map.65 = bf16[8,16,16,128]{3,2,1,0:T(8,128)(2,1)} custom-call(bf16[8,2,2,2,2,4,16,128]{7,6,5,4,3,2,1,0:T(8,128)(2,1)} %copy-done.3, bf16[2,1,1024,1024]{3,2,1,0:T(8,128)(2,1)} %w_ref.7, bf16[1024,2048]{1,0:T(8,128)(2,1)} %fusion.1.sel_ref), custom_call_target="tpu_custom_call" | custom-call | flops 4831838208 | bytes 11010048 | tf_op jit(solution)/shard_map/pallas_call | solution.py:189
  131.4 1.9 copy.11
  133.3 10.0 %all-to-all-done.6.cal_ref = bf16[8,2,2,2,2,4,16,128]{7,6,5,4,3,2,1,0:T(8,128)(2,1)S(1)} async-done(((bf16[8,2,2,2,2,4,16,128]{7,6,5,4,3,2,1,0:T(8,128)(2,1)}), bf16[8,2,2,2,2,4,16,128]{7,6,5,4,3,2,1,0:T(8,128)(2,1)S(1)}, u32[]{:S(2)}, u32[]{:S(2)}) %all-to-all-start.6) | async-done | bytes 2097184 | tf_op jit(solution)/shard_map/all_to_all | solution.py:219
  143.3 0.0 copy-start
  143.3 7.6 %all-to-all-start.1 = ((bf16[8,16,16,128]{3,2,0,1:T(8,128)(2,1)}), bf16[8,16,16,128]{3,2,0,1:T(8,128)(2,1)S(1)}, u32[]{:S(2)}, u32[]{:S(2)}) async-start(bf16[8,16,16,128]{3,2,0,1:T(8,128)(2,1)} %copy.11), calls=%async_computation.1 | async-start | bytes 1048576 | tf_op jit(solution)/shard_map/all_to_all | solution.py:221
  150.9 10.7 %shard_map.67 = bf16[8,16,16,128]{3,2,1,0:T(8,128)(2,1)} custom-call(bf16[8,2,2,2,2,4,16,128]{7,6,5,4,3,2,1,0:T(8,128)(2,1)} %copy-done.2, bf16[2,1,1024,1024]{3,2,1,0:T(8,128)(2,1)} %w_ref.7, bf16[1024,2048]{1,0:T(8,128)(2,1)} %fusion.1.sel_ref), custom_call_target="tpu_custom_call" | custom-call | flops 4831838208 | bytes 11010048 | tf_op jit(solution)/shard_map/pallas_call | solution.py:189
  161.6 0.0 copy-done
  161.6 1.9 copy.12
  163.5 0.0 all-to-all-done.1
  163.5 6.7 %all-to-all-start.3 = ((bf16[8,16,16,128]{3,2,0,1:T(8,128)(2,1)}), bf16[8,16,16,128]{3,2,0,1:T(8,128)(2,1)S(1)}, u32[]{:S(2)}, u32[]{:S(2)}) async-start(bf16[8,16,16,128]{3,2,0,1:T(8,128)(2,1)} %copy.12), calls=%async_computation.3 | async-start | bytes 1048576 | tf_op jit(solution)/shard_map/all_to_all | solution.py:221
  170.2 10.7 %shard_map.69 = bf16[8,16,16,128]{3,2,1,0:T(8,128)(2,1)} custom-call(bf16[8,2,2,2,2,4,16,128]{7,6,5,4,3,2,1,0:T(8,128)(2,1)} %copy-done.1, bf16[2,1,1024,1024]{3,2,1,0:T(8,128)(2,1)} %w_ref.7, bf16[1024,2048]{1,0:T(8,128)(2,1)} %fusion.1.sel_ref), custom_call_target="tpu_custom_call" | custom-call | flops 4831838208 | bytes 11010048 | tf_op jit(solution)/shard_map/pallas_call | solution.py:189
  180.9 1.9 copy.13
  182.8 0.0 all-to-all-done.3
  182.8 6.6 %all-to-all-start.5 = ((bf16[8,16,16,128]{3,2,0,1:T(8,128)(2,1)}), bf16[8,16,16,128]{3,2,0,1:T(8,128)(2,1)S(1)}, u32[]{:S(2)}, u32[]{:S(2)}) async-start(bf16[8,16,16,128]{3,2,0,1:T(8,128)(2,1)} %copy.13), calls=%async_computation.5 | async-start | bytes 1048576 | tf_op jit(solution)/shard_map/all_to_all | solution.py:221
  189.4 10.7 %shard_map.71 = bf16[8,16,16,128]{3,2,1,0:T(8,128)(2,1)} custom-call(bf16[8,2,2,2,2,4,16,128]{7,6,5,4,3,2,1,0:T(8,128)(2,1)} %copy-done, bf16[2,1,1024,1024]{3,2,1,0:T(8,128)(2,1)} %w_ref.7, bf16[1024,2048]{1,0:T(8,128)(2,1)} %fusion.1.sel_ref), custom_call_target="tpu_custom_call" | custom-call | flops 4831838208 | bytes 11010048 | tf_op jit(solution)/shard_map/pallas_call | solution.py:189
  200.2 1.1 copy.14
  201.2 0.0 all-to-all-done.5
  201.3 15.5 %all_to_all.40 = bf16[8,16,16,128]{3,2,0,1:T(8,128)(2,1)S(1)} all-to-all(bf16[8,16,16,128]{3,2,0,1:T(8,128)(2,1)S(1)} %copy.14), channel_id=1, replica_groups=mesh['feed'=8,'chan'=16] {'chan'}, dimensions={1} | all-to-all | bytes 1048576 | tf_op jit(solution)/shard_map/all_to_all | solution.py:221
  216.7 0.3 pad_maximum_fusion
  217.0 1.9 copy.19
Async XLA Ops:
  14.7 32.3 %all-to-all-start = ((bf16[8,2,2,2,2,4,16,128]{7,6,5,4,3,2,1,0:T(8,128)(2,1)}), bf16[8,2,2,2,2,4,16,128]{7,6,5,4,3,2,1,0:T(8,128)(2,1)S(1)}, u32[]{:S(2)}, u32[]{:S(2)}) async-start(bf16[8,2,2,2,2,4,16,128]{7,6,5,4,3,2,1,0:T(8,128)(2,1)} %shard_map.64), calls=%async_computation | async-start | bytes 4194304 | tf_op jit(solution)/shard_map/all_to_all | solution.py:219
  47.0 1.4 copy-start.3
  48.4 30.7 %all-to-all-start.2 = ((bf16[8,2,2,2,2,4,16,128]{7,6,5,4,3,2,1,0:T(8,128)(2,1)}), bf16[8,2,2,2,2,4,16,128]{7,6,5,4,3,2,1,0:T(8,128)(2,1)S(1)}, u32[]{:S(2)}, u32[]{:S(2)}) async-start(bf16[8,2,2,2,2,4,16,128]{7,6,5,4,3,2,1,0:T(8,128)(2,1)} %shard_map.66), calls=%async_computation.2 | async-start | bytes 4194304 | tf_op jit(solution)/shard_map/all_to_all | solution.py:219
  79.1 1.4 copy-start.2
  80.5 30.7 %all-to-all-start.4 = ((bf16[8,2,2,2,2,4,16,128]{7,6,5,4,3,2,1,0:T(8,128)(2,1)}), bf16[8,2,2,2,2,4,16,128]{7,6,5,4,3,2,1,0:T(8,128)(2,1)S(1)}, u32[]{:S(2)}, u32[]{:S(2)}) async-start(bf16[8,2,2,2,2,4,16,128]{7,6,5,4,3,2,1,0:T(8,128)(2,1)} %shard_map.68), calls=%async_computation.4 | async-start | bytes 4194304 | tf_op jit(solution)/shard_map/all_to_all | solution.py:219
  99.4 17.5 %copy-start.5 = (s32[16]{0:T(128)S(1)}, s32[16]{0:T(128)}, u32[]{:S(2)}) copy-start(s32[16]{0:T(128)} %param.11) | copy-start | bytes 196
  99.4 17.6 %copy-start.4 = (s32[16,128]{1,0:T(8,128)S(1)}, s32[16,128]{1,0:T(8,128)}, u32[]{:S(2)}) copy-start(s32[16,128]{1,0:T(8,128)} %param.10) | copy-start | bytes 24580
  111.2 1.4 copy-start.1
  112.6 30.7 %all-to-all-start.6 = ((bf16[8,2,2,2,2,4,16,128]{7,6,5,4,3,2,1,0:T(8,128)(2,1)}), bf16[8,2,2,2,2,4,16,128]{7,6,5,4,3,2,1,0:T(8,128)(2,1)S(1)}, u32[]{:S(2)}, u32[]{:S(2)}) async-start(bf16[8,2,2,2,2,4,16,128]{7,6,5,4,3,2,1,0:T(8,128)(2,1)} %shard_map.70), calls=%async_computation.6 | async-start | bytes 4194304 | tf_op jit(solution)/shard_map/all_to_all | solution.py:219
  143.3 18.3 %copy-start = (bf16[8,2,2,2,2,4,16,128]{7,6,5,4,3,2,1,0:T(8,128)(2,1)}, bf16[8,2,2,2,2,4,16,128]{7,6,5,4,3,2,1,0:T(8,128)(2,1)S(1)}, u32[]{:S(2)}) copy-start(bf16[8,2,2,2,2,4,16,128]{7,6,5,4,3,2,1,0:T(8,128)(2,1)S(1)} %all-to-all-done.6.cal_ref) | copy-start | bytes 6291460
  143.3 20.2 %all-to-all-start.1 = ((bf16[8,16,16,128]{3,2,0,1:T(8,128)(2,1)}), bf16[8,16,16,128]{3,2,0,1:T(8,128)(2,1)S(1)}, u32[]{:S(2)}, u32[]{:S(2)}) async-start(bf16[8,16,16,128]{3,2,0,1:T(8,128)(2,1)} %copy.11), calls=%async_computation.1 | async-start | bytes 1048576 | tf_op jit(solution)/shard_map/all_to_all | solution.py:221
  163.5 19.3 %all-to-all-start.3 = ((bf16[8,16,16,128]{3,2,0,1:T(8,128)(2,1)}), bf16[8,16,16,128]{3,2,0,1:T(8,128)(2,1)S(1)}, u32[]{:S(2)}, u32[]{:S(2)}) async-start(bf16[8,16,16,128]{3,2,0,1:T(8,128)(2,1)} %copy.12), calls=%async_computation.3 | async-start | bytes 1048576 | tf_op jit(solution)/shard_map/all_to_all | solution.py:221
  182.8 18.5 %all-to-all-start.5 = ((bf16[8,16,16,128]{3,2,0,1:T(8,128)(2,1)}), bf16[8,16,16,128]{3,2,0,1:T(8,128)(2,1)S(1)}, u32[]{:S(2)}, u32[]{:S(2)}) async-start(bf16[8,16,16,128]{3,2,0,1:T(8,128)(2,1)} %copy.13), calls=%async_computation.5 | async-start | bytes 1048576 | tf_op jit(solution)/shard_map/all_to_all | solution.py:221

commit v3 on v2

v3 whole, which is shorter than its diff:
```python
import math

import numpy as np
import jax
import jax.numpy as jnp
from jax import lax
from jax.experimental import pallas as pl
from jax.experimental.pallas import tpu as pltpu
from jax.sharding import PartitionSpec as P

U = 16
TAPS = 4
TINT = 2
IB = 4
CHUNKS = 4
FRAMES = 2 * IB


def window_taps_np():
    length = TAPS * U
    positions = np.arange(length, dtype=np.float64)
    offsets = (positions - (length - 1) / 2.0) / U
    hann_taper = 0.5 - 0.5 * np.cos(2.0 * math.pi * (positions + 0.5) / length)
    taps_window = np.sinc(offsets) * hann_taper
    taps_window = taps_window / np.sqrt(np.sum(taps_window * taps_window) / U)
    return taps_window.astype(np.float32)


def band_matrix():
    taps = window_taps_np().astype(np.float64)
    span = (FRAMES + TAPS - 1) * U
    index_n = np.arange(U)
    phases = 2.0 * math.pi * ((index_n[:, None] * index_n[None, :]) % U) / U
    cosine = np.cos(phases) / math.sqrt(U)
    sine = np.sin(phases) / math.sqrt(U)
    table = np.array([[cosine, -sine], [sine, cosine]])
    band = np.zeros((2, FRAMES, U, 2, span))
    for t in range(FRAMES):
        for m in range(TAPS * U):
            for r in range(2):
                band[:, t, :, r, t * U + m] = taps[m] * table[r, :, m % U, :]
    band = band.reshape(2 * FRAMES * U, 2 * span).astype(np.float32)
    high = band.astype(jnp.bfloat16)
    low = (band - high.astype(np.float32)).astype(jnp.bfloat16)
    return np.stack([high, low])


def _filter_kernel(chunk, main_ref, pre0_ref, pre1_ref, pre2_ref, hist_ref, gain_ref, band_ref, out_ref, xs_ref):
    rows_main = main_ref.shape[4]
    nblk = main_ref.shape[2]
    nb = out_ref.shape[1]
    span = (FRAMES + TAPS - 1) * U
    half = FRAMES * U
    g_re = gain_ref[0, 0]
    g_im = gain_ref[1, 0]

    def block(tdev, carry):
        for r in range(2):
            xs_ref[r, pl.ds(48, rows_main), :] = main_ref[r, 0, tdev, 0]
        if chunk == 0:
            prev = jnp.maximum(tdev - 1, 0)
            for r in range(2):
                for m, pre in enumerate((pre0_ref, pre1_ref, pre2_ref)):
                    xs_ref[r, pl.ds(16 * m, 16), :] = pre[r, 0, prev, 0]

            @pl.when(tdev == 0)
            def _():
                for r in range(2):
                    xs_ref[r, pl.ds(0, 48), :] = hist_ref[r, 0, 0]
        else:
            for r in range(2):
                for m, pre in enumerate((pre0_ref, pre1_ref, pre2_ref)):
                    xs_ref[r, pl.ds(16 * m, 16), :] = pre[r, 0, tdev, 0]

        for ib in range(nb):
            rhs = jnp.concatenate(
                [xs_ref[r, pl.ds(ib * half, span), :] for r in range(2)], axis=0
            )
            spec = jnp.dot(band_ref[0], rhs, preferred_element_type=jnp.float32)
            spec = spec + jnp.dot(band_ref[1], rhs, preferred_element_type=jnp.float32)
            s_re = spec[:half]
            s_im = spec[half:]
            c_re = g_re * s_re - g_im * s_im
            c_im = g_re * s_im + g_im * s_re
            out_ref[tdev, ib, 0, 0] = c_re.astype(jnp.bfloat16).reshape(IB, TINT, U, 128)
            out_ref[tdev, ib, 1, 0] = c_im.astype(jnp.bfloat16).reshape(IB, TINT, U, 128)
        return carry

    lax.fori_loop(0, nblk, block, 0)


def filterbank(voltages, history, gains, band, chunk, chunks):
    _, pols, _, samples, feeds = voltages.shape
    nblk = 8
    rows_blk = samples // nblk
    rows_main = rows_blk // chunks
    nb = rows_main // U // FRAMES
    main = voltages.reshape(2, pols, nblk, chunks, rows_main, feeds)
    units = voltages.reshape(2, pols, nblk, rows_blk // 16, 16, feeds)
    if chunk == 0:
        first = rows_blk // 16 - 3
    else:
        first = chunk * rows_main // 16 - 3

    def pre_map(m):
        return lambda p: (0, p, 0, first + m, 0, 0)

    return pl.pallas_call(
        lambda *refs: _filter_kernel(chunk, *refs),
        grid=(pols,),
        in_specs=[
            pl.BlockSpec((2, 1, nblk, 1, rows_main, feeds), lambda p: (0, p, 0, chunk, 0, 0)),
            pl.BlockSpec((2, 1, nblk, 1, 16, feeds), pre_map(0)),
            pl.BlockSpec((2, 1, nblk, 1, 16, feeds), pre_map(1)),
            pl.BlockSpec((2, 1, nblk, 1, 16, feeds), pre_map(2)),
            pl.BlockSpec((2, 1, 1, 48, feeds), lambda p: (0, p, 0, 0, 0)),
            pl.BlockSpec((2, 1, 1, feeds), lambda p: (0, p, 0, 0)),
            pl.BlockSpec(band.shape, lambda p: (0, 0, 0)),
        ],
        out_specs=pl.BlockSpec((nblk, nb, 2, 1, IB, TINT, U, feeds), lambda p: (0, 0, 0, p, 0, 0, 0, 0)),
        out_shape=jax.ShapeDtypeStruct((nblk, nb, 2, pols, IB, TINT, U, feeds), jnp.bfloat16),
        scratch_shapes=[
            pltpu.VMEM((2, rows_main + 48, feeds), jnp.bfloat16),
        ],
        cost_estimate=pl.CostEstimate(
            flops=2 * band.size * feeds * pols * nblk * nb,
            bytes_accessed=2 * voltages.size * 2 // chunks,
            transcendentals=0,
        ),
    )(main, units, units, units, history, gains, band)


def _beam_kernel(cal_ref, w_ref, sel_ref, out_ref):
    nsrc = cal_ref.shape[0]
    rows = 2 * 2 * IB * U
    halves = []
    for s in range(2):
        pieces = [cal_ref[d, 0, s].reshape(rows, 128) for d in range(nsrc)]
        halves.append(jnp.concatenate(pieces, axis=1))
    lhs = jnp.concatenate(halves, axis=0)
    prod_re = jnp.dot(lhs, w_ref[0, 0], preferred_element_type=jnp.float32)
    prod_im = jnp.dot(lhs, w_ref[1, 0], preferred_element_type=jnp.float32)
    real_part = prod_re[:rows] - prod_im[rows:]
    imag_part = prod_im[:rows] + prod_re[rows:]
    power = real_part * real_part + imag_part * imag_part
    quarter = rows // 2
    power = power[:quarter] + power[quarter:]
    power = power.reshape(IB, TINT, U, power.shape[-1])
    power = (power[:, 0] + power[:, 1]).reshape(IB * U, power.shape[-1])
    detected = (power * (1.0 / (4.0 * TINT))).astype(jnp.bfloat16)
    picked = jnp.dot(detected, sel_ref[...], preferred_element_type=jnp.float32).astype(jnp.bfloat16)
    nodes = out_ref.shape[1]
    for n in range(nodes):
        out_ref[:, n] = picked[:, n * 128 : (n + 1) * 128].reshape(IB, U, 128)


def beamform(cal, weights, select):
    nsrc, nb = cal.shape[0], cal.shape[1]
    feeds, beams = weights.shape[2], weights.shape[3]
    slots = select.shape[1]
    nodes = slots // 128
    return pl.pallas_call(
        _beam_kernel,
        grid=(nb,),
        in_specs=[
            pl.BlockSpec((nsrc, 1, 2, 2, IB, TINT, U, 128), lambda i: (0, i, 0, 0, 0, 0, 0, 0)),
            pl.BlockSpec((2, 1, feeds, beams), lambda i: (0, 0, 0, 0)),
            pl.BlockSpec((beams, slots), lambda i: (0, 0)),
        ],
        out_specs=pl.BlockSpec((IB, nodes, U, 128), lambda i: (i, 0, 0, 0)),
        out_shape=jax.ShapeDtypeStruct((nb * IB, nodes, U, 128), jnp.bfloat16),
        cost_estimate=pl.CostEstimate(
            flops=2 * 2 * (4 * nb * IB * U * TINT) * feeds * beams + 2 * nb * IB * U * beams * slots,
            bytes_accessed=cal.size * 2 + weights.size * 2 + select.size * 2 + nb * IB * U * slots * 2,
            transcendentals=0,
        ),
        compiler_params=pltpu.CompilerParams(vmem_limit_bytes=60 * 1024 * 1024),
    )(cal, weights, select)


def on_device(voltages, history, gains, weights, beam_lists, beam_counts):
    capacity = beam_lists.shape[1]
    beams = weights.shape[3]
    flat_ids = beam_lists.reshape(-1)
    live_slots = (jnp.arange(capacity, dtype=jnp.int32)[None, :] < beam_counts[:, None]).reshape(-1)
    select = (
        (jnp.arange(beams, dtype=jnp.int32)[:, None] == flat_ids[None, :]) & live_slots[None, :]
    ).astype(jnp.bfloat16)
    band = jnp.asarray(band_matrix())
    outs = []
    for chunk in range(CHUNKS):
        calibrated = filterbank(voltages, history, gains, band, chunk, CHUNKS)
        gathered = lax.all_to_all(calibrated, "feed", split_axis=0, concat_axis=0, tiled=True)
        picked = beamform(gathered, weights, select)
        outs.append(lax.all_to_all(picked, "chan", split_axis=1, concat_axis=1, tiled=True))
    exchanged = jnp.concatenate(outs, axis=0)
    bins, nodes, fine, width = exchanged.shape
    return exchanged.reshape(bins, nodes * fine, width)


def solution(mesh):
    in_specs = (
        P(None, None, "chan", None, "feed"),
        P(None, None, "chan", None, "feed"),
        P(None, None, "chan", "feed"),
        P(None, "chan", None, None),
        P(),
        P(),
    )
    out_specs = P("feed", None, "chan")
    return jax.shard_map(
        on_device, mesh=mesh, in_specs=in_specs, out_specs=out_specs, check_vma=False
    )
```

time: 222 us -> 216 us (0.973)
  Pallas kernels: 101 us -> 76.6 us
  waiting for transfers between devices: 45.2 us -> 63.6 us
    pallas_call x4, Pallas kernels: 58.5 us -> 33.9 us  [filterbank(): pl.pallas_call(lambda *refs: _filter_kernel(chunk, *refs), grid=(pols,),...]
    all_to_all x4, waiting for transfers between devices: 45.2 us -> 63.6 us  [on_device(): lax.all_to_all(calibrated, 'feed', split_axis=0, concat_axis=0, tiled=True)]
  transfers between devices with their start and end apart: 7 -> 7, of which waited for: 4 -> 4; matrix products, arithmetic and copies ran while one was open for 5% -> 5% of each run, Pallas kernels for 40% -> 32%
where the time goes in v3:
time: 216 us; the launch traced here: 213 us
  Pallas kernels  76.6 us (35%)
  waiting for transfers between devices  63.6 us (29%)
  starting transfers between devices  40 us (19%)
  blocking collectives  15.4 us (7%)
  local copies, waits for them, and re-layouts  12.8 us (6%)
  other arithmetic  3.99 us (2%)
    all_to_all x4, waiting for transfers between devices, on_device(): lax.all_to_all(calibrated, 'feed', split_axis=0, concat_axis=0, tiled=True)  63.6 us
    pallas_call x4, Pallas kernels, beamform(): pl.pallas_call(_beam_kernel, grid=(nb,), in_specs=[pl.BlockSpec((nsrc, 1,...  42.7 us
    pallas_call x4, Pallas kernels, filterbank(): pl.pallas_call(lambda *refs: _filter_kernel(chunk, *refs), grid=(pols,),...  33.9 us
    all_to_all x3, starting transfers between devices, on_device(): lax.all_to_all(picked, 'chan', split_axis=1, concat_axis=1, tiled=True)  20.9 us
    all_to_all x4, starting transfers between devices, on_device(): lax.all_to_all(calibrated, 'feed', split_axis=0, concat_axis=0, tiled=True)  19.1 us
    all_to_all x1, blocking collectives, on_device(): lax.all_to_all(picked, 'chan', split_axis=1, concat_axis=1, tiled=True)  15.4 us
    pallas_call x4, local copies, waits for them, and re-layouts, beamform(): pl.pallas_call(_beam_kernel, grid=(nb,), in_specs=[pl.BlockSpec((nsrc, 1,...  6.8 us
  transfers between devices with their start and end apart: 7, of which 4 were waited for; matrix products, arithmetic and copies ran while one was open for 5% of the time, Pallas kernels for 32%

profile of v3, /device:TPU:1, one launch (start us, length us, event | category | flops | bytes accessed | tf_op | source)
XLA Modules:
  0.0 212.6 jit_solution(17314792347597562298)
XLA Ops:
  0.0 8.5 %shard_map.73 = bf16[8,2,2,2,4,2,16,128]{7,6,5,4,3,2,1,0:T(8,128)(2,1)} custom-call(bf16[2,2,8,4,256,128]{5,4,3,2,1,0:T(8,128)(2,1)} %bitcast.6, bf16[2,2,8,64,16,128]{5,4,3,2,1,0:T(8,128)(2,1)} %bitcast.7, bf16[2,2,8,64,16,128]{5,4,3,2,1,0:T(8,128)(2,1)} %bitcast.8, bf16[2,2,8,64,16,128]{5,4,3,2,1,0:T(8,128)(2,1)} %bitcast.9, ...), custom_call_target="tpu_custom_call" | custom-call | flops 1476395008 | bytes 4194304 | tf_op jit(solution)/shard_map/pallas_call | solution.py:108
  8.5 6.0 %all-to-all-start = ((bf16[8,2,2,2,4,2,16,128]{7,6,5,4,3,2,1,0:T(8,128)(2,1)}), bf16[8,2,2,2,4,2,16,128]{7,6,5,4,3,2,1,0:T(8,128)(2,1)S(1)}, u32[]{:S(2)}, u32[]{:S(2)}) async-start(bf16[8,2,2,2,4,2,16,128]{7,6,5,4,3,2,1,0:T(8,128)(2,1)} %shard_map.73), calls=%async_computation | async-start | bytes 4194304 | tf_op jit(solution)/shard_map/all_to_all | solution.py:193
  14.4 8.5 %shard_map.75 = bf16[8,2,2,2,4,2,16,128]{7,6,5,4,3,2,1,0:T(8,128)(2,1)} custom-call(bf16[2,2,8,4,256,128]{5,4,3,2,1,0:T(8,128)(2,1)} %bitcast.10, bf16[2,2,8,64,16,128]{5,4,3,2,1,0:T(8,128)(2,1)} %bitcast.11, bf16[2,2,8,64,16,128]{5,4,3,2,1,0:T(8,128)(2,1)} %bitcast.12, bf16[2,2,8,64,16,128]{5,4,3,2,1,0:T(8,128)(2,1)} %bitcast.13, ...), custom_call_target="tpu_custom_call" | custom-call | flops 1476395008 | bytes 4194304 | tf_op jit(solution)/shard_map/pallas_call | solution.py:108
  22.9 17.9 %all-to-all-done.cal_ref = bf16[8,2,2,2,4,2,16,128]{7,6,5,4,3,2,1,0:T(8,128)(2,1)S(1)} async-done(((bf16[8,2,2,2,4,2,16,128]{7,6,5,4,3,2,1,0:T(8,128)(2,1)}), bf16[8,2,2,2,4,2,16,128]{7,6,5,4,3,2,1,0:T(8,128)(2,1)S(1)}, u32[]{:S(2)}, u32[]{:S(2)}) %all-to-all-start) | async-done | bytes 2097184 | tf_op jit(solution)/shard_map/all_to_all | solution.py:193
  40.8 0.0 copy-start.3
  40.8 1.4 copy-done.3
  42.2 4.4 %all-to-all-start.2 = ((bf16[8,2,2,2,4,2,16,128]{7,6,5,4,3,2,1,0:T(8,128)(2,1)}), bf16[8,2,2,2,4,2,16,128]{7,6,5,4,3,2,1,0:T(8,128)(2,1)S(1)}, u32[]{:S(2)}, u32[]{:S(2)}) async-start(bf16[8,2,2,2,4,2,16,128]{7,6,5,4,3,2,1,0:T(8,128)(2,1)} %shard_map.75), calls=%async_computation.2 | async-start | bytes 4194304 | tf_op jit(solution)/shard_map/all_to_all | solution.py:193
  46.5 8.5 %shard_map.77 = bf16[8,2,2,2,4,2,16,128]{7,6,5,4,3,2,1,0:T(8,128)(2,1)} custom-call(bf16[2,2,8,4,256,128]{5,4,3,2,1,0:T(8,128)(2,1)} %bitcast.14, bf16[2,2,8,64,16,128]{5,4,3,2,1,0:T(8,128)(2,1)} %bitcast.15, bf16[2,2,8,64,16,128]{5,4,3,2,1,0:T(8,128)(2,1)} %bitcast.16, bf16[2,2,8,64,16,128]{5,4,3,2,1,0:T(8,128)(2,1)} %bitcast.17, ...), custom_call_target="tpu_custom_call" | custom-call | flops 1476395008 | bytes 4194304 | tf_op jit(solution)/shard_map/pallas_call | solution.py:108
  55.0 17.9 %all-to-all-done.2.cal_ref = bf16[8,2,2,2,4,2,16,128]{7,6,5,4,3,2,1,0:T(8,128)(2,1)S(1)} async-done(((bf16[8,2,2,2,4,2,16,128]{7,6,5,4,3,2,1,0:T(8,128)(2,1)}), bf16[8,2,2,2,4,2,16,128]{7,6,5,4,3,2,1,0:T(8,128)(2,1)S(1)}, u32[]{:S(2)}, u32[]{:S(2)}) %all-to-all-start.2) | async-done | bytes 2097184 | tf_op jit(solution)/shard_map/all_to_all | solution.py:193
  72.9 0.0 copy-start.2
  72.9 1.4 copy-done.2
  74.2 4.4 %all-to-all-start.4 = ((bf16[8,2,2,2,4,2,16,128]{7,6,5,4,3,2,1,0:T(8,128)(2,1)}), bf16[8,2,2,2,4,2,16,128]{7,6,5,4,3,2,1,0:T(8,128)(2,1)S(1)}, u32[]{:S(2)}, u32[]{:S(2)}) async-start(bf16[8,2,2,2,4,2,16,128]{7,6,5,4,3,2,1,0:T(8,128)(2,1)} %shard_map.77), calls=%async_computation.4 | async-start | bytes 4194304 | tf_op jit(solution)/shard_map/all_to_all | solution.py:193
  78.6 8.5 %shard_map.79 = bf16[8,2,2,2,4,2,16,128]{7,6,5,4,3,2,1,0:T(8,128)(2,1)} custom-call(bf16[2,2,8,4,256,128]{5,4,3,2,1,0:T(8,128)(2,1)} %bitcast.18, bf16[2,2,8,64,16,128]{5,4,3,2,1,0:T(8,128)(2,1)} %bitcast.19, bf16[2,2,8,64,16,128]{5,4,3,2,1,0:T(8,128)(2,1)} %bitcast.20, bf16[2,2,8,64,16,128]{5,4,3,2,1,0:T(8,128)(2,1)} %bitcast.21, ...), custom_call_target="tpu_custom_call" | custom-call | flops 1476395008 | bytes 4194304 | tf_op jit(solution)/shard_map/pallas_call | solution.py:108
  87.1 0.0 copy-start.5
  87.1 0.0 copy-start.4
  87.1 17.9 %all-to-all-done.4.cal_ref = bf16[8,2,2,2,4,2,16,128]{7,6,5,4,3,2,1,0:T(8,128)(2,1)S(1)} async-done(((bf16[8,2,2,2,4,2,16,128]{7,6,5,4,3,2,1,0:T(8,128)(2,1)}), bf16[8,2,2,2,4,2,16,128]{7,6,5,4,3,2,1,0:T(8,128)(2,1)S(1)}, u32[]{:S(2)}, u32[]{:S(2)}) %all-to-all-start.4) | async-done | bytes 2097184 | tf_op jit(solution)/shard_map/all_to_all | solution.py:193
  105.0 0.0 copy-start.1
  105.0 1.4 copy-done.1
  106.3 4.4 %all-to-all-start.6 = ((bf16[8,2,2,2,4,2,16,128]{7,6,5,4,3,2,1,0:T(8,128)(2,1)}), bf16[8,2,2,2,4,2,16,128]{7,6,5,4,3,2,1,0:T(8,128)(2,1)S(1)}, u32[]{:S(2)}, u32[]{:S(2)}) async-start(bf16[8,2,2,2,4,2,16,128]{7,6,5,4,3,2,1,0:T(8,128)(2,1)} %shard_map.79), calls=%async_computation.6 | async-start | bytes 4194304 | tf_op jit(solution)/shard_map/all_to_all | solution.py:193
  110.7 0.0 copy-done.5
  110.7 0.1 fusion.2
  110.8 0.0 copy-done.4
  110.8 3.7 %fusion.1.sel_ref = bf16[1024,2048]{1,0:T(8,128)(2,1)} fusion(s32[2048]{0:T(1024)S(1)} %bitcast.22, pred[2048]{0:T(1024)(128)(4,1)S(1)} %fusion.2), kind=kLoop, calls=%fused_computation.2 | loop fusion | flops 6291456 | bytes 4204544 | tf_op jit(solution)/shard_map/convert_element_type | solution.py:188
  114.5 10.7 %shard_map.74 = bf16[8,16,16,128]{3,2,1,0:T(8,128)(2,1)} custom-call(bf16[8,2,2,2,4,2,16,128]{7,6,5,4,3,2,1,0:T(8,128)(2,1)} %copy-done.3, bf16[2,1,1024,1024]{3,2,1,0:T(8,128)(2,1)} %w_ref.7, bf16[1024,2048]{1,0:T(8,128)(2,1)} %fusion.1.sel_ref), custom_call_target="tpu_custom_call" | custom-call | flops 4831838208 | bytes 11010048 | tf_op jit(solution)/shard_map/pallas_call | solution.py:162
  125.1 1.9 copy.12
  127.1 10.0 %all-to-all-done.6.cal_ref = bf16[8,2,2,2,4,2,16,128]{7,6,5,4,3,2,1,0:T(8,128)(2,1)S(1)} async-done(((bf16[8,2,2,2,4,2,16,128]{7,6,5,4,3,2,1,0:T(8,128)(2,1)}), bf16[8,2,2,2,4,2,16,128]{7,6,5,4,3,2,1,0:T(8,128)(2,1)S(1)}, u32[]{:S(2)}, u32[]{:S(2)}) %all-to-all-start.6) | async-done | bytes 2097184 | tf_op jit(solution)/shard_map/all_to_all | solution.py:193
  137.1 0.0 copy-start
  137.1 7.6 %all-to-all-start.1 = ((bf16[8,16,16,128]{3,2,0,1:T(8,128)(2,1)}), bf16[8,16,16,128]{3,2,0,1:T(8,128)(2,1)S(1)}, u32[]{:S(2)}, u32[]{:S(2)}) async-start(bf16[8,16,16,128]{3,2,0,1:T(8,128)(2,1)} %copy.12), calls=%async_computation.1 | async-start | bytes 1048576 | tf_op jit(solution)/shard_map/all_to_all | solution.py:195
  144.7 10.7 %shard_map.76 = bf16[8,16,16,128]{3,2,1,0:T(8,128)(2,1)} custom-call(bf16[8,2,2,2,4,2,16,128]{7,6,5,4,3,2,1,0:T(8,128)(2,1)} %copy-done.2, bf16[2,1,1024,1024]{3,2,1,0:T(8,128)(2,1)} %w_ref.7, bf16[1024,2048]{1,0:T(8,128)(2,1)} %fusion.1.sel_ref), custom_call_target="tpu_custom_call" | custom-call | flops 4831838208 | bytes 11010048 | tf_op jit(solution)/shard_map/pallas_call | solution.py:162
  155.4 0.0 copy-done
  155.4 1.9 copy.13
  157.3 0.0 all-to-all-done.1
  157.3 6.7 %all-to-all-start.3 = ((bf16[8,16,16,128]{3,2,0,1:T(8,128)(2,1)}), bf16[8,16,16,128]{3,2,0,1:T(8,128)(2,1)S(1)}, u32[]{:S(2)}, u32[]{:S(2)}) async-start(bf16[8,16,16,128]{3,2,0,1:T(8,128)(2,1)} %copy.13), calls=%async_computation.3 | async-start | bytes 1048576 | tf_op jit(solution)/shard_map/all_to_all | solution.py:195
  163.9 10.7 %shard_map.78 = bf16[8,16,16,128]{3,2,1,0:T(8,128)(2,1)} custom-call(bf16[8,2,2,2,4,2,16,128]{7,6,5,4,3,2,1,0:T(8,128)(2,1)} %copy-done.1, bf16[2,1,1024,1024]{3,2,1,0:T(8,128)(2,1)} %w_ref.7, bf16[1024,2048]{1,0:T(8,128)(2,1)} %fusion.1.sel_ref), custom_call_target="tpu_custom_call" | custom-call | flops 4831838208 | bytes 11010048 | tf_op jit(solution)/shard_map/pallas_call | solution.py:162
  174.6 1.9 copy.14
  176.5 0.0 all-to-all-done.3
  176.5 6.7 %all-to-all-start.5 = ((bf16[8,16,16,128]{3,2,0,1:T(8,128)(2,1)}), bf16[8,16,16,128]{3,2,0,1:T(8,128)(2,1)S(1)}, u32[]{:S(2)}, u32[]{:S(2)}) async-start(bf16[8,16,16,128]{3,2,0,1:T(8,128)(2,1)} %copy.14), calls=%async_computation.5 | async-start | bytes 1048576 | tf_op jit(solution)/shard_map/all_to_all | solution.py:195
  183.2 10.7 %shard_map.80 = bf16[8,16,16,128]{3,2,1,0:T(8,128)(2,1)} custom-call(bf16[8,2,2,2,4,2,16,128]{7,6,5,4,3,2,1,0:T(8,128)(2,1)} %copy-done, bf16[2,1,1024,1024]{3,2,1,0:T(8,128)(2,1)} %w_ref.7, bf16[1024,2048]{1,0:T(8,128)(2,1)} %fusion.1.sel_ref), custom_call_target="tpu_custom_call" | custom-call | flops 4831838208 | bytes 11010048 | tf_op jit(solution)/shard_map/pallas_call | solution.py:162
  193.9 1.1 copy.15
  195.0 0.0 all-to-all-done.5
  195.0 15.4 %all_to_all.40 = bf16[8,16,16,128]{3,2,0,1:T(8,128)(2,1)S(1)} all-to-all(bf16[8,16,16,128]{3,2,0,1:T(8,128)(2,1)S(1)} %copy.15), channel_id=1, replica_groups=mesh['feed'=8,'chan'=16] {'chan'}, dimensions={1} | all-to-all | bytes 1048576 | tf_op jit(solution)/shard_map/all_to_all | solution.py:195
  210.4 0.3 pad_maximum_fusion
  210.7 1.9 copy.20
Async XLA Ops:
  8.5 32.3 %all-to-all-start = ((bf16[8,2,2,2,4,2,16,128]{7,6,5,4,3,2,1,0:T(8,128)(2,1)}), bf16[8,2,2,2,4,2,16,128]{7,6,5,4,3,2,1,0:T(8,128)(2,1)S(1)}, u32[]{:S(2)}, u32[]{:S(2)}) async-start(bf16[8,2,2,2,4,2,16,128]{7,6,5,4,3,2,1,0:T(8,128)(2,1)} %shard_map.73), calls=%async_computation | async-start | bytes 4194304 | tf_op jit(solution)/shard_map/all_to_all | solution.py:193
  40.8 1.4 copy-start.3
  42.2 30.7 %all-to-all-start.2 = ((bf16[8,2,2,2,4,2,16,128]{7,6,5,4,3,2,1,0:T(8,128)(2,1)}), bf16[8,2,2,2,4,2,16,128]{7,6,5,4,3,2,1,0:T(8,128)(2,1)S(1)}, u32[]{:S(2)}, u32[]{:S(2)}) async-start(bf16[8,2,2,2,4,2,16,128]{7,6,5,4,3,2,1,0:T(8,128)(2,1)} %shard_map.75), calls=%async_computation.2 | async-start | bytes 4194304 | tf_op jit(solution)/shard_map/all_to_all | solution.py:193
  72.9 1.4 copy-start.2
  74.2 30.7 %all-to-all-start.4 = ((bf16[8,2,2,2,4,2,16,128]{7,6,5,4,3,2,1,0:T(8,128)(2,1)}), bf16[8,2,2,2,4,2,16,128]{7,6,5,4,3,2,1,0:T(8,128)(2,1)S(1)}, u32[]{:S(2)}, u32[]{:S(2)}) async-start(bf16[8,2,2,2,4,2,16,128]{7,6,5,4,3,2,1,0:T(8,128)(2,1)} %shard_map.77), calls=%async_computation.4 | async-start | bytes 4194304 | tf_op jit(solution)/shard_map/all_to_all | solution.py:193
  87.1 23.6 %copy-start.5 = (s32[16]{0:T(128)S(1)}, s32[16]{0:T(128)}, u32[]{:S(2)}) copy-start(s32[16]{0:T(128)} %param.12) | copy-start | bytes 196
  87.1 23.7 %copy-start.4 = (s32[16,128]{1,0:T(8,128)S(1)}, s32[16,128]{1,0:T(8,128)}, u32[]{:S(2)}) copy-start(s32[16,128]{1,0:T(8,128)} %param.11) | copy-start | bytes 24580
  105.0 1.4 copy-start.1
  106.3 30.7 %all-to-all-start.6 = ((bf16[8,2,2,2,4,2,16,128]{7,6,5,4,3,2,1,0:T(8,128)(2,1)}), bf16[8,2,2,2,4,2,16,128]{7,6,5,4,3,2,1,0:T(8,128)(2,1)S(1)}, u32[]{:S(2)}, u32[]{:S(2)}) async-start(bf16[8,2,2,2,4,2,16,128]{7,6,5,4,3,2,1,0:T(8,128)(2,1)} %shard_map.79), calls=%async_computation.6 | async-start | bytes 4194304 | tf_op jit(solution)/shard_map/all_to_all | solution.py:193
  137.1 18.3 %copy-start = (bf16[8,2,2,2,4,2,16,128]{7,6,5,4,3,2,1,0:T(8,128)(2,1)}, bf16[8,2,2,2,4,2,16,128]{7,6,5,4,3,2,1,0:T(8,128)(2,1)S(1)}, u32[]{:S(2)}) copy-start(bf16[8,2,2,2,4,2,16,128]{7,6,5,4,3,2,1,0:T(8,128)(2,1)S(1)} %all-to-all-done.6.cal_ref) | copy-start | bytes 6291460
  137.1 20.2 %all-to-all-start.1 = ((bf16[8,16,16,128]{3,2,0,1:T(8,128)(2,1)}), bf16[8,16,16,128]{3,2,0,1:T(8,128)(2,1)S(1)}, u32[]{:S(2)}, u32[]{:S(2)}) async-start(bf16[8,16,16,128]{3,2,0,1:T(8,128)(2,1)} %copy.12), calls=%async_computation.1 | async-start | bytes 1048576 | tf_op jit(solution)/shard_map/all_to_all | solution.py:195
  157.3 19.2 %all-to-all-start.3 = ((bf16[8,16,16,128]{3,2,0,1:T(8,128)(2,1)}), bf16[8,16,16,128]{3,2,0,1:T(8,128)(2,1)S(1)}, u32[]{:S(2)}, u32[]{:S(2)}) async-start(bf16[8,16,16,128]{3,2,0,1:T(8,128)(2,1)} %copy.13), calls=%async_computation.3 | async-start | bytes 1048576 | tf_op jit(solution)/shard_map/all_to_all | solution.py:195
  176.5 18.5 %all-to-all-start.5 = ((bf16[8,16,16,128]{3,2,0,1:T(8,128)(2,1)}), bf16[8,16,16,128]{3,2,0,1:T(8,128)(2,1)S(1)}, u32[]{:S(2)}, u32[]{:S(2)}) async-start(bf16[8,16,16,128]{3,2,0,1:T(8,128)(2,1)} %copy.14), calls=%async_computation.5 | async-start | bytes 1048576 | tf_op jit(solution)/shard_map/all_to_all | solution.py:195

commit v4 on v3

--- a/solution.py
+++ b/solution.py
@@ -45,7 +45,7 @@
     return np.stack([high, low])
 
 
-def _filter_kernel(chunk, main_ref, pre0_ref, pre1_ref, pre2_ref, hist_ref, gain_ref, band_ref, out_ref, xs_ref):
+def _filter_kernel(chunk, me_ref, main_ref, pre0_ref, pre1_ref, pre2_ref, hist_ref, gain_ref, band_ref, out_ref, xs_ref):
     rows_main = main_ref.shape[4]
     nblk = main_ref.shape[2]
     nb = out_ref.shape[1]
@@ -54,7 +54,8 @@
     g_re = gain_ref[0, 0]
     g_im = gain_ref[1, 0]
 
-    def block(tdev, carry):
+    def block(shift, carry):
+        tdev = lax.rem(me_ref[0] + shift, nblk)
         for r in range(2):
             xs_ref[r, pl.ds(48, rows_main), :] = main_ref[r, 0, tdev, 0]
         if chunk == 0:
@@ -82,14 +83,14 @@
             s_im = spec[half:]
             c_re = g_re * s_re - g_im * s_im
             c_im = g_re * s_im + g_im * s_re
-            out_ref[tdev, ib, 0, 0] = c_re.astype(jnp.bfloat16).reshape(IB, TINT, U, 128)
-            out_ref[tdev, ib, 1, 0] = c_im.astype(jnp.bfloat16).reshape(IB, TINT, U, 128)
+            out_ref[shift, ib, 0, 0] = c_re.astype(jnp.bfloat16).reshape(IB, TINT, U, 128)
+            out_ref[shift, ib, 1, 0] = c_im.astype(jnp.bfloat16).reshape(IB, TINT, U, 128)
         return carry
 
     lax.fori_loop(0, nblk, block, 0)
 
 
-def filterbank(voltages, history, gains, band, chunk, chunks):
+def filterbank(me, voltages, history, gains, band, chunk, chunks):
     _, pols, _, samples, feeds = voltages.shape
     nblk = 8
     rows_blk = samples // nblk
@@ -109,6 +110,7 @@
         lambda *refs: _filter_kernel(chunk, *refs),
         grid=(pols,),
         in_specs=[
+            pl.BlockSpec(memory_space=pltpu.SMEM),
             pl.BlockSpec((2, 1, nblk, 1, rows_main, feeds), lambda p: (0, p, 0, chunk, 0, 0)),
             pl.BlockSpec((2, 1, nblk, 1, 16, feeds), pre_map(0)),
             pl.BlockSpec((2, 1, nblk, 1, 16, feeds), pre_map(1)),
@@ -127,15 +129,16 @@
             bytes_accessed=2 * voltages.size * 2 // chunks,
             transcendentals=0,
         ),
-    )(main, units, units, units, history, gains, band)
-
-
-def _beam_kernel(cal_ref, w_ref, sel_ref, out_ref):
-    nsrc = cal_ref.shape[0]
+    )(me, main, units, units, units, history, gains, band)
+
+
+def _beam_kernel(*refs):
+    cal_refs = refs[:-3]
+    w_ref, sel_ref, out_ref = refs[-3:]
     rows = 2 * 2 * IB * U
     halves = []
     for s in range(2):
-        pieces = [cal_ref[d, 0, s].reshape(rows, 128) for d in range(nsrc)]
+        pieces = [c[0, 0, s].reshape(rows, 128) for c in cal_refs]
         halves.append(jnp.concatenate(pieces, axis=1))
     lhs = jnp.concatenate(halves, axis=0)
     prod_re = jnp.dot(lhs, w_ref[0, 0], preferred_element_type=jnp.float32)
@@ -154,16 +157,17 @@
         out_ref[:, n] = picked[:, n * 128 : (n + 1) * 128].reshape(IB, U, 128)
 
 
-def beamform(cal, weights, select):
-    nsrc, nb = cal.shape[0], cal.shape[1]
+def beamform(pieces, weights, select):
+    nsrc, nb = len(pieces), pieces[0].shape[1]
     feeds, beams = weights.shape[2], weights.shape[3]
     slots = select.shape[1]
     nodes = slots // 128
+    piece_spec = pl.BlockSpec((1, 1, 2, 2, IB, TINT, U, 128), lambda i: (0, i, 0, 0, 0, 0, 0, 0))
     return pl.pallas_call(
         _beam_kernel,
         grid=(nb,),
-        in_specs=[
-            pl.BlockSpec((nsrc, 1, 2, 2, IB, TINT, U, 128), lambda i: (0, i, 0, 0, 0, 0, 0, 0)),
+        in_specs=[piece_spec] * nsrc
+        + [
             pl.BlockSpec((2, 1, feeds, beams), lambda i: (0, 0, 0, 0)),
             pl.BlockSpec((beams, slots), lambda i: (0, 0)),
         ],
@@ -171,11 +175,11 @@
         out_shape=jax.ShapeDtypeStruct((nb * IB, nodes, U, 128), jnp.bfloat16),
         cost_estimate=pl.CostEstimate(
             flops=2 * 2 * (4 * nb * IB * U * TINT) * feeds * beams + 2 * nb * IB * U * beams * slots,
-            bytes_accessed=cal.size * 2 + weights.size * 2 + select.size * 2 + nb * IB * U * slots * 2,
+            bytes_accessed=sum(p.size for p in pieces) * 2 + weights.size * 2 + select.size * 2 + nb * IB * U * slots * 2,
             transcendentals=0,
         ),
         compiler_params=pltpu.CompilerParams(vmem_limit_bytes=60 * 1024 * 1024),
-    )(cal, weights, select)
+    )(*pieces, weights, select)
 
 
 def on_device(voltages, history, gains, weights, beam_lists, beam_counts):
@@ -187,11 +191,20 @@
         (jnp.arange(beams, dtype=jnp.int32)[:, None] == flat_ids[None, :]) & live_slots[None, :]
     ).astype(jnp.bfloat16)
     band = jnp.asarray(band_matrix())
+    nfeed = lax.axis_size("feed")
+    me = lax.axis_index("feed")
+    order = lax.rem(me - jnp.arange(nfeed, dtype=jnp.int32) + nfeed, nfeed)
+    feeds_local = weights.shape[2] // nfeed
+    wperm = jnp.take(weights.reshape(2, 1, nfeed, feeds_local, beams), order, axis=2).reshape(weights.shape)
+    me_arr = me.astype(jnp.int32).reshape(1)
     outs = []
     for chunk in range(CHUNKS):
-        calibrated = filterbank(voltages, history, gains, band, chunk, CHUNKS)
-        gathered = lax.all_to_all(calibrated, "feed", split_axis=0, concat_axis=0, tiled=True)
-        picked = beamform(gathered, weights, select)
+        calibrated = filterbank(me_arr, voltages, history, gains, band, chunk, CHUNKS)
+        pieces = [calibrated[0:1]]
+        for shift in range(1, nfeed):
+            pairs = [(i, (i + shift) % nfeed) for i in range(nfeed)]
+            pieces.append(lax.ppermute(calibrated[shift : shift + 1], "feed", perm=pairs))
+        picked = beamform(pieces, wperm, select)
         outs.append(lax.all_to_all(picked, "chan", split_axis=1, concat_axis=1, tiled=True))
     exchanged = jnp.concatenate(outs, axis=0)
     bins, nodes, fine, width = exchanged.shape

time: 216 us -> 213 us (0.986)
  waiting for transfers between devices: 63.6 us -> 27.3 us
  starting transfers between devices: 40 us -> 57.7 us
  local copies, waits for them, and re-layouts: 12.8 us -> 25.5 us
  other arithmetic: 3.99 us -> 6.51 us
    all_to_all x4 -> x0, waiting for transfers between devices: 63.6 us -> none  [on_device(): lax.all_to_all(calibrated, 'feed', split_axis=0, concat_axis=0, tiled=True)]
    ppermute x0 -> x28, starting transfers between devices: none -> 36.5 us  [on_device(): pieces.append(lax.ppermute(calibrated[shift:shift + 1], 'feed', perm=pairs))]
    ppermute x0 -> x28, waiting for transfers between devices: none -> 27.3 us  [on_device(): pieces.append(lax.ppermute(calibrated[shift:shift + 1], 'feed', perm=pairs))]
    all_to_all x4 -> x0, starting transfers between devices: 19.1 us -> none  [on_device(): lax.all_to_all(calibrated, 'feed', split_axis=0, concat_axis=0, tiled=True)]
    gather x0 -> x2, local copies, waits for them, and re-layouts: none -> 7.67 us  [on_device(): jnp.take(weights.reshape(2, 1, nfeed, feeds_local, beams), order, axis=2)]
    slice x0 -> x4, local copies, waits for them, and re-layouts: none -> 6.55 us  [on_device(): pieces.append(lax.ppermute(calibrated[shift:shift + 1], 'feed', perm=pairs))]
    select_n x0 -> x2, other arithmetic: none -> 2.45 us  [on_device(): jnp.take(weights.reshape(2, 1, nfeed, feeds_local, beams), order, axis=2)]
  transfers between devices with their start and end apart: 7 -> 31, of which waited for: 4 -> 6; matrix products, arithmetic and copies ran while one was open for 5% -> 12% of each run, Pallas kernels for 32% -> 33%
where the time goes in v4:
time: 213 us; the launch traced here: 212 us
  Pallas kernels  77.6 us (36%)
  starting transfers between devices  57.7 us (27%)
  waiting for transfers between devices  27.3 us (13%)
  local copies, waits for them, and re-layouts  25.5 us (12%)
  blocking collectives  16.9 us (8%)
  other arithmetic  6.51 us (3%)
    pallas_call x4, Pallas kernels, beamform(): pl.pallas_call(_beam_kernel, grid=(nb,), in_specs=[piece_spec] * nsrc + [...  43.8 us
    ppermute x28, starting transfers between devices, on_device(): pieces.append(lax.ppermute(calibrated[shift:shift + 1], 'feed', perm=pairs))  36.5 us
    pallas_call x4, Pallas kernels, filterbank(): pl.pallas_call(lambda *refs: _filter_kernel(chunk, *refs), grid=(pols,),...  33.8 us
    ppermute x28, waiting for transfers between devices, on_device(): pieces.append(lax.ppermute(calibrated[shift:shift + 1], 'feed', perm=pairs))  27.3 us
    all_to_all x3, starting transfers between devices, on_device(): lax.all_to_all(picked, 'chan', split_axis=1, concat_axis=1, tiled=True)  21.2 us
    all_to_all x1, blocking collectives, on_device(): lax.all_to_all(picked, 'chan', split_axis=1, concat_axis=1, tiled=True)  16.9 us
    gather x2, local copies, waits for them, and re-layouts, on_device(): jnp.take(weights.reshape(2, 1, nfeed, feeds_local, beams), order, axis=2)  7.67 us
    pallas_call x4, local copies, waits for them, and re-layouts, beamform(): pl.pallas_call(_beam_kernel, grid=(nb,), in_specs=[piece_spec] * nsrc + [...  6.98 us
  transfers between devices with their start and end apart: 31, of which 6 were waited for; matrix products, arithmetic and copies ran while one was open for 12% of the time, Pallas kernels for 33%

profile of v4, /device:TPU:1, one launch (start us, length us, event | category | flops | bytes accessed | tf_op | source)
XLA Modules:
  0.0 211.7 jit_solution(20031969716128234)
XLA Ops:
  0.0 8.5 %shard_map.73 = bf16[8,2,2,2,4,2,16,128]{7,6,5,4,3,2,1,0:T(8,128)(2,1)} custom-call(s32[1]{0:T(128)} %bitcast.refs_0_, bf16[2,2,8,4,256,128]{5,4,3,2,1,0:T(8,128)(2,1)} %bitcast.16, bf16[2,2,8,64,16,128]{5,4,3,2,1,0:T(8,128)(2,1)} %bitcast.17, bf16[2,2,8,64,16,128]{5,4,3,2,1,0:T(8,128)(2,1)} %bitcast.18, bf16[2,2,8,64,16,128]{5,4,3,2,1,0:T(8,128)(2,1)} %bitcast.19, ...), custom_call_target="tpu_custom_call" | custom-call | flops 1476395008 | bytes 4194304 | tf_op jit(solution)/shard_map/pallas_call | solution.py:109
  8.5 2.7 %fusion.6 = (bf16[1,2,2,2,4,2,16,128]{7,6,5,4,3,2,1,0:T(8,128)(2,1)S(1)}, bf16[1,2,2,2,4,2,16,128]{7,6,5,4,3,2,1,0:T(8,128)(2,1)S(1)}, bf16[1,2,2,2,4,2,16,128]{...) fusion(bf16[8,2,2,2,4,2,16,128]{7,6,5,4,3,2,1,0:T(8,128)(2,1)} , ...), kind=kLoop, calls=%fused_computation.20 | loop fusion | bytes 4194304 | tf_op jit(solution)/shard_map/slice | solution.py:206
  11.2 2.7 %collective-permute-start = (bf16[1,2,2,2,4,2,16,128]{7,6,5,4,3,2,1,0:T(8,128)(2,1)S(1)}, bf16[1,2,2,2,4,2,16,128]{7,6,5,4,3,2,1,0:T(8,128)(2,1)S(1)}, u32[]{:S(2)}, u32[]{:S(2)}) collective-permute-start(bf16[1,2,2,2,4,2,16,128]{7,6,5,4,3,2,1,0:T(8,128)(2,1)S(1)} %get-tuple-element.11), channel_id=1, source_target_pairs={{0,16},{16,32},{32,48},{48,64},{64,80},{80,96},{96,112},{112,0},{1... | collective-permute-start | bytes 786440 | tf_op jit(solution)/shard_map/ppermute | solution.py:206
  13.8 1.3 collective-permute-start.1
  15.1 1.6 collective-permute-start.2
  16.8 0.3 collective-permute-start.3
  17.1 2.0 collective-permute-start.4
  19.2 8.5 %shard_map.75 = bf16[8,2,2,2,4,2,16,128]{7,6,5,4,3,2,1,0:T(8,128)(2,1)} custom-call(s32[1]{0:T(128)} %bitcast.refs_0_, bf16[2,2,8,4,256,128]{5,4,3,2,1,0:T(8,128)(2,1)} %bitcast.20, bf16[2,2,8,64,16,128]{5,4,3,2,1,0:T(8,128)(2,1)} %bitcast.21, bf16[2,2,8,64,16,128]{5,4,3,2,1,0:T(8,128)(2,1)} %bitcast.22, bf16[2,2,8,64,16,128]{5,4,3,2,1,0:T(8,128)(2,1)} %bitcast.23, ...), custom_call_target="tpu_custom_call" | custom-call | flops 1476395008 | bytes 4194304 | tf_op jit(solution)/shard_map/pallas_call | solution.py:109
  27.7 8.4 %shard_map.77 = bf16[8,2,2,2,4,2,16,128]{7,6,5,4,3,2,1,0:T(8,128)(2,1)} custom-call(s32[1]{0:T(128)} %bitcast.refs_0_, bf16[2,2,8,4,256,128]{5,4,3,2,1,0:T(8,128)(2,1)} %bitcast.24, bf16[2,2,8,64,16,128]{5,4,3,2,1,0:T(8,128)(2,1)} %bitcast.25, bf16[2,2,8,64,16,128]{5,4,3,2,1,0:T(8,128)(2,1)} %bitcast.26, bf16[2,2,8,64,16,128]{5,4,3,2,1,0:T(8,128)(2,1)} %bitcast.27, ...), custom_call_target="tpu_custom_call" | custom-call | flops 1476395008 | bytes 4194304 | tf_op jit(solution)/shard_map/pallas_call | solution.py:109
  36.1 8.4 %shard_map.79 = bf16[8,2,2,2,4,2,16,128]{7,6,5,4,3,2,1,0:T(8,128)(2,1)} custom-call(s32[1]{0:T(128)} %bitcast.refs_0_, bf16[2,2,8,4,256,128]{5,4,3,2,1,0:T(8,128)(2,1)} %bitcast.28, bf16[2,2,8,64,16,128]{5,4,3,2,1,0:T(8,128)(2,1)} %bitcast.29, bf16[2,2,8,64,16,128]{5,4,3,2,1,0:T(8,128)(2,1)} %bitcast.30, bf16[2,2,8,64,16,128]{5,4,3,2,1,0:T(8,128)(2,1)} %bitcast.31, ...), custom_call_target="tpu_custom_call" | custom-call | flops 1476395008 | bytes 4194304 | tf_op jit(solution)/shard_map/pallas_call | solution.py:109
  44.5 5.0 %gather_fusion = bf16[8,2,128,1024]{3,2,1,0:T(8,128)(2,1)} fusion(bf16[2,8,128,1024]{3,2,1,0:T(8,128)(2,1)} %bitcast.34, s32[1024]{0:T(1024)S(1)} %pad_clamp_fusion), kind=kCustom, calls=%fused_computation | custom fusion | bytes 8388640 | tf_op jit(solution)/shard_map/jit(_take)/gather | solution.py:198
  49.5 2.7 %copy.14 = bf16[2,8,128,1024]{3,2,1,0:T(8,128)(2,1)S(1)} copy(bf16[2,8,128,1024]{3,2,0,1:T(8,128)(2,1)} %bitcast.33) | data formatting | bytes 8388608 | tf_op jit(solution)/shard_map/jit(_take)/gather | solution.py:198
  52.2 0.1 broadcast_bitcast_fusion
  52.2 0.1 fusion.2
  52.3 2.4 %bitcast_select_fusion.refs_8_ = bf16[2,1,1024,1024]{3,2,1,0:T(8,128)(2,1)} fusion(pred[1024]{0:T(1024)(128)(4,1)S(1)} %broadcast_bitcast_fusion, bf16[2,1,1024,1024]{3,2,1,0:T(8,128)(2,1)S(1)} %bitcast.32), kind=kLoop, calls=%fused_computation.4 | loop fusion | flops 2097152 | bytes 8389632 | tf_op jit(solution)/shard_map/jit(_take)/select_n | solution.py:198
  54.8 3.7 %fusion.1.refs_9_ = bf16[1024,2048]{1,0:T(8,128)(2,1)} fusion(s32[2048]{0:T(1024)S(1)} %bitcast.35, pred[2048]{0:T(1024)(128)(4,1)S(1)} %fusion.2), kind=kLoop, calls=%fused_computation.3 | loop fusion | flops 6291456 | bytes 4204544 | tf_op jit(solution)/shard_map/convert_element_type | solution.py:192
  58.5 1.3 fusion.7
  59.8 0.9 collective-permute-start.5
  60.6 0.0 collective-permute-done.1.refs_2_
  60.7 1.5 collective-permute-start.6
  62.2 0.7 copy-done.15
  62.9 0.1 collective-permute-start.10
  63.0 1.2 fusion.8
  64.2 0.0 collective-permute-done.3.refs_4_
  64.2 2.9 %collective-permute-start.11 = (bf16[1,2,2,2,4,2,16,128]{7,6,5,4,3,2,1,0:T(8,128)(2,1)}, bf16[1,2,2,2,4,2,16,128]{7,6,5,4,3,2,1,0:T(8,128)(2,1)}, u32[]{:S(2)}, u32[]{:S(2)}) collective-permute-start(bf16[1,2,2,2,4,2,16,128]{7,6,5,4,3,2,1,0:T(8,128)(2,1)} %get-tuple-element.15), channel_id=1, source_target_pairs={{0,80},{16,96},{32,112},{48,0},{64,16},{80,32},{96,48},{112,64},{1... | collective-permute-start | bytes 786440 | tf_op jit(solution)/shard_map/ppermute | solution.py:206
  67.2 0.0 collective-permute-done.4.refs_5_
  67.2 0.5 collective-permute-start.12
  67.6 0.0 collective-permute-done.5.refs_6_
  67.7 2.4 %collective-permute-start.13 = (bf16[1,2,2,2,4,2,16,128]{7,6,5,4,3,2,1,0:T(8,128)(2,1)}, bf16[1,2,2,2,4,2,16,128]{7,6,5,4,3,2,1,0:T(8,128)(2,1)}, u32[]{:S(2)}, u32[]{:S(2)}) collective-permute-start(bf16[1,2,2,2,4,2,16,128]{7,6,5,4,3,2,1,0:T(8,128)(2,1)} %get-tuple-element.13), channel_id=1, source_target_pairs={{0,112},{16,0},{32,16},{48,32},{64,48},{80,64},{96,80},{112,96},{1... | collective-permute-start | bytes 786440 | tf_op jit(solution)/shard_map/ppermute | solution.py:206
  70.1 5.3 %collective-permute-done.6.refs_7_ = bf16[1,2,2,2,4,2,16,128]{7,6,5,4,3,2,1,0:T(8,128)(2,1)S(1)} collective-permute-done((bf16[1,2,2,2,4,2,16,128]{7,6,5,4,3,2,1,0:T(8,128)(2,1)S(1)}, bf16[1,2,2,2,4,2,16,128]{7,6,5,4,3,2,1,0:T(8,128)(2,1)S(1)}, u32[]{:S(2)}, u32[]{:S(2)}) %collective-permute-start.6) | collective-permute-done | bytes 262176 | tf_op jit(solution)/shard_map/ppermute | solution.py:206
  75.4 4.3 %collective-permute-start.8 = (bf16[1,2,2,2,4,2,16,128]{7,6,5,4,3,2,1,0:T(8,128)(2,1)}, bf16[1,2,2,2,4,2,16,128]{7,6,5,4,3,2,1,0:T(8,128)(2,1)}, u32[]{:S(2)}, u32[]{:S(2)}) collective-permute-start(bf16[1,2,2,2,4,2,16,128]{7,6,5,4,3,2,1,0:T(8,128)(2,1)} %get-tuple-element.18), channel_id=1, source_target_pairs={{0,32},{16,48},{32,64},{48,80},{64,96},{80,112},{96,0},{112,16},{1... | collective-permute-start | bytes 786440 | tf_op jit(solution)/shard_map/ppermute | solution.py:206
  79.8 10.9 %shard_map.74 = bf16[8,16,16,128]{3,2,1,0:T(8,128)(2,1)} custom-call(bf16[1,2,2,2,4,2,16,128]{7,6,5,4,3,2,1,0:T(8,128)(2,1)} %get-tuple-element.12.refs_0_, bf16[1,2,2,2,4,2,16,128]{7,6,5,4,3,2,1,0:T(8,128)(2,1)} %copy-done.13, bf16[1,2,2,2,4,2,16,128]{7,6,5,4,3,2,1,0:T(8,128)(2,1)} %copy-done.14, bf16[1,2,2,2,4,2,16,128]{7,6,5,4,3,2,1,0:T(8,128)(2,1)} %copy-done.15, ...), custom_call_target="tpu_custom_call" | custom-call | flops 4831838208 | bytes 11010048 | tf_op jit(solution)/shard_map/pallas_call | solution.py:166
  90.7 2.0 copy.15
  92.7 7.6 %all-to-all-start = ((bf16[8,16,16,128]{3,2,0,1:T(8,128)(2,1)}), bf16[8,16,16,128]{3,2,0,1:T(8,128)(2,1)S(1)}, u32[]{:S(2)}, u32[]{:S(2)}) async-start(bf16[8,16,16,128]{3,2,0,1:T(8,128)(2,1)} %copy.15), calls=%async_computation | async-start | bytes 1048576 | tf_op jit(solution)/shard_map/all_to_all | solution.py:208
  100.4 5.8 %collective-permute-start.9 = (bf16[1,2,2,2,4,2,16,128]{7,6,5,4,3,2,1,0:T(8,128)(2,1)}, bf16[1,2,2,2,4,2,16,128]{7,6,5,4,3,2,1,0:T(8,128)(2,1)S(1)}, u32[]{:S(2)}, u32[]{:S(2)}) collective-permute-start(bf16[1,2,2,2,4,2,16,128]{7,6,5,4,3,2,1,0:T(8,128)(2,1)} %get-tuple-element.17), channel_id=1, source_target_pairs={{0,48},{16,64},{32,80},{48,96},{64,112},{80,0},{96,16},{112,32},{1... | collective-permute-start | bytes 786440 | tf_op jit(solution)/shard_map/ppermute | solution.py:206
  106.2 0.1 collective-permute-start.15
  106.3 0.7 collective-permute-start.16
  107.0 2.6 %collective-permute-start.17 = (bf16[1,2,2,2,4,2,16,128]{7,6,5,4,3,2,1,0:T(8,128)(2,1)}, bf16[1,2,2,2,4,2,16,128]{7,6,5,4,3,2,1,0:T(8,128)(2,1)}, u32[]{:S(2)}, u32[]{:S(2)}) collective-permute-start(bf16[1,2,2,2,4,2,16,128]{7,6,5,4,3,2,1,0:T(8,128)(2,1)} %get-tuple-element.24), channel_id=1, source_target_pairs={{0,64},{16,80},{32,96},{48,112},{64,0},{80,16},{96,32},{112,48},{1... | collective-permute-start | bytes 786440 | tf_op jit(solution)/shard_map/ppermute | solution.py:206
  109.7 1.4 fusion.9
  111.0 4.0 %collective-permute-done.9.refs_3_ = bf16[1,2,2,2,4,2,16,128]{7,6,5,4,3,2,1,0:T(8,128)(2,1)S(1)} collective-permute-done((bf16[1,2,2,2,4,2,16,128]{7,6,5,4,3,2,1,0:T(8,128)(2,1)}, bf16[1,2,2,2,4,2,16,128]{7,6,5,4,3,2,1,0:T(8,128)(2,1)S(1)}, u32[]{:S(2)}, u32[]{:S(2)}) %collective-permute-start.9) | collective-permute-done | bytes 262176 | tf_op jit(solution)/shard_map/ppermute | solution.py:206
  115.0 2.5 %collective-permute-done.14.refs_1_ = bf16[1,2,2,2,4,2,16,128]{7,6,5,4,3,2,1,0:T(8,128)(2,1)S(1)} collective-permute-done((bf16[1,2,2,2,4,2,16,128]{7,6,5,4,3,2,1,0:T(8,128)(2,1)}, bf16[1,2,2,2,4,2,16,128]{7,6,5,4,3,2,1,0:T(8,128)(2,1)S(1)}, u32[]{:S(2)}, u32[]{:S(2)}) %collective-permute-start.14) | collective-permute-done | bytes 262176 | tf_op jit(solution)/shard_map/ppermute | solution.py:206
  117.5 5.6 %collective-permute-done.15.refs_2_ = bf16[1,2,2,2,4,2,16,128]{7,6,5,4,3,2,1,0:T(8,128)(2,1)S(1)} collective-permute-done((bf16[1,2,2,2,4,2,16,128]{7,6,5,4,3,2,1,0:T(8,128)(2,1)}, bf16[1,2,2,2,4,2,16,128]{7,6,5,4,3,2,1,0:T(8,128)(2,1)S(1)}, u32[]{:S(2)}, u32[]{:S(2)}) %collective-permute-start.15) | collective-permute-done | bytes 262176 | tf_op jit(solution)/shard_map/ppermute | solution.py:206
  123.1 5.6 %collective-permute-done.16.refs_3_ = bf16[1,2,2,2,4,2,16,128]{7,6,5,4,3,2,1,0:T(8,128)(2,1)S(1)} collective-permute-done((bf16[1,2,2,2,4,2,16,128]{7,6,5,4,3,2,1,0:T(8,128)(2,1)}, bf16[1,2,2,2,4,2,16,128]{7,6,5,4,3,2,1,0:T(8,128)(2,1)S(1)}, u32[]{:S(2)}, u32[]{:S(2)}) %collective-permute-start.16) | collective-permute-done | bytes 262176 | tf_op jit(solution)/shard_map/ppermute | solution.py:206
  128.8 0.7 copy-done.12
  129.5 4.2 %collective-permute-done.17.refs_4_ = bf16[1,2,2,2,4,2,16,128]{7,6,5,4,3,2,1,0:T(8,128)(2,1)} collective-permute-done((bf16[1,2,2,2,4,2,16,128]{7,6,5,4,3,2,1,0:T(8,128)(2,1)}, bf16[1,2,2,2,4,2,16,128]{7,6,5,4,3,2,1,0:T(8,128)(2,1)}, u32[]{:S(2)}, u32[]{:S(2)}) %collective-permute-start.17) | collective-permute-done | bytes 262176 | tf_op jit(solution)/shard_map/ppermute | solution.py:206
  133.7 10.9 %shard_map.76 = bf16[8,16,16,128]{3,2,1,0:T(8,128)(2,1)} custom-call(bf16[1,2,2,2,4,2,16,128]{7,6,5,4,3,2,1,0:T(8,128)(2,1)} %get-tuple-element.20.refs_0_, bf16[1,2,2,2,4,2,16,128]{7,6,5,4,3,2,1,0:T(8,128)(2,1)} %collective-permute-done.7.refs_1_, bf16[1,2,2,2,4,2,16,128]{7,6,5,4,3,2,1,0:T(8,128)(2,1)} %collective-permute-done.8.refs_2_, ...), custom_call_target="tpu_custom_call" | custom-call | flops 4831838208 | bytes 11010048 | tf_op jit(solution)/shard_map/pallas_call | solution.py:166
  144.6 2.0 copy.16
  146.6 6.9 %all-to-all-start.1 = ((bf16[8,16,16,128]{3,2,0,1:T(8,128)(2,1)}), bf16[8,16,16,128]{3,2,0,1:T(8,128)(2,1)S(1)}, u32[]{:S(2)}, u32[]{:S(2)}) async-start(bf16[8,16,16,128]{3,2,0,1:T(8,128)(2,1)} %copy.16), calls=%async_computation.1 | async-start | bytes 1048576 | tf_op jit(solution)/shard_map/all_to_all | solution.py:208
  153.5 0.1 collective-permute-start.23
  153.7 2.4 %collective-permute-start.24 = (bf16[1,2,2,2,4,2,16,128]{7,6,5,4,3,2,1,0:T(8,128)(2,1)S(1)}, bf16[1,2,2,2,4,2,16,128]{7,6,5,4,3,2,1,0:T(8,128)(2,1)S(1)}, u32[]{:S(2)}, u32[]{:S(2)}) collective-permute-start(bf16[1,2,2,2,4,2,16,128]{7,6,5,4,3,2,1,0:T(8,128)(2,1)S(1)} %copy-done.6), channel_id=1, source_target_pairs={{0,64},{16,80},{32,96},{48,112},{64,0},{80,16},{96,32},{112,48},{1... | collective-permute-start | bytes 786440 | tf_op jit(solution)/shard_map/ppermute | solution.py:206
  156.1 2.5 %collective-permute-start.25 = (bf16[1,2,2,2,4,2,16,128]{7,6,5,4,3,2,1,0:T(8,128)(2,1)S(1)}, bf16[1,2,2,2,4,2,16,128]{7,6,5,4,3,2,1,0:T(8,128)(2,1)S(1)}, u32[]{:S(2)}, u32[]{:S(2)}) collective-permute-start(bf16[1,2,2,2,4,2,16,128]{7,6,5,4,3,2,1,0:T(8,128)(2,1)S(1)} %copy-done.5), channel_id=1, source_target_pairs={{0,80},{16,96},{32,112},{48,0},{64,16},{80,32},{96,48},{112,64},{1... | collective-permute-start | bytes 786440 | tf_op jit(solution)/shard_map/ppermute | solution.py:206
  158.6 0.9 collective-permute-start.26
  159.6 0.6 collective-permute-start.27
  160.1 10.9 %shard_map.78 = bf16[8,16,16,128]{3,2,1,0:T(8,128)(2,1)} custom-call(bf16[1,2,2,2,4,2,16,128]{7,6,5,4,3,2,1,0:T(8,128)(2,1)} %get-tuple-element.28.refs_0_, bf16[1,2,2,2,4,2,16,128]{7,6,5,4,3,2,1,0:T(8,128)(2,1)} %copy-done.10, bf16[1,2,2,2,4,2,16,128]{7,6,5,4,3,2,1,0:T(8,128)(2,1)} %copy-done.11, bf16[1,2,2,2,4,2,16,128]{7,6,5,4,3,2,1,0:T(8,128)(2,1)} %copy-done.12, ...), custom_call_target="tpu_custom_call" | custom-call | flops 4831838208 | bytes 11010048 | tf_op jit(solution)/shard_map/pallas_call | solution.py:166
  171.1 1.9 copy.17
  173.0 6.7 %all-to-all-start.2 = ((bf16[8,16,16,128]{3,2,0,1:T(8,128)(2,1)}), bf16[8,16,16,128]{3,2,0,1:T(8,128)(2,1)S(1)}, u32[]{:S(2)}, u32[]{:S(2)}) async-start(bf16[8,16,16,128]{3,2,0,1:T(8,128)(2,1)} %copy.17), calls=%async_computation.2 | async-start | bytes 1048576 | tf_op jit(solution)/shard_map/all_to_all | solution.py:208
  179.7 0.6 copy-done.19
  180.4 0.1 copy-done.21
  180.4 0.1 copy-done.23
  180.5 10.9 %shard_map.80 = bf16[8,16,16,128]{3,2,1,0:T(8,128)(2,1)} custom-call(bf16[1,2,2,2,4,2,16,128]{7,6,5,4,3,2,1,0:T(8,128)(2,1)} %get-tuple-element.36.refs_0_, bf16[1,2,2,2,4,2,16,128]{7,6,5,4,3,2,1,0:T(8,128)(2,1)} %copy-done.16, bf16[1,2,2,2,4,2,16,128]{7,6,5,4,3,2,1,0:T(8,128)(2,1)} %copy-done.17, bf16[1,2,2,2,4,2,16,128]{7,6,5,4,3,2,1,0:T(8,128)(2,1)} %copy-done.19, ...), custom_call_target="tpu_custom_call" | custom-call | flops 4831838208 | bytes 11010048 | tf_op jit(solution)/shard_map/pallas_call | solution.py:166
  191.5 1.1 copy.18
  192.6 16.9 %all_to_all.20 = bf16[8,16,16,128]{3,2,0,1:T(8,128)(2,1)S(1)} all-to-all(bf16[8,16,16,128]{3,2,0,1:T(8,128)(2,1)S(1)} %copy.18), channel_id=1, replica_groups=mesh['feed'=8,'chan'=16] {'chan'}, dimensions={1} | all-to-all | bytes 1048576 | tf_op jit(solution)/shard_map/all_to_all | solution.py:208
  209.5 0.3 pad_maximum_fusion
  209.7 1.9 copy.23
  (74 shorter events, 0.2 us)
Async XLA Ops:
  11.2 48.6 %collective-permute-start = (bf16[1,2,2,2,4,2,16,128]{7,6,5,4,3,2,1,0:T(8,128)(2,1)S(1)}, bf16[1,2,2,2,4,2,16,128]{7,6,5,4,3,2,1,0:T(8,128)(2,1)S(1)}, u32[]{:S(2)}, u32[]{:S(2)}) collective-permute-start(bf16[1,2,2,2,4,2,16,128]{7,6,5,4,3,2,1,0:T(8,128)(2,1)S(1)} %get-tuple-element.11), channel_id=1, source_target_pairs={{0,16},{16,32},{32,48},{48,64},{64,80},{80,96},{96,112},{112,0},{1... | collective-permute-start | bytes 786440 | tf_op jit(solution)/shard_map/ppermute | solution.py:206
  13.8 46.8 %collective-permute-start.1 = (bf16[1,2,2,2,4,2,16,128]{7,6,5,4,3,2,1,0:T(8,128)(2,1)S(1)}, bf16[1,2,2,2,4,2,16,128]{7,6,5,4,3,2,1,0:T(8,128)(2,1)S(1)}, u32[]{:S(2)}, u32[]{:S(2)}) collective-permute-start(bf16[1,2,2,2,4,2,16,128]{7,6,5,4,3,2,1,0:T(8,128)(2,1)S(1)} %get-tuple-element.10), channel_id=1, source_target_pairs={{0,32},{16,48},{32,64},{48,80},{64,96},{80,112},{96,0},{112,16},{1... | collective-permute-start | bytes 786440 | tf_op jit(solution)/shard_map/ppermute | solution.py:206
  15.1 47.0 %collective-permute-start.2 = (bf16[1,2,2,2,4,2,16,128]{7,6,5,4,3,2,1,0:T(8,128)(2,1)S(1)}, bf16[1,2,2,2,4,2,16,128]{7,6,5,4,3,2,1,0:T(8,128)(2,1)S(1)}, u32[]{:S(2)}, u32[]{:S(2)}) collective-permute-start(bf16[1,2,2,2,4,2,16,128]{7,6,5,4,3,2,1,0:T(8,128)(2,1)S(1)} %get-tuple-element.9), channel_id=1, source_target_pairs={{0,48},{16,64},{32,80},{48,96},{64,112},{80,0},{96,16},{112,32},{1... | collective-permute-start | bytes 786440 | tf_op jit(solution)/shard_map/ppermute | solution.py:206
  16.8 47.5 %collective-permute-start.3 = (bf16[1,2,2,2,4,2,16,128]{7,6,5,4,3,2,1,0:T(8,128)(2,1)S(1)}, bf16[1,2,2,2,4,2,16,128]{7,6,5,4,3,2,1,0:T(8,128)(2,1)}, u32[]{:S(2)}, u32[]{:S(2)}) collective-permute-start(bf16[1,2,2,2,4,2,16,128]{7,6,5,4,3,2,1,0:T(8,128)(2,1)S(1)} %get-tuple-element.8), channel_id=1, source_target_pairs={{0,64},{16,80},{32,96},{48,112},{64,0},{80,16},{96,32},{112,48},{1... | collective-permute-start | bytes 786440 | tf_op jit(solution)/shard_map/ppermute | solution.py:206
  17.1 50.1 %collective-permute-start.4 = (bf16[1,2,2,2,4,2,16,128]{7,6,5,4,3,2,1,0:T(8,128)(2,1)S(1)}, bf16[1,2,2,2,4,2,16,128]{7,6,5,4,3,2,1,0:T(8,128)(2,1)}, u32[]{:S(2)}, u32[]{:S(2)}) collective-permute-start(bf16[1,2,2,2,4,2,16,128]{7,6,5,4,3,2,1,0:T(8,128)(2,1)S(1)} %get-tuple-element.7), channel_id=1, source_target_pairs={{0,80},{16,96},{32,112},{48,0},{64,16},{80,32},{96,48},{112,64},{1... | collective-permute-start | bytes 786440 | tf_op jit(solution)/shard_map/ppermute | solution.py:206
  49.5 2.8 %copy-start.8 = (s32[16]{0:T(128)S(1)}, s32[16]{0:T(128)}, u32[]{:S(2)}) copy-start(s32[16]{0:T(128)} %param.12) | copy-start | bytes 196
  52.3 2.4 %copy-start.7 = (s32[16,128]{1,0:T(8,128)S(1)}, s32[16,128]{1,0:T(8,128)}, u32[]{:S(2)}) copy-start(s32[16,128]{1,0:T(8,128)} %param.11) | copy-start | bytes 24580
  54.8 3.7 %copy-start.2 = (bf16[8,2,2,2,4,2,16,128]{7,6,5,4,3,2,1,0:T(8,128)(2,1)S(1)}, bf16[8,2,2,2,4,2,16,128]{7,6,5,4,3,2,1,0:T(8,128)(2,1)}, u32[]{:S(2)}) copy-start(bf16[8,2,2,2,4,2,16,128]{7,6,5,4,3,2,1,0:T(8,128)(2,1)} %shard_map.75) | copy-start | bytes 6291460
  58.5 4.6 %copy-start.1 = (bf16[8,2,2,2,4,2,16,128]{7,6,5,4,3,2,1,0:T(8,128)(2,1)S(1)}, bf16[8,2,2,2,4,2,16,128]{7,6,5,4,3,2,1,0:T(8,128)(2,1)}, u32[]{:S(2)}) copy-start(bf16[8,2,2,2,4,2,16,128]{7,6,5,4,3,2,1,0:T(8,128)(2,1)} %shard_map.77) | copy-start | bytes 6291460
  59.8 4.5 %copy-start.13 = (bf16[1,2,2,2,4,2,16,128]{7,6,5,4,3,2,1,0:T(8,128)(2,1)}, bf16[1,2,2,2,4,2,16,128]{7,6,5,4,3,2,1,0:T(8,128)(2,1)S(1)}, u32[]{:S(2)}) copy-start(bf16[1,2,2,2,4,2,16,128]{7,6,5,4,3,2,1,0:T(8,128)(2,1)S(1)} %collective-permute-done.refs_1_) | copy-start | bytes 786436
  59.8 7.9 %collective-permute-start.5 = (bf16[1,2,2,2,4,2,16,128]{7,6,5,4,3,2,1,0:T(8,128)(2,1)S(1)}, bf16[1,2,2,2,4,2,16,128]{7,6,5,4,3,2,1,0:T(8,128)(2,1)S(1)}, u32[]{:S(2)}, u32[]{:S(2)}) collective-permute-start(bf16[1,2,2,2,4,2,16,128]{7,6,5,4,3,2,1,0:T(8,128)(2,1)S(1)} %get-tuple-element.6), channel_id=1, source_target_pairs={{0,96},{16,112},{32,0},{48,16},{64,32},{80,48},{96,64},{112,80},{1... | collective-permute-start | bytes 786440 | tf_op jit(solution)/shard_map/ppermute | solution.py:206
  60.6 3.6 %copy-start.14 = (bf16[1,2,2,2,4,2,16,128]{7,6,5,4,3,2,1,0:T(8,128)(2,1)}, bf16[1,2,2,2,4,2,16,128]{7,6,5,4,3,2,1,0:T(8,128)(2,1)S(1)}, u32[]{:S(2)}) copy-start(bf16[1,2,2,2,4,2,16,128]{7,6,5,4,3,2,1,0:T(8,128)(2,1)S(1)} %collective-permute-done.1.refs_2_) | copy-start | bytes 786436
  60.7 14.8 %collective-permute-start.6 = (bf16[1,2,2,2,4,2,16,128]{7,6,5,4,3,2,1,0:T(8,128)(2,1)S(1)}, bf16[1,2,2,2,4,2,16,128]{7,6,5,4,3,2,1,0:T(8,128)(2,1)S(1)}, u32[]{:S(2)}, u32[]{:S(2)}) collective-permute-start(bf16[1,2,2,2,4,2,16,128]{7,6,5,4,3,2,1,0:T(8,128)(2,1)S(1)} %get-tuple-element.5), channel_id=1, source_target_pairs={{0,112},{16,0},{32,16},{48,32},{64,48},{80,64},{96,80},{112,96},{1... | collective-permute-start | bytes 786440 | tf_op jit(solution)/shard_map/ppermute | solution.py:206
  62.2 0.7 copy-start.15
  62.9 12.5 %collective-permute-start.10 = (bf16[1,2,2,2,4,2,16,128]{7,6,5,4,3,2,1,0:T(8,128)(2,1)S(1)}, bf16[1,2,2,2,4,2,16,128]{7,6,5,4,3,2,1,0:T(8,128)(2,1)S(1)}, u32[]{:S(2)}, u32[]{:S(2)}) collective-permute-start(bf16[1,2,2,2,4,2,16,128]{7,6,5,4,3,2,1,0:T(8,128)(2,1)S(1)} %get-tuple-element.16), channel_id=1, source_target_pairs={{0,64},{16,80},{32,96},{48,112},{64,0},{80,16},{96,32},{112,48},{1... | collective-permute-start | bytes 786440 | tf_op jit(solution)/shard_map/ppermute | solution.py:206
  64.2 36.1 %collective-permute-start.11 = (bf16[1,2,2,2,4,2,16,128]{7,6,5,4,3,2,1,0:T(8,128)(2,1)}, bf16[1,2,2,2,4,2,16,128]{7,6,5,4,3,2,1,0:T(8,128)(2,1)}, u32[]{:S(2)}, u32[]{:S(2)}) collective-permute-start(bf16[1,2,2,2,4,2,16,128]{7,6,5,4,3,2,1,0:T(8,128)(2,1)} %get-tuple-element.15), channel_id=1, source_target_pairs={{0,80},{16,96},{32,112},{48,0},{64,16},{80,32},{96,48},{112,64},{1... | collective-permute-start | bytes 786440 | tf_op jit(solution)/shard_map/ppermute | solution.py:206
  67.2 39.0 %collective-permute-start.12 = (bf16[1,2,2,2,4,2,16,128]{7,6,5,4,3,2,1,0:T(8,128)(2,1)}, bf16[1,2,2,2,4,2,16,128]{7,6,5,4,3,2,1,0:T(8,128)(2,1)}, u32[]{:S(2)}, u32[]{:S(2)}) collective-permute-start(bf16[1,2,2,2,4,2,16,128]{7,6,5,4,3,2,1,0:T(8,128)(2,1)} %get-tuple-element.14), channel_id=1, source_target_pairs={{0,96},{16,112},{32,0},{48,16},{64,32},{80,48},{96,64},{112,80},{1... | collective-permute-start | bytes 786440 | tf_op jit(solution)/shard_map/ppermute | solution.py:206
  67.6 12.1 %copy-start.20 = (bf16[1,2,2,2,4,2,16,128]{7,6,5,4,3,2,1,0:T(8,128)(2,1)}, bf16[1,2,2,2,4,2,16,128]{7,6,5,4,3,2,1,0:T(8,128)(2,1)S(1)}, u32[]{:S(2)}) copy-start(bf16[1,2,2,2,4,2,16,128]{7,6,5,4,3,2,1,0:T(8,128)(2,1)S(1)} %collective-permute-done.5.refs_6_) | copy-start | bytes 786436
  67.7 38.6 %collective-permute-start.13 = (bf16[1,2,2,2,4,2,16,128]{7,6,5,4,3,2,1,0:T(8,128)(2,1)}, bf16[1,2,2,2,4,2,16,128]{7,6,5,4,3,2,1,0:T(8,128)(2,1)}, u32[]{:S(2)}, u32[]{:S(2)}) collective-permute-start(bf16[1,2,2,2,4,2,16,128]{7,6,5,4,3,2,1,0:T(8,128)(2,1)} %get-tuple-element.13), channel_id=1, source_target_pairs={{0,112},{16,0},{32,16},{48,32},{64,48},{80,64},{96,80},{112,96},{1... | collective-permute-start | bytes 786440 | tf_op jit(solution)/shard_map/ppermute | solution.py:206
  75.4 4.3 %copy-start.22 = (bf16[1,2,2,2,4,2,16,128]{7,6,5,4,3,2,1,0:T(8,128)(2,1)}, bf16[1,2,2,2,4,2,16,128]{7,6,5,4,3,2,1,0:T(8,128)(2,1)S(1)}, u32[]{:S(2)}) copy-start(bf16[1,2,2,2,4,2,16,128]{7,6,5,4,3,2,1,0:T(8,128)(2,1)S(1)} %collective-permute-done.6.refs_7_) | copy-start | bytes 786436
  75.4 30.9 %collective-permute-start.7 = (bf16[1,2,2,2,4,2,16,128]{7,6,5,4,3,2,1,0:T(8,128)(2,1)}, bf16[1,2,2,2,4,2,16,128]{7,6,5,4,3,2,1,0:T(8,128)(2,1)}, u32[]{:S(2)}, u32[]{:S(2)}) collective-permute-start(bf16[1,2,2,2,4,2,16,128]{7,6,5,4,3,2,1,0:T(8,128)(2,1)} %get-tuple-element.19), channel_id=1, source_target_pairs={{0,16},{16,32},{32,48},{48,64},{64,80},{80,96},{96,112},{112,0},{1... | collective-permute-start | bytes 786440 | tf_op jit(solution)/shard_map/ppermute | solution.py:206
  75.4 4.3 %copy-start.9 = (bf16[1,2,2,2,4,2,16,128]{7,6,5,4,3,2,1,0:T(8,128)(2,1)}, bf16[1,2,2,2,4,2,16,128]{7,6,5,4,3,2,1,0:T(8,128)(2,1)S(1)}, u32[]{:S(2)}) copy-start(bf16[1,2,2,2,4,2,16,128]{7,6,5,4,3,2,1,0:T(8,128)(2,1)S(1)} %collective-permute-done.10.refs_4_) | copy-start | bytes 786436
  75.4 31.6 %collective-permute-start.8 = (bf16[1,2,2,2,4,2,16,128]{7,6,5,4,3,2,1,0:T(8,128)(2,1)}, bf16[1,2,2,2,4,2,16,128]{7,6,5,4,3,2,1,0:T(8,128)(2,1)}, u32[]{:S(2)}, u32[]{:S(2)}) collective-permute-start(bf16[1,2,2,2,4,2,16,128]{7,6,5,4,3,2,1,0:T(8,128)(2,1)} %get-tuple-element.18), channel_id=1, source_target_pairs={{0,32},{16,48},{32,64},{48,80},{64,96},{80,112},{96,0},{112,16},{1... | collective-permute-start | bytes 786440 | tf_op jit(solution)/shard_map/ppermute | solution.py:206
  90.7 19.0 %copy-start = (bf16[8,2,2,2,4,2,16,128]{7,6,5,4,3,2,1,0:T(8,128)(2,1)S(1)}, bf16[8,2,2,2,4,2,16,128]{7,6,5,4,3,2,1,0:T(8,128)(2,1)}, u32[]{:S(2)}) copy-start(bf16[8,2,2,2,4,2,16,128]{7,6,5,4,3,2,1,0:T(8,128)(2,1)} %shard_map.79) | copy-start | bytes 6291460
  92.7 53.9 %all-to-all-start = ((bf16[8,16,16,128]{3,2,0,1:T(8,128)(2,1)}), bf16[8,16,16,128]{3,2,0,1:T(8,128)(2,1)S(1)}, u32[]{:S(2)}, u32[]{:S(2)}) async-start(bf16[8,16,16,128]{3,2,0,1:T(8,128)(2,1)} %copy.15), calls=%async_computation | async-start | bytes 1048576 | tf_op jit(solution)/shard_map/all_to_all | solution.py:208
  100.4 14.7 %collective-permute-start.9 = (bf16[1,2,2,2,4,2,16,128]{7,6,5,4,3,2,1,0:T(8,128)(2,1)}, bf16[1,2,2,2,4,2,16,128]{7,6,5,4,3,2,1,0:T(8,128)(2,1)S(1)}, u32[]{:S(2)}, u32[]{:S(2)}) collective-permute-start(bf16[1,2,2,2,4,2,16,128]{7,6,5,4,3,2,1,0:T(8,128)(2,1)} %get-tuple-element.17), channel_id=1, source_target_pairs={{0,48},{16,64},{32,80},{48,96},{64,112},{80,0},{96,16},{112,32},{1... | collective-permute-start | bytes 786440 | tf_op jit(solution)/shard_map/ppermute | solution.py:206
  106.2 11.3 %collective-permute-start.14 = (bf16[1,2,2,2,4,2,16,128]{7,6,5,4,3,2,1,0:T(8,128)(2,1)}, bf16[1,2,2,2,4,2,16,128]{7,6,5,4,3,2,1,0:T(8,128)(2,1)S(1)}, u32[]{:S(2)}, u32[]{:S(2)}) collective-permute-start(bf16[1,2,2,2,4,2,16,128]{7,6,5,4,3,2,1,0:T(8,128)(2,1)} %get-tuple-element.27), channel_id=1, source_target_pairs={{0,16},{16,32},{32,48},{48,64},{64,80},{80,96},{96,112},{112,0},{1... | collective-permute-start | bytes 786440 | tf_op jit(solution)/shard_map/ppermute | solution.py:206
  106.2 16.9 %collective-permute-start.15 = (bf16[1,2,2,2,4,2,16,128]{7,6,5,4,3,2,1,0:T(8,128)(2,1)}, bf16[1,2,2,2,4,2,16,128]{7,6,5,4,3,2,1,0:T(8,128)(2,1)S(1)}, u32[]{:S(2)}, u32[]{:S(2)}) collective-permute-start(bf16[1,2,2,2,4,2,16,128]{7,6,5,4,3,2,1,0:T(8,128)(2,1)} %get-tuple-element.26), channel_id=1, source_target_pairs={{0,32},{16,48},{32,64},{48,80},{64,96},{80,112},{96,0},{112,16},{1... | collective-permute-start | bytes 786440 | tf_op jit(solution)/shard_map/ppermute | solution.py:206
  106.3 22.4 %collective-permute-start.16 = (bf16[1,2,2,2,4,2,16,128]{7,6,5,4,3,2,1,0:T(8,128)(2,1)}, bf16[1,2,2,2,4,2,16,128]{7,6,5,4,3,2,1,0:T(8,128)(2,1)S(1)}, u32[]{:S(2)}, u32[]{:S(2)}) collective-permute-start(bf16[1,2,2,2,4,2,16,128]{7,6,5,4,3,2,1,0:T(8,128)(2,1)} %get-tuple-element.25), channel_id=1, source_target_pairs={{0,48},{16,64},{32,80},{48,96},{64,112},{80,0},{96,16},{112,32},{1... | collective-permute-start | bytes 786440 | tf_op jit(solution)/shard_map/ppermute | solution.py:206
  107.0 26.6 %collective-permute-start.17 = (bf16[1,2,2,2,4,2,16,128]{7,6,5,4,3,2,1,0:T(8,128)(2,1)}, bf16[1,2,2,2,4,2,16,128]{7,6,5,4,3,2,1,0:T(8,128)(2,1)}, u32[]{:S(2)}, u32[]{:S(2)}) collective-permute-start(bf16[1,2,2,2,4,2,16,128]{7,6,5,4,3,2,1,0:T(8,128)(2,1)} %get-tuple-element.24), channel_id=1, source_target_pairs={{0,64},{16,80},{32,96},{48,112},{64,0},{80,16},{96,32},{112,48},{1... | collective-permute-start | bytes 786440 | tf_op jit(solution)/shard_map/ppermute | solution.py:206
  115.0 18.6 %copy-start.18 = (bf16[1,2,2,2,4,2,16,128]{7,6,5,4,3,2,1,0:T(8,128)(2,1)}, bf16[1,2,2,2,4,2,16,128]{7,6,5,4,3,2,1,0:T(8,128)(2,1)S(1)}, u32[]{:S(2)}) copy-start(bf16[1,2,2,2,4,2,16,128]{7,6,5,4,3,2,1,0:T(8,128)(2,1)S(1)} %collective-permute-done.9.refs_3_) | copy-start | bytes 786436
  115.0 38.5 %collective-permute-start.18 = (bf16[1,2,2,2,4,2,16,128]{7,6,5,4,3,2,1,0:T(8,128)(2,1)S(1)}, bf16[1,2,2,2,4,2,16,128]{7,6,5,4,3,2,1,0:T(8,128)(2,1)}, u32[]{:S(2)}, u32[]{:S(2)}) collective-permute-start(bf16[1,2,2,2,4,2,16,128]{7,6,5,4,3,2,1,0:T(8,128)(2,1)S(1)} %get-tuple-element.23), channel_id=1, source_target_pairs={{0,80},{16,96},{32,112},{48,0},{64,16},{80,32},{96,48},{112,64},{1... | collective-permute-start | bytes 786440 | tf_op jit(solution)/shard_map/ppermute | solution.py:206
  117.5 5.6 %copy-start.10 = (bf16[1,2,2,2,4,2,16,128]{7,6,5,4,3,2,1,0:T(8,128)(2,1)}, bf16[1,2,2,2,4,2,16,128]{7,6,5,4,3,2,1,0:T(8,128)(2,1)S(1)}, u32[]{:S(2)}) copy-start(bf16[1,2,2,2,4,2,16,128]{7,6,5,4,3,2,1,0:T(8,128)(2,1)S(1)} %collective-permute-done.14.refs_1_) | copy-start | bytes 786436
  117.5 36.1 %collective-permute-start.19 = (bf16[1,2,2,2,4,2,16,128]{7,6,5,4,3,2,1,0:T(8,128)(2,1)S(1)}, bf16[1,2,2,2,4,2,16,128]{7,6,5,4,3,2,1,0:T(8,128)(2,1)}, u32[]{:S(2)}, u32[]{:S(2)}) collective-permute-start(bf16[1,2,2,2,4,2,16,128]{7,6,5,4,3,2,1,0:T(8,128)(2,1)S(1)} %get-tuple-element.22), channel_id=1, source_target_pairs={{0,96},{16,112},{32,0},{48,16},{64,32},{80,48},{96,64},{112,80},{1... | collective-permute-start | bytes 786440 | tf_op jit(solution)/shard_map/ppermute | solution.py:206
  123.1 5.6 %copy-start.11 = (bf16[1,2,2,2,4,2,16,128]{7,6,5,4,3,2,1,0:T(8,128)(2,1)}, bf16[1,2,2,2,4,2,16,128]{7,6,5,4,3,2,1,0:T(8,128)(2,1)S(1)}, u32[]{:S(2)}) copy-start(bf16[1,2,2,2,4,2,16,128]{7,6,5,4,3,2,1,0:T(8,128)(2,1)S(1)} %collective-permute-done.15.refs_2_) | copy-start | bytes 786436
  123.1 33.0 %collective-permute-start.20 = (bf16[1,2,2,2,4,2,16,128]{7,6,5,4,3,2,1,0:T(8,128)(2,1)S(1)}, bf16[1,2,2,2,4,2,16,128]{7,6,5,4,3,2,1,0:T(8,128)(2,1)}, u32[]{:S(2)}, u32[]{:S(2)}) collective-permute-start(bf16[1,2,2,2,4,2,16,128]{7,6,5,4,3,2,1,0:T(8,128)(2,1)S(1)} %get-tuple-element.21), channel_id=1, source_target_pairs={{0,112},{16,0},{32,16},{48,32},{64,48},{80,64},{96,80},{112,96},{1... | collective-permute-start | bytes 786440 | tf_op jit(solution)/shard_map/ppermute | solution.py:206
  128.8 0.7 copy-start.12
  129.5 29.2 %collective-permute-start.21 = (bf16[1,2,2,2,4,2,16,128]{7,6,5,4,3,2,1,0:T(8,128)(2,1)}, bf16[1,2,2,2,4,2,16,128]{7,6,5,4,3,2,1,0:T(8,128)(2,1)S(1)}, u32[]{:S(2)}, u32[]{:S(2)}) collective-permute-start(bf16[1,2,2,2,4,2,16,128]{7,6,5,4,3,2,1,0:T(8,128)(2,1)} %get-tuple-element.35), channel_id=1, source_target_pairs={{0,16},{16,32},{32,48},{48,64},{64,80},{80,96},{96,112},{112,0},{1... | collective-permute-start | bytes 786440 | tf_op jit(solution)/shard_map/ppermute | solution.py:206
  133.6 25.9 %collective-permute-start.22 = (bf16[1,2,2,2,4,2,16,128]{7,6,5,4,3,2,1,0:T(8,128)(2,1)}, bf16[1,2,2,2,4,2,16,128]{7,6,5,4,3,2,1,0:T(8,128)(2,1)S(1)}, u32[]{:S(2)}, u32[]{:S(2)}) collective-permute-start(bf16[1,2,2,2,4,2,16,128]{7,6,5,4,3,2,1,0:T(8,128)(2,1)} %get-tuple-element.34), channel_id=1, source_target_pairs={{0,32},{16,48},{32,64},{48,80},{64,96},{80,112},{96,0},{112,16},{1... | collective-permute-start | bytes 786440 | tf_op jit(solution)/shard_map/ppermute | solution.py:206
  144.6 9.0 %copy-start.6 = (bf16[1,2,2,2,4,2,16,128]{7,6,5,4,3,2,1,0:T(8,128)(2,1)S(1)}, bf16[1,2,2,2,4,2,16,128]{7,6,5,4,3,2,1,0:T(8,128)(2,1)}, u32[]{:S(2)}) copy-start(bf16[1,2,2,2,4,2,16,128]{7,6,5,4,3,2,1,0:T(8,128)(2,1)} %get-tuple-element.32) | copy-start | bytes 786436
  144.6 11.5 %copy-start.5 = (bf16[1,2,2,2,4,2,16,128]{7,6,5,4,3,2,1,0:T(8,128)(2,1)S(1)}, bf16[1,2,2,2,4,2,16,128]{7,6,5,4,3,2,1,0:T(8,128)(2,1)}, u32[]{:S(2)}) copy-start(bf16[1,2,2,2,4,2,16,128]{7,6,5,4,3,2,1,0:T(8,128)(2,1)} %get-tuple-element.31) | copy-start | bytes 786436
  144.6 14.0 %copy-start.4 = (bf16[1,2,2,2,4,2,16,128]{7,6,5,4,3,2,1,0:T(8,128)(2,1)S(1)}, bf16[1,2,2,2,4,2,16,128]{7,6,5,4,3,2,1,0:T(8,128)(2,1)}, u32[]{:S(2)}) copy-start(bf16[1,2,2,2,4,2,16,128]{7,6,5,4,3,2,1,0:T(8,128)(2,1)} %get-tuple-element.30) | copy-start | bytes 786436
  144.6 14.9 %copy-start.3 = (bf16[1,2,2,2,4,2,16,128]{7,6,5,4,3,2,1,0:T(8,128)(2,1)S(1)}, bf16[1,2,2,2,4,2,16,128]{7,6,5,4,3,2,1,0:T(8,128)(2,1)}, u32[]{:S(2)}) copy-start(bf16[1,2,2,2,4,2,16,128]{7,6,5,4,3,2,1,0:T(8,128)(2,1)} %get-tuple-element.29) | copy-start | bytes 786436
  146.6 26.4 %all-to-all-start.1 = ((bf16[8,16,16,128]{3,2,0,1:T(8,128)(2,1)}), bf16[8,16,16,128]{3,2,0,1:T(8,128)(2,1)S(1)}, u32[]{:S(2)}, u32[]{:S(2)}) async-start(bf16[8,16,16,128]{3,2,0,1:T(8,128)(2,1)} %copy.16), calls=%async_computation.1 | async-start | bytes 1048576 | tf_op jit(solution)/shard_map/all_to_all | solution.py:208
  153.5 26.1 %collective-permute-start.23 = (bf16[1,2,2,2,4,2,16,128]{7,6,5,4,3,2,1,0:T(8,128)(2,1)}, bf16[1,2,2,2,4,2,16,128]{7,6,5,4,3,2,1,0:T(8,128)(2,1)S(1)}, u32[]{:S(2)}, u32[]{:S(2)}) collective-permute-start(bf16[1,2,2,2,4,2,16,128]{7,6,5,4,3,2,1,0:T(8,128)(2,1)} %get-tuple-element.33), channel_id=1, source_target_pairs={{0,48},{16,64},{32,80},{48,96},{64,112},{80,0},{96,16},{112,32},{1... | collective-permute-start | bytes 786440 | tf_op jit(solution)/shard_map/ppermute | solution.py:206
  153.7 26.0 %collective-permute-start.24 = (bf16[1,2,2,2,4,2,16,128]{7,6,5,4,3,2,1,0:T(8,128)(2,1)S(1)}, bf16[1,2,2,2,4,2,16,128]{7,6,5,4,3,2,1,0:T(8,128)(2,1)S(1)}, u32[]{:S(2)}, u32[]{:S(2)}) collective-permute-start(bf16[1,2,2,2,4,2,16,128]{7,6,5,4,3,2,1,0:T(8,128)(2,1)S(1)} %copy-done.6), channel_id=1, source_target_pairs={{0,64},{16,80},{32,96},{48,112},{64,0},{80,16},{96,32},{112,48},{1... | collective-permute-start | bytes 786440 | tf_op jit(solution)/shard_map/ppermute | solution.py:206
  156.1 23.6 %collective-permute-start.25 = (bf16[1,2,2,2,4,2,16,128]{7,6,5,4,3,2,1,0:T(8,128)(2,1)S(1)}, bf16[1,2,2,2,4,2,16,128]{7,6,5,4,3,2,1,0:T(8,128)(2,1)S(1)}, u32[]{:S(2)}, u32[]{:S(2)}) collective-permute-start(bf16[1,2,2,2,4,2,16,128]{7,6,5,4,3,2,1,0:T(8,128)(2,1)S(1)} %copy-done.5), channel_id=1, source_target_pairs={{0,80},{16,96},{32,112},{48,0},{64,16},{80,32},{96,48},{112,64},{1... | collective-permute-start | bytes 786440 | tf_op jit(solution)/shard_map/ppermute | solution.py:206
  158.6 12.4 %copy-start.16 = (bf16[1,2,2,2,4,2,16,128]{7,6,5,4,3,2,1,0:T(8,128)(2,1)}, bf16[1,2,2,2,4,2,16,128]{7,6,5,4,3,2,1,0:T(8,128)(2,1)S(1)}, u32[]{:S(2)}) copy-start(bf16[1,2,2,2,4,2,16,128]{7,6,5,4,3,2,1,0:T(8,128)(2,1)S(1)} %collective-permute-done.21.refs_1_) | copy-start | bytes 786436
  158.6 21.1 %collective-permute-start.26 = (bf16[1,2,2,2,4,2,16,128]{7,6,5,4,3,2,1,0:T(8,128)(2,1)S(1)}, bf16[1,2,2,2,4,2,16,128]{7,6,5,4,3,2,1,0:T(8,128)(2,1)}, u32[]{:S(2)}, u32[]{:S(2)}) collective-permute-start(bf16[1,2,2,2,4,2,16,128]{7,6,5,4,3,2,1,0:T(8,128)(2,1)S(1)} %copy-done.4), channel_id=1, source_target_pairs={{0,96},{16,112},{32,0},{48,16},{64,32},{80,48},{96,64},{112,80},{1... | collective-permute-start | bytes 786440 | tf_op jit(solution)/shard_map/ppermute | solution.py:206
  159.6 11.5 %copy-start.17 = (bf16[1,2,2,2,4,2,16,128]{7,6,5,4,3,2,1,0:T(8,128)(2,1)}, bf16[1,2,2,2,4,2,16,128]{7,6,5,4,3,2,1,0:T(8,128)(2,1)S(1)}, u32[]{:S(2)}) copy-start(bf16[1,2,2,2,4,2,16,128]{7,6,5,4,3,2,1,0:T(8,128)(2,1)S(1)} %collective-permute-done.22.refs_2_) | copy-start | bytes 786436
  159.6 20.2 %collective-permute-start.27 = (bf16[1,2,2,2,4,2,16,128]{7,6,5,4,3,2,1,0:T(8,128)(2,1)S(1)}, bf16[1,2,2,2,4,2,16,128]{7,6,5,4,3,2,1,0:T(8,128)(2,1)}, u32[]{:S(2)}, u32[]{:S(2)}) collective-permute-start(bf16[1,2,2,2,4,2,16,128]{7,6,5,4,3,2,1,0:T(8,128)(2,1)S(1)} %copy-done.3), channel_id=1, source_target_pairs={{0,112},{16,0},{32,16},{48,32},{64,48},{80,64},{96,80},{112,96},{1... | collective-permute-start | bytes 786440 | tf_op jit(solution)/shard_map/ppermute | solution.py:206
  173.0 19.6 %all-to-all-start.2 = ((bf16[8,16,16,128]{3,2,0,1:T(8,128)(2,1)}), bf16[8,16,16,128]{3,2,0,1:T(8,128)(2,1)S(1)}, u32[]{:S(2)}, u32[]{:S(2)}) async-start(bf16[8,16,16,128]{3,2,0,1:T(8,128)(2,1)} %copy.17), calls=%async_computation.2 | async-start | bytes 1048576 | tf_op jit(solution)/shard_map/all_to_all | solution.py:208
  179.7 0.7 copy-start.19
  179.7 0.8 copy-start.21
  179.7 0.8 copy-start.23

commit v5 on v3

--- a/solution.py
+++ b/solution.py
@@ -12,7 +12,7 @@
 TAPS = 4
 TINT = 2
 IB = 4
-CHUNKS = 4
+CHUNKS = 2
 FRAMES = 2 * IB
 
 
@@ -42,54 +42,52 @@
     band = band.reshape(2 * FRAMES * U, 2 * span).astype(np.float32)
     high = band.astype(jnp.bfloat16)
     low = (band - high.astype(np.float32)).astype(jnp.bfloat16)
-    return np.stack([high, low])
-
-
-def _filter_kernel(chunk, main_ref, pre0_ref, pre1_ref, pre2_ref, hist_ref, gain_ref, band_ref, out_ref, xs_ref):
+    return np.concatenate([high, low], axis=0)
+
+
+def _filter_kernel(chunk, main_ref, pre0_ref, pre1_ref, pre2_ref, hist_ref, gain_ref, band_ref, *rest):
+    out_ref = rest[-1]
+    tdev = pl.program_id(0)
     rows_main = main_ref.shape[4]
-    nblk = main_ref.shape[2]
     nb = out_ref.shape[1]
     span = (FRAMES + TAPS - 1) * U
     half = FRAMES * U
-    g_re = gain_ref[0, 0]
-    g_im = gain_ref[1, 0]
-
-    def block(tdev, carry):
+    lanes = main_ref.shape[5]
+    g_re = jnp.concatenate([gain_ref[0, p] for p in range(2)], axis=1)
+    g_im = jnp.concatenate([gain_ref[1, p] for p in range(2)], axis=1)
+
+    def rows_of(r, start, size):
+        return jnp.concatenate([main_ref[r, p, 0, 0, pl.ds(start, size), :] for p in range(2)], axis=1)
+
+    def prefix_of(r):
+        pre = [jnp.concatenate([ref[r, p, 0, 0] for p in range(2)], axis=1) for ref in (pre0_ref, pre1_ref, pre2_ref)]
+        pre = jnp.concatenate(pre, axis=0)
+        if chunk == 0:
+            hist = jnp.concatenate([hist_ref[r, p, 0] for p in range(2)], axis=1)
+            pre = jnp.where(tdev == 0, hist, pre)
+        return pre
+
+    for ib in range(nb):
+        parts = []
         for r in range(2):
-            xs_ref[r, pl.ds(48, rows_main), :] = main_ref[r, 0, tdev, 0]
-        if chunk == 0:
-            prev = jnp.maximum(tdev - 1, 0)
-            for r in range(2):
-                for m, pre in enumerate((pre0_ref, pre1_ref, pre2_ref)):
-                    xs_ref[r, pl.ds(16 * m, 16), :] = pre[r, 0, prev, 0]
-
-            @pl.when(tdev == 0)
-            def _():
-                for r in range(2):
-                    xs_ref[r, pl.ds(0, 48), :] = hist_ref[r, 0, 0]
-        else:
-            for r in range(2):
-                for m, pre in enumerate((pre0_ref, pre1_ref, pre2_ref)):
-                    xs_ref[r, pl.ds(16 * m, 16), :] = pre[r, 0, tdev, 0]
-
-        for ib in range(nb):
-            rhs = jnp.concatenate(
-                [xs_ref[r, pl.ds(ib * half, span), :] for r in range(2)], axis=0
-            )
-            spec = jnp.dot(band_ref[0], rhs, preferred_element_type=jnp.float32)
-            spec = spec + jnp.dot(band_ref[1], rhs, preferred_element_type=jnp.float32)
-            s_re = spec[:half]
-            s_im = spec[half:]
-            c_re = g_re * s_re - g_im * s_im
-            c_im = g_re * s_im + g_im * s_re
-            out_ref[tdev, ib, 0, 0] = c_re.astype(jnp.bfloat16).reshape(IB, TINT, U, 128)
-            out_ref[tdev, ib, 1, 0] = c_im.astype(jnp.bfloat16).reshape(IB, TINT, U, 128)
-        return carry
-
-    lax.fori_loop(0, nblk, block, 0)
-
-
-def filterbank(voltages, history, gains, band, chunk, chunks):
+            if ib == 0:
+                parts.append(jnp.concatenate([prefix_of(r), rows_of(r, 0, span - 48)], axis=0))
+            else:
+                parts.append(rows_of(r, ib * half - 48, span))
+        rhs = jnp.concatenate(parts, axis=0)
+        both = jnp.dot(band_ref[...], rhs, preferred_element_type=jnp.float32)
+        rows = both.shape[0] // 2
+        spec = both[:rows] + both[rows:]
+        s_re = spec[:half]
+        s_im = spec[half:]
+        c_re = (g_re * s_re - g_im * s_im).astype(jnp.bfloat16)
+        c_im = (g_re * s_im + g_im * s_re).astype(jnp.bfloat16)
+        for p in range(2):
+            out_ref[0, ib, 0, p] = c_re[:, p * lanes : (p + 1) * lanes].reshape(IB, TINT, U, lanes)
+            out_ref[0, ib, 1, p] = c_im[:, p * lanes : (p + 1) * lanes].reshape(IB, TINT, U, lanes)
+
+
+def filterbank(voltages, history, gains, band, chunk, chunks, after=None):
     _, pols, _, samples, feeds = voltages.shape
     nblk = 8
     rows_blk = samples // nblk
@@ -97,37 +95,34 @@
     nb = rows_main // U // FRAMES
     main = voltages.reshape(2, pols, nblk, chunks, rows_main, feeds)
     units = voltages.reshape(2, pols, nblk, rows_blk // 16, 16, feeds)
-    if chunk == 0:
-        first = rows_blk // 16 - 3
-    else:
-        first = chunk * rows_main // 16 - 3
 
     def pre_map(m):
-        return lambda p: (0, p, 0, first + m, 0, 0)
-
+        if chunk == 0:
+            return lambda t: (0, 0, jnp.maximum(t - 1, 0), rows_blk // 16 - 3 + m, 0, 0)
+        return lambda t: (0, 0, t, chunk * rows_main // 16 - 3 + m, 0, 0)
+
+    extra = [] if after is None else [after]
     return pl.pallas_call(
         lambda *refs: _filter_kernel(chunk, *refs),
-        grid=(pols,),
+        grid=(nblk,),
         in_specs=[
-            pl.BlockSpec((2, 1, nblk, 1, rows_main, feeds), lambda p: (0, p, 0, chunk, 0, 0)),
-            pl.BlockSpec((2, 1, nblk, 1, 16, feeds), pre_map(0)),
-            pl.BlockSpec((2, 1, nblk, 1, 16, feeds), pre_map(1)),
-            pl.BlockSpec((2, 1, nblk, 1, 16, feeds), pre_map(2)),
-            pl.BlockSpec((2, 1, 1, 48, feeds), lambda p: (0, p, 0, 0, 0)),
-            pl.BlockSpec((2, 1, 1, feeds), lambda p: (0, p, 0, 0)),
-            pl.BlockSpec(band.shape, lambda p: (0, 0, 0)),
-        ],
-        out_specs=pl.BlockSpec((nblk, nb, 2, 1, IB, TINT, U, feeds), lambda p: (0, 0, 0, p, 0, 0, 0, 0)),
+            pl.BlockSpec((2, pols, 1, 1, rows_main, feeds), lambda t: (0, 0, t, chunk, 0, 0)),
+            pl.BlockSpec((2, pols, 1, 1, 16, feeds), pre_map(0)),
+            pl.BlockSpec((2, pols, 1, 1, 16, feeds), pre_map(1)),
+            pl.BlockSpec((2, pols, 1, 1, 16, feeds), pre_map(2)),
+            pl.BlockSpec((2, pols, 1, 48, feeds), lambda t: (0, 0, 0, 0, 0)),
+            pl.BlockSpec((2, pols, 1, feeds), lambda t: (0, 0, 0, 0)),
+            pl.BlockSpec(band.shape, lambda t: (0, 0)),
+        ]
+        + [pl.BlockSpec((1, 1, U, 128), lambda t: (0, 0, 0, 0)) for _ in extra],
+        out_specs=pl.BlockSpec((1, nb, 2, pols, IB, TINT, U, feeds), lambda t: (t, 0, 0, 0, 0, 0, 0, 0)),
         out_shape=jax.ShapeDtypeStruct((nblk, nb, 2, pols, IB, TINT, U, feeds), jnp.bfloat16),
-        scratch_shapes=[
-            pltpu.VMEM((2, rows_main + 48, feeds), jnp.bfloat16),
-        ],
         cost_estimate=pl.CostEstimate(
             flops=2 * band.size * feeds * pols * nblk * nb,
             bytes_accessed=2 * voltages.size * 2 // chunks,
             transcendentals=0,
         ),
-    )(main, units, units, units, history, gains, band)
+    )(main, units, units, units, history, gains, band, *extra)
 
 
 def _beam_kernel(cal_ref, w_ref, sel_ref, out_ref):
@@ -187,12 +182,16 @@
         (jnp.arange(beams, dtype=jnp.int32)[:, None] == flat_ids[None, :]) & live_slots[None, :]
     ).astype(jnp.bfloat16)
     band = jnp.asarray(band_matrix())
+    gathered = []
     outs = []
-    for chunk in range(CHUNKS):
-        calibrated = filterbank(voltages, history, gains, band, chunk, CHUNKS)
-        gathered = lax.all_to_all(calibrated, "feed", split_axis=0, concat_axis=0, tiled=True)
-        picked = beamform(gathered, weights, select)
-        outs.append(lax.all_to_all(picked, "chan", split_axis=1, concat_axis=1, tiled=True))
+    for chunk in range(CHUNKS + 1):
+        if chunk < CHUNKS:
+            after = outs[-1] if outs else None
+            calibrated = filterbank(voltages, history, gains, band, chunk, CHUNKS, after)
+            gathered.append(lax.all_to_all(calibrated, "feed", split_axis=0, concat_axis=0, tiled=True))
+        if chunk >= 1:
+            picked = beamform(gathered[chunk - 1], weights, select)
+            outs.append(lax.all_to_all(picked, "chan", split_axis=1, concat_axis=1, tiled=True))
     exchanged = jnp.concatenate(outs, axis=0)
     bins, nodes, fine, width = exchanged.shape
     return exchanged.reshape(bins, nodes * fine, width)

time: 216 us -> 171 us (0.79)
  Pallas kernels: 76.6 us -> 53.2 us
  starting transfers between devices: 40 us -> 18.9 us
  local copies, waits for them, and re-layouts: 12.8 us -> 5.95 us
  blocking collectives: 15.4 us -> 22.1 us
    pallas_call x4 -> x2, Pallas kernels: 33.9 us -> 19.4 us  [filterbank(): pl.pallas_call(lambda *refs: _filter_kernel(chunk, *refs), grid=(nblk,),...]
    all_to_all x3 -> x1, starting transfers between devices: 20.9 us -> 7.62 us  [on_device(): lax.all_to_all(picked, 'chan', split_axis=1, concat_axis=1, tiled=True)]
    pallas_call x4 -> x2, Pallas kernels: 42.7 us -> 33.8 us  [beamform(): pl.pallas_call(_beam_kernel, grid=(nb,), in_specs=[pl.BlockSpec((nsrc, 1,...]
    all_to_all x4 -> x2, starting transfers between devices: 19.1 us -> 11.3 us  [on_device(): lax.all_to_all(calibrated, 'feed', split_axis=0, concat_axis=0, tiled=True)]
    all_to_all x1, blocking collectives: 15.4 us -> 22.1 us  [on_device(): lax.all_to_all(picked, 'chan', split_axis=1, concat_axis=1, tiled=True)]
    unnamed x12 -> x4, local copies, waits for them, and re-layouts: 4.12 us -> 0.01 us
    pallas_call x4 -> x2, local copies, waits for them, and re-layouts: 6.8 us -> 4.03 us  [beamform(): pl.pallas_call(_beam_kernel, grid=(nb,), in_specs=[pl.BlockSpec((nsrc, 1,...]
    all_to_all x4 -> x2, waiting for transfers between devices: 63.6 us -> 65 us  [on_device(): lax.all_to_all(calibrated, 'feed', split_axis=0, concat_axis=0, tiled=True)]
  transfers between devices with their start and end apart: 7 -> 3, of which waited for: 4 -> 2; matrix products, arithmetic and copies ran while one was open for 5% -> 5% of each run, Pallas kernels for 32% -> 26%
where the time goes in v5:
time: 171 us; the launch traced here: 169 us
  waiting for transfers between devices  65 us (38%)
  Pallas kernels  53.2 us (31%)
  blocking collectives  22.1 us (13%)
  starting transfers between devices  18.9 us (11%)
  local copies, waits for them, and re-layouts  5.95 us (3%)
  other arithmetic  3.91 us (2%)
    all_to_all x2, waiting for transfers between devices, on_device(): lax.all_to_all(calibrated, 'feed', split_axis=0, concat_axis=0, tiled=True)  65 us
    pallas_call x2, Pallas kernels, beamform(): pl.pallas_call(_beam_kernel, grid=(nb,), in_specs=[pl.BlockSpec((nsrc, 1,...  33.8 us
    all_to_all x1, blocking collectives, on_device(): lax.all_to_all(picked, 'chan', split_axis=1, concat_axis=1, tiled=True)  22.1 us
    pallas_call x2, Pallas kernels, filterbank(): pl.pallas_call(lambda *refs: _filter_kernel(chunk, *refs), grid=(nblk,),...  19.4 us
    all_to_all x2, starting transfers between devices, on_device(): lax.all_to_all(calibrated, 'feed', split_axis=0, concat_axis=0, tiled=True)  11.3 us
    all_to_all x1, starting transfers between devices, on_device(): lax.all_to_all(picked, 'chan', split_axis=1, concat_axis=1, tiled=True)  7.62 us
    pallas_call x2, local copies, waits for them, and re-layouts, beamform(): pl.pallas_call(_beam_kernel, grid=(nb,), in_specs=[pl.BlockSpec((nsrc, 1,...  4.03 us
    convert_element_type x1, other arithmetic, on_device(): select = ((jnp.arange(beams, dtype=jnp.int32)[:, None] == flat_ids[None,...  3.65 us
  transfers between devices with their start and end apart: 3, of which 2 were waited for; matrix products, arithmetic and copies ran while one was open for 5% of the time, Pallas kernels for 26%

profile of v5, /device:TPU:1, one launch (start us, length us, event | category | flops | bytes accessed | tf_op | source)
XLA Modules:
  0.0 169.1 jit_solution(17383485280384616507)
XLA Ops:
  0.0 9.7 %shard_map.75 = bf16[8,4,2,2,4,2,16,128]{7,6,5,4,3,2,1,0:T(8,128)(2,1)} custom-call(bf16[2,2,8,2,512,128]{5,4,3,2,1,0:T(8,128)(2,1)} %bitcast.6, bf16[2,2,8,64,16,128]{5,4,3,2,1,0:T(8,128)(2,1)} %bitcast.7, bf16[2,2,8,64,16,128]{5,4,3,2,1,0:T(8,128)(2,1)} %bitcast.8, bf16[2,2,8,64,16,128]{5,4,3,2,1,0:T(8,128)(2,1)} %bitcast.9, ...), custom_call_target="tpu_custom_call" | custom-call | flops 2952790016 | bytes 8388608 | tf_op jit(solution)/shard_map/pallas_call | solution.py:105
  9.7 6.0 %all-to-all-start.2 = ((bf16[8,4,2,2,4,2,16,128]{7,6,5,4,3,2,1,0:T(8,128)(2,1)}), bf16[8,4,2,2,4,2,16,128]{7,6,5,4,3,2,1,0:T(8,128)(2,1)}, u32[]{:S(2)}, u32[]{:S(2)}) async-start(bf16[8,4,2,2,4,2,16,128]{7,6,5,4,3,2,1,0:T(8,128)(2,1)} %shard_map.75), calls=%async_computation.2 | async-start | bytes 8388608 | tf_op jit(solution)/shard_map/all_to_all | solution.py:191
  15.7 9.7 %shard_map.73 = bf16[8,4,2,2,4,2,16,128]{7,6,5,4,3,2,1,0:T(8,128)(2,1)} custom-call(bf16[2,2,8,2,512,128]{5,4,3,2,1,0:T(8,128)(2,1)} %bitcast.10, bf16[2,2,8,64,16,128]{5,4,3,2,1,0:T(8,128)(2,1)} %bitcast.11, bf16[2,2,8,64,16,128]{5,4,3,2,1,0:T(8,128)(2,1)} %bitcast.12, bf16[2,2,8,64,16,128]{5,4,3,2,1,0:T(8,128)(2,1)} %bitcast.13, ...), custom_call_target="tpu_custom_call" | custom-call | flops 2952790016 | bytes 8388608 | tf_op jit(solution)/shard_map/pallas_call | solution.py:105
  25.4 0.0 copy-start.1
  25.4 0.0 copy-start
  25.4 39.2 %all-to-all-done.2.cal_ref = bf16[8,4,2,2,4,2,16,128]{7,6,5,4,3,2,1,0:T(8,128)(2,1)} async-done(((bf16[8,4,2,2,4,2,16,128]{7,6,5,4,3,2,1,0:T(8,128)(2,1)}), bf16[8,4,2,2,4,2,16,128]{7,6,5,4,3,2,1,0:T(8,128)(2,1)}, u32[]{:S(2)}, u32[]{:S(2)}) %all-to-all-start.2) | async-done | bytes 4194336 | tf_op jit(solution)/shard_map/all_to_all | solution.py:191
  64.6 5.3 %all-to-all-start = ((bf16[8,4,2,2,4,2,16,128]{7,6,5,4,3,2,1,0:T(8,128)(2,1)}), bf16[8,4,2,2,4,2,16,128]{7,6,5,4,3,2,1,0:T(8,128)(2,1)}, u32[]{:S(2)}, u32[]{:S(2)}) async-start(bf16[8,4,2,2,4,2,16,128]{7,6,5,4,3,2,1,0:T(8,128)(2,1)} %shard_map.73), calls=%async_computation | async-start | bytes 8388608 | tf_op jit(solution)/shard_map/all_to_all | solution.py:191
  69.9 0.0 copy-done.1
  69.9 0.1 fusion.2
  70.0 0.0 copy-done
  70.0 3.6 %fusion.1.sel_ref = bf16[1024,2048]{1,0:T(8,128)(2,1)} fusion(s32[2048]{0:T(1024)S(1)} %bitcast.14, pred[2048]{0:T(1024)(128)(4,1)S(1)} %fusion.2), kind=kLoop, calls=%fused_computation.2 | loop fusion | flops 6291456 | bytes 4204544 | tf_op jit(solution)/shard_map/convert_element_type | solution.py:183
  73.6 16.9 %shard_map.76 = bf16[16,16,16,128]{3,2,1,0:T(8,128)(2,1)} custom-call(bf16[8,4,2,2,4,2,16,128]{7,6,5,4,3,2,1,0:T(8,128)(2,1)} %all-to-all-done.2.cal_ref, bf16[2,1,1024,1024]{3,2,1,0:T(8,128)(2,1)} %w_ref.3, bf16[1024,2048]{1,0:T(8,128)(2,1)} %fusion.1.sel_ref), custom_call_target="tpu_custom_call" | custom-call | flops 9663676416 | bytes 13631488 | tf_op jit(solution)/shard_map/pallas_call | solution.py:157
  90.5 2.5 %copy.11 = bf16[16,16,16,128]{3,2,0,1:T(8,128)(2,1)} copy(bf16[16,16,16,128]{3,2,1,0:T(8,128)(2,1)} %shard_map.76) | data formatting | bytes 2097152 | tf_op jit(solution)/shard_map/pallas_call | solution.py:157
  93.1 25.8 %all-to-all-done.cal_ref = bf16[8,4,2,2,4,2,16,128]{7,6,5,4,3,2,1,0:T(8,128)(2,1)} async-done(((bf16[8,4,2,2,4,2,16,128]{7,6,5,4,3,2,1,0:T(8,128)(2,1)}), bf16[8,4,2,2,4,2,16,128]{7,6,5,4,3,2,1,0:T(8,128)(2,1)}, u32[]{:S(2)}, u32[]{:S(2)}) %all-to-all-start) | async-done | bytes 4194336 | tf_op jit(solution)/shard_map/all_to_all | solution.py:191
  118.8 7.6 %all-to-all-start.3 = ((bf16[16,16,16,128]{3,2,0,1:T(8,128)(2,1)}), bf16[16,16,16,128]{3,2,0,1:T(8,128)(2,1)S(1)}, u32[]{:S(2)}, u32[]{:S(2)}) async-start(bf16[16,16,16,128]{3,2,0,1:T(8,128)(2,1)} %copy.11), calls=%async_computation.3 | async-start | bytes 2097152 | tf_op jit(solution)/shard_map/all_to_all | solution.py:194
  126.5 16.9 %shard_map.74 = bf16[16,16,16,128]{3,2,1,0:T(8,128)(2,1)} custom-call(bf16[8,4,2,2,4,2,16,128]{7,6,5,4,3,2,1,0:T(8,128)(2,1)} %all-to-all-done.cal_ref, bf16[2,1,1024,1024]{3,2,1,0:T(8,128)(2,1)} %w_ref.3, bf16[1024,2048]{1,0:T(8,128)(2,1)} %fusion.1.sel_ref), custom_call_target="tpu_custom_call" | custom-call | flops 9663676416 | bytes 13631488 | tf_op jit(solution)/shard_map/pallas_call | solution.py:157
  143.4 1.5 copy.10
  144.9 0.0 all-to-all-done.3
  144.9 22.1 %all_to_all.20 = bf16[16,16,16,128]{3,2,0,1:T(8,128)(2,1)S(1)} all-to-all(bf16[16,16,16,128]{3,2,0,1:T(8,128)(2,1)S(1)} %copy.10), channel_id=1, replica_groups=mesh['feed'=8,'chan'=16] {'chan'}, dimensions={1} | all-to-all | bytes 2097152 | tf_op jit(solution)/shard_map/all_to_all | solution.py:194
  167.0 0.2 pad_maximum_fusion
  167.2 1.9 %copy.14 = bf16[32,16,16,128]{3,2,1,0:T(8,128)(2,1)} copy(bf16[32,16,16,128]{3,2,0,1:T(8,128)(2,1)S(1)} %pad_maximum_fusion) | data formatting | bytes 4194304 | tf_op jit(solution)/shard_map/concatenate | solution.py:195
Async XLA Ops:
  9.7 54.9 %all-to-all-start.2 = ((bf16[8,4,2,2,4,2,16,128]{7,6,5,4,3,2,1,0:T(8,128)(2,1)}), bf16[8,4,2,2,4,2,16,128]{7,6,5,4,3,2,1,0:T(8,128)(2,1)}, u32[]{:S(2)}, u32[]{:S(2)}) async-start(bf16[8,4,2,2,4,2,16,128]{7,6,5,4,3,2,1,0:T(8,128)(2,1)} %shard_map.75), calls=%async_computation.2 | async-start | bytes 8388608 | tf_op jit(solution)/shard_map/all_to_all | solution.py:191
  25.4 44.5 %copy-start.1 = (s32[16]{0:T(128)S(1)}, s32[16]{0:T(128)}, u32[]{:S(2)}) copy-start(s32[16]{0:T(128)} %param.12) | copy-start | bytes 196
  25.4 44.6 %copy-start = (s32[16,128]{1,0:T(8,128)S(1)}, s32[16,128]{1,0:T(8,128)}, u32[]{:S(2)}) copy-start(s32[16,128]{1,0:T(8,128)} %param.11) | copy-start | bytes 24580
  64.6 54.2 %all-to-all-start = ((bf16[8,4,2,2,4,2,16,128]{7,6,5,4,3,2,1,0:T(8,128)(2,1)}), bf16[8,4,2,2,4,2,16,128]{7,6,5,4,3,2,1,0:T(8,128)(2,1)}, u32[]{:S(2)}, u32[]{:S(2)}) async-start(bf16[8,4,2,2,4,2,16,128]{7,6,5,4,3,2,1,0:T(8,128)(2,1)} %shard_map.73), calls=%async_computation | async-start | bytes 8388608 | tf_op jit(solution)/shard_map/all_to_all | solution.py:191
  118.8 26.0 %all-to-all-start.3 = ((bf16[16,16,16,128]{3,2,0,1:T(8,128)(2,1)}), bf16[16,16,16,128]{3,2,0,1:T(8,128)(2,1)S(1)}, u32[]{:S(2)}, u32[]{:S(2)}) async-start(bf16[16,16,16,128]{3,2,0,1:T(8,128)(2,1)} %copy.11), calls=%async_computation.3 | async-start | bytes 2097152 | tf_op jit(solution)/shard_map/all_to_all | solution.py:194

commit v6 on v5

--- a/solution.py
+++ b/solution.py
@@ -144,9 +144,9 @@
     power = (power[:, 0] + power[:, 1]).reshape(IB * U, power.shape[-1])
     detected = (power * (1.0 / (4.0 * TINT))).astype(jnp.bfloat16)
     picked = jnp.dot(detected, sel_ref[...], preferred_element_type=jnp.float32).astype(jnp.bfloat16)
-    nodes = out_ref.shape[1]
+    nodes = out_ref.shape[0]
     for n in range(nodes):
-        out_ref[:, n] = picked[:, n * 128 : (n + 1) * 128].reshape(IB, U, 128)
+        out_ref[n] = picked[:, n * 128 : (n + 1) * 128].reshape(IB, U, 128)
 
 
 def beamform(cal, weights, select):
@@ -162,8 +162,8 @@
             pl.BlockSpec((2, 1, feeds, beams), lambda i: (0, 0, 0, 0)),
             pl.BlockSpec((beams, slots), lambda i: (0, 0)),
         ],
-        out_specs=pl.BlockSpec((IB, nodes, U, 128), lambda i: (i, 0, 0, 0)),
-        out_shape=jax.ShapeDtypeStruct((nb * IB, nodes, U, 128), jnp.bfloat16),
+        out_specs=pl.BlockSpec((nodes, IB, U, 128), lambda i: (0, i, 0, 0)),
+        out_shape=jax.ShapeDtypeStruct((nodes, nb * IB, U, 128), jnp.bfloat16),
         cost_estimate=pl.CostEstimate(
             flops=2 * 2 * (4 * nb * IB * U * TINT) * feeds * beams + 2 * nb * IB * U * beams * slots,
             bytes_accessed=cal.size * 2 + weights.size * 2 + select.size * 2 + nb * IB * U * slots * 2,
@@ -191,10 +191,10 @@
             gathered.append(lax.all_to_all(calibrated, "feed", split_axis=0, concat_axis=0, tiled=True))
         if chunk >= 1:
             picked = beamform(gathered[chunk - 1], weights, select)
-            outs.append(lax.all_to_all(picked, "chan", split_axis=1, concat_axis=1, tiled=True))
-    exchanged = jnp.concatenate(outs, axis=0)
-    bins, nodes, fine, width = exchanged.shape
-    return exchanged.reshape(bins, nodes * fine, width)
+            outs.append(lax.all_to_all(picked, "chan", split_axis=0, concat_axis=0, tiled=True))
+    exchanged = jnp.concatenate(outs, axis=1)
+    nodes, bins, fine, width = exchanged.shape
+    return jnp.transpose(exchanged, (1, 0, 2, 3)).reshape(bins, nodes * fine, width)
 
 
 def solution(mesh):

time: 171 us -> 170 us (level)
  local copies, waits for them, and re-layouts: 5.95 us -> 1.92 us
  waiting for transfers between devices: 65 us -> 67.5 us
    pallas_call x2 -> x0, local copies, waits for them, and re-layouts: 4.03 us -> none  [beamform(): pl.pallas_call(_beam_kernel, grid=(nb,), in_specs=[pl.BlockSpec((nsrc, 1,...]
    all_to_all x2, waiting for transfers between devices: 65 us -> 67.5 us  [on_device(): lax.all_to_all(calibrated, 'feed', split_axis=0, concat_axis=0, tiled=True)]
    transpose x0 -> x1, local copies, waits for them, and re-layouts: none -> 1.91 us  [on_device(): jnp.transpose(exchanged, (1, 0, 2, 3)).reshape(bins, nodes * fine, width)]
    concatenate x1 -> x0, local copies, waits for them, and re-layouts: 1.91 us -> none  [on_device(): exchanged = jnp.concatenate(outs, axis=0)]
  transfers between devices with their start and end apart: 3 -> 3, of which waited for: 2 -> 2; matrix products, arithmetic and copies ran while one was open for 5% -> 2% of each run, Pallas kernels for 26% -> 26%
where the time goes in v6:
time: 170 us; the launch traced here: 168 us
  waiting for transfers between devices  67.5 us (40%)
  Pallas kernels  53.2 us (31%)
  blocking collectives  22.3 us (13%)
  starting transfers between devices  18.9 us (11%)
  other arithmetic  3.93 us (2%)
  local copies, waits for them, and re-layouts  1.92 us (1%)
    all_to_all x2, waiting for transfers between devices, on_device(): lax.all_to_all(calibrated, 'feed', split_axis=0, concat_axis=0, tiled=True)  67.5 us
    pallas_call x2, Pallas kernels, beamform(): pl.pallas_call(_beam_kernel, grid=(nb,), in_specs=[pl.BlockSpec((nsrc, 1,...  33.9 us
    all_to_all x1, blocking collectives, on_device(): lax.all_to_all(picked, 'chan', split_axis=0, concat_axis=0, tiled=True)  22.3 us
    pallas_call x2, Pallas kernels, filterbank(): pl.pallas_call(lambda *refs: _filter_kernel(chunk, *refs), grid=(nblk,),...  19.4 us
    all_to_all x2, starting transfers between devices, on_device(): lax.all_to_all(calibrated, 'feed', split_axis=0, concat_axis=0, tiled=True)  11.3 us
    all_to_all x1, starting transfers between devices, on_device(): lax.all_to_all(picked, 'chan', split_axis=0, concat_axis=0, tiled=True)  7.6 us
    convert_element_type x1, other arithmetic, on_device(): select = ((jnp.arange(beams, dtype=jnp.int32)[:, None] == flat_ids[None,...  3.67 us
  transfers between devices with their start and end apart: 3, of which 2 were waited for; matrix products, arithmetic and copies ran while one was open for 2% of the time, Pallas kernels for 26%

profile of v6, /device:TPU:1, one launch (start us, length us, event | category | flops | bytes accessed | tf_op | source)
XLA Modules:
  0.0 167.8 jit_solution(9059902228675543833)
XLA Ops:
  0.0 9.7 %shard_map.75 = bf16[8,4,2,2,4,2,16,128]{7,6,5,4,3,2,1,0:T(8,128)(2,1)} custom-call(bf16[2,2,8,2,512,128]{5,4,3,2,1,0:T(8,128)(2,1)} %bitcast.8, bf16[2,2,8,64,16,128]{5,4,3,2,1,0:T(8,128)(2,1)} %bitcast.9, bf16[2,2,8,64,16,128]{5,4,3,2,1,0:T(8,128)(2,1)} %bitcast.10, bf16[2,2,8,64,16,128]{5,4,3,2,1,0:T(8,128)(2,1)} %bitcast.11, ...), custom_call_target="tpu_custom_call" | custom-call | flops 2952790016 | bytes 8388608 | tf_op jit(solution)/shard_map/pallas_call | solution.py:105
  9.7 6.0 %all-to-all-start.2 = ((bf16[8,4,2,2,4,2,16,128]{7,6,5,4,3,2,1,0:T(8,128)(2,1)}), bf16[8,4,2,2,4,2,16,128]{7,6,5,4,3,2,1,0:T(8,128)(2,1)}, u32[]{:S(2)}, u32[]{:S(2)}) async-start(bf16[8,4,2,2,4,2,16,128]{7,6,5,4,3,2,1,0:T(8,128)(2,1)} %shard_map.75), calls=%async_computation.2 | async-start | bytes 8388608 | tf_op jit(solution)/shard_map/all_to_all | solution.py:191
  15.6 9.7 %shard_map.73 = bf16[8,4,2,2,4,2,16,128]{7,6,5,4,3,2,1,0:T(8,128)(2,1)} custom-call(bf16[2,2,8,2,512,128]{5,4,3,2,1,0:T(8,128)(2,1)} %bitcast.12, bf16[2,2,8,64,16,128]{5,4,3,2,1,0:T(8,128)(2,1)} %bitcast.13, bf16[2,2,8,64,16,128]{5,4,3,2,1,0:T(8,128)(2,1)} %bitcast.14, bf16[2,2,8,64,16,128]{5,4,3,2,1,0:T(8,128)(2,1)} %bitcast.15, ...), custom_call_target="tpu_custom_call" | custom-call | flops 2952790016 | bytes 8388608 | tf_op jit(solution)/shard_map/pallas_call | solution.py:105
  25.3 0.0 copy-start.1
  25.3 0.0 copy-start
  25.3 39.2 %all-to-all-done.2.cal_ref = bf16[8,4,2,2,4,2,16,128]{7,6,5,4,3,2,1,0:T(8,128)(2,1)} async-done(((bf16[8,4,2,2,4,2,16,128]{7,6,5,4,3,2,1,0:T(8,128)(2,1)}), bf16[8,4,2,2,4,2,16,128]{7,6,5,4,3,2,1,0:T(8,128)(2,1)}, u32[]{:S(2)}, u32[]{:S(2)}) %all-to-all-start.2) | async-done | bytes 4194336 | tf_op jit(solution)/shard_map/all_to_all | solution.py:191
  64.5 5.3 %all-to-all-start = ((bf16[8,4,2,2,4,2,16,128]{7,6,5,4,3,2,1,0:T(8,128)(2,1)}), bf16[8,4,2,2,4,2,16,128]{7,6,5,4,3,2,1,0:T(8,128)(2,1)}, u32[]{:S(2)}, u32[]{:S(2)}) async-start(bf16[8,4,2,2,4,2,16,128]{7,6,5,4,3,2,1,0:T(8,128)(2,1)} %shard_map.73), calls=%async_computation | async-start | bytes 8388608 | tf_op jit(solution)/shard_map/all_to_all | solution.py:191
  69.8 0.0 copy-done.1
  69.8 0.1 fusion.2
  69.9 0.0 copy-done
  69.9 3.7 %fusion.1.sel_ref = bf16[1024,2048]{1,0:T(8,128)(2,1)} fusion(s32[2048]{0:T(1024)S(1)} %bitcast.16, pred[2048]{0:T(1024)(128)(4,1)S(1)} %fusion.2), kind=kLoop, calls=%fused_computation.2 | loop fusion | flops 6291456 | bytes 4204544 | tf_op jit(solution)/shard_map/convert_element_type | solution.py:183
  73.6 16.9 %shard_map.76 = bf16[16,16,16,128]{3,2,1,0:T(8,128)(2,1)} custom-call(bf16[8,4,2,2,4,2,16,128]{7,6,5,4,3,2,1,0:T(8,128)(2,1)} %all-to-all-done.2.cal_ref, bf16[2,1,1024,1024]{3,2,1,0:T(8,128)(2,1)} %w_ref.3, bf16[1024,2048]{1,0:T(8,128)(2,1)} %fusion.1.sel_ref), custom_call_target="tpu_custom_call" | custom-call | flops 9663676416 | bytes 13631488 | tf_op jit(solution)/shard_map/pallas_call | solution.py:157
  90.5 28.3 %all-to-all-done.cal_ref = bf16[8,4,2,2,4,2,16,128]{7,6,5,4,3,2,1,0:T(8,128)(2,1)} async-done(((bf16[8,4,2,2,4,2,16,128]{7,6,5,4,3,2,1,0:T(8,128)(2,1)}), bf16[8,4,2,2,4,2,16,128]{7,6,5,4,3,2,1,0:T(8,128)(2,1)}, u32[]{:S(2)}, u32[]{:S(2)}) %all-to-all-start) | async-done | bytes 4194336 | tf_op jit(solution)/shard_map/all_to_all | solution.py:191
  118.8 7.6 %all-to-all-start.3 = ((bf16[16,16,16,128]{3,2,1,0:T(8,128)(2,1)}), bf16[16,16,16,128]{3,2,1,0:T(8,128)(2,1)S(1)}, u32[]{:S(2)}, u32[]{:S(2)}) async-start(bf16[16,16,16,128]{3,2,1,0:T(8,128)(2,1)} %shard_map.76), calls=%async_computation.3 | async-start | bytes 2097152 | tf_op jit(solution)/shard_map/all_to_all | solution.py:194
  126.4 17.0 %shard_map.74 = bf16[16,16,16,128]{3,2,1,0:T(8,128)(2,1)} custom-call(bf16[8,4,2,2,4,2,16,128]{7,6,5,4,3,2,1,0:T(8,128)(2,1)} %all-to-all-done.cal_ref, bf16[2,1,1024,1024]{3,2,1,0:T(8,128)(2,1)} %w_ref.3, bf16[1024,2048]{1,0:T(8,128)(2,1)} %fusion.1.sel_ref), custom_call_target="tpu_custom_call" | custom-call | flops 9663676416 | bytes 13631488 | tf_op jit(solution)/shard_map/pallas_call | solution.py:157
  143.3 0.0 all-to-all-done.3
  143.3 22.3 %all_to_all.20 = bf16[16,16,16,128]{3,2,1,0:T(8,128)(2,1)S(1)} all-to-all(bf16[16,16,16,128]{3,2,1,0:T(8,128)(2,1)} %shard_map.74), channel_id=1, replica_groups=mesh['feed'=8,'chan'=16] {'chan'}, dimensions={0} | all-to-all | bytes 2097152 | tf_op jit(solution)/shard_map/all_to_all | solution.py:194
  165.7 0.2 maximum_bitcast_fusion
  165.9 1.9 %copy.8 = bf16[32,16,16,128]{3,2,1,0:T(8,128)(2,1)} copy(bf16[32,16,16,128]{3,2,0,1:T(8,128)(2,1)S(1)} %maximum_bitcast_fusion) | data formatting | bytes 4194304 | tf_op jit(solution)/shard_map/transpose | solution.py:197
Async XLA Ops:
  9.7 54.9 %all-to-all-start.2 = ((bf16[8,4,2,2,4,2,16,128]{7,6,5,4,3,2,1,0:T(8,128)(2,1)}), bf16[8,4,2,2,4,2,16,128]{7,6,5,4,3,2,1,0:T(8,128)(2,1)}, u32[]{:S(2)}, u32[]{:S(2)}) async-start(bf16[8,4,2,2,4,2,16,128]{7,6,5,4,3,2,1,0:T(8,128)(2,1)} %shard_map.75), calls=%async_computation.2 | async-start | bytes 8388608 | tf_op jit(solution)/shard_map/all_to_all | solution.py:191
  25.3 44.5 %copy-start.1 = (s32[16]{0:T(128)S(1)}, s32[16]{0:T(128)}, u32[]{:S(2)}) copy-start(s32[16]{0:T(128)} %param.12) | copy-start | bytes 196
  25.3 44.6 %copy-start = (s32[16,128]{1,0:T(8,128)S(1)}, s32[16,128]{1,0:T(8,128)}, u32[]{:S(2)}) copy-start(s32[16,128]{1,0:T(8,128)} %param.11) | copy-start | bytes 24580
  64.5 54.2 %all-to-all-start = ((bf16[8,4,2,2,4,2,16,128]{7,6,5,4,3,2,1,0:T(8,128)(2,1)}), bf16[8,4,2,2,4,2,16,128]{7,6,5,4,3,2,1,0:T(8,128)(2,1)}, u32[]{:S(2)}, u32[]{:S(2)}) async-start(bf16[8,4,2,2,4,2,16,128]{7,6,5,4,3,2,1,0:T(8,128)(2,1)} %shard_map.73), calls=%async_computation | async-start | bytes 8388608 | tf_op jit(solution)/shard_map/all_to_all | solution.py:191
  118.8 24.6 %all-to-all-start.3 = ((bf16[16,16,16,128]{3,2,1,0:T(8,128)(2,1)}), bf16[16,16,16,128]{3,2,1,0:T(8,128)(2,1)S(1)}, u32[]{:S(2)}, u32[]{:S(2)}) async-start(bf16[16,16,16,128]{3,2,1,0:T(8,128)(2,1)} %shard_map.76), calls=%async_computation.3 | async-start | bytes 2097152 | tf_op jit(solution)/shard_map/all_to_all | solution.py:194

commit v7 on v6

--- a/solution.py
+++ b/solution.py
@@ -12,7 +12,7 @@
 TAPS = 4
 TINT = 2
 IB = 4
-CHUNKS = 2
+CHUNK_BLOCKS = (6, 2)
 FRAMES = 2 * IB
 
 
@@ -48,16 +48,15 @@
 def _filter_kernel(chunk, main_ref, pre0_ref, pre1_ref, pre2_ref, hist_ref, gain_ref, band_ref, *rest):
     out_ref = rest[-1]
     tdev = pl.program_id(0)
-    rows_main = main_ref.shape[4]
     nb = out_ref.shape[1]
     span = (FRAMES + TAPS - 1) * U
     half = FRAMES * U
-    lanes = main_ref.shape[5]
+    lanes = main_ref.shape[4]
     g_re = jnp.concatenate([gain_ref[0, p] for p in range(2)], axis=1)
     g_im = jnp.concatenate([gain_ref[1, p] for p in range(2)], axis=1)
 
     def rows_of(r, start, size):
-        return jnp.concatenate([main_ref[r, p, 0, 0, pl.ds(start, size), :] for p in range(2)], axis=1)
+        return jnp.concatenate([main_ref[r, p, 0, pl.ds(start, size), :] for p in range(2)], axis=1)
 
     def prefix_of(r):
         pre = [jnp.concatenate([ref[r, p, 0, 0] for p in range(2)], axis=1) for ref in (pre0_ref, pre1_ref, pre2_ref)]
@@ -87,26 +86,27 @@
             out_ref[0, ib, 1, p] = c_im[:, p * lanes : (p + 1) * lanes].reshape(IB, TINT, U, lanes)
 
 
-def filterbank(voltages, history, gains, band, chunk, chunks, after=None):
+def filterbank(voltages, history, gains, band, first_blk, nb, after=None):
     _, pols, _, samples, feeds = voltages.shape
     nblk = 8
     rows_blk = samples // nblk
-    rows_main = rows_blk // chunks
-    nb = rows_main // U // FRAMES
-    main = voltages.reshape(2, pols, nblk, chunks, rows_main, feeds)
+    rows_main = nb * FRAMES * U
+    assert (first_blk * FRAMES * U) % rows_main == 0
+    chunk = first_blk * FRAMES * U // rows_main
+    main = voltages.reshape(2, pols, nblk, rows_blk, feeds)
     units = voltages.reshape(2, pols, nblk, rows_blk // 16, 16, feeds)
 
     def pre_map(m):
-        if chunk == 0:
+        if first_blk == 0:
             return lambda t: (0, 0, jnp.maximum(t - 1, 0), rows_blk // 16 - 3 + m, 0, 0)
-        return lambda t: (0, 0, t, chunk * rows_main // 16 - 3 + m, 0, 0)
+        return lambda t: (0, 0, t, first_blk * FRAMES - 3 + m, 0, 0)
 
     extra = [] if after is None else [after]
     return pl.pallas_call(
-        lambda *refs: _filter_kernel(chunk, *refs),
+        lambda *refs: _filter_kernel(first_blk, *refs),
         grid=(nblk,),
         in_specs=[
-            pl.BlockSpec((2, pols, 1, 1, rows_main, feeds), lambda t: (0, 0, t, chunk, 0, 0)),
+            pl.BlockSpec((2, pols, 1, rows_main, feeds), lambda t: (0, 0, t, chunk, 0)),
             pl.BlockSpec((2, pols, 1, 1, 16, feeds), pre_map(0)),
             pl.BlockSpec((2, pols, 1, 1, 16, feeds), pre_map(1)),
             pl.BlockSpec((2, pols, 1, 1, 16, feeds), pre_map(2)),
@@ -119,13 +119,14 @@
         out_shape=jax.ShapeDtypeStruct((nblk, nb, 2, pols, IB, TINT, U, feeds), jnp.bfloat16),
         cost_estimate=pl.CostEstimate(
             flops=2 * band.size * feeds * pols * nblk * nb,
-            bytes_accessed=2 * voltages.size * 2 // chunks,
+            bytes_accessed=2 * voltages.size * 2 * nb // (rows_blk // (FRAMES * U)),
             transcendentals=0,
         ),
     )(main, units, units, units, history, gains, band, *extra)
 
 
-def _beam_kernel(cal_ref, w_ref, sel_ref, out_ref):
+def _beam_kernel(cal_ref, w_ref, sel_ref, *rest):
+    out_ref = rest[-1]
     nsrc = cal_ref.shape[0]
     rows = 2 * 2 * IB * U
     halves = []
@@ -149,7 +150,8 @@
         out_ref[n] = picked[:, n * 128 : (n + 1) * 128].reshape(IB, U, 128)
 
 
-def beamform(cal, weights, select):
+def beamform(cal, weights, select, after=None):
+    extra = [] if after is None else [after]
     nsrc, nb = cal.shape[0], cal.shape[1]
     feeds, beams = weights.shape[2], weights.shape[3]
     slots = select.shape[1]
@@ -161,7 +163,8 @@
             pl.BlockSpec((nsrc, 1, 2, 2, IB, TINT, U, 128), lambda i: (0, i, 0, 0, 0, 0, 0, 0)),
             pl.BlockSpec((2, 1, feeds, beams), lambda i: (0, 0, 0, 0)),
             pl.BlockSpec((beams, slots), lambda i: (0, 0)),
-        ],
+        ]
+        + [pl.BlockSpec((1, 1, U, 128), lambda i: (0, 0, 0, 0)) for _ in extra],
         out_specs=pl.BlockSpec((nodes, IB, U, 128), lambda i: (0, i, 0, 0)),
         out_shape=jax.ShapeDtypeStruct((nodes, nb * IB, U, 128), jnp.bfloat16),
         cost_estimate=pl.CostEstimate(
@@ -170,7 +173,7 @@
             transcendentals=0,
         ),
         compiler_params=pltpu.CompilerParams(vmem_limit_bytes=60 * 1024 * 1024),
-    )(cal, weights, select)
+    )(cal, weights, select, *extra)
 
 
 def on_device(voltages, history, gains, weights, beam_lists, beam_counts):
@@ -182,16 +185,18 @@
         (jnp.arange(beams, dtype=jnp.int32)[:, None] == flat_ids[None, :]) & live_slots[None, :]
     ).astype(jnp.bfloat16)
     band = jnp.asarray(band_matrix())
+    starts = [sum(CHUNK_BLOCKS[:c]) for c in range(len(CHUNK_BLOCKS))]
     gathered = []
+    calibrated = []
     outs = []
-    for chunk in range(CHUNKS + 1):
-        if chunk < CHUNKS:
-            after = outs[-1] if outs else None
-            calibrated = filterbank(voltages, history, gains, band, chunk, CHUNKS, after)
-            gathered.append(lax.all_to_all(calibrated, "feed", split_axis=0, concat_axis=0, tiled=True))
-        if chunk >= 1:
-            picked = beamform(gathered[chunk - 1], weights, select)
-            outs.append(lax.all_to_all(picked, "chan", split_axis=0, concat_axis=0, tiled=True))
+    for chunk in range(len(CHUNK_BLOCKS)):
+        after = None if chunk == 0 else gathered[-1].reshape(-1, 1, U, 128)
+        calibrated.append(filterbank(voltages, history, gains, band, starts[chunk], CHUNK_BLOCKS[chunk], after))
+        gathered.append(lax.all_to_all(calibrated[-1], "feed", split_axis=0, concat_axis=0, tiled=True))
+    for chunk in range(len(CHUNK_BLOCKS)):
+        after = calibrated[chunk + 1].reshape(-1, 1, U, 128) if chunk + 1 < len(CHUNK_BLOCKS) else None
+        picked = beamform(gathered[chunk], weights, select, after)
+        outs.append(lax.all_to_all(picked, "chan", split_axis=0, concat_axis=0, tiled=True))
     exchanged = jnp.concatenate(outs, axis=1)
     nodes, bins, fine, width = exchanged.shape
     return jnp.transpose(exchanged, (1, 0, 2, 3)).reshape(bins, nodes * fine, width)

time: 170 us -> 180 us (1.059)
  waiting for transfers between devices: 67.5 us -> 85.2 us
  blocking collectives: 22.3 us -> 14 us
    all_to_all x1, waiting for transfers between devices: 0.01 us -> 13.9 us  [on_device(): lax.all_to_all(picked, 'chan', split_axis=0, concat_axis=0, tiled=True)]
    all_to_all x1, blocking collectives: 22.3 us -> 14 us  [on_device(): lax.all_to_all(picked, 'chan', split_axis=0, concat_axis=0, tiled=True)]
    all_to_all x2, waiting for transfers between devices: 67.5 us -> 71.3 us  [on_device(): lax.all_to_all(calibrated[-1], 'feed', split_axis=0, concat_axis=0, tiled...]
  transfers between devices with their start and end apart: 3 -> 3, of which waited for: 2 -> 2; matrix products, arithmetic and copies ran while one was open for 2% -> 2% of each run, Pallas kernels for 26% -> 19%
where the time goes in v7:
time: 180 us; the launch traced here: 178 us
  waiting for transfers between devices  85.2 us (47%)
  Pallas kernels  53.4 us (30%)
  starting transfers between devices  18.4 us (10%)
  blocking collectives  14 us (8%)
  other arithmetic  4 us (2%)
  local copies, waits for them, and re-layouts  3.24 us (2%)
    all_to_all x2, waiting for transfers between devices, on_device(): lax.all_to_all(calibrated[-1], 'feed', split_axis=0, concat_axis=0, tiled...  71.3 us
    pallas_call x2, Pallas kernels, beamform(): pl.pallas_call(_beam_kernel, grid=(nb,), in_specs=[pl.BlockSpec((nsrc, 1,...  34 us
    pallas_call x2, Pallas kernels, filterbank(): pl.pallas_call(lambda *refs: _filter_kernel(first_blk, *refs), grid=(nblk...  19.4 us
    all_to_all x1, blocking collectives, on_device(): lax.all_to_all(picked, 'chan', split_axis=0, concat_axis=0, tiled=True)  14 us
    all_to_all x1, waiting for transfers between devices, on_device(): lax.all_to_all(picked, 'chan', split_axis=0, concat_axis=0, tiled=True)  13.9 us
    all_to_all x2, starting transfers between devices, on_device(): lax.all_to_all(calibrated[-1], 'feed', split_axis=0, concat_axis=0, tiled...  10.7 us
    all_to_all x1, starting transfers between devices, on_device(): lax.all_to_all(picked, 'chan', split_axis=0, concat_axis=0, tiled=True)  7.72 us
    convert_element_type x1, other arithmetic, on_device(): select = ((jnp.arange(beams, dtype=jnp.int32)[:, None] == flat_ids[None,...  3.74 us
  transfers between devices with their start and end apart: 3, of which 2 were waited for; matrix products, arithmetic and copies ran while one was open for 2% of the time, Pallas kernels for 19%

profile of v7, /device:TPU:1, one launch (start us, length us, event | category | flops | bytes accessed | tf_op | source)
XLA Modules:
  0.0 178.2 jit_solution(12271398301698990408)
XLA Ops:
  0.0 11.9 %shard_map.73 = bf16[8,6,2,2,4,2,16,128]{7,6,5,4,3,2,1,0:T(8,128)(2,1)} custom-call(bf16[2,2,8,1024,128]{4,3,2,1,0:T(8,128)(2,1)} %bitcast.12, bf16[2,2,8,64,16,128]{5,4,3,2,1,0:T(8,128)(2,1)} %bitcast.13, bf16[2,2,8,64,16,128]{5,4,3,2,1,0:T(8,128)(2,1)} %bitcast.14, bf16[2,2,8,64,16,128]{5,4,3,2,1,0:T(8,128)(2,1)} %bitcast.15, ...), custom_call_target="tpu_custom_call" | custom-call | flops 4429185024 | bytes 12582912 | tf_op jit(solution)/shard_map/pallas_call | solution.py:105
  11.9 0.0 copy-start.2
  11.9 6.1 %all-to-all-start = ((bf16[8,6,2,2,4,2,16,128]{7,6,5,4,3,2,1,0:T(8,128)(2,1)}), bf16[8,6,2,2,4,2,16,128]{7,6,5,4,3,2,1,0:T(8,128)(2,1)}, u32[]{:S(2)}, u32[]{:S(2)}) async-start(bf16[8,6,2,2,4,2,16,128]{7,6,5,4,3,2,1,0:T(8,128)(2,1)} %shard_map.73), calls=%async_computation | async-start | bytes 12582912 | tf_op jit(solution)/shard_map/all_to_all | solution.py:195
  18.1 0.0 copy-done.2
  18.1 0.1 fusion.2
  18.1 71.3 %all-to-all-done.cal_ref = bf16[8,6,2,2,4,2,16,128]{7,6,5,4,3,2,1,0:T(8,128)(2,1)} async-done(((bf16[8,6,2,2,4,2,16,128]{7,6,5,4,3,2,1,0:T(8,128)(2,1)}), bf16[8,6,2,2,4,2,16,128]{7,6,5,4,3,2,1,0:T(8,128)(2,1)}, u32[]{:S(2)}, u32[]{:S(2)}) %all-to-all-start) | async-done | bytes 6291488 | tf_op jit(solution)/shard_map/all_to_all | solution.py:195
  89.5 7.5 %shard_map.74 = bf16[8,2,2,2,4,2,16,128]{7,6,5,4,3,2,1,0:T(8,128)(2,1)} custom-call(bf16[2,2,8,1024,128]{4,3,2,1,0:T(8,128)(2,1)} %bitcast.16, bf16[2,2,8,64,16,128]{5,4,3,2,1,0:T(8,128)(2,1)} %bitcast.17, bf16[2,2,8,64,16,128]{5,4,3,2,1,0:T(8,128)(2,1)} %bitcast.18, bf16[2,2,8,64,16,128]{5,4,3,2,1,0:T(8,128)(2,1)} %bitcast.19, ...), custom_call_target="tpu_custom_call" | custom-call | flops 1476395008 | bytes 4194304 | tf_op jit(solution)/shard_map/pallas_call | solution.py:105
  97.0 0.0 copy-start.1
  97.0 4.5 %all-to-all-start.2 = ((bf16[8,2,2,2,4,2,16,128]{7,6,5,4,3,2,1,0:T(8,128)(2,1)}), bf16[8,2,2,2,4,2,16,128]{7,6,5,4,3,2,1,0:T(8,128)(2,1)S(1)}, u32[]{:S(2)}, u32[]{:S(2)}) async-start(bf16[8,2,2,2,4,2,16,128]{7,6,5,4,3,2,1,0:T(8,128)(2,1)} %shard_map.74), calls=%async_computation.2 | async-start | bytes 4194304 | tf_op jit(solution)/shard_map/all_to_all | solution.py:195
  101.5 0.0 copy-done.1
  101.5 3.7 %fusion.1.sel_ref = bf16[1024,2048]{1,0:T(8,128)(2,1)} fusion(s32[2048]{0:T(1024)S(1)} %bitcast.21, pred[2048]{0:T(1024)(128)(4,1)S(1)} %fusion.2), kind=kLoop, calls=%fused_computation.2 | loop fusion | flops 6291456 | bytes 4204544 | tf_op jit(solution)/shard_map/convert_element_type | solution.py:186
  105.2 23.2 %shard_map.75 = bf16[16,24,16,128]{3,2,1,0:T(8,128)(2,1)} custom-call(bf16[8,6,2,2,4,2,16,128]{7,6,5,4,3,2,1,0:T(8,128)(2,1)} %all-to-all-done.cal_ref, bf16[2,1,1024,1024]{3,2,1,0:T(8,128)(2,1)} %w_ref.3, bf16[1024,2048]{1,0:T(8,128)(2,1)} %fusion.1.sel_ref, bf16[512,1,16,128]{3,2,1,0:T(8,128)(2,1)} %bitcast.20), custom_call_target="tpu_custom_call" | custom-call | flops 14495514624 | bytes 16252928 | tf_op jit(solution)/shard_map/pallas_call | solution.py:159
  128.5 0.0 all-to-all-done.2.cal_ref
  128.5 0.0 copy-start
  128.5 1.3 copy-done
  129.8 7.7 %all-to-all-start.1 = ((bf16[16,24,16,128]{3,2,1,0:T(8,128)(2,1)}), bf16[16,24,16,128]{3,2,1,0:T(8,128)(2,1)S(1)}, u32[]{:S(2)}, u32[]{:S(2)}) async-start(bf16[16,24,16,128]{3,2,1,0:T(8,128)(2,1)} %shard_map.75), calls=%async_computation.1 | async-start | bytes 3145728 | tf_op jit(solution)/shard_map/all_to_all | solution.py:199
  137.5 10.7 %shard_map.76 = bf16[16,8,16,128]{3,2,1,0:T(8,128)(2,1)} custom-call(bf16[8,2,2,2,4,2,16,128]{7,6,5,4,3,2,1,0:T(8,128)(2,1)} %copy-done, bf16[2,1,1024,1024]{3,2,1,0:T(8,128)(2,1)} %w_ref.3, bf16[1024,2048]{1,0:T(8,128)(2,1)} %fusion.1.sel_ref), custom_call_target="tpu_custom_call" | custom-call | flops 4831838208 | bytes 11010048 | tf_op jit(solution)/shard_map/pallas_call | solution.py:159
  148.2 13.9 %all-to-all-done.1 = bf16[16,24,16,128]{3,2,1,0:T(8,128)(2,1)S(1)} async-done(((bf16[16,24,16,128]{3,2,1,0:T(8,128)(2,1)}), bf16[16,24,16,128]{3,2,1,0:T(8,128)(2,1)S(1)}, u32[]{:S(2)}, u32[]{:S(2)}) %all-to-all-start.1) | async-done | bytes 1572896 | tf_op jit(solution)/shard_map/all_to_all | solution.py:199
  162.1 14.0 %all_to_all.20 = bf16[16,8,16,128]{3,2,1,0:T(8,128)(2,1)S(1)} all-to-all(bf16[16,8,16,128]{3,2,1,0:T(8,128)(2,1)} %shard_map.76), channel_id=1, replica_groups=mesh['feed'=8,'chan'=16] {'chan'}, dimensions={0} | all-to-all | bytes 1048576 | tf_op jit(solution)/shard_map/all_to_all | solution.py:199
  176.1 0.2 maximum_bitcast_fusion
  176.3 1.9 %copy.10 = bf16[32,16,16,128]{3,2,1,0:T(8,128)(2,1)} copy(bf16[32,16,16,128]{3,2,0,1:T(8,128)(2,1)S(1)} %maximum_bitcast_fusion) | data formatting | bytes 4194304 | tf_op jit(solution)/shard_map/transpose | solution.py:202
Async XLA Ops:
  11.9 6.1 %copy-start.2 = (s32[16]{0:T(128)S(1)}, s32[16]{0:T(128)}, u32[]{:S(2)}) copy-start(s32[16]{0:T(128)} %param.12) | copy-start | bytes 196
  11.9 77.5 %all-to-all-start = ((bf16[8,6,2,2,4,2,16,128]{7,6,5,4,3,2,1,0:T(8,128)(2,1)}), bf16[8,6,2,2,4,2,16,128]{7,6,5,4,3,2,1,0:T(8,128)(2,1)}, u32[]{:S(2)}, u32[]{:S(2)}) async-start(bf16[8,6,2,2,4,2,16,128]{7,6,5,4,3,2,1,0:T(8,128)(2,1)} %shard_map.73), calls=%async_computation | async-start | bytes 12582912 | tf_op jit(solution)/shard_map/all_to_all | solution.py:195
  97.0 4.5 %copy-start.1 = (s32[16,128]{1,0:T(8,128)S(1)}, s32[16,128]{1,0:T(8,128)}, u32[]{:S(2)}) copy-start(s32[16,128]{1,0:T(8,128)} %param.11) | copy-start | bytes 24580
  97.0 31.5 %all-to-all-start.2 = ((bf16[8,2,2,2,4,2,16,128]{7,6,5,4,3,2,1,0:T(8,128)(2,1)}), bf16[8,2,2,2,4,2,16,128]{7,6,5,4,3,2,1,0:T(8,128)(2,1)S(1)}, u32[]{:S(2)}, u32[]{:S(2)}) async-start(bf16[8,2,2,2,4,2,16,128]{7,6,5,4,3,2,1,0:T(8,128)(2,1)} %shard_map.74), calls=%async_computation.2 | async-start | bytes 4194304 | tf_op jit(solution)/shard_map/all_to_all | solution.py:195
  128.5 1.3 copy-start
  129.8 32.3 %all-to-all-start.1 = ((bf16[16,24,16,128]{3,2,1,0:T(8,128)(2,1)}), bf16[16,24,16,128]{3,2,1,0:T(8,128)(2,1)S(1)}, u32[]{:S(2)}, u32[]{:S(2)}) async-start(bf16[16,24,16,128]{3,2,1,0:T(8,128)(2,1)} %shard_map.75), calls=%async_computation.1 | async-start | bytes 3145728 | tf_op jit(solution)/shard_map/all_to_all | solution.py:199

commit v8 on v6

--- a/solution.py
+++ b/solution.py
@@ -173,6 +173,19 @@
     )(cal, weights, select)
 
 
+def exchange_by_permutes(blocks, axis):
+    count = lax.axis_size(axis)
+    me = lax.axis_index(axis)
+    received = [lax.dynamic_index_in_dim(blocks, me, axis=0, keepdims=False)]
+    for shift in range(1, count):
+        pairs = [(i, (i + shift) % count) for i in range(count)]
+        piece = lax.dynamic_index_in_dim(blocks, lax.rem(me + shift, count), axis=0, keepdims=False)
+        received.append(lax.ppermute(piece, axis, perm=pairs))
+    stacked = jnp.stack(received)
+    order = lax.rem(me - jnp.arange(count, dtype=jnp.int32) + count, count)
+    return jnp.take(stacked, order, axis=0)
+
+
 def on_device(voltages, history, gains, weights, beam_lists, beam_counts):
     capacity = beam_lists.shape[1]
     beams = weights.shape[3]
@@ -191,7 +204,10 @@
             gathered.append(lax.all_to_all(calibrated, "feed", split_axis=0, concat_axis=0, tiled=True))
         if chunk >= 1:
             picked = beamform(gathered[chunk - 1], weights, select)
-            outs.append(lax.all_to_all(picked, "chan", split_axis=0, concat_axis=0, tiled=True))
+            if chunk < CHUNKS:
+                outs.append(exchange_by_permutes(picked, "chan"))
+            else:
+                outs.append(lax.all_to_all(picked, "chan", split_axis=0, concat_axis=0, tiled=True))
     exchanged = jnp.concatenate(outs, axis=1)
     nodes, bins, fine, width = exchanged.shape
     return jnp.transpose(exchanged, (1, 0, 2, 3)).reshape(bins, nodes * fine, width)

time: 170 us -> 179 us (1.053)
  starting transfers between devices: 18.9 us -> 50.5 us
  blocking collectives: 22.3 us -> 0 us
  waiting for transfers between devices: 67.5 us -> 64.2 us
  local copies, waits for them, and re-layouts: 1.92 us -> 4.3 us
    ppermute x0 -> x15, starting transfers between devices: none -> 31.6 us  [exchange_by_permutes(): received.append(lax.ppermute(piece, axis, perm=pairs))]
    all_to_all x1 -> x0, blocking collectives: 22.3 us -> none  [on_device(): lax.all_to_all(picked, 'chan', split_axis=0, concat_axis=0, tiled=True)]
    all_to_all x2, waiting for transfers between devices: 67.5 us -> 56.7 us  [on_device(): lax.all_to_all(calibrated, 'feed', split_axis=0, concat_axis=0, tiled=True)]
    ppermute x0 -> x15, waiting for transfers between devices: none -> 7.43 us  [exchange_by_permutes(): received.append(lax.ppermute(piece, axis, perm=pairs))]
  transfers between devices with their start and end apart: 3 -> 18, of which waited for: 2 -> 5; matrix products, arithmetic and copies ran while one was open for 2% -> 4% of each run, Pallas kernels for 26% -> 25%
where the time goes in v8:
time: 179 us; the launch traced here: 177 us
  waiting for transfers between devices  64.2 us (36%)
  Pallas kernels  53.2 us (30%)
  starting transfers between devices  50.5 us (28%)
  local copies, waits for them, and re-layouts  4.3 us (2%)
  other arithmetic  4.11 us (2%)
    all_to_all x2, waiting for transfers between devices, on_device(): lax.all_to_all(calibrated, 'feed', split_axis=0, concat_axis=0, tiled=True)  56.7 us
    pallas_call x2, Pallas kernels, beamform(): pl.pallas_call(_beam_kernel, grid=(nb,), in_specs=[pl.BlockSpec((nsrc, 1,...  33.8 us
    ppermute x15, starting transfers between devices, exchange_by_permutes(): received.append(lax.ppermute(piece, axis, perm=pairs))  31.6 us
    pallas_call x2, Pallas kernels, filterbank(): pl.pallas_call(lambda *refs: _filter_kernel(chunk, *refs), grid=(nblk,),...  19.4 us
    all_to_all x2, starting transfers between devices, on_device(): lax.all_to_all(calibrated, 'feed', split_axis=0, concat_axis=0, tiled=True)  11.3 us
    all_to_all x1, starting transfers between devices, on_device(): lax.all_to_all(picked, 'chan', split_axis=0, concat_axis=0, tiled=True)  7.6 us
    ppermute x15, waiting for transfers between devices, exchange_by_permutes(): received.append(lax.ppermute(piece, axis, perm=pairs))  7.43 us
    convert_element_type x1, other arithmetic, on_device(): select = ((jnp.arange(beams, dtype=jnp.int32)[:, None] == flat_ids[None,...  3.66 us
  transfers between devices with their start and end apart: 18, of which 5 were waited for; matrix products, arithmetic and copies ran while one was open for 4% of the time, Pallas kernels for 25%

profile of v8, /device:TPU:1, one launch (start us, length us, event | category | flops | bytes accessed | tf_op | source)
XLA Modules:
  0.0 176.5 jit_solution(11612469207465767202)
XLA Ops:
  0.0 9.7 %shard_map.73 = bf16[8,4,2,2,4,2,16,128]{7,6,5,4,3,2,1,0:T(8,128)(2,1)} custom-call(bf16[2,2,8,2,512,128]{5,4,3,2,1,0:T(8,128)(2,1)} %bitcast.70, bf16[2,2,8,64,16,128]{5,4,3,2,1,0:T(8,128)(2,1)} %bitcast.71, bf16[2,2,8,64,16,128]{5,4,3,2,1,0:T(8,128)(2,1)} %bitcast.72, bf16[2,2,8,64,16,128]{5,4,3,2,1,0:T(8,128)(2,1)} %bitcast.73, ...), custom_call_target="tpu_custom_call" | custom-call | flops 2952790016 | bytes 8388608 | tf_op jit(solution)/shard_map/pallas_call | solution.py:105
  9.7 6.0 %all-to-all-start = ((bf16[8,4,2,2,4,2,16,128]{7,6,5,4,3,2,1,0:T(8,128)(2,1)}), bf16[8,4,2,2,4,2,16,128]{7,6,5,4,3,2,1,0:T(8,128)(2,1)}, u32[]{:S(2)}, u32[]{:S(2)}) async-start(bf16[8,4,2,2,4,2,16,128]{7,6,5,4,3,2,1,0:T(8,128)(2,1)} %shard_map.73), calls=%async_computation | async-start | bytes 8388608 | tf_op jit(solution)/shard_map/all_to_all | solution.py:204
  15.7 9.7 %shard_map.75 = bf16[8,4,2,2,4,2,16,128]{7,6,5,4,3,2,1,0:T(8,128)(2,1)} custom-call(bf16[2,2,8,2,512,128]{5,4,3,2,1,0:T(8,128)(2,1)} %bitcast.74, bf16[2,2,8,64,16,128]{5,4,3,2,1,0:T(8,128)(2,1)} %bitcast.75, bf16[2,2,8,64,16,128]{5,4,3,2,1,0:T(8,128)(2,1)} %bitcast.76, bf16[2,2,8,64,16,128]{5,4,3,2,1,0:T(8,128)(2,1)} %bitcast.77, ...), custom_call_target="tpu_custom_call" | custom-call | flops 2952790016 | bytes 8388608 | tf_op jit(solution)/shard_map/pallas_call | solution.py:105
  25.4 0.0 copy-start.1
  25.4 0.0 copy-start
  25.4 39.2 %all-to-all-done.cal_ref = bf16[8,4,2,2,4,2,16,128]{7,6,5,4,3,2,1,0:T(8,128)(2,1)} async-done(((bf16[8,4,2,2,4,2,16,128]{7,6,5,4,3,2,1,0:T(8,128)(2,1)}), bf16[8,4,2,2,4,2,16,128]{7,6,5,4,3,2,1,0:T(8,128)(2,1)}, u32[]{:S(2)}, u32[]{:S(2)}) %all-to-all-start) | async-done | bytes 4194336 | tf_op jit(solution)/shard_map/all_to_all | solution.py:204
  64.6 5.4 %all-to-all-start.1 = ((bf16[8,4,2,2,4,2,16,128]{7,6,5,4,3,2,1,0:T(8,128)(2,1)}), bf16[8,4,2,2,4,2,16,128]{7,6,5,4,3,2,1,0:T(8,128)(2,1)}, u32[]{:S(2)}, u32[]{:S(2)}) async-start(bf16[8,4,2,2,4,2,16,128]{7,6,5,4,3,2,1,0:T(8,128)(2,1)} %shard_map.75), calls=%async_computation.1 | async-start | bytes 8388608 | tf_op jit(solution)/shard_map/all_to_all | solution.py:204
  70.0 0.0 copy-done.1
  70.0 0.1 fusion.2
  70.1 0.0 copy-done
  70.1 3.7 %fusion.1.sel_ref = bf16[1024,2048]{1,0:T(8,128)(2,1)} fusion(s32[2048]{0:T(1024)S(1)} %bitcast.78, pred[2048]{0:T(1024)(128)(4,1)S(1)} %fusion.2), kind=kLoop, calls=%fused_computation.3 | loop fusion | flops 6291456 | bytes 4204544 | tf_op jit(solution)/shard_map/convert_element_type | solution.py:196
  73.7 16.9 %shard_map.74 = bf16[16,16,16,128]{3,2,1,0:T(8,128)(2,1)} custom-call(bf16[8,4,2,2,4,2,16,128]{7,6,5,4,3,2,1,0:T(8,128)(2,1)} %all-to-all-done.cal_ref, bf16[2,1,1024,1024]{3,2,1,0:T(8,128)(2,1)} %w_ref.3, bf16[1024,2048]{1,0:T(8,128)(2,1)} %fusion.1.sel_ref), custom_call_target="tpu_custom_call" | custom-call | flops 9663676416 | bytes 13631488 | tf_op jit(solution)/shard_map/pallas_call | solution.py:157
  90.6 1.4 dynamic-slice_bitcast_fusion
  92.1 1.3 collective-permute-start
  93.4 2.5 %collective-permute-start.1 = (bf16[16,16,128]{2,1,0:T(8,128)(2,1)S(1)}, bf16[16,16,128]{2,1,0:T(8,128)(2,1)S(1)}, u32[]{:S(2)}, u32[]{:S(2)}) collective-permute-start(bf16[16,16,128]{2,1,0:T(8,128)(2,1)S(1)} %get-tuple-element.18), channel_id=1, source_target_pairs={{0,2},{1,3},{2,4},{3,5},{4,6},{5,7},{6,8},{7,9},{8,10},{9,11},{10,... | collective-permute-start | bytes 196616 | tf_op jit(solution)/shard_map/ppermute | solution.py:183
  95.8 2.5 %collective-permute-start.2 = (bf16[16,16,128]{2,1,0:T(8,128)(2,1)S(1)}, bf16[16,16,128]{2,1,0:T(8,128)(2,1)S(1)}, u32[]{:S(2)}, u32[]{:S(2)}) collective-permute-start(bf16[16,16,128]{2,1,0:T(8,128)(2,1)S(1)} %get-tuple-element.17), channel_id=1, source_target_pairs={{0,3},{1,4},{2,5},{3,6},{4,7},{5,8},{6,9},{7,10},{8,11},{9,12},{10... | collective-permute-start | bytes 196616 | tf_op jit(solution)/shard_map/ppermute | solution.py:183
  98.3 1.6 collective-permute-start.3
  100.0 1.4 collective-permute-start.4
  101.3 17.5 %all-to-all-done.1.cal_ref = bf16[8,4,2,2,4,2,16,128]{7,6,5,4,3,2,1,0:T(8,128)(2,1)} async-done(((bf16[8,4,2,2,4,2,16,128]{7,6,5,4,3,2,1,0:T(8,128)(2,1)}), bf16[8,4,2,2,4,2,16,128]{7,6,5,4,3,2,1,0:T(8,128)(2,1)}, u32[]{:S(2)}, u32[]{:S(2)}) %all-to-all-start.1) | async-done | bytes 4194336 | tf_op jit(solution)/shard_map/all_to_all | solution.py:204
  118.9 16.9 %shard_map.76 = bf16[16,16,16,128]{3,2,1,0:T(8,128)(2,1)} custom-call(bf16[8,4,2,2,4,2,16,128]{7,6,5,4,3,2,1,0:T(8,128)(2,1)} %all-to-all-done.1.cal_ref, bf16[2,1,1024,1024]{3,2,1,0:T(8,128)(2,1)} %w_ref.3, bf16[1024,2048]{1,0:T(8,128)(2,1)} %fusion.1.sel_ref), custom_call_target="tpu_custom_call" | custom-call | flops 9663676416 | bytes 13631488 | tf_op jit(solution)/shard_map/pallas_call | solution.py:157
  135.8 7.6 %all-to-all-start.2 = ((bf16[16,16,16,128]{3,2,1,0:T(8,128)(2,1)}), bf16[16,16,16,128]{3,2,1,0:T(8,128)(2,1)S(1)}, u32[]{:S(2)}, u32[]{:S(2)}) async-start(bf16[16,16,16,128]{3,2,1,0:T(8,128)(2,1)} %shard_map.76), calls=%async_computation.2 | async-start | bytes 2097152 | tf_op jit(solution)/shard_map/all_to_all | solution.py:210
  143.4 0.0 collective-permute-done
  143.4 3.8 %collective-permute-start.5 = (bf16[16,16,128]{2,1,0:T(8,128)(2,1)S(1)}, bf16[16,16,128]{2,1,0:T(8,128)(2,1)S(1)}, u32[]{:S(2)}, u32[]{:S(2)}) collective-permute-start(bf16[16,16,128]{2,1,0:T(8,128)(2,1)S(1)} %get-tuple-element.14), channel_id=1, source_target_pairs={{0,6},{1,7},{2,8},{3,9},{4,10},{5,11},{6,12},{7,13},{8,14},{9,15},... | collective-permute-start | bytes 196616 | tf_op jit(solution)/shard_map/ppermute | solution.py:183
  147.3 0.0 collective-permute-done.1
  147.3 2.5 %collective-permute-start.6 = (bf16[16,16,128]{2,1,0:T(8,128)(2,1)S(1)}, bf16[16,16,128]{2,1,0:T(8,128)(2,1)S(1)}, u32[]{:S(2)}, u32[]{:S(2)}) collective-permute-start(bf16[16,16,128]{2,1,0:T(8,128)(2,1)S(1)} %get-tuple-element.13), channel_id=1, source_target_pairs={{0,7},{1,8},{2,9},{3,10},{4,11},{5,12},{6,13},{7,14},{8,15},{9,0},... | collective-permute-start | bytes 196616 | tf_op jit(solution)/shard_map/ppermute | solution.py:183
  149.7 0.0 collective-permute-done.2
  149.8 1.9 %collective-permute-start.7 = (bf16[16,16,128]{2,1,0:T(8,128)(2,1)S(1)}, bf16[16,16,128]{2,1,0:T(8,128)(2,1)S(1)}, u32[]{:S(2)}, u32[]{:S(2)}) collective-permute-start(bf16[16,16,128]{2,1,0:T(8,128)(2,1)S(1)} %get-tuple-element.12), channel_id=1, source_target_pairs={{0,8},{1,9},{2,10},{3,11},{4,12},{5,13},{6,14},{7,15},{8,0},{9,1},... | collective-permute-start | bytes 196616 | tf_op jit(solution)/shard_map/ppermute | solution.py:183
  151.6 0.0 collective-permute-done.3
  151.6 2.2 %collective-permute-start.8 = (bf16[16,16,128]{2,1,0:T(8,128)(2,1)S(1)}, bf16[16,16,128]{2,1,0:T(8,128)(2,1)S(1)}, u32[]{:S(2)}, u32[]{:S(2)}) collective-permute-start(bf16[16,16,128]{2,1,0:T(8,128)(2,1)S(1)} %get-tuple-element.11), channel_id=1, source_target_pairs={{0,9},{1,10},{2,11},{3,12},{4,13},{5,14},{6,15},{7,0},{8,1},{9,2},... | collective-permute-start | bytes 196616 | tf_op jit(solution)/shard_map/ppermute | solution.py:183
  153.8 0.0 collective-permute-done.4
  153.8 2.1 %collective-permute-start.9 = (bf16[16,16,128]{2,1,0:T(8,128)(2,1)S(1)}, bf16[16,16,128]{2,1,0:T(8,128)(2,1)S(1)}, u32[]{:S(2)}, u32[]{:S(2)}) collective-permute-start(bf16[16,16,128]{2,1,0:T(8,128)(2,1)S(1)} %get-tuple-element.10), channel_id=1, source_target_pairs={{0,10},{1,11},{2,12},{3,13},{4,14},{5,15},{6,0},{7,1},{8,2},{9,3},... | collective-permute-start | bytes 196616 | tf_op jit(solution)/shard_map/ppermute | solution.py:183
  156.0 5.0 %collective-permute-done.5 = bf16[16,16,128]{2,1,0:T(8,128)(2,1)S(1)} collective-permute-done((bf16[16,16,128]{2,1,0:T(8,128)(2,1)S(1)}, bf16[16,16,128]{2,1,0:T(8,128)(2,1)S(1)}, u32[]{:S(2)}, u32[]{:S(2)}) %collective-permute-start.5) | collective-permute-done | bytes 65568 | tf_op jit(solution)/shard_map/ppermute | solution.py:183
  160.9 0.9 collective-permute-start.10
  161.8 0.0 collective-permute-done.6
  161.8 1.2 collective-permute-start.11
  163.0 0.0 collective-permute-done.7
  163.0 5.3 %collective-permute-start.12 = (bf16[16,16,128]{2,1,0:T(8,128)(2,1)S(1)}, bf16[16,16,128]{2,1,0:T(8,128)(2,1)S(1)}, u32[]{:S(2)}, u32[]{:S(2)}) collective-permute-start(bf16[16,16,128]{2,1,0:T(8,128)(2,1)S(1)} %get-tuple-element.7), channel_id=1, source_target_pairs={{0,13},{1,14},{2,15},{3,0},{4,1},{5,2},{6,3},{7,4},{8,5},{9,6},{10... | collective-permute-start | bytes 196616 | tf_op jit(solution)/shard_map/ppermute | solution.py:183
  168.3 0.0 collective-permute-done.8
  168.3 0.7 collective-permute-start.13
  169.1 0.0 collective-permute-done.9
  169.1 1.8 %collective-permute-start.14 = (bf16[16,16,128]{2,1,0:T(8,128)(2,1)S(1)}, bf16[16,16,128]{2,1,0:T(8,128)(2,1)S(1)}, u32[]{:S(2)}, u32[]{:S(2)}) collective-permute-start(bf16[16,16,128]{2,1,0:T(8,128)(2,1)S(1)} %get-tuple-element.5), channel_id=1, source_target_pairs={{0,15},{1,0},{2,1},{3,2},{4,3},{5,4},{6,5},{7,6},{8,7},{9,8},{10,9... | collective-permute-start | bytes 196616 | tf_op jit(solution)/shard_map/ppermute | solution.py:183
  170.9 0.0 collective-permute-done.10
  170.9 0.0 collective-permute-done.11
  171.0 0.0 collective-permute-done.12
  171.0 2.1 %collective-permute-done.13 = bf16[16,16,128]{2,1,0:T(8,128)(2,1)S(1)} collective-permute-done((bf16[16,16,128]{2,1,0:T(8,128)(2,1)S(1)}, bf16[16,16,128]{2,1,0:T(8,128)(2,1)S(1)}, u32[]{:S(2)}, u32[]{:S(2)}) %collective-permute-start.13) | collective-permute-done | bytes 65568 | tf_op jit(solution)/shard_map/ppermute | solution.py:183
  173.1 0.3 collective-permute-done.14
  173.5 0.7 gather_fusion
  174.2 0.2 broadcast_select_fusion
  174.4 0.0 all-to-all-done.2
  174.4 0.2 maximum_bitcast_fusion
  174.6 1.9 %copy.8 = bf16[32,16,16,128]{3,2,1,0:T(8,128)(2,1)} copy(bf16[32,16,16,128]{3,2,0,1:T(8,128)(2,1)S(1)} %maximum_bitcast_fusion) | data formatting | bytes 4194304 | tf_op jit(solution)/shard_map/transpose | solution.py:213
  (18 shorter events, 0.2 us)
Async XLA Ops:
  9.7 54.9 %all-to-all-start = ((bf16[8,4,2,2,4,2,16,128]{7,6,5,4,3,2,1,0:T(8,128)(2,1)}), bf16[8,4,2,2,4,2,16,128]{7,6,5,4,3,2,1,0:T(8,128)(2,1)}, u32[]{:S(2)}, u32[]{:S(2)}) async-start(bf16[8,4,2,2,4,2,16,128]{7,6,5,4,3,2,1,0:T(8,128)(2,1)} %shard_map.73), calls=%async_computation | async-start | bytes 8388608 | tf_op jit(solution)/shard_map/all_to_all | solution.py:204
  25.4 44.6 %copy-start.1 = (s32[16]{0:T(128)S(1)}, s32[16]{0:T(128)}, u32[]{:S(2)}) copy-start(s32[16]{0:T(128)} %param.12) | copy-start | bytes 196
  25.4 44.7 %copy-start = (s32[16,128]{1,0:T(8,128)S(1)}, s32[16,128]{1,0:T(8,128)}, u32[]{:S(2)}) copy-start(s32[16,128]{1,0:T(8,128)} %param.11) | copy-start | bytes 24580
  64.6 54.3 %all-to-all-start.1 = ((bf16[8,4,2,2,4,2,16,128]{7,6,5,4,3,2,1,0:T(8,128)(2,1)}), bf16[8,4,2,2,4,2,16,128]{7,6,5,4,3,2,1,0:T(8,128)(2,1)}, u32[]{:S(2)}, u32[]{:S(2)}) async-start(bf16[8,4,2,2,4,2,16,128]{7,6,5,4,3,2,1,0:T(8,128)(2,1)} %shard_map.75), calls=%async_computation.1 | async-start | bytes 8388608 | tf_op jit(solution)/shard_map/all_to_all | solution.py:204
  92.1 51.3 %collective-permute-start = (bf16[16,16,128]{2,1,0:T(8,128)(2,1)S(1)}, bf16[16,16,128]{2,1,0:T(8,128)(2,1)S(1)}, u32[]{:S(2)}, u32[]{:S(2)}) collective-permute-start(bf16[16,16,128]{2,1,0:T(8,128)(2,1)S(1)} %get-tuple-element.19), channel_id=1, source_target_pairs={{0,1},{1,2},{2,3},{3,4},{4,5},{5,6},{6,7},{7,8},{8,9},{9,10},{10,1... | collective-permute-start | bytes 196616 | tf_op jit(solution)/shard_map/ppermute | solution.py:183
  93.4 53.9 %collective-permute-start.1 = (bf16[16,16,128]{2,1,0:T(8,128)(2,1)S(1)}, bf16[16,16,128]{2,1,0:T(8,128)(2,1)S(1)}, u32[]{:S(2)}, u32[]{:S(2)}) collective-permute-start(bf16[16,16,128]{2,1,0:T(8,128)(2,1)S(1)} %get-tuple-element.18), channel_id=1, source_target_pairs={{0,2},{1,3},{2,4},{3,5},{4,6},{5,7},{6,8},{7,9},{8,10},{9,11},{10,... | collective-permute-start | bytes 196616 | tf_op jit(solution)/shard_map/ppermute | solution.py:183
  95.8 53.9 %collective-permute-start.2 = (bf16[16,16,128]{2,1,0:T(8,128)(2,1)S(1)}, bf16[16,16,128]{2,1,0:T(8,128)(2,1)S(1)}, u32[]{:S(2)}, u32[]{:S(2)}) collective-permute-start(bf16[16,16,128]{2,1,0:T(8,128)(2,1)S(1)} %get-tuple-element.17), channel_id=1, source_target_pairs={{0,3},{1,4},{2,5},{3,6},{4,7},{5,8},{6,9},{7,10},{8,11},{9,12},{10... | collective-permute-start | bytes 196616 | tf_op jit(solution)/shard_map/ppermute | solution.py:183
  98.3 53.3 %collective-permute-start.3 = (bf16[16,16,128]{2,1,0:T(8,128)(2,1)S(1)}, bf16[16,16,128]{2,1,0:T(8,128)(2,1)S(1)}, u32[]{:S(2)}, u32[]{:S(2)}) collective-permute-start(bf16[16,16,128]{2,1,0:T(8,128)(2,1)S(1)} %get-tuple-element.16), channel_id=1, source_target_pairs={{0,4},{1,5},{2,6},{3,7},{4,8},{5,9},{6,10},{7,11},{8,12},{9,13},{1... | collective-permute-start | bytes 196616 | tf_op jit(solution)/shard_map/ppermute | solution.py:183
  100.0 53.9 %collective-permute-start.4 = (bf16[16,16,128]{2,1,0:T(8,128)(2,1)S(1)}, bf16[16,16,128]{2,1,0:T(8,128)(2,1)S(1)}, u32[]{:S(2)}, u32[]{:S(2)}) collective-permute-start(bf16[16,16,128]{2,1,0:T(8,128)(2,1)S(1)} %get-tuple-element.15), channel_id=1, source_target_pairs={{0,5},{1,6},{2,7},{3,8},{4,9},{5,10},{6,11},{7,12},{8,13},{9,14},{... | collective-permute-start | bytes 196616 | tf_op jit(solution)/shard_map/ppermute | solution.py:183
  135.8 38.6 %all-to-all-start.2 = ((bf16[16,16,16,128]{3,2,1,0:T(8,128)(2,1)}), bf16[16,16,16,128]{3,2,1,0:T(8,128)(2,1)S(1)}, u32[]{:S(2)}, u32[]{:S(2)}) async-start(bf16[16,16,16,128]{3,2,1,0:T(8,128)(2,1)} %shard_map.76), calls=%async_computation.2 | async-start | bytes 2097152 | tf_op jit(solution)/shard_map/all_to_all | solution.py:210
  143.4 17.5 %collective-permute-start.5 = (bf16[16,16,128]{2,1,0:T(8,128)(2,1)S(1)}, bf16[16,16,128]{2,1,0:T(8,128)(2,1)S(1)}, u32[]{:S(2)}, u32[]{:S(2)}) collective-permute-start(bf16[16,16,128]{2,1,0:T(8,128)(2,1)S(1)} %get-tuple-element.14), channel_id=1, source_target_pairs={{0,6},{1,7},{2,8},{3,9},{4,10},{5,11},{6,12},{7,13},{8,14},{9,15},... | collective-permute-start | bytes 196616 | tf_op jit(solution)/shard_map/ppermute | solution.py:183
  147.3 14.5 %collective-permute-start.6 = (bf16[16,16,128]{2,1,0:T(8,128)(2,1)S(1)}, bf16[16,16,128]{2,1,0:T(8,128)(2,1)S(1)}, u32[]{:S(2)}, u32[]{:S(2)}) collective-permute-start(bf16[16,16,128]{2,1,0:T(8,128)(2,1)S(1)} %get-tuple-element.13), channel_id=1, source_target_pairs={{0,7},{1,8},{2,9},{3,10},{4,11},{5,12},{6,13},{7,14},{8,15},{9,0},... | collective-permute-start | bytes 196616 | tf_op jit(solution)/shard_map/ppermute | solution.py:183
  149.8 13.3 %collective-permute-start.7 = (bf16[16,16,128]{2,1,0:T(8,128)(2,1)S(1)}, bf16[16,16,128]{2,1,0:T(8,128)(2,1)S(1)}, u32[]{:S(2)}, u32[]{:S(2)}) collective-permute-start(bf16[16,16,128]{2,1,0:T(8,128)(2,1)S(1)} %get-tuple-element.12), channel_id=1, source_target_pairs={{0,8},{1,9},{2,10},{3,11},{4,12},{5,13},{6,14},{7,15},{8,0},{9,1},... | collective-permute-start | bytes 196616 | tf_op jit(solution)/shard_map/ppermute | solution.py:183
  151.6 16.7 %collective-permute-start.8 = (bf16[16,16,128]{2,1,0:T(8,128)(2,1)S(1)}, bf16[16,16,128]{2,1,0:T(8,128)(2,1)S(1)}, u32[]{:S(2)}, u32[]{:S(2)}) collective-permute-start(bf16[16,16,128]{2,1,0:T(8,128)(2,1)S(1)} %get-tuple-element.11), channel_id=1, source_target_pairs={{0,9},{1,10},{2,11},{3,12},{4,13},{5,14},{6,15},{7,0},{8,1},{9,2},... | collective-permute-start | bytes 196616 | tf_op jit(solution)/shard_map/ppermute | solution.py:183
  153.8 15.2 %collective-permute-start.9 = (bf16[16,16,128]{2,1,0:T(8,128)(2,1)S(1)}, bf16[16,16,128]{2,1,0:T(8,128)(2,1)S(1)}, u32[]{:S(2)}, u32[]{:S(2)}) collective-permute-start(bf16[16,16,128]{2,1,0:T(8,128)(2,1)S(1)} %get-tuple-element.10), channel_id=1, source_target_pairs={{0,10},{1,11},{2,12},{3,13},{4,14},{5,15},{6,0},{7,1},{8,2},{9,3},... | collective-permute-start | bytes 196616 | tf_op jit(solution)/shard_map/ppermute | solution.py:183
  160.9 10.0 %collective-permute-start.10 = (bf16[16,16,128]{2,1,0:T(8,128)(2,1)S(1)}, bf16[16,16,128]{2,1,0:T(8,128)(2,1)S(1)}, u32[]{:S(2)}, u32[]{:S(2)}) collective-permute-start(bf16[16,16,128]{2,1,0:T(8,128)(2,1)S(1)} %get-tuple-element.9), channel_id=1, source_target_pairs={{0,11},{1,12},{2,13},{3,14},{4,15},{5,0},{6,1},{7,2},{8,3},{9,4},{... | collective-permute-start | bytes 196616 | tf_op jit(solution)/shard_map/ppermute | solution.py:183
  161.8 9.1 %collective-permute-start.11 = (bf16[16,16,128]{2,1,0:T(8,128)(2,1)S(1)}, bf16[16,16,128]{2,1,0:T(8,128)(2,1)S(1)}, u32[]{:S(2)}, u32[]{:S(2)}) collective-permute-start(bf16[16,16,128]{2,1,0:T(8,128)(2,1)S(1)} %get-tuple-element.8), channel_id=1, source_target_pairs={{0,12},{1,13},{2,14},{3,15},{4,0},{5,1},{6,2},{7,3},{8,4},{9,5},{1... | collective-permute-start | bytes 196616 | tf_op jit(solution)/shard_map/ppermute | solution.py:183
  163.0 7.9 %collective-permute-start.12 = (bf16[16,16,128]{2,1,0:T(8,128)(2,1)S(1)}, bf16[16,16,128]{2,1,0:T(8,128)(2,1)S(1)}, u32[]{:S(2)}, u32[]{:S(2)}) collective-permute-start(bf16[16,16,128]{2,1,0:T(8,128)(2,1)S(1)} %get-tuple-element.7), channel_id=1, source_target_pairs={{0,13},{1,14},{2,15},{3,0},{4,1},{5,2},{6,3},{7,4},{8,5},{9,6},{10... | collective-permute-start | bytes 196616 | tf_op jit(solution)/shard_map/ppermute | solution.py:183
  168.3 4.8 %collective-permute-start.13 = (bf16[16,16,128]{2,1,0:T(8,128)(2,1)S(1)}, bf16[16,16,128]{2,1,0:T(8,128)(2,1)S(1)}, u32[]{:S(2)}, u32[]{:S(2)}) collective-permute-start(bf16[16,16,128]{2,1,0:T(8,128)(2,1)S(1)} %get-tuple-element.6), channel_id=1, source_target_pairs={{0,14},{1,15},{2,0},{3,1},{4,2},{5,3},{6,4},{7,5},{8,6},{9,7},{10,... | collective-permute-start | bytes 196616 | tf_op jit(solution)/shard_map/ppermute | solution.py:183
  169.1 4.4 %collective-permute-start.14 = (bf16[16,16,128]{2,1,0:T(8,128)(2,1)S(1)}, bf16[16,16,128]{2,1,0:T(8,128)(2,1)S(1)}, u32[]{:S(2)}, u32[]{:S(2)}) collective-permute-start(bf16[16,16,128]{2,1,0:T(8,128)(2,1)S(1)} %get-tuple-element.5), channel_id=1, source_target_pairs={{0,15},{1,0},{2,1},{3,2},{4,3},{5,4},{6,5},{7,6},{8,7},{9,8},{10,9... | collective-permute-start | bytes 196616 | tf_op jit(solution)/shard_map/ppermute | solution.py:183

commit v9 on v6

--- a/solution.py
+++ b/solution.py
@@ -173,6 +173,33 @@
     )(cal, weights, select)
 
 
+def exchange_by_permutes(blocks, axis, inner):
+    count = lax.axis_size(axis)
+    outer = count // inner
+    me = lax.axis_index(axis)
+    lo, hi = lax.rem(me, inner), me // inner
+    rest = blocks.shape[1:]
+    grid = blocks.reshape((outer, inner) + rest)
+
+    def stage(values, mine, size, place):
+        got = [lax.dynamic_index_in_dim(values, mine, axis=1, keepdims=False)]
+        for shift in range(1, size):
+            pairs = [(i, place(i, shift)) for i in range(count)]
+            piece = lax.dynamic_index_in_dim(values, lax.rem(mine + shift, size), axis=1, keepdims=False)
+            got.append(lax.ppermute(piece, axis, perm=pairs))
+        return jnp.stack(got)
+
+    first = stage(
+        grid, lo, inner,
+        lambda i, s: (i // inner) * inner + (i % inner + s) % inner,
+    )
+    second = stage(first, hi, outer, lambda i, s: ((i // inner + s) % outer) * inner + i % inner)
+    order_hi = lax.rem(hi - jnp.arange(outer, dtype=jnp.int32) + outer, outer)
+    order_lo = lax.rem(lo - jnp.arange(inner, dtype=jnp.int32) + inner, inner)
+    out = jnp.take(jnp.take(second, order_hi, axis=0), order_lo, axis=1)
+    return out.reshape((count,) + rest)
+
+
 def on_device(voltages, history, gains, weights, beam_lists, beam_counts):
     capacity = beam_lists.shape[1]
     beams = weights.shape[3]
@@ -191,7 +218,10 @@
             gathered.append(lax.all_to_all(calibrated, "feed", split_axis=0, concat_axis=0, tiled=True))
         if chunk >= 1:
             picked = beamform(gathered[chunk - 1], weights, select)
-            outs.append(lax.all_to_all(picked, "chan", split_axis=0, concat_axis=0, tiled=True))
+            if chunk < CHUNKS:
+                outs.append(exchange_by_permutes(picked, "chan", 4))
+            else:
+                outs.append(lax.all_to_all(picked, "chan", split_axis=0, concat_axis=0, tiled=True))
     exchanged = jnp.concatenate(outs, axis=1)
     nodes, bins, fine, width = exchanged.shape
     return jnp.transpose(exchanged, (1, 0, 2, 3)).reshape(bins, nodes * fine, width)

time: 170 us -> 176 us (1.035)
  blocking collectives: 22.3 us -> 0 us
  waiting for transfers between devices: 67.5 us -> 81.3 us
  starting transfers between devices: 18.9 us -> 28.2 us
  local copies, waits for them, and re-layouts: 1.92 us -> 6 us
    all_to_all x1 -> x0, blocking collectives: 22.3 us -> none  [on_device(): lax.all_to_all(picked, 'chan', split_axis=0, concat_axis=0, tiled=True)]
    ppermute x0 -> x6, waiting for transfers between devices: none -> 19.6 us  [stage(): got.append(lax.ppermute(piece, axis, perm=pairs))]
    ppermute x0 -> x6, starting transfers between devices: none -> 9.29 us  [stage(): got.append(lax.ppermute(piece, axis, perm=pairs))]
    all_to_all x2, waiting for transfers between devices: 67.5 us -> 61.8 us  [on_device(): lax.all_to_all(calibrated, 'feed', split_axis=0, concat_axis=0, tiled=True)]
  transfers between devices with their start and end apart: 3 -> 9, of which waited for: 2 -> 4; matrix products, arithmetic and copies ran while one was open for 2% -> 5% of each run, Pallas kernels for 26% -> 25%
where the time goes in v9:
time: 176 us; the launch traced here: 174 us
  waiting for transfers between devices  81.3 us (46%)
  Pallas kernels  53.2 us (30%)
  starting transfers between devices  28.2 us (16%)
  local copies, waits for them, and re-layouts  6 us (3%)
  other arithmetic  5.5 us (3%)
    all_to_all x2, waiting for transfers between devices, on_device(): lax.all_to_all(calibrated, 'feed', split_axis=0, concat_axis=0, tiled=True)  61.8 us
    pallas_call x2, Pallas kernels, beamform(): pl.pallas_call(_beam_kernel, grid=(nb,), in_specs=[pl.BlockSpec((nsrc, 1,...  33.8 us
    ppermute x6, waiting for transfers between devices, stage(): got.append(lax.ppermute(piece, axis, perm=pairs))  19.6 us
    pallas_call x2, Pallas kernels, filterbank(): pl.pallas_call(lambda *refs: _filter_kernel(chunk, *refs), grid=(nblk,),...  19.4 us
    all_to_all x2, starting transfers between devices, on_device(): lax.all_to_all(calibrated, 'feed', split_axis=0, concat_axis=0, tiled=True)  11.3 us
    ppermute x6, starting transfers between devices, stage(): got.append(lax.ppermute(piece, axis, perm=pairs))  9.29 us
    all_to_all x1, starting transfers between devices, on_device(): lax.all_to_all(picked, 'chan', split_axis=0, concat_axis=0, tiled=True)  7.6 us
    convert_element_type x1, other arithmetic, on_device(): select = ((jnp.arange(beams, dtype=jnp.int32)[:, None] == flat_ids[None,...  3.64 us
  transfers between devices with their start and end apart: 9, of which 4 were waited for; matrix products, arithmetic and copies ran while one was open for 5% of the time, Pallas kernels for 25%

profile of v9, /device:TPU:1, one launch (start us, length us, event | category | flops | bytes accessed | tf_op | source)
XLA Modules:
  0.0 174.4 jit_solution(7344106461069083495)
XLA Ops:
  0.0 9.7 %shard_map.73 = bf16[8,4,2,2,4,2,16,128]{7,6,5,4,3,2,1,0:T(8,128)(2,1)} custom-call(bf16[2,2,8,2,512,128]{5,4,3,2,1,0:T(8,128)(2,1)} %bitcast.38, bf16[2,2,8,64,16,128]{5,4,3,2,1,0:T(8,128)(2,1)} %bitcast.39, bf16[2,2,8,64,16,128]{5,4,3,2,1,0:T(8,128)(2,1)} %bitcast.40, bf16[2,2,8,64,16,128]{5,4,3,2,1,0:T(8,128)(2,1)} %bitcast.41, ...), custom_call_target="tpu_custom_call" | custom-call | flops 2952790016 | bytes 8388608 | tf_op jit(solution)/shard_map/pallas_call | solution.py:105
  9.7 6.0 %all-to-all-start = ((bf16[8,4,2,2,4,2,16,128]{7,6,5,4,3,2,1,0:T(8,128)(2,1)}), bf16[8,4,2,2,4,2,16,128]{7,6,5,4,3,2,1,0:T(8,128)(2,1)}, u32[]{:S(2)}, u32[]{:S(2)}) async-start(bf16[8,4,2,2,4,2,16,128]{7,6,5,4,3,2,1,0:T(8,128)(2,1)} %shard_map.73), calls=%async_computation | async-start | bytes 8388608 | tf_op jit(solution)/shard_map/all_to_all | solution.py:218
  15.7 9.7 %shard_map.75 = bf16[8,4,2,2,4,2,16,128]{7,6,5,4,3,2,1,0:T(8,128)(2,1)} custom-call(bf16[2,2,8,2,512,128]{5,4,3,2,1,0:T(8,128)(2,1)} %bitcast.42, bf16[2,2,8,64,16,128]{5,4,3,2,1,0:T(8,128)(2,1)} %bitcast.43, bf16[2,2,8,64,16,128]{5,4,3,2,1,0:T(8,128)(2,1)} %bitcast.44, bf16[2,2,8,64,16,128]{5,4,3,2,1,0:T(8,128)(2,1)} %bitcast.45, ...), custom_call_target="tpu_custom_call" | custom-call | flops 2952790016 | bytes 8388608 | tf_op jit(solution)/shard_map/pallas_call | solution.py:105
  25.4 0.0 copy-start.2
  25.4 0.0 copy-start.1
  25.4 39.2 %all-to-all-done.cal_ref = bf16[8,4,2,2,4,2,16,128]{7,6,5,4,3,2,1,0:T(8,128)(2,1)} async-done(((bf16[8,4,2,2,4,2,16,128]{7,6,5,4,3,2,1,0:T(8,128)(2,1)}), bf16[8,4,2,2,4,2,16,128]{7,6,5,4,3,2,1,0:T(8,128)(2,1)}, u32[]{:S(2)}, u32[]{:S(2)}) %all-to-all-start) | async-done | bytes 4194336 | tf_op jit(solution)/shard_map/all_to_all | solution.py:218
  64.6 5.3 %all-to-all-start.1 = ((bf16[8,4,2,2,4,2,16,128]{7,6,5,4,3,2,1,0:T(8,128)(2,1)}), bf16[8,4,2,2,4,2,16,128]{7,6,5,4,3,2,1,0:T(8,128)(2,1)}, u32[]{:S(2)}, u32[]{:S(2)}) async-start(bf16[8,4,2,2,4,2,16,128]{7,6,5,4,3,2,1,0:T(8,128)(2,1)} %shard_map.75), calls=%async_computation.1 | async-start | bytes 8388608 | tf_op jit(solution)/shard_map/all_to_all | solution.py:218
  69.9 0.0 copy-done.2
  70.0 0.1 fusion.2
  70.0 0.0 copy-done.1
  70.0 3.6 %fusion.1.sel_ref = bf16[1024,2048]{1,0:T(8,128)(2,1)} fusion(s32[2048]{0:T(1024)S(1)} %bitcast.54, pred[2048]{0:T(1024)(128)(4,1)S(1)} %fusion.2), kind=kLoop, calls=%fused_computation.4 | loop fusion | flops 6291456 | bytes 4204544 | tf_op jit(solution)/shard_map/convert_element_type | solution.py:210
  73.7 16.9 %shard_map.74 = bf16[16,16,16,128]{3,2,1,0:T(8,128)(2,1)} custom-call(bf16[8,4,2,2,4,2,16,128]{7,6,5,4,3,2,1,0:T(8,128)(2,1)} %all-to-all-done.cal_ref, bf16[2,1,1024,1024]{3,2,1,0:T(8,128)(2,1)} %w_ref.3, bf16[1024,2048]{1,0:T(8,128)(2,1)} %fusion.1.sel_ref), custom_call_target="tpu_custom_call" | custom-call | flops 9663676416 | bytes 13631488 | tf_op jit(solution)/shard_map/pallas_call | solution.py:157
  90.6 1.4 dynamic-slice_bitcast_fusion.7
  92.0 2.5 %collective-permute-start.2 = (bf16[4,16,16,128]{3,2,1,0:T(8,128)(2,1)S(1)}, bf16[4,16,16,128]{3,2,1,0:T(8,128)(2,1)S(1)}, u32[]{:S(2)}, u32[]{:S(2)}) collective-permute-start(bf16[4,16,16,128]{3,2,1,0:T(8,128)(2,1)S(1)} %get-tuple-element.10), channel_id=1, source_target_pairs={{0,3},{1,0},{2,1},{3,2},{4,7},{5,4},{6,5},{7,6},{8,11},{9,8},{10,9... | collective-permute-start | bytes 786440 | tf_op jit(solution)/shard_map/ppermute | solution.py:189
  94.5 0.0 collective-permute-start
  94.5 1.7 collective-permute-start.1
  96.3 22.6 %all-to-all-done.1.cal_ref = bf16[8,4,2,2,4,2,16,128]{7,6,5,4,3,2,1,0:T(8,128)(2,1)} async-done(((bf16[8,4,2,2,4,2,16,128]{7,6,5,4,3,2,1,0:T(8,128)(2,1)}), bf16[8,4,2,2,4,2,16,128]{7,6,5,4,3,2,1,0:T(8,128)(2,1)}, u32[]{:S(2)}, u32[]{:S(2)}) %all-to-all-start.1) | async-done | bytes 4194336 | tf_op jit(solution)/shard_map/all_to_all | solution.py:218
  118.8 16.9 %shard_map.76 = bf16[16,16,16,128]{3,2,1,0:T(8,128)(2,1)} custom-call(bf16[8,4,2,2,4,2,16,128]{7,6,5,4,3,2,1,0:T(8,128)(2,1)} %all-to-all-done.1.cal_ref, bf16[2,1,1024,1024]{3,2,1,0:T(8,128)(2,1)} %w_ref.3, bf16[1024,2048]{1,0:T(8,128)(2,1)} %fusion.1.sel_ref), custom_call_target="tpu_custom_call" | custom-call | flops 9663676416 | bytes 13631488 | tf_op jit(solution)/shard_map/pallas_call | solution.py:157
  135.8 7.6 %all-to-all-start.2 = ((bf16[16,16,16,128]{3,2,1,0:T(8,128)(2,1)}), bf16[16,16,16,128]{3,2,1,0:T(8,128)(2,1)S(1)}, u32[]{:S(2)}, u32[]{:S(2)}) async-start(bf16[16,16,16,128]{3,2,1,0:T(8,128)(2,1)} %shard_map.76), calls=%async_computation.2 | async-start | bytes 2097152 | tf_op jit(solution)/shard_map/all_to_all | solution.py:224
  143.4 0.0 collective-permute-done.2
  143.4 0.0 collective-permute-done
  143.4 0.0 collective-permute-done.1
  143.4 0.1 pad_maximum_fusion
  143.5 0.2 dynamic-slice_bitcast_fusion.3
  143.8 1.4 collective-permute-start.3
  145.2 2.4 %collective-permute-start.4 = (bf16[4,16,16,128]{3,2,1,0:T(8,128)(2,1)S(1)}, bf16[4,16,16,128]{3,2,1,0:T(8,128)(2,1)S(1)}, u32[]{:S(2)}, u32[]{:S(2)}) collective-permute-start(bf16[4,16,16,128]{3,2,1,0:T(8,128)(2,1)S(1)} %get-tuple-element.7), channel_id=1, source_target_pairs={{0,8},{1,9},{2,10},{3,11},{4,12},{5,13},{6,14},{7,15},{8,0},{9,1},... | collective-permute-start | bytes 786440 | tf_op jit(solution)/shard_map/ppermute | solution.py:189
  147.6 1.2 collective-permute-start.5
  148.8 0.1 broadcast_in_dim.28
  148.9 14.4 %collective-permute-done.3 = bf16[4,16,16,128]{3,2,1,0:T(8,128)(2,1)S(1)} collective-permute-done((bf16[4,16,16,128]{3,2,1,0:T(8,128)(2,1)S(1)}, bf16[4,16,16,128]{3,2,1,0:T(8,128)(2,1)S(1)}, u32[]{:S(2)}, u32[]{:S(2)}) %collective-permute-start.3) | collective-permute-done | bytes 262176 | tf_op jit(solution)/shard_map/ppermute | solution.py:189
  163.3 5.2 %collective-permute-done.4 = bf16[4,16,16,128]{3,2,1,0:T(8,128)(2,1)S(1)} collective-permute-done((bf16[4,16,16,128]{3,2,1,0:T(8,128)(2,1)S(1)}, bf16[4,16,16,128]{3,2,1,0:T(8,128)(2,1)S(1)}, u32[]{:S(2)}, u32[]{:S(2)}) %collective-permute-start.4) | collective-permute-done | bytes 262176 | tf_op jit(solution)/shard_map/ppermute | solution.py:189
  168.5 0.0 collective-permute-done.5
  168.5 0.0 copy-start
  168.5 0.7 copy-done
  169.2 1.1 pad_maximum_fusion.1
  170.3 0.7 gather_fusion
  171.0 0.2 broadcast_select_fusion
  171.2 0.7 gather_fusion.1
  172.0 0.2 copy.8
  172.1 0.2 bitcast_select_fusion
  172.3 0.0 all-to-all-done.2
  172.3 0.2 maximum_bitcast_fusion
  172.5 1.9 %copy.9 = bf16[32,16,16,128]{3,2,1,0:T(8,128)(2,1)} copy(bf16[32,16,16,128]{3,2,0,1:T(8,128)(2,1)S(1)} %maximum_bitcast_fusion) | data formatting | bytes 4194304 | tf_op jit(solution)/shard_map/transpose | solution.py:227
  (6 shorter events, 0.1 us)
Async XLA Ops:
  9.7 54.9 %all-to-all-start = ((bf16[8,4,2,2,4,2,16,128]{7,6,5,4,3,2,1,0:T(8,128)(2,1)}), bf16[8,4,2,2,4,2,16,128]{7,6,5,4,3,2,1,0:T(8,128)(2,1)}, u32[]{:S(2)}, u32[]{:S(2)}) async-start(bf16[8,4,2,2,4,2,16,128]{7,6,5,4,3,2,1,0:T(8,128)(2,1)} %shard_map.73), calls=%async_computation | async-start | bytes 8388608 | tf_op jit(solution)/shard_map/all_to_all | solution.py:218
  25.4 44.6 %copy-start.2 = (s32[16]{0:T(128)S(1)}, s32[16]{0:T(128)}, u32[]{:S(2)}) copy-start(s32[16]{0:T(128)} %param.12) | copy-start | bytes 196
  25.4 44.6 %copy-start.1 = (s32[16,128]{1,0:T(8,128)S(1)}, s32[16,128]{1,0:T(8,128)}, u32[]{:S(2)}) copy-start(s32[16,128]{1,0:T(8,128)} %param.11) | copy-start | bytes 24580
  64.6 54.3 %all-to-all-start.1 = ((bf16[8,4,2,2,4,2,16,128]{7,6,5,4,3,2,1,0:T(8,128)(2,1)}), bf16[8,4,2,2,4,2,16,128]{7,6,5,4,3,2,1,0:T(8,128)(2,1)}, u32[]{:S(2)}, u32[]{:S(2)}) async-start(bf16[8,4,2,2,4,2,16,128]{7,6,5,4,3,2,1,0:T(8,128)(2,1)} %shard_map.75), calls=%async_computation.1 | async-start | bytes 8388608 | tf_op jit(solution)/shard_map/all_to_all | solution.py:218
  92.0 51.4 %collective-permute-start.2 = (bf16[4,16,16,128]{3,2,1,0:T(8,128)(2,1)S(1)}, bf16[4,16,16,128]{3,2,1,0:T(8,128)(2,1)S(1)}, u32[]{:S(2)}, u32[]{:S(2)}) collective-permute-start(bf16[4,16,16,128]{3,2,1,0:T(8,128)(2,1)S(1)} %get-tuple-element.10), channel_id=1, source_target_pairs={{0,3},{1,0},{2,1},{3,2},{4,7},{5,4},{6,5},{7,6},{8,11},{9,8},{10,9... | collective-permute-start | bytes 786440 | tf_op jit(solution)/shard_map/ppermute | solution.py:189
  94.5 48.9 %collective-permute-start = (bf16[4,16,16,128]{3,2,1,0:T(8,128)(2,1)S(1)}, bf16[4,16,16,128]{3,2,1,0:T(8,128)(2,1)S(1)}, u32[]{:S(2)}, u32[]{:S(2)}) collective-permute-start(bf16[4,16,16,128]{3,2,1,0:T(8,128)(2,1)S(1)} %get-tuple-element.12), channel_id=1, source_target_pairs={{0,1},{1,2},{2,3},{3,0},{4,5},{5,6},{6,7},{7,4},{8,9},{9,10},{10,1... | collective-permute-start | bytes 786440 | tf_op jit(solution)/shard_map/ppermute | solution.py:189
  94.5 48.9 %collective-permute-start.1 = (bf16[4,16,16,128]{3,2,1,0:T(8,128)(2,1)S(1)}, bf16[4,16,16,128]{3,2,1,0:T(8,128)(2,1)S(1)}, u32[]{:S(2)}, u32[]{:S(2)}) collective-permute-start(bf16[4,16,16,128]{3,2,1,0:T(8,128)(2,1)S(1)} %get-tuple-element.11), channel_id=1, source_target_pairs={{0,2},{1,3},{2,0},{3,1},{4,6},{5,7},{6,4},{7,5},{8,10},{9,11},{10,... | collective-permute-start | bytes 786440 | tf_op jit(solution)/shard_map/ppermute | solution.py:189
  135.8 36.6 %all-to-all-start.2 = ((bf16[16,16,16,128]{3,2,1,0:T(8,128)(2,1)}), bf16[16,16,16,128]{3,2,1,0:T(8,128)(2,1)S(1)}, u32[]{:S(2)}, u32[]{:S(2)}) async-start(bf16[16,16,16,128]{3,2,1,0:T(8,128)(2,1)} %shard_map.76), calls=%async_computation.2 | async-start | bytes 2097152 | tf_op jit(solution)/shard_map/all_to_all | solution.py:224
  143.8 19.5 %collective-permute-start.3 = (bf16[4,16,16,128]{3,2,1,0:T(8,128)(2,1)S(1)}, bf16[4,16,16,128]{3,2,1,0:T(8,128)(2,1)S(1)}, u32[]{:S(2)}, u32[]{:S(2)}) collective-permute-start(bf16[4,16,16,128]{3,2,1,0:T(8,128)(2,1)S(1)} %get-tuple-element.8), channel_id=1, source_target_pairs={{0,4},{1,5},{2,6},{3,7},{4,8},{5,9},{6,10},{7,11},{8,12},{9,13},{1... | collective-permute-start | bytes 786440 | tf_op jit(solution)/shard_map/ppermute | solution.py:189
  145.2 23.3 %collective-permute-start.4 = (bf16[4,16,16,128]{3,2,1,0:T(8,128)(2,1)S(1)}, bf16[4,16,16,128]{3,2,1,0:T(8,128)(2,1)S(1)}, u32[]{:S(2)}, u32[]{:S(2)}) collective-permute-start(bf16[4,16,16,128]{3,2,1,0:T(8,128)(2,1)S(1)} %get-tuple-element.7), channel_id=1, source_target_pairs={{0,8},{1,9},{2,10},{3,11},{4,12},{5,13},{6,14},{7,15},{8,0},{9,1},... | collective-permute-start | bytes 786440 | tf_op jit(solution)/shard_map/ppermute | solution.py:189
  147.6 20.9 %collective-permute-start.5 = (bf16[4,16,16,128]{3,2,1,0:T(8,128)(2,1)S(1)}, bf16[4,16,16,128]{3,2,1,0:T(8,128)(2,1)S(1)}, u32[]{:S(2)}, u32[]{:S(2)}) collective-permute-start(bf16[4,16,16,128]{3,2,1,0:T(8,128)(2,1)S(1)} %get-tuple-element.6), channel_id=1, source_target_pairs={{0,12},{1,13},{2,14},{3,15},{4,0},{5,1},{6,2},{7,3},{8,4},{9,5},{1... | collective-permute-start | bytes 786440 | tf_op jit(solution)/shard_map/ppermute | solution.py:189
  168.5 0.7 copy-start

commit v10 on v9

--- a/solution.py
+++ b/solution.py
@@ -125,7 +125,8 @@
     )(main, units, units, units, history, gains, band, *extra)
 
 
-def _beam_kernel(cal_ref, w_ref, sel_ref, out_ref):
+def _beam_kernel(cal_ref, w_ref, sel_ref, *rest):
+    out_ref = rest[-1]
     nsrc = cal_ref.shape[0]
     rows = 2 * 2 * IB * U
     halves = []
@@ -149,7 +150,8 @@
         out_ref[n] = picked[:, n * 128 : (n + 1) * 128].reshape(IB, U, 128)
 
 
-def beamform(cal, weights, select):
+def beamform(cal, weights, select, after=None):
+    extra = [] if after is None else [after]
     nsrc, nb = cal.shape[0], cal.shape[1]
     feeds, beams = weights.shape[2], weights.shape[3]
     slots = select.shape[1]
@@ -161,7 +163,8 @@
             pl.BlockSpec((nsrc, 1, 2, 2, IB, TINT, U, 128), lambda i: (0, i, 0, 0, 0, 0, 0, 0)),
             pl.BlockSpec((2, 1, feeds, beams), lambda i: (0, 0, 0, 0)),
             pl.BlockSpec((beams, slots), lambda i: (0, 0)),
-        ],
+        ]
+        + [pl.BlockSpec((1, 1, U, 128), lambda i: (0, 0, 0, 0)) for _ in extra],
         out_specs=pl.BlockSpec((nodes, IB, U, 128), lambda i: (0, i, 0, 0)),
         out_shape=jax.ShapeDtypeStruct((nodes, nb * IB, U, 128), jnp.bfloat16),
         cost_estimate=pl.CostEstimate(
@@ -170,7 +173,7 @@
             transcendentals=0,
         ),
         compiler_params=pltpu.CompilerParams(vmem_limit_bytes=60 * 1024 * 1024),
-    )(cal, weights, select)
+    )(cal, weights, select, *extra)
 
 
 def exchange_by_permutes(blocks, axis, inner):
@@ -217,7 +220,8 @@
             calibrated = filterbank(voltages, history, gains, band, chunk, CHUNKS, after)
             gathered.append(lax.all_to_all(calibrated, "feed", split_axis=0, concat_axis=0, tiled=True))
         if chunk >= 1:
-            picked = beamform(gathered[chunk - 1], weights, select)
+            after = outs[-1].reshape(-1, 1, U, 128) if outs else None
+            picked = beamform(gathered[chunk - 1], weights, select, after)
             if chunk < CHUNKS:
                 outs.append(exchange_by_permutes(picked, "chan", 4))
             else:

time: 176 us -> 171 us (0.972)
  waiting for transfers between devices: 81.3 us -> 75.7 us
    all_to_all x2, waiting for transfers between devices: 61.8 us -> 39.2 us  [on_device(): lax.all_to_all(calibrated, 'feed', split_axis=0, concat_axis=0, tiled=True)]
    all_to_all x1, waiting for transfers between devices: 0.01 us -> 15.8 us  [on_device(): lax.all_to_all(picked, 'chan', split_axis=0, concat_axis=0, tiled=True)]
  transfers between devices with their start and end apart: 9 -> 9, of which waited for: 4 -> 7; matrix products, arithmetic and copies ran while one was open for 5% -> 6% of each run, Pallas kernels for 25% -> 16%
where the time goes in v10:
time: 171 us; the launch traced here: 169 us
  waiting for transfers between devices  75.7 us (44%)
  Pallas kernels  53.3 us (31%)
  starting transfers between devices  28.3 us (17%)
  other arithmetic  6.26 us (4%)
  local copies, waits for them, and re-layouts  5.52 us (3%)
    all_to_all x2, waiting for transfers between devices, on_device(): lax.all_to_all(calibrated, 'feed', split_axis=0, concat_axis=0, tiled=True)  39.2 us
    pallas_call x2, Pallas kernels, beamform(): pl.pallas_call(_beam_kernel, grid=(nb,), in_specs=[pl.BlockSpec((nsrc, 1,...  33.9 us
    ppermute x6, waiting for transfers between devices, stage(): got.append(lax.ppermute(piece, axis, perm=pairs))  20.6 us
    pallas_call x2, Pallas kernels, filterbank(): pl.pallas_call(lambda *refs: _filter_kernel(chunk, *refs), grid=(nblk,),...  19.4 us
    all_to_all x1, waiting for transfers between devices, on_device(): lax.all_to_all(picked, 'chan', split_axis=0, concat_axis=0, tiled=True)  15.8 us
    all_to_all x2, starting transfers between devices, on_device(): lax.all_to_all(calibrated, 'feed', split_axis=0, concat_axis=0, tiled=True)  11.3 us
    ppermute x6, starting transfers between devices, stage(): got.append(lax.ppermute(piece, axis, perm=pairs))  10 us
    all_to_all x1, starting transfers between devices, on_device(): lax.all_to_all(picked, 'chan', split_axis=0, concat_axis=0, tiled=True)  7.05 us
  transfers between devices with their start and end apart: 9, of which 7 were waited for; matrix products, arithmetic and copies ran while one was open for 6% of the time, Pallas kernels for 16%

profile of v10, /device:TPU:1, one launch (start us, length us, event | category | flops | bytes accessed | tf_op | source)
XLA Modules:
  0.0 169.2 jit_solution(1098736873580874655)
XLA Ops:
  0.0 9.7 %shard_map.73 = bf16[8,4,2,2,4,2,16,128]{7,6,5,4,3,2,1,0:T(8,128)(2,1)} custom-call(bf16[2,2,8,2,512,128]{5,4,3,2,1,0:T(8,128)(2,1)} %bitcast.39, bf16[2,2,8,64,16,128]{5,4,3,2,1,0:T(8,128)(2,1)} %bitcast.40, bf16[2,2,8,64,16,128]{5,4,3,2,1,0:T(8,128)(2,1)} %bitcast.41, bf16[2,2,8,64,16,128]{5,4,3,2,1,0:T(8,128)(2,1)} %bitcast.42, ...), custom_call_target="tpu_custom_call" | custom-call | flops 2952790016 | bytes 8388608 | tf_op jit(solution)/shard_map/pallas_call | solution.py:105
  9.7 6.0 %all-to-all-start = ((bf16[8,4,2,2,4,2,16,128]{7,6,5,4,3,2,1,0:T(8,128)(2,1)}), bf16[8,4,2,2,4,2,16,128]{7,6,5,4,3,2,1,0:T(8,128)(2,1)}, u32[]{:S(2)}, u32[]{:S(2)}) async-start(bf16[8,4,2,2,4,2,16,128]{7,6,5,4,3,2,1,0:T(8,128)(2,1)} %shard_map.73), calls=%async_computation | async-start | bytes 8388608 | tf_op jit(solution)/shard_map/all_to_all | solution.py:221
  15.7 9.7 %shard_map.75 = bf16[8,4,2,2,4,2,16,128]{7,6,5,4,3,2,1,0:T(8,128)(2,1)} custom-call(bf16[2,2,8,2,512,128]{5,4,3,2,1,0:T(8,128)(2,1)} %bitcast.43, bf16[2,2,8,64,16,128]{5,4,3,2,1,0:T(8,128)(2,1)} %bitcast.44, bf16[2,2,8,64,16,128]{5,4,3,2,1,0:T(8,128)(2,1)} %bitcast.45, bf16[2,2,8,64,16,128]{5,4,3,2,1,0:T(8,128)(2,1)} %bitcast.46, ...), custom_call_target="tpu_custom_call" | custom-call | flops 2952790016 | bytes 8388608 | tf_op jit(solution)/shard_map/pallas_call | solution.py:105
  25.4 0.0 copy-start.1
  25.4 0.0 copy-start
  25.4 39.2 %all-to-all-done.cal_ref = bf16[8,4,2,2,4,2,16,128]{7,6,5,4,3,2,1,0:T(8,128)(2,1)} async-done(((bf16[8,4,2,2,4,2,16,128]{7,6,5,4,3,2,1,0:T(8,128)(2,1)}), bf16[8,4,2,2,4,2,16,128]{7,6,5,4,3,2,1,0:T(8,128)(2,1)}, u32[]{:S(2)}, u32[]{:S(2)}) %all-to-all-start) | async-done | bytes 4194336 | tf_op jit(solution)/shard_map/all_to_all | solution.py:221
  64.6 5.3 %all-to-all-start.1 = ((bf16[8,4,2,2,4,2,16,128]{7,6,5,4,3,2,1,0:T(8,128)(2,1)}), bf16[8,4,2,2,4,2,16,128]{7,6,5,4,3,2,1,0:T(8,128)(2,1)}, u32[]{:S(2)}, u32[]{:S(2)}) async-start(bf16[8,4,2,2,4,2,16,128]{7,6,5,4,3,2,1,0:T(8,128)(2,1)} %shard_map.75), calls=%async_computation.1 | async-start | bytes 8388608 | tf_op jit(solution)/shard_map/all_to_all | solution.py:221
  69.9 0.0 copy-done.1
  69.9 0.1 fusion.2
  70.0 0.0 copy-done
  70.0 3.6 %fusion.1.sel_ref = bf16[1024,2048]{1,0:T(8,128)(2,1)} fusion(s32[2048]{0:T(1024)S(1)} %bitcast.56, pred[2048]{0:T(1024)(128)(4,1)S(1)} %fusion.2), kind=kLoop, calls=%fused_computation.4 | loop fusion | flops 6291456 | bytes 4204544 | tf_op jit(solution)/shard_map/convert_element_type | solution.py:213
  73.7 16.9 %shard_map.74 = bf16[16,16,16,128]{3,2,1,0:T(8,128)(2,1)} custom-call(bf16[8,4,2,2,4,2,16,128]{7,6,5,4,3,2,1,0:T(8,128)(2,1)} %all-to-all-done.cal_ref, bf16[2,1,1024,1024]{3,2,1,0:T(8,128)(2,1)} %w_ref.3, bf16[1024,2048]{1,0:T(8,128)(2,1)} %fusion.1.sel_ref), custom_call_target="tpu_custom_call" | custom-call | flops 9663676416 | bytes 13631488 | tf_op jit(solution)/shard_map/pallas_call | solution.py:159
  90.6 1.4 dynamic-slice_bitcast_fusion.7
  92.0 2.5 %collective-permute-start.2 = (bf16[4,16,16,128]{3,2,1,0:T(8,128)(2,1)S(1)}, bf16[4,16,16,128]{3,2,1,0:T(8,128)(2,1)S(1)}, u32[]{:S(2)}, u32[]{:S(2)}) collective-permute-start(bf16[4,16,16,128]{3,2,1,0:T(8,128)(2,1)S(1)} %get-tuple-element.10), channel_id=1, source_target_pairs={{0,3},{1,0},{2,1},{3,2},{4,7},{5,4},{6,5},{7,6},{8,11},{9,8},{10,9... | collective-permute-start | bytes 786440 | tf_op jit(solution)/shard_map/ppermute | solution.py:192
  94.5 0.0 collective-permute-start
  94.5 1.7 %collective-permute-start.1 = (bf16[4,16,16,128]{3,2,1,0:T(8,128)(2,1)S(1)}, bf16[4,16,16,128]{3,2,1,0:T(8,128)(2,1)S(1)}, u32[]{:S(2)}, u32[]{:S(2)}) collective-permute-start(bf16[4,16,16,128]{3,2,1,0:T(8,128)(2,1)S(1)} %get-tuple-element.11), channel_id=1, source_target_pairs={{0,2},{1,3},{2,0},{3,1},{4,6},{5,7},{6,4},{7,5},{8,10},{9,11},{10,... | collective-permute-start | bytes 786440 | tf_op jit(solution)/shard_map/ppermute | solution.py:192
  96.3 9.2 %collective-permute-done.2 = bf16[4,16,16,128]{3,2,1,0:T(8,128)(2,1)S(1)} collective-permute-done((bf16[4,16,16,128]{3,2,1,0:T(8,128)(2,1)S(1)}, bf16[4,16,16,128]{3,2,1,0:T(8,128)(2,1)S(1)}, u32[]{:S(2)}, u32[]{:S(2)}) %collective-permute-start.2) | collective-permute-done | bytes 262176 | tf_op jit(solution)/shard_map/ppermute | solution.py:192
  105.5 0.0 collective-permute-done
  105.5 2.3 %collective-permute-done.1 = bf16[4,16,16,128]{3,2,1,0:T(8,128)(2,1)S(1)} collective-permute-done((bf16[4,16,16,128]{3,2,1,0:T(8,128)(2,1)S(1)}, bf16[4,16,16,128]{3,2,1,0:T(8,128)(2,1)S(1)}, u32[]{:S(2)}, u32[]{:S(2)}) %collective-permute-start.1) | collective-permute-done | bytes 262176 | tf_op jit(solution)/shard_map/ppermute | solution.py:192
  107.9 0.1 pad_maximum_fusion
  108.0 0.2 dynamic-slice_bitcast_fusion.3
  108.2 1.7 collective-permute-start.3
  109.9 3.3 %collective-permute-start.4 = (bf16[4,16,16,128]{3,2,1,0:T(8,128)(2,1)S(1)}, bf16[4,16,16,128]{3,2,1,0:T(8,128)(2,1)S(1)}, u32[]{:S(2)}, u32[]{:S(2)}) collective-permute-start(bf16[4,16,16,128]{3,2,1,0:T(8,128)(2,1)S(1)} %get-tuple-element.7), channel_id=1, source_target_pairs={{0,8},{1,9},{2,10},{3,11},{4,12},{5,13},{6,14},{7,15},{8,0},{9,1},... | collective-permute-start | bytes 786440 | tf_op jit(solution)/shard_map/ppermute | solution.py:192
  113.2 0.7 collective-permute-start.5
  114.0 0.1 broadcast_in_dim.41
  114.1 0.1 broadcast_in_dim.42
  114.2 2.4 %collective-permute-done.3 = bf16[4,16,16,128]{3,2,1,0:T(8,128)(2,1)S(1)} collective-permute-done((bf16[4,16,16,128]{3,2,1,0:T(8,128)(2,1)S(1)}, bf16[4,16,16,128]{3,2,1,0:T(8,128)(2,1)S(1)}, u32[]{:S(2)}, u32[]{:S(2)}) %collective-permute-start.3) | collective-permute-done | bytes 262176 | tf_op jit(solution)/shard_map/ppermute | solution.py:192
  116.6 6.4 %collective-permute-done.4 = bf16[4,16,16,128]{3,2,1,0:T(8,128)(2,1)S(1)} collective-permute-done((bf16[4,16,16,128]{3,2,1,0:T(8,128)(2,1)S(1)}, bf16[4,16,16,128]{3,2,1,0:T(8,128)(2,1)S(1)}, u32[]{:S(2)}, u32[]{:S(2)}) %collective-permute-start.4) | collective-permute-done | bytes 262176 | tf_op jit(solution)/shard_map/ppermute | solution.py:192
  123.0 0.2 collective-permute-done.5
  123.2 0.1 pad_maximum_fusion.1
  123.3 0.7 gather_fusion
  124.1 0.2 broadcast_select_fusion.1
  124.2 0.7 gather_fusion.1
  125.0 0.2 copy.8
  125.2 1.7 %broadcast_select_fusion.rest_0_ = bf16[256,1,16,128]{3,2,1,0:T(8,128)(2,1)} fusion(bf16[256,1,16,128]{3,2,1,0:T(8,128)(2,1)S(1)} %bitcast.47, pred[256]{0:T(512)(128)(4,1)S(1)} %broadcast_in_dim.42), kind=kLoop, calls=%fused_computation.9 | loop fusion | flops 524288 | bytes 2097408 | tf_op jit(solution)/shard_map/jit(_take)/select_n | solution.py:202
  127.0 0.0 all-to-all-done.1.cal_ref
  127.0 17.0 %shard_map.76 = bf16[16,16,16,128]{3,2,1,0:T(8,128)(2,1)} custom-call(bf16[8,4,2,2,4,2,16,128]{7,6,5,4,3,2,1,0:T(8,128)(2,1)} %all-to-all-done.1.cal_ref, bf16[2,1,1024,1024]{3,2,1,0:T(8,128)(2,1)} %w_ref.3, bf16[1024,2048]{1,0:T(8,128)(2,1)} %fusion.1.sel_ref, bf16[256,1,16,128]{3,2,1,0:T(8,128)(2,1)} %broadcast_select_fusion.rest_0_), custom_call_target="tpu_custom_call" | custom-call | flops 9663676416 | bytes 13631488 | tf_op jit(solution)/shard_map/pallas_call | solution.py:159
  143.9 7.1 %all-to-all-start.2 = ((bf16[16,16,16,128]{3,2,1,0:T(8,128)(2,1)}), bf16[16,16,16,128]{3,2,1,0:T(8,128)(2,1)S(1)}, u32[]{:S(2)}, u32[]{:S(2)}) async-start(bf16[16,16,16,128]{3,2,1,0:T(8,128)(2,1)} %shard_map.76), calls=%async_computation.2 | async-start | bytes 2097152 | tf_op jit(solution)/shard_map/all_to_all | solution.py:228
  151.0 0.1 broadcast_in_dim.36
  151.1 0.2 bitcast_select_fusion
  151.3 15.8 %all-to-all-done.2 = bf16[16,16,16,128]{3,2,1,0:T(8,128)(2,1)S(1)} async-done(((bf16[16,16,16,128]{3,2,1,0:T(8,128)(2,1)}), bf16[16,16,16,128]{3,2,1,0:T(8,128)(2,1)S(1)}, u32[]{:S(2)}, u32[]{:S(2)}) %all-to-all-start.2) | async-done | bytes 1048608 | tf_op jit(solution)/shard_map/all_to_all | solution.py:228
  167.1 0.2 maximum_bitcast_fusion
  167.3 1.9 %copy.10 = bf16[32,16,16,128]{3,2,1,0:T(8,128)(2,1)} copy(bf16[32,16,16,128]{3,2,0,1:T(8,128)(2,1)S(1)} %maximum_bitcast_fusion) | data formatting | bytes 4194304 | tf_op jit(solution)/shard_map/transpose | solution.py:231
  (6 shorter events, 0.1 us)
Async XLA Ops:
  9.7 54.9 %all-to-all-start = ((bf16[8,4,2,2,4,2,16,128]{7,6,5,4,3,2,1,0:T(8,128)(2,1)}), bf16[8,4,2,2,4,2,16,128]{7,6,5,4,3,2,1,0:T(8,128)(2,1)}, u32[]{:S(2)}, u32[]{:S(2)}) async-start(bf16[8,4,2,2,4,2,16,128]{7,6,5,4,3,2,1,0:T(8,128)(2,1)} %shard_map.73), calls=%async_computation | async-start | bytes 8388608 | tf_op jit(solution)/shard_map/all_to_all | solution.py:221
  25.4 44.5 %copy-start.1 = (s32[16]{0:T(128)S(1)}, s32[16]{0:T(128)}, u32[]{:S(2)}) copy-start(s32[16]{0:T(128)} %param.12) | copy-start | bytes 196
  25.4 44.6 %copy-start = (s32[16,128]{1,0:T(8,128)S(1)}, s32[16,128]{1,0:T(8,128)}, u32[]{:S(2)}) copy-start(s32[16,128]{1,0:T(8,128)} %param.11) | copy-start | bytes 24580
  64.6 62.3 %all-to-all-start.1 = ((bf16[8,4,2,2,4,2,16,128]{7,6,5,4,3,2,1,0:T(8,128)(2,1)}), bf16[8,4,2,2,4,2,16,128]{7,6,5,4,3,2,1,0:T(8,128)(2,1)}, u32[]{:S(2)}, u32[]{:S(2)}) async-start(bf16[8,4,2,2,4,2,16,128]{7,6,5,4,3,2,1,0:T(8,128)(2,1)} %shard_map.75), calls=%async_computation.1 | async-start | bytes 8388608 | tf_op jit(solution)/shard_map/all_to_all | solution.py:221
  92.0 13.6 %collective-permute-start.2 = (bf16[4,16,16,128]{3,2,1,0:T(8,128)(2,1)S(1)}, bf16[4,16,16,128]{3,2,1,0:T(8,128)(2,1)S(1)}, u32[]{:S(2)}, u32[]{:S(2)}) collective-permute-start(bf16[4,16,16,128]{3,2,1,0:T(8,128)(2,1)S(1)} %get-tuple-element.10), channel_id=1, source_target_pairs={{0,3},{1,0},{2,1},{3,2},{4,7},{5,4},{6,5},{7,6},{8,11},{9,8},{10,9... | collective-permute-start | bytes 786440 | tf_op jit(solution)/shard_map/ppermute | solution.py:192
  94.5 11.0 %collective-permute-start = (bf16[4,16,16,128]{3,2,1,0:T(8,128)(2,1)S(1)}, bf16[4,16,16,128]{3,2,1,0:T(8,128)(2,1)S(1)}, u32[]{:S(2)}, u32[]{:S(2)}) collective-permute-start(bf16[4,16,16,128]{3,2,1,0:T(8,128)(2,1)S(1)} %get-tuple-element.12), channel_id=1, source_target_pairs={{0,1},{1,2},{2,3},{3,0},{4,5},{5,6},{6,7},{7,4},{8,9},{9,10},{10,1... | collective-permute-start | bytes 786440 | tf_op jit(solution)/shard_map/ppermute | solution.py:192
  94.5 13.4 %collective-permute-start.1 = (bf16[4,16,16,128]{3,2,1,0:T(8,128)(2,1)S(1)}, bf16[4,16,16,128]{3,2,1,0:T(8,128)(2,1)S(1)}, u32[]{:S(2)}, u32[]{:S(2)}) collective-permute-start(bf16[4,16,16,128]{3,2,1,0:T(8,128)(2,1)S(1)} %get-tuple-element.11), channel_id=1, source_target_pairs={{0,2},{1,3},{2,0},{3,1},{4,6},{5,7},{6,4},{7,5},{8,10},{9,11},{10,... | collective-permute-start | bytes 786440 | tf_op jit(solution)/shard_map/ppermute | solution.py:192
  108.2 8.3 %collective-permute-start.3 = (bf16[4,16,16,128]{3,2,1,0:T(8,128)(2,1)S(1)}, bf16[4,16,16,128]{3,2,1,0:T(8,128)(2,1)S(1)}, u32[]{:S(2)}, u32[]{:S(2)}) collective-permute-start(bf16[4,16,16,128]{3,2,1,0:T(8,128)(2,1)S(1)} %get-tuple-element.8), channel_id=1, source_target_pairs={{0,4},{1,5},{2,6},{3,7},{4,8},{5,9},{6,10},{7,11},{8,12},{9,13},{1... | collective-permute-start | bytes 786440 | tf_op jit(solution)/shard_map/ppermute | solution.py:192
  109.9 13.0 %collective-permute-start.4 = (bf16[4,16,16,128]{3,2,1,0:T(8,128)(2,1)S(1)}, bf16[4,16,16,128]{3,2,1,0:T(8,128)(2,1)S(1)}, u32[]{:S(2)}, u32[]{:S(2)}) collective-permute-start(bf16[4,16,16,128]{3,2,1,0:T(8,128)(2,1)S(1)} %get-tuple-element.7), channel_id=1, source_target_pairs={{0,8},{1,9},{2,10},{3,11},{4,12},{5,13},{6,14},{7,15},{8,0},{9,1},... | collective-permute-start | bytes 786440 | tf_op jit(solution)/shard_map/ppermute | solution.py:192
  113.2 9.9 %collective-permute-start.5 = (bf16[4,16,16,128]{3,2,1,0:T(8,128)(2,1)S(1)}, bf16[4,16,16,128]{3,2,1,0:T(8,128)(2,1)S(1)}, u32[]{:S(2)}, u32[]{:S(2)}) collective-permute-start(bf16[4,16,16,128]{3,2,1,0:T(8,128)(2,1)S(1)} %get-tuple-element.6), channel_id=1, source_target_pairs={{0,12},{1,13},{2,14},{3,15},{4,0},{5,1},{6,2},{7,3},{8,4},{9,5},{1... | collective-permute-start | bytes 786440 | tf_op jit(solution)/shard_map/ppermute | solution.py:192
  143.9 23.2 %all-to-all-start.2 = ((bf16[16,16,16,128]{3,2,1,0:T(8,128)(2,1)}), bf16[16,16,16,128]{3,2,1,0:T(8,128)(2,1)S(1)}, u32[]{:S(2)}, u32[]{:S(2)}) async-start(bf16[16,16,16,128]{3,2,1,0:T(8,128)(2,1)} %shard_map.76), calls=%async_computation.2 | async-start | bytes 2097152 | tf_op jit(solution)/shard_map/all_to_all | solution.py:228

commit v11 on v6

--- a/solution.py
+++ b/solution.py
@@ -149,6 +149,44 @@
         out_ref[n] = picked[:, n * 128 : (n + 1) * 128].reshape(IB, U, 128)
 
 
+def _beam_pieces_kernel(*refs):
+    count = len(refs) - 3
+
+    class Stacked:
+        def __getitem__(self, index):
+            return refs[index[0]][(0,) + index[1:]]
+
+    shape = (count,) + refs[0].shape[1:]
+    stacked = Stacked()
+    stacked.shape = shape
+    _beam_kernel(stacked, *refs[count:])
+
+
+def beamform_pieces(pieces, weights, select):
+    nb = pieces[0].shape[1]
+    feeds, beams = weights.shape[2], weights.shape[3]
+    slots = select.shape[1]
+    nodes = slots // 128
+    piece_spec = pl.BlockSpec((1, 1, 2, 2, IB, TINT, U, 128), lambda i: (0, i, 0, 0, 0, 0, 0, 0))
+    return pl.pallas_call(
+        _beam_pieces_kernel,
+        grid=(nb,),
+        in_specs=[piece_spec] * len(pieces)
+        + [
+            pl.BlockSpec((2, 1, feeds, beams), lambda i: (0, 0, 0, 0)),
+            pl.BlockSpec((beams, slots), lambda i: (0, 0)),
+        ],
+        out_specs=pl.BlockSpec((nodes, IB, U, 128), lambda i: (0, i, 0, 0)),
+        out_shape=jax.ShapeDtypeStruct((nodes, nb * IB, U, 128), jnp.bfloat16),
+        cost_estimate=pl.CostEstimate(
+            flops=2 * 2 * (4 * nb * IB * U * TINT) * feeds * beams + 2 * nb * IB * U * beams * slots,
+            bytes_accessed=sum(p.size for p in pieces) * 2 + weights.size * 2 + select.size * 2 + nb * IB * U * slots * 2,
+            transcendentals=0,
+        ),
+        compiler_params=pltpu.CompilerParams(vmem_limit_bytes=60 * 1024 * 1024),
+    )(*pieces, weights, select)
+
+
 def beamform(cal, weights, select):
     nsrc, nb = cal.shape[0], cal.shape[1]
     feeds, beams = weights.shape[2], weights.shape[3]
@@ -182,16 +220,24 @@
         (jnp.arange(beams, dtype=jnp.int32)[:, None] == flat_ids[None, :]) & live_slots[None, :]
     ).astype(jnp.bfloat16)
     band = jnp.asarray(band_matrix())
-    gathered = []
+    nfeed = lax.axis_size("feed")
+    me = lax.axis_index("feed")
+    order = lax.rem(me - jnp.arange(nfeed, dtype=jnp.int32) + nfeed, nfeed)
+    feeds_local = weights.shape[2] // nfeed
+    wperm = jnp.take(weights.reshape(2, 1, nfeed, feeds_local, beams), order, axis=2).reshape(weights.shape)
+    first = filterbank(voltages, history, gains, band, 0, CHUNKS)
+    gathered = lax.all_to_all(first, "feed", split_axis=0, concat_axis=0, tiled=True)
+    second = filterbank(voltages, history, gains, band, 1, CHUNKS)
+    pieces = [lax.dynamic_slice_in_dim(second, me, 1, axis=0)]
+    for shift in range(1, nfeed):
+        pairs = [(i, (i + shift) % nfeed) for i in range(nfeed)]
+        piece = lax.dynamic_slice_in_dim(second, lax.rem(me + shift, nfeed), 1, axis=0)
+        pieces.append(lax.ppermute(piece, "feed", perm=pairs))
     outs = []
-    for chunk in range(CHUNKS + 1):
-        if chunk < CHUNKS:
-            after = outs[-1] if outs else None
-            calibrated = filterbank(voltages, history, gains, band, chunk, CHUNKS, after)
-            gathered.append(lax.all_to_all(calibrated, "feed", split_axis=0, concat_axis=0, tiled=True))
-        if chunk >= 1:
-            picked = beamform(gathered[chunk - 1], weights, select)
-            outs.append(lax.all_to_all(picked, "chan", split_axis=0, concat_axis=0, tiled=True))
+    picked = beamform(gathered, weights, select)
+    outs.append(lax.all_to_all(picked, "chan", split_axis=0, concat_axis=0, tiled=True))
+    picked = beamform_pieces(pieces, wperm, select)
+    outs.append(lax.all_to_all(picked, "chan", split_axis=0, concat_axis=0, tiled=True))
     exchanged = jnp.concatenate(outs, axis=1)
     nodes, bins, fine, width = exchanged.shape
     return jnp.transpose(exchanged, (1, 0, 2, 3)).reshape(bins, nodes * fine, width)

time: 170 us -> 178 us (1.047)
  local copies, waits for them, and re-layouts: 1.92 us -> 14.7 us
  waiting for transfers between devices: 67.5 us -> 57.3 us
  starting transfers between devices: 18.9 us -> 22.7 us
  other arithmetic: 3.93 us -> 6.34 us
    all_to_all x2 -> x1, waiting for transfers between devices: 67.5 us -> 0.01 us  [on_device(): lax.all_to_all(first, 'feed', split_axis=0, concat_axis=0, tiled=True)]
    ppermute x0 -> x7, waiting for transfers between devices: none -> 57.3 us  [on_device(): pieces.append(lax.ppermute(piece, 'feed', perm=pairs))]
    pallas_call x0 -> x1, Pallas kernels: none -> 17.2 us  [beamform_pieces(): pl.pallas_call(_beam_pieces_kernel, grid=(nb,), in_specs=[piece_spec] * l...]
    pallas_call x2 -> x1, Pallas kernels: 33.9 us -> 16.9 us  [beamform(): pl.pallas_call(_beam_kernel, grid=(nb,), in_specs=[pl.BlockSpec((nsrc, 1,...]
    ppermute x0 -> x7, starting transfers between devices: none -> 9.1 us  [on_device(): pieces.append(lax.ppermute(piece, 'feed', perm=pairs))]
    gather x0 -> x2, local copies, waits for them, and re-layouts: none -> 7.63 us  [on_device(): jnp.take(weights.reshape(2, 1, nfeed, feeds_local, beams), order, axis=2)]
    all_to_all x2 -> x1, starting transfers between devices: 11.3 us -> 5.97 us  [on_device(): lax.all_to_all(first, 'feed', split_axis=0, concat_axis=0, tiled=True)]
    dynamic_slice x0 -> x1, local copies, waits for them, and re-layouts: none -> 4.13 us  [on_device(): lax.dynamic_slice_in_dim(second, lax.rem(me + shift, nfeed), 1, axis=0)]
  transfers between devices with their start and end apart: 3 -> 9, of which waited for: 2 -> 5; matrix products, arithmetic and copies ran while one was open for 2% -> 10% of each run, Pallas kernels for 26% -> 25%
where the time goes in v11:
time: 178 us; the launch traced here: 177 us
  waiting for transfers between devices  57.3 us (32%)
  Pallas kernels  53.6 us (30%)
  starting transfers between devices  22.7 us (13%)
  blocking collectives  22.3 us (13%)
  local copies, waits for them, and re-layouts  14.7 us (8%)
  other arithmetic  6.34 us (4%)
    ppermute x7, waiting for transfers between devices, on_device(): pieces.append(lax.ppermute(piece, 'feed', perm=pairs))  57.3 us
    all_to_all x1, blocking collectives, on_device(): lax.all_to_all(picked, 'chan', split_axis=0, concat_axis=0, tiled=True)  22.3 us
    pallas_call x2, Pallas kernels, filterbank(): pl.pallas_call(lambda *refs: _filter_kernel(chunk, *refs), grid=(nblk,),...  19.4 us
    pallas_call x1, Pallas kernels, beamform_pieces(): pl.pallas_call(_beam_pieces_kernel, grid=(nb,), in_specs=[piece_spec] * l...  17.2 us
    pallas_call x1, Pallas kernels, beamform(): pl.pallas_call(_beam_kernel, grid=(nb,), in_specs=[pl.BlockSpec((nsrc, 1,...  16.9 us
    ppermute x7, starting transfers between devices, on_device(): pieces.append(lax.ppermute(piece, 'feed', perm=pairs))  9.1 us
    gather x2, local copies, waits for them, and re-layouts, on_device(): jnp.take(weights.reshape(2, 1, nfeed, feeds_local, beams), order, axis=2)  7.63 us
    all_to_all x1, starting transfers between devices, on_device(): lax.all_to_all(picked, 'chan', split_axis=0, concat_axis=0, tiled=True)  7.61 us
  transfers between devices with their start and end apart: 9, of which 5 were waited for; matrix products, arithmetic and copies ran while one was open for 10% of the time, Pallas kernels for 25%

profile of v11, /device:TPU:1, one launch (start us, length us, event | category | flops | bytes accessed | tf_op | source)
XLA Modules:
  0.0 177.0 jit_solution(7665946482985566456)
XLA Ops:
  0.0 9.7 %shard_map.73 = bf16[8,4,2,2,4,2,16,128]{7,6,5,4,3,2,1,0:T(8,128)(2,1)} custom-call(bf16[2,2,8,2,512,128]{5,4,3,2,1,0:T(8,128)(2,1)} %bitcast.17, bf16[2,2,8,64,16,128]{5,4,3,2,1,0:T(8,128)(2,1)} %bitcast.18, bf16[2,2,8,64,16,128]{5,4,3,2,1,0:T(8,128)(2,1)} %bitcast.19, bf16[2,2,8,64,16,128]{5,4,3,2,1,0:T(8,128)(2,1)} %bitcast.20, ...), custom_call_target="tpu_custom_call" | custom-call | flops 2952790016 | bytes 8388608 | tf_op jit(solution)/shard_map/pallas_call | solution.py:105
  9.7 6.0 %all-to-all-start = ((bf16[8,4,2,2,4,2,16,128]{7,6,5,4,3,2,1,0:T(8,128)(2,1)}), bf16[8,4,2,2,4,2,16,128]{7,6,5,4,3,2,1,0:T(8,128)(2,1)}, u32[]{:S(2)}, u32[]{:S(2)}) async-start(bf16[8,4,2,2,4,2,16,128]{7,6,5,4,3,2,1,0:T(8,128)(2,1)} %shard_map.73), calls=%async_computation | async-start | bytes 8388608 | tf_op jit(solution)/shard_map/all_to_all | solution.py:229
  15.7 9.7 %shard_map.75 = bf16[8,4,2,2,4,2,16,128]{7,6,5,4,3,2,1,0:T(8,128)(2,1)} custom-call(bf16[2,2,8,2,512,128]{5,4,3,2,1,0:T(8,128)(2,1)} %bitcast.21, bf16[2,2,8,64,16,128]{5,4,3,2,1,0:T(8,128)(2,1)} %bitcast.22, bf16[2,2,8,64,16,128]{5,4,3,2,1,0:T(8,128)(2,1)} %bitcast.23, bf16[2,2,8,64,16,128]{5,4,3,2,1,0:T(8,128)(2,1)} %bitcast.24, ...), custom_call_target="tpu_custom_call" | custom-call | flops 2952790016 | bytes 8388608 | tf_op jit(solution)/shard_map/pallas_call | solution.py:105
  25.4 0.0 copy-start.1
  25.4 4.1 %constant_dynamic-slice_fusion = (bf16[1,4,2,2,4,2,16,128]{7,6,5,4,3,2,1,0:T(8,128)(2,1)S(1)}, bf16[1,4,2,2,4,2,16,128]{7,6,5,4,3,2,1,0:T(8,128)(2,1)S(1)}, bf16...) fusion(bf16[8,4,2,2,4,2,16,128]{7,6,5,4,3,2,1,0:T(8,128)(2,1)} , ...), kind=kLoop, calls=%fused_computation.15 | loop fusion | bytes 8388640 | tf_op jit(solution)/shard_map/dynamic_slice | solution.py:234
  29.5 1.6 collective-permute-start
  31.1 1.2 collective-permute-start.1
  32.3 1.6 collective-permute-start.2
  34.0 0.6 collective-permute-start.3
  34.5 1.7 collective-permute-start.4
  36.2 0.1 broadcast_bitcast_fusion
  36.3 0.0 copy-done.1
  36.3 0.1 fusion.2
  36.4 5.0 %gather_fusion = bf16[8,2,128,1024]{3,2,1,0:T(8,128)(2,1)} fusion(bf16[2,8,128,1024]{3,2,1,0:T(8,128)(2,1)} %bitcast.27, s32[1024]{0:T(1024)S(1)} %pad_clamp_fusion), kind=kCustom, calls=%fused_computation | custom fusion | bytes 8388640 | tf_op jit(solution)/shard_map/jit(_take)/gather | solution.py:227
  41.4 2.7 %copy.8 = bf16[2,8,128,1024]{3,2,1,0:T(8,128)(2,1)S(1)} copy(bf16[2,8,128,1024]{3,2,0,1:T(8,128)(2,1)} %bitcast.26) | data formatting | bytes 8388608 | tf_op jit(solution)/shard_map/jit(_take)/gather | solution.py:227
  44.0 0.0 copy-start
  44.0 2.4 %bitcast_select_fusion.refs_8_ = bf16[2,1,1024,1024]{3,2,1,0:T(8,128)(2,1)} fusion(pred[1024]{0:T(1024)(128)(4,1)S(1)} %broadcast_bitcast_fusion, bf16[2,1,1024,1024]{3,2,1,0:T(8,128)(2,1)S(1)} %bitcast.25), kind=kLoop, calls=%fused_computation.4 | loop fusion | flops 2097152 | bytes 8389632 | tf_op jit(solution)/shard_map/jit(_take)/select_n | solution.py:227
  46.4 26.1 %collective-permute-done.refs_1_ = bf16[1,4,2,2,4,2,16,128]{7,6,5,4,3,2,1,0:T(8,128)(2,1)} collective-permute-done((bf16[1,4,2,2,4,2,16,128]{7,6,5,4,3,2,1,0:T(8,128)(2,1)}, bf16[1,4,2,2,4,2,16,128]{7,6,5,4,3,2,1,0:T(8,128)(2,1)}, u32[]{:S(2)}, u32[]{:S(2)}) %collective-permute-start) | collective-permute-done | bytes 524320 | tf_op jit(solution)/shard_map/ppermute | solution.py:235
  72.6 2.4 %collective-permute-start.5 = (bf16[1,4,2,2,4,2,16,128]{7,6,5,4,3,2,1,0:T(8,128)(2,1)S(1)}, bf16[1,4,2,2,4,2,16,128]{7,6,5,4,3,2,1,0:T(8,128)(2,1)S(1)}, u32[]{:S(2)}, u32[]{:S(2)}) collective-permute-start(bf16[1,4,2,2,4,2,16,128]{7,6,5,4,3,2,1,0:T(8,128)(2,1)S(1)} %get-tuple-element.6), channel_id=1, source_target_pairs={{0,96},{16,112},{32,0},{48,16},{64,32},{80,48},{96,64},{112,80},{1... | collective-permute-start | bytes 1572872 | tf_op jit(solution)/shard_map/ppermute | solution.py:235
  75.0 11.7 %collective-permute-done.1.refs_2_ = bf16[1,4,2,2,4,2,16,128]{7,6,5,4,3,2,1,0:T(8,128)(2,1)} collective-permute-done((bf16[1,4,2,2,4,2,16,128]{7,6,5,4,3,2,1,0:T(8,128)(2,1)S(1)}, bf16[1,4,2,2,4,2,16,128]{7,6,5,4,3,2,1,0:T(8,128)(2,1)}, u32[]{:S(2)}, u32[]{:S(2)}) %collective-permute-start.1) | collective-permute-done | bytes 524320 | tf_op jit(solution)/shard_map/ppermute | solution.py:235
  86.6 0.0 collective-permute-start.6
  86.7 0.0 copy-done
  86.7 3.7 %fusion.1.sel_ref.refs_9_ = bf16[1024,2048]{1,0:T(8,128)(2,1)} fusion(s32[2048]{0:T(1024)S(1)} %bitcast.28, pred[2048]{0:T(1024)(128)(4,1)S(1)} %fusion.2), kind=kLoop, calls=%fused_computation.3 | loop fusion | flops 6291456 | bytes 4204544 | tf_op jit(solution)/shard_map/convert_element_type | solution.py:221
  90.3 4.6 %collective-permute-done.2.refs_3_ = bf16[1,4,2,2,4,2,16,128]{7,6,5,4,3,2,1,0:T(8,128)(2,1)} collective-permute-done((bf16[1,4,2,2,4,2,16,128]{7,6,5,4,3,2,1,0:T(8,128)(2,1)S(1)}, bf16[1,4,2,2,4,2,16,128]{7,6,5,4,3,2,1,0:T(8,128)(2,1)}, u32[]{:S(2)}, u32[]{:S(2)}) %collective-permute-start.2) | collective-permute-done | bytes 524320 | tf_op jit(solution)/shard_map/ppermute | solution.py:235
  94.9 14.4 %collective-permute-done.3.refs_4_ = bf16[1,4,2,2,4,2,16,128]{7,6,5,4,3,2,1,0:T(8,128)(2,1)} collective-permute-done((bf16[1,4,2,2,4,2,16,128]{7,6,5,4,3,2,1,0:T(8,128)(2,1)S(1)}, bf16[1,4,2,2,4,2,16,128]{7,6,5,4,3,2,1,0:T(8,128)(2,1)}, u32[]{:S(2)}, u32[]{:S(2)}) %collective-permute-start.3) | collective-permute-done | bytes 524320 | tf_op jit(solution)/shard_map/ppermute | solution.py:235
  109.3 0.5 collective-permute-done.4.refs_5_
  109.8 0.0 collective-permute-done.5.refs_6_
  109.8 0.0 copy-start.2
  109.8 0.0 collective-permute-done.6.refs_7_
  109.8 0.0 copy-start.3
  109.8 0.8 copy-done.2
  110.6 0.2 copy-done.3
  110.8 17.2 %shard_map.76 = bf16[16,16,16,128]{3,2,1,0:T(8,128)(2,1)} custom-call(bf16[1,4,2,2,4,2,16,128]{7,6,5,4,3,2,1,0:T(8,128)(2,1)} %get-tuple-element.12.refs_0_, bf16[1,4,2,2,4,2,16,128]{7,6,5,4,3,2,1,0:T(8,128)(2,1)} %collective-permute-done.refs_1_, bf16[1,4,2,2,4,2,16,128]{7,6,5,4,3,2,1,0:T(8,128)(2,1)} %collective-permute-done.1.refs_2_, ...), custom_call_target="tpu_custom_call" | custom-call | flops 9663676416 | bytes 13631488 | tf_op jit(solution)/shard_map/pallas_call | solution.py:171
  128.0 0.0 all-to-all-done.cal_ref
  128.0 7.6 %all-to-all-start.2 = ((bf16[16,16,16,128]{3,2,1,0:T(8,128)(2,1)}), bf16[16,16,16,128]{3,2,1,0:T(8,128)(2,1)S(1)}, u32[]{:S(2)}, u32[]{:S(2)}) async-start(bf16[16,16,16,128]{3,2,1,0:T(8,128)(2,1)} %shard_map.76), calls=%async_computation.2 | async-start | bytes 2097152 | tf_op jit(solution)/shard_map/all_to_all | solution.py:240
  135.6 16.9 %shard_map.74 = bf16[16,16,16,128]{3,2,1,0:T(8,128)(2,1)} custom-call(bf16[8,4,2,2,4,2,16,128]{7,6,5,4,3,2,1,0:T(8,128)(2,1)} %all-to-all-done.cal_ref, bf16[2,1,1024,1024]{3,2,1,0:T(8,128)(2,1)} %w_ref.1, bf16[1024,2048]{1,0:T(8,128)(2,1)} %fusion.1.sel_ref.refs_9_), custom_call_target="tpu_custom_call" | custom-call | flops 9663676416 | bytes 13631488 | tf_op jit(solution)/shard_map/pallas_call | solution.py:195
  152.6 0.0 all-to-all-done.2
  152.6 22.3 %all_to_all.15 = bf16[16,16,16,128]{3,2,1,0:T(8,128)(2,1)S(1)} all-to-all(bf16[16,16,16,128]{3,2,1,0:T(8,128)(2,1)} %shard_map.74), channel_id=1, replica_groups=mesh['feed'=8,'chan'=16] {'chan'}, dimensions={0} | all-to-all | bytes 2097152 | tf_op jit(solution)/shard_map/all_to_all | solution.py:238
  174.9 0.2 maximum_bitcast_fusion
  175.1 1.9 %copy.9 = bf16[32,16,16,128]{3,2,1,0:T(8,128)(2,1)} copy(bf16[32,16,16,128]{3,2,0,1:T(8,128)(2,1)S(1)} %maximum_bitcast_fusion) | data formatting | bytes 4194304 | tf_op jit(solution)/shard_map/transpose | solution.py:243
  (3 shorter events, 0.0 us)
Async XLA Ops:
  9.7 118.3 %all-to-all-start = ((bf16[8,4,2,2,4,2,16,128]{7,6,5,4,3,2,1,0:T(8,128)(2,1)}), bf16[8,4,2,2,4,2,16,128]{7,6,5,4,3,2,1,0:T(8,128)(2,1)}, u32[]{:S(2)}, u32[]{:S(2)}) async-start(bf16[8,4,2,2,4,2,16,128]{7,6,5,4,3,2,1,0:T(8,128)(2,1)} %shard_map.73), calls=%async_computation | async-start | bytes 8388608 | tf_op jit(solution)/shard_map/all_to_all | solution.py:229
  25.4 10.9 %copy-start.1 = (s32[16]{0:T(128)S(1)}, s32[16]{0:T(128)}, u32[]{:S(2)}) copy-start(s32[16]{0:T(128)} %param.12) | copy-start | bytes 196
  29.5 43.0 %collective-permute-start = (bf16[1,4,2,2,4,2,16,128]{7,6,5,4,3,2,1,0:T(8,128)(2,1)}, bf16[1,4,2,2,4,2,16,128]{7,6,5,4,3,2,1,0:T(8,128)(2,1)}, u32[]{:S(2)}, u32[]{:S(2)}) collective-permute-start(bf16[1,4,2,2,4,2,16,128]{7,6,5,4,3,2,1,0:T(8,128)(2,1)} %get-tuple-element.11), channel_id=1, source_target_pairs={{0,16},{16,32},{32,48},{48,64},{64,80},{80,96},{96,112},{112,0},{1... | collective-permute-start | bytes 1572872 | tf_op jit(solution)/shard_map/ppermute | solution.py:235
  31.1 55.5 %collective-permute-start.1 = (bf16[1,4,2,2,4,2,16,128]{7,6,5,4,3,2,1,0:T(8,128)(2,1)S(1)}, bf16[1,4,2,2,4,2,16,128]{7,6,5,4,3,2,1,0:T(8,128)(2,1)}, u32[]{:S(2)}, u32[]{:S(2)}) collective-permute-start(bf16[1,4,2,2,4,2,16,128]{7,6,5,4,3,2,1,0:T(8,128)(2,1)S(1)} %get-tuple-element.10), channel_id=1, source_target_pairs={{0,32},{16,48},{32,64},{48,80},{64,96},{80,112},{96,0},{112,16},{1... | collective-permute-start | bytes 1572872 | tf_op jit(solution)/shard_map/ppermute | solution.py:235
  32.3 62.6 %collective-permute-start.2 = (bf16[1,4,2,2,4,2,16,128]{7,6,5,4,3,2,1,0:T(8,128)(2,1)S(1)}, bf16[1,4,2,2,4,2,16,128]{7,6,5,4,3,2,1,0:T(8,128)(2,1)}, u32[]{:S(2)}, u32[]{:S(2)}) collective-permute-start(bf16[1,4,2,2,4,2,16,128]{7,6,5,4,3,2,1,0:T(8,128)(2,1)S(1)} %get-tuple-element.9), channel_id=1, source_target_pairs={{0,48},{16,64},{32,80},{48,96},{64,112},{80,0},{96,16},{112,32},{1... | collective-permute-start | bytes 1572872 | tf_op jit(solution)/shard_map/ppermute | solution.py:235
  34.0 75.3 %collective-permute-start.3 = (bf16[1,4,2,2,4,2,16,128]{7,6,5,4,3,2,1,0:T(8,128)(2,1)S(1)}, bf16[1,4,2,2,4,2,16,128]{7,6,5,4,3,2,1,0:T(8,128)(2,1)}, u32[]{:S(2)}, u32[]{:S(2)}) collective-permute-start(bf16[1,4,2,2,4,2,16,128]{7,6,5,4,3,2,1,0:T(8,128)(2,1)S(1)} %get-tuple-element.8), channel_id=1, source_target_pairs={{0,64},{16,80},{32,96},{48,112},{64,0},{80,16},{96,32},{112,48},{1... | collective-permute-start | bytes 1572872 | tf_op jit(solution)/shard_map/ppermute | solution.py:235
  34.5 75.2 %collective-permute-start.4 = (bf16[1,4,2,2,4,2,16,128]{7,6,5,4,3,2,1,0:T(8,128)(2,1)S(1)}, bf16[1,4,2,2,4,2,16,128]{7,6,5,4,3,2,1,0:T(8,128)(2,1)}, u32[]{:S(2)}, u32[]{:S(2)}) collective-permute-start(bf16[1,4,2,2,4,2,16,128]{7,6,5,4,3,2,1,0:T(8,128)(2,1)S(1)} %get-tuple-element.7), channel_id=1, source_target_pairs={{0,80},{16,96},{32,112},{48,0},{64,16},{80,32},{96,48},{112,64},{1... | collective-permute-start | bytes 1572872 | tf_op jit(solution)/shard_map/ppermute | solution.py:235
  44.0 42.6 %copy-start = (s32[16,128]{1,0:T(8,128)S(1)}, s32[16,128]{1,0:T(8,128)}, u32[]{:S(2)}) copy-start(s32[16,128]{1,0:T(8,128)} %param.11) | copy-start | bytes 24580
  72.6 37.2 %collective-permute-start.5 = (bf16[1,4,2,2,4,2,16,128]{7,6,5,4,3,2,1,0:T(8,128)(2,1)S(1)}, bf16[1,4,2,2,4,2,16,128]{7,6,5,4,3,2,1,0:T(8,128)(2,1)S(1)}, u32[]{:S(2)}, u32[]{:S(2)}) collective-permute-start(bf16[1,4,2,2,4,2,16,128]{7,6,5,4,3,2,1,0:T(8,128)(2,1)S(1)} %get-tuple-element.6), channel_id=1, source_target_pairs={{0,96},{16,112},{32,0},{48,16},{64,32},{80,48},{96,64},{112,80},{1... | collective-permute-start | bytes 1572872 | tf_op jit(solution)/shard_map/ppermute | solution.py:235
  86.6 23.1 %collective-permute-start.6 = (bf16[1,4,2,2,4,2,16,128]{7,6,5,4,3,2,1,0:T(8,128)(2,1)S(1)}, bf16[1,4,2,2,4,2,16,128]{7,6,5,4,3,2,1,0:T(8,128)(2,1)S(1)}, u32[]{:S(2)}, u32[]{:S(2)}) collective-permute-start(bf16[1,4,2,2,4,2,16,128]{7,6,5,4,3,2,1,0:T(8,128)(2,1)S(1)} %get-tuple-element.5), channel_id=1, source_target_pairs={{0,112},{16,0},{32,16},{48,32},{64,48},{80,64},{96,80},{112,96},{1... | collective-permute-start | bytes 1572872 | tf_op jit(solution)/shard_map/ppermute | solution.py:235
  109.8 0.8 copy-start.2
  109.8 1.0 copy-start.3
  128.0 24.6 %all-to-all-start.2 = ((bf16[16,16,16,128]{3,2,1,0:T(8,128)(2,1)}), bf16[16,16,16,128]{3,2,1,0:T(8,128)(2,1)S(1)}, u32[]{:S(2)}, u32[]{:S(2)}) async-start(bf16[16,16,16,128]{3,2,1,0:T(8,128)(2,1)} %shard_map.76), calls=%async_computation.2 | async-start | bytes 2097152 | tf_op jit(solution)/shard_map/all_to_all | solution.py:240

commit v12 on v11

--- a/solution.py
+++ b/solution.py
@@ -149,8 +149,8 @@
         out_ref[n] = picked[:, n * 128 : (n + 1) * 128].reshape(IB, U, 128)
 
 
-def _beam_pieces_kernel(*refs):
-    count = len(refs) - 3
+def _beam_pieces_kernel(count, *refs):
+    refs = refs[:count + 2] + refs[-1:]
 
     class Stacked:
         def __getitem__(self, index):
@@ -162,19 +162,20 @@
     _beam_kernel(stacked, *refs[count:])
 
 
-def beamform_pieces(pieces, weights, select):
+def beamform_pieces(pieces, weights, select, after):
     nb = pieces[0].shape[1]
     feeds, beams = weights.shape[2], weights.shape[3]
     slots = select.shape[1]
     nodes = slots // 128
     piece_spec = pl.BlockSpec((1, 1, 2, 2, IB, TINT, U, 128), lambda i: (0, i, 0, 0, 0, 0, 0, 0))
     return pl.pallas_call(
-        _beam_pieces_kernel,
+        lambda *refs: _beam_pieces_kernel(len(pieces), *refs),
         grid=(nb,),
         in_specs=[piece_spec] * len(pieces)
         + [
             pl.BlockSpec((2, 1, feeds, beams), lambda i: (0, 0, 0, 0)),
             pl.BlockSpec((beams, slots), lambda i: (0, 0)),
+            pl.BlockSpec((1, 1, U, 128), lambda i: (0, 0, 0, 0)),
         ],
         out_specs=pl.BlockSpec((nodes, IB, U, 128), lambda i: (0, i, 0, 0)),
         out_shape=jax.ShapeDtypeStruct((nodes, nb * IB, U, 128), jnp.bfloat16),
@@ -184,7 +185,7 @@
             transcendentals=0,
         ),
         compiler_params=pltpu.CompilerParams(vmem_limit_bytes=60 * 1024 * 1024),
-    )(*pieces, weights, select)
+    )(*pieces, weights, select, after)
 
 
 def beamform(cal, weights, select):
@@ -236,7 +237,7 @@
     outs = []
     picked = beamform(gathered, weights, select)
     outs.append(lax.all_to_all(picked, "chan", split_axis=0, concat_axis=0, tiled=True))
-    picked = beamform_pieces(pieces, wperm, select)
+    picked = beamform_pieces(pieces, wperm, select, outs[0].reshape(-1, 1, U, 128))
     outs.append(lax.all_to_all(picked, "chan", split_axis=0, concat_axis=0, tiled=True))
     exchanged = jnp.concatenate(outs, axis=1)
     nodes, bins, fine, width = exchanged.shape

time: 178 us -> 155 us (0.87)
  waiting for transfers between devices: 57.3 us -> 32.1 us
    ppermute x7, waiting for transfers between devices: 57.3 us -> 7.58 us  [on_device(): pieces.append(lax.ppermute(piece, 'feed', perm=pairs))]
    all_to_all x1, waiting for transfers between devices: 0.01 us -> 24.5 us  [on_device(): lax.all_to_all(first, 'feed', split_axis=0, concat_axis=0, tiled=True)]
  transfers between devices with their start and end apart: 9 -> 9, of which waited for: 5 -> 3; matrix products, arithmetic and copies ran while one was open for 10% -> 12% of each run, Pallas kernels for 25% -> 17%
where the time goes in v12:
time: 155 us; the launch traced here: 154 us
  Pallas kernels  53.6 us (35%)
  waiting for transfers between devices  32.1 us (21%)
  starting transfers between devices  23.1 us (15%)
  blocking collectives  23 us (15%)
  local copies, waits for them, and re-layouts  14.9 us (10%)
  other arithmetic  7.59 us (5%)
    all_to_all x1, waiting for transfers between devices, on_device(): lax.all_to_all(first, 'feed', split_axis=0, concat_axis=0, tiled=True)  24.5 us
    all_to_all x1, blocking collectives, on_device(): lax.all_to_all(picked, 'chan', split_axis=0, concat_axis=0, tiled=True)  23 us
    pallas_call x2, Pallas kernels, filterbank(): pl.pallas_call(lambda *refs: _filter_kernel(chunk, *refs), grid=(nblk,),...  19.4 us
    pallas_call x1, Pallas kernels, beamform_pieces(): pl.pallas_call(lambda *refs: _beam_pieces_kernel(len(pieces), *refs), gri...  17.3 us
    pallas_call x1, Pallas kernels, beamform(): pl.pallas_call(_beam_kernel, grid=(nb,), in_specs=[pl.BlockSpec((nsrc, 1,...  16.9 us
    ppermute x7, starting transfers between devices, on_device(): pieces.append(lax.ppermute(piece, 'feed', perm=pairs))  9.55 us
    gather x2, local copies, waits for them, and re-layouts, on_device(): jnp.take(weights.reshape(2, 1, nfeed, feeds_local, beams), order, axis=2)  7.63 us
    all_to_all x1, starting transfers between devices, on_device(): lax.all_to_all(picked, 'chan', split_axis=0, concat_axis=0, tiled=True)  7.6 us
  transfers between devices with their start and end apart: 9, of which 3 were waited for; matrix products, arithmetic and copies ran while one was open for 12% of the time, Pallas kernels for 17%

profile of v12, /device:TPU:1, one launch (start us, length us, event | category | flops | bytes accessed | tf_op | source)
XLA Modules:
  0.0 154.3 jit_solution(16520806925545006556)
XLA Ops:
  0.0 9.7 %shard_map.73 = bf16[8,4,2,2,4,2,16,128]{7,6,5,4,3,2,1,0:T(8,128)(2,1)} custom-call(bf16[2,2,8,2,512,128]{5,4,3,2,1,0:T(8,128)(2,1)} %bitcast.18, bf16[2,2,8,64,16,128]{5,4,3,2,1,0:T(8,128)(2,1)} %bitcast.19, bf16[2,2,8,64,16,128]{5,4,3,2,1,0:T(8,128)(2,1)} %bitcast.20, bf16[2,2,8,64,16,128]{5,4,3,2,1,0:T(8,128)(2,1)} %bitcast.21, ...), custom_call_target="tpu_custom_call" | custom-call | flops 2952790016 | bytes 8388608 | tf_op jit(solution)/shard_map/pallas_call | solution.py:105
  9.7 6.0 %all-to-all-start = ((bf16[8,4,2,2,4,2,16,128]{7,6,5,4,3,2,1,0:T(8,128)(2,1)}), bf16[8,4,2,2,4,2,16,128]{7,6,5,4,3,2,1,0:T(8,128)(2,1)}, u32[]{:S(2)}, u32[]{:S(2)}) async-start(bf16[8,4,2,2,4,2,16,128]{7,6,5,4,3,2,1,0:T(8,128)(2,1)} %shard_map.73), calls=%async_computation | async-start | bytes 8388608 | tf_op jit(solution)/shard_map/all_to_all | solution.py:230
  15.7 9.7 %shard_map.75 = bf16[8,4,2,2,4,2,16,128]{7,6,5,4,3,2,1,0:T(8,128)(2,1)} custom-call(bf16[2,2,8,2,512,128]{5,4,3,2,1,0:T(8,128)(2,1)} %bitcast.22, bf16[2,2,8,64,16,128]{5,4,3,2,1,0:T(8,128)(2,1)} %bitcast.23, bf16[2,2,8,64,16,128]{5,4,3,2,1,0:T(8,128)(2,1)} %bitcast.24, bf16[2,2,8,64,16,128]{5,4,3,2,1,0:T(8,128)(2,1)} %bitcast.25, ...), custom_call_target="tpu_custom_call" | custom-call | flops 2952790016 | bytes 8388608 | tf_op jit(solution)/shard_map/pallas_call | solution.py:105
  25.3 0.0 copy-start.2
  25.3 0.0 copy-start.1
  25.3 4.4 %constant_dynamic-slice_fusion = (bf16[1,4,2,2,4,2,16,128]{7,6,5,4,3,2,1,0:T(8,128)(2,1)S(1)}, bf16[1,4,2,2,4,2,16,128]{7,6,5,4,3,2,1,0:T(8,128)(2,1)S(1)}, bf16...) fusion(bf16[8,4,2,2,4,2,16,128]{7,6,5,4,3,2,1,0:T(8,128)(2,1)} , ...), kind=kLoop, calls=%fused_computation.15 | loop fusion | bytes 8388640 | tf_op jit(solution)/shard_map/dynamic_slice | solution.py:235
  29.7 1.6 %collective-permute-start = (bf16[1,4,2,2,4,2,16,128]{7,6,5,4,3,2,1,0:T(8,128)(2,1)}, bf16[1,4,2,2,4,2,16,128]{7,6,5,4,3,2,1,0:T(8,128)(2,1)}, u32[]{:S(2)}, u32[]{:S(2)}) collective-permute-start(bf16[1,4,2,2,4,2,16,128]{7,6,5,4,3,2,1,0:T(8,128)(2,1)} %get-tuple-element.11), channel_id=1, source_target_pairs={{0,16},{16,32},{32,48},{48,64},{64,80},{80,96},{96,112},{112,0},{1... | collective-permute-start | bytes 1572872 | tf_op jit(solution)/shard_map/ppermute | solution.py:236
  31.3 1.2 collective-permute-start.1
  32.5 1.6 %collective-permute-start.2 = (bf16[1,4,2,2,4,2,16,128]{7,6,5,4,3,2,1,0:T(8,128)(2,1)}, bf16[1,4,2,2,4,2,16,128]{7,6,5,4,3,2,1,0:T(8,128)(2,1)}, u32[]{:S(2)}, u32[]{:S(2)}) collective-permute-start(bf16[1,4,2,2,4,2,16,128]{7,6,5,4,3,2,1,0:T(8,128)(2,1)} %get-tuple-element.9), channel_id=1, source_target_pairs={{0,48},{16,64},{32,80},{48,96},{64,112},{80,0},{96,16},{112,32},{1... | collective-permute-start | bytes 1572872 | tf_op jit(solution)/shard_map/ppermute | solution.py:236
  34.2 0.6 collective-permute-start.3
  34.7 1.7 %collective-permute-start.4 = (bf16[1,4,2,2,4,2,16,128]{7,6,5,4,3,2,1,0:T(8,128)(2,1)S(1)}, bf16[1,4,2,2,4,2,16,128]{7,6,5,4,3,2,1,0:T(8,128)(2,1)}, u32[]{:S(2)}, u32[]{:S(2)}) collective-permute-start(bf16[1,4,2,2,4,2,16,128]{7,6,5,4,3,2,1,0:T(8,128)(2,1)S(1)} %get-tuple-element.7), channel_id=1, source_target_pairs={{0,80},{16,96},{32,112},{48,0},{64,16},{80,32},{96,48},{112,64},{1... | collective-permute-start | bytes 1572872 | tf_op jit(solution)/shard_map/ppermute | solution.py:236
  36.4 0.0 copy-done.2
  36.4 0.1 fusion.2
  36.5 0.0 copy-done.1
  36.5 3.7 %fusion.1.sel_ref.refs_9_ = bf16[1024,2048]{1,0:T(8,128)(2,1)} fusion(s32[2048]{0:T(1024)S(1)} %bitcast.30, pred[2048]{0:T(1024)(128)(4,1)S(1)} %fusion.2), kind=kLoop, calls=%fused_computation.3 | loop fusion | flops 6291456 | bytes 4204544 | tf_op jit(solution)/shard_map/convert_element_type | solution.py:222
  40.1 24.5 %all-to-all-done.cal_ref = bf16[8,4,2,2,4,2,16,128]{7,6,5,4,3,2,1,0:T(8,128)(2,1)} async-done(((bf16[8,4,2,2,4,2,16,128]{7,6,5,4,3,2,1,0:T(8,128)(2,1)}), bf16[8,4,2,2,4,2,16,128]{7,6,5,4,3,2,1,0:T(8,128)(2,1)}, u32[]{:S(2)}, u32[]{:S(2)}) %all-to-all-start) | async-done | bytes 4194336 | tf_op jit(solution)/shard_map/all_to_all | solution.py:230
  64.6 16.9 %shard_map.74 = bf16[16,16,16,128]{3,2,1,0:T(8,128)(2,1)} custom-call(bf16[8,4,2,2,4,2,16,128]{7,6,5,4,3,2,1,0:T(8,128)(2,1)} %all-to-all-done.cal_ref, bf16[2,1,1024,1024]{3,2,1,0:T(8,128)(2,1)} %w_ref.1, bf16[1024,2048]{1,0:T(8,128)(2,1)} %fusion.1.sel_ref.refs_9_), custom_call_target="tpu_custom_call" | custom-call | flops 9663676416 | bytes 13631488 | tf_op jit(solution)/shard_map/pallas_call | solution.py:196
  81.5 7.6 %all-to-all-start.1 = ((bf16[16,16,16,128]{3,2,1,0:T(8,128)(2,1)}), bf16[16,16,16,128]{3,2,1,0:T(8,128)(2,1)S(1)}, u32[]{:S(2)}, u32[]{:S(2)}) async-start(bf16[16,16,16,128]{3,2,1,0:T(8,128)(2,1)} %shard_map.74), calls=%async_computation.1 | async-start | bytes 2097152 | tf_op jit(solution)/shard_map/all_to_all | solution.py:239
  89.2 0.1 broadcast_bitcast_fusion
  89.2 0.0 collective-permute-done.refs_1_
  89.2 0.9 collective-permute-start.5
  90.1 0.0 collective-permute-done.1.refs_2_
  90.2 2.0 %collective-permute-start.6 = (bf16[1,4,2,2,4,2,16,128]{7,6,5,4,3,2,1,0:T(8,128)(2,1)S(1)}, bf16[1,4,2,2,4,2,16,128]{7,6,5,4,3,2,1,0:T(8,128)(2,1)}, u32[]{:S(2)}, u32[]{:S(2)}) collective-permute-start(bf16[1,4,2,2,4,2,16,128]{7,6,5,4,3,2,1,0:T(8,128)(2,1)S(1)} %get-tuple-element.5), channel_id=1, source_target_pairs={{0,112},{16,0},{32,16},{48,32},{64,48},{80,64},{96,80},{112,96},{1... | collective-permute-start | bytes 1572872 | tf_op jit(solution)/shard_map/ppermute | solution.py:236
  92.1 5.0 %gather_fusion = bf16[8,2,128,1024]{3,2,1,0:T(8,128)(2,1)} fusion(bf16[2,8,128,1024]{3,2,1,0:T(8,128)(2,1)} %bitcast.28, s32[1024]{0:T(1024)S(1)} %pad_clamp_fusion), kind=kCustom, calls=%fused_computation | custom fusion | bytes 8388640 | tf_op jit(solution)/shard_map/jit(_take)/gather | solution.py:228
  97.1 2.7 %copy.8 = bf16[2,8,128,1024]{3,2,1,0:T(8,128)(2,1)S(1)} copy(bf16[2,8,128,1024]{3,2,0,1:T(8,128)(2,1)} %bitcast.27) | data formatting | bytes 8388608 | tf_op jit(solution)/shard_map/jit(_take)/gather | solution.py:228
  99.8 2.4 %bitcast_select_fusion.refs_8_ = bf16[2,1,1024,1024]{3,2,1,0:T(8,128)(2,1)} fusion(pred[1024]{0:T(1024)(128)(4,1)S(1)} %broadcast_bitcast_fusion, bf16[2,1,1024,1024]{3,2,1,0:T(8,128)(2,1)S(1)} %bitcast.26), kind=kLoop, calls=%fused_computation.4 | loop fusion | flops 2097152 | bytes 8389632 | tf_op jit(solution)/shard_map/jit(_take)/select_n | solution.py:228
  102.2 0.0 collective-permute-done.2.refs_3_
  102.2 7.1 %collective-permute-done.3.refs_4_ = bf16[1,4,2,2,4,2,16,128]{7,6,5,4,3,2,1,0:T(8,128)(2,1)} collective-permute-done((bf16[1,4,2,2,4,2,16,128]{7,6,5,4,3,2,1,0:T(8,128)(2,1)S(1)}, bf16[1,4,2,2,4,2,16,128]{7,6,5,4,3,2,1,0:T(8,128)(2,1)}, u32[]{:S(2)}, u32[]{:S(2)}) %collective-permute-start.3) | collective-permute-done | bytes 524320 | tf_op jit(solution)/shard_map/ppermute | solution.py:236
  109.3 0.5 collective-permute-done.4.refs_5_
  109.7 0.0 collective-permute-done.5.refs_6_
  109.7 0.0 collective-permute-done.6.refs_7_
  109.7 0.0 all-to-all-done.1
  109.8 0.0 copy-start
  109.8 1.0 copy-done
  110.7 17.3 %shard_map.76 = bf16[16,16,16,128]{3,2,1,0:T(8,128)(2,1)} custom-call(bf16[1,4,2,2,4,2,16,128]{7,6,5,4,3,2,1,0:T(8,128)(2,1)} %get-tuple-element.12.refs_0_, bf16[1,4,2,2,4,2,16,128]{7,6,5,4,3,2,1,0:T(8,128)(2,1)} %collective-permute-done.refs_1_, bf16[1,4,2,2,4,2,16,128]{7,6,5,4,3,2,1,0:T(8,128)(2,1)} %collective-permute-done.1.refs_2_, ...), custom_call_target="tpu_custom_call" | custom-call | flops 9663676416 | bytes 13631488 | tf_op jit(solution)/shard_map/pallas_call | solution.py:171
  128.0 23.0 %all_to_all.15 = bf16[16,16,16,128]{3,2,1,0:T(8,128)(2,1)S(1)} all-to-all(bf16[16,16,16,128]{3,2,1,0:T(8,128)(2,1)} %shard_map.76), channel_id=1, replica_groups=mesh['feed'=8,'chan'=16] {'chan'}, dimensions={0} | all-to-all | bytes 2097152 | tf_op jit(solution)/shard_map/all_to_all | solution.py:241
  151.0 1.4 maximum_bitcast_fusion
  152.4 1.9 %copy.9 = bf16[32,16,16,128]{3,2,1,0:T(8,128)(2,1)} copy(bf16[32,16,16,128]{3,2,0,1:T(8,128)(2,1)S(1)} %maximum_bitcast_fusion) | data formatting | bytes 4194304 | tf_op jit(solution)/shard_map/transpose | solution.py:244
  (3 shorter events, 0.0 us)
Async XLA Ops:
  9.7 54.9 %all-to-all-start = ((bf16[8,4,2,2,4,2,16,128]{7,6,5,4,3,2,1,0:T(8,128)(2,1)}), bf16[8,4,2,2,4,2,16,128]{7,6,5,4,3,2,1,0:T(8,128)(2,1)}, u32[]{:S(2)}, u32[]{:S(2)}) async-start(bf16[8,4,2,2,4,2,16,128]{7,6,5,4,3,2,1,0:T(8,128)(2,1)} %shard_map.73), calls=%async_computation | async-start | bytes 8388608 | tf_op jit(solution)/shard_map/all_to_all | solution.py:230
  25.3 11.1 %copy-start.2 = (s32[16]{0:T(128)S(1)}, s32[16]{0:T(128)}, u32[]{:S(2)}) copy-start(s32[16]{0:T(128)} %param.12) | copy-start | bytes 196
  25.3 11.1 %copy-start.1 = (s32[16,128]{1,0:T(8,128)S(1)}, s32[16,128]{1,0:T(8,128)}, u32[]{:S(2)}) copy-start(s32[16,128]{1,0:T(8,128)} %param.11) | copy-start | bytes 24580
  29.7 59.5 %collective-permute-start = (bf16[1,4,2,2,4,2,16,128]{7,6,5,4,3,2,1,0:T(8,128)(2,1)}, bf16[1,4,2,2,4,2,16,128]{7,6,5,4,3,2,1,0:T(8,128)(2,1)}, u32[]{:S(2)}, u32[]{:S(2)}) collective-permute-start(bf16[1,4,2,2,4,2,16,128]{7,6,5,4,3,2,1,0:T(8,128)(2,1)} %get-tuple-element.11), channel_id=1, source_target_pairs={{0,16},{16,32},{32,48},{48,64},{64,80},{80,96},{96,112},{112,0},{1... | collective-permute-start | bytes 1572872 | tf_op jit(solution)/shard_map/ppermute | solution.py:236
  31.3 58.8 %collective-permute-start.1 = (bf16[1,4,2,2,4,2,16,128]{7,6,5,4,3,2,1,0:T(8,128)(2,1)}, bf16[1,4,2,2,4,2,16,128]{7,6,5,4,3,2,1,0:T(8,128)(2,1)}, u32[]{:S(2)}, u32[]{:S(2)}) collective-permute-start(bf16[1,4,2,2,4,2,16,128]{7,6,5,4,3,2,1,0:T(8,128)(2,1)} %get-tuple-element.10), channel_id=1, source_target_pairs={{0,32},{16,48},{32,64},{48,80},{64,96},{80,112},{96,0},{112,16},{1... | collective-permute-start | bytes 1572872 | tf_op jit(solution)/shard_map/ppermute | solution.py:236
  32.5 69.7 %collective-permute-start.2 = (bf16[1,4,2,2,4,2,16,128]{7,6,5,4,3,2,1,0:T(8,128)(2,1)}, bf16[1,4,2,2,4,2,16,128]{7,6,5,4,3,2,1,0:T(8,128)(2,1)}, u32[]{:S(2)}, u32[]{:S(2)}) collective-permute-start(bf16[1,4,2,2,4,2,16,128]{7,6,5,4,3,2,1,0:T(8,128)(2,1)} %get-tuple-element.9), channel_id=1, source_target_pairs={{0,48},{16,64},{32,80},{48,96},{64,112},{80,0},{96,16},{112,32},{1... | collective-permute-start | bytes 1572872 | tf_op jit(solution)/shard_map/ppermute | solution.py:236
  34.2 75.1 %collective-permute-start.3 = (bf16[1,4,2,2,4,2,16,128]{7,6,5,4,3,2,1,0:T(8,128)(2,1)S(1)}, bf16[1,4,2,2,4,2,16,128]{7,6,5,4,3,2,1,0:T(8,128)(2,1)}, u32[]{:S(2)}, u32[]{:S(2)}) collective-permute-start(bf16[1,4,2,2,4,2,16,128]{7,6,5,4,3,2,1,0:T(8,128)(2,1)S(1)} %get-tuple-element.8), channel_id=1, source_target_pairs={{0,64},{16,80},{32,96},{48,112},{64,0},{80,16},{96,32},{112,48},{1... | collective-permute-start | bytes 1572872 | tf_op jit(solution)/shard_map/ppermute | solution.py:236
  34.7 75.0 %collective-permute-start.4 = (bf16[1,4,2,2,4,2,16,128]{7,6,5,4,3,2,1,0:T(8,128)(2,1)S(1)}, bf16[1,4,2,2,4,2,16,128]{7,6,5,4,3,2,1,0:T(8,128)(2,1)}, u32[]{:S(2)}, u32[]{:S(2)}) collective-permute-start(bf16[1,4,2,2,4,2,16,128]{7,6,5,4,3,2,1,0:T(8,128)(2,1)S(1)} %get-tuple-element.7), channel_id=1, source_target_pairs={{0,80},{16,96},{32,112},{48,0},{64,16},{80,32},{96,48},{112,64},{1... | collective-permute-start | bytes 1572872 | tf_op jit(solution)/shard_map/ppermute | solution.py:236
  81.5 28.2 %all-to-all-start.1 = ((bf16[16,16,16,128]{3,2,1,0:T(8,128)(2,1)}), bf16[16,16,16,128]{3,2,1,0:T(8,128)(2,1)S(1)}, u32[]{:S(2)}, u32[]{:S(2)}) async-start(bf16[16,16,16,128]{3,2,1,0:T(8,128)(2,1)} %shard_map.74), calls=%async_computation.1 | async-start | bytes 2097152 | tf_op jit(solution)/shard_map/all_to_all | solution.py:239
  89.2 20.5 %collective-permute-start.5 = (bf16[1,4,2,2,4,2,16,128]{7,6,5,4,3,2,1,0:T(8,128)(2,1)S(1)}, bf16[1,4,2,2,4,2,16,128]{7,6,5,4,3,2,1,0:T(8,128)(2,1)}, u32[]{:S(2)}, u32[]{:S(2)}) collective-permute-start(bf16[1,4,2,2,4,2,16,128]{7,6,5,4,3,2,1,0:T(8,128)(2,1)S(1)} %get-tuple-element.6), channel_id=1, source_target_pairs={{0,96},{16,112},{32,0},{48,16},{64,32},{80,48},{96,64},{112,80},{1... | collective-permute-start | bytes 1572872 | tf_op jit(solution)/shard_map/ppermute | solution.py:236
  90.2 19.6 %collective-permute-start.6 = (bf16[1,4,2,2,4,2,16,128]{7,6,5,4,3,2,1,0:T(8,128)(2,1)S(1)}, bf16[1,4,2,2,4,2,16,128]{7,6,5,4,3,2,1,0:T(8,128)(2,1)}, u32[]{:S(2)}, u32[]{:S(2)}) collective-permute-start(bf16[1,4,2,2,4,2,16,128]{7,6,5,4,3,2,1,0:T(8,128)(2,1)S(1)} %get-tuple-element.5), channel_id=1, source_target_pairs={{0,112},{16,0},{32,16},{48,32},{64,48},{80,64},{96,80},{112,96},{1... | collective-permute-start | bytes 1572872 | tf_op jit(solution)/shard_map/ppermute | solution.py:236
  109.8 1.0 copy-start

commit v13 on v12

--- a/solution.py
+++ b/solution.py
@@ -45,7 +45,13 @@
     return np.concatenate([high, low], axis=0)
 
 
-def _filter_kernel(chunk, main_ref, pre0_ref, pre1_ref, pre2_ref, hist_ref, gain_ref, band_ref, *rest):
+def _filter_kernel(chunk, shifted, *refs):
+    if shifted:
+        refs = refs[1:]
+    _filter_body(chunk, *refs)
+
+
+def _filter_body(chunk, main_ref, pre0_ref, pre1_ref, pre2_ref, hist_ref, gain_ref, band_ref, *rest):
     out_ref = rest[-1]
     tdev = pl.program_id(0)
     rows_main = main_ref.shape[4]
@@ -87,7 +93,7 @@
             out_ref[0, ib, 1, p] = c_im[:, p * lanes : (p + 1) * lanes].reshape(IB, TINT, U, lanes)
 
 
-def filterbank(voltages, history, gains, band, chunk, chunks, after=None):
+def filterbank(voltages, history, gains, band, chunk, chunks, after=None, me=None):
     _, pols, _, samples, feeds = voltages.shape
     nblk = 8
     rows_blk = samples // nblk
@@ -102,27 +108,43 @@
         return lambda t: (0, 0, t, chunk * rows_main // 16 - 3 + m, 0, 0)
 
     extra = [] if after is None else [after]
+    shifted = me is not None
+
+    def spec(shape, index):
+        if shifted:
+            return pl.BlockSpec(shape, lambda t, me_ref: index(t))
+        return pl.BlockSpec(shape, index)
+
+    if shifted:
+        out_spec = pl.BlockSpec(
+            (1, nb, 2, pols, IB, TINT, U, feeds),
+            lambda t, me_ref: (lax.rem(t - me_ref[0] + nblk, nblk), 0, 0, 0, 0, 0, 0, 0),
+        )
+    else:
+        out_spec = pl.BlockSpec((1, nb, 2, pols, IB, TINT, U, feeds), lambda t: (t, 0, 0, 0, 0, 0, 0, 0))
+    in_specs = [
+        spec((2, pols, 1, 1, rows_main, feeds), lambda t: (0, 0, t, chunk, 0, 0)),
+        spec((2, pols, 1, 1, 16, feeds), pre_map(0)),
+        spec((2, pols, 1, 1, 16, feeds), pre_map(1)),
+        spec((2, pols, 1, 1, 16, feeds), pre_map(2)),
+        spec((2, pols, 1, 48, feeds), lambda t: (0, 0, 0, 0, 0)),
+        spec((2, pols, 1, feeds), lambda t: (0, 0, 0, 0)),
+        spec(band.shape, lambda t: (0, 0)),
+    ] + [spec((1, 1, U, 128), lambda t: (0, 0, 0, 0)) for _ in extra]
+    grid_spec = pltpu.PrefetchScalarGridSpec(
+        num_scalar_prefetch=1 if shifted else 0, grid=(nblk,), in_specs=in_specs, out_specs=out_spec
+    )
+    lead = [me] if shifted else []
     return pl.pallas_call(
-        lambda *refs: _filter_kernel(chunk, *refs),
-        grid=(nblk,),
-        in_specs=[
-            pl.BlockSpec((2, pols, 1, 1, rows_main, feeds), lambda t: (0, 0, t, chunk, 0, 0)),
-            pl.BlockSpec((2, pols, 1, 1, 16, feeds), pre_map(0)),
-            pl.BlockSpec((2, pols, 1, 1, 16, feeds), pre_map(1)),
-            pl.BlockSpec((2, pols, 1, 1, 16, feeds), pre_map(2)),
-            pl.BlockSpec((2, pols, 1, 48, feeds), lambda t: (0, 0, 0, 0, 0)),
-            pl.BlockSpec((2, pols, 1, feeds), lambda t: (0, 0, 0, 0)),
-            pl.BlockSpec(band.shape, lambda t: (0, 0)),
-        ]
-        + [pl.BlockSpec((1, 1, U, 128), lambda t: (0, 0, 0, 0)) for _ in extra],
-        out_specs=pl.BlockSpec((1, nb, 2, pols, IB, TINT, U, feeds), lambda t: (t, 0, 0, 0, 0, 0, 0, 0)),
+        lambda *refs: _filter_kernel(chunk, shifted, *refs),
+        grid_spec=grid_spec,
         out_shape=jax.ShapeDtypeStruct((nblk, nb, 2, pols, IB, TINT, U, feeds), jnp.bfloat16),
         cost_estimate=pl.CostEstimate(
             flops=2 * band.size * feeds * pols * nblk * nb,
             bytes_accessed=2 * voltages.size * 2 // chunks,
             transcendentals=0,
         ),
-    )(main, units, units, units, history, gains, band, *extra)
+    )(*lead, main, units, units, units, history, gains, band, *extra)
 
 
 def _beam_kernel(cal_ref, w_ref, sel_ref, out_ref):
@@ -228,12 +250,11 @@
     wperm = jnp.take(weights.reshape(2, 1, nfeed, feeds_local, beams), order, axis=2).reshape(weights.shape)
     first = filterbank(voltages, history, gains, band, 0, CHUNKS)
     gathered = lax.all_to_all(first, "feed", split_axis=0, concat_axis=0, tiled=True)
-    second = filterbank(voltages, history, gains, band, 1, CHUNKS)
-    pieces = [lax.dynamic_slice_in_dim(second, me, 1, axis=0)]
+    second = filterbank(voltages, history, gains, band, 1, CHUNKS, me=me.astype(jnp.int32).reshape(1))
+    pieces = [second[0:1]]
     for shift in range(1, nfeed):
         pairs = [(i, (i + shift) % nfeed) for i in range(nfeed)]
-        piece = lax.dynamic_slice_in_dim(second, lax.rem(me + shift, nfeed), 1, axis=0)
-        pieces.append(lax.ppermute(piece, "feed", perm=pairs))
+        pieces.append(lax.ppermute(second[shift : shift + 1], "feed", perm=pairs))
     outs = []
     picked = beamform(gathered, weights, select)
     outs.append(lax.all_to_all(picked, "chan", split_axis=0, concat_axis=0, tiled=True))

time: 155 us -> 155 us (level)
    dynamic_slice x1 -> x0, local copies, waits for them, and re-layouts: 4.36 us -> none  [on_device(): lax.dynamic_slice_in_dim(second, lax.rem(me + shift, nfeed), 1, axis=0)]
    slice x0 -> x1, local copies, waits for them, and re-layouts: none -> 4.36 us  [on_device(): pieces.append(lax.ppermute(second[shift:shift + 1], 'feed', perm=pairs))]
where the time goes in v13:
time: 155 us; the launch traced here: 154 us
  Pallas kernels  53.6 us (35%)
  waiting for transfers between devices  32.1 us (21%)
  starting transfers between devices  23.1 us (15%)
  blocking collectives  23 us (15%)
  local copies, waits for them, and re-layouts  14.9 us (10%)
  other arithmetic  7.59 us (5%)
    all_to_all x1, waiting for transfers between devices, on_device(): lax.all_to_all(first, 'feed', split_axis=0, concat_axis=0, tiled=True)  24.5 us
    all_to_all x1, blocking collectives, on_device(): lax.all_to_all(picked, 'chan', split_axis=0, concat_axis=0, tiled=True)  23 us
    pallas_call x2, Pallas kernels, filterbank(): pl.pallas_call(lambda *refs: _filter_kernel(chunk, shifted, *refs), grid_...  19.4 us
    pallas_call x1, Pallas kernels, beamform_pieces(): pl.pallas_call(lambda *refs: _beam_pieces_kernel(len(pieces), *refs), gri...  17.3 us
    pallas_call x1, Pallas kernels, beamform(): pl.pallas_call(_beam_kernel, grid=(nb,), in_specs=[pl.BlockSpec((nsrc, 1,...  16.9 us
    ppermute x7, starting transfers between devices, on_device(): pieces.append(lax.ppermute(second[shift:shift + 1], 'feed', perm=pairs))  9.54 us
    gather x2, local copies, waits for them, and re-layouts, on_device(): jnp.take(weights.reshape(2, 1, nfeed, feeds_local, beams), order, axis=2)  7.63 us
    all_to_all x1, starting transfers between devices, on_device(): lax.all_to_all(picked, 'chan', split_axis=0, concat_axis=0, tiled=True)  7.6 us
  transfers between devices with their start and end apart: 9, of which 3 were waited for; matrix products, arithmetic and copies ran while one was open for 12% of the time, Pallas kernels for 17%

profile of v13, /device:TPU:1, one launch (start us, length us, event | category | flops | bytes accessed | tf_op | source)
XLA Modules:
  0.0 154.3 jit_solution(6586358002509614799)
XLA Ops:
  0.0 9.7 %shard_map.73 = bf16[8,4,2,2,4,2,16,128]{7,6,5,4,3,2,1,0:T(8,128)(2,1)} custom-call(bf16[2,2,8,2,512,128]{5,4,3,2,1,0:T(8,128)(2,1)} %bitcast.19, bf16[2,2,8,64,16,128]{5,4,3,2,1,0:T(8,128)(2,1)} %bitcast.20, bf16[2,2,8,64,16,128]{5,4,3,2,1,0:T(8,128)(2,1)} %bitcast.21, bf16[2,2,8,64,16,128]{5,4,3,2,1,0:T(8,128)(2,1)} %bitcast.22, ...), custom_call_target="tpu_custom_call" | custom-call | flops 2952790016 | bytes 8388608 | tf_op jit(solution)/shard_map/pallas_call | solution.py:138
  9.7 6.0 %all-to-all-start = ((bf16[8,4,2,2,4,2,16,128]{7,6,5,4,3,2,1,0:T(8,128)(2,1)}), bf16[8,4,2,2,4,2,16,128]{7,6,5,4,3,2,1,0:T(8,128)(2,1)}, u32[]{:S(2)}, u32[]{:S(2)}) async-start(bf16[8,4,2,2,4,2,16,128]{7,6,5,4,3,2,1,0:T(8,128)(2,1)} %shard_map.73), calls=%async_computation | async-start | bytes 8388608 | tf_op jit(solution)/shard_map/all_to_all | solution.py:252
  15.7 9.7 %shard_map.75 = bf16[8,4,2,2,4,2,16,128]{7,6,5,4,3,2,1,0:T(8,128)(2,1)} custom-call(s32[1]{0:T(128)} %bitcast.4.refs_0_, bf16[2,2,8,2,512,128]{5,4,3,2,1,0:T(8,128)(2,1)} %bitcast.23, bf16[2,2,8,64,16,128]{5,4,3,2,1,0:T(8,128)(2,1)} %bitcast.24, bf16[2,2,8,64,16,128]{5,4,3,2,1,0:T(8,128)(2,1)} %bitcast.25, bf16[2,2,8,64,16,128]{5,4,3,2,1,0:T(8,128)(2,1)} %bitcast.26, ...), custom_call_target="tpu_custom_call" | custom-call | flops 2952790016 | bytes 8388608 | tf_op jit(solution)/shard_map/pallas_call | solution.py:138
  25.4 0.0 copy-start.2
  25.4 0.0 copy-start.1
  25.4 4.4 %fusion.6 = (bf16[1,4,2,2,4,2,16,128]{7,6,5,4,3,2,1,0:T(8,128)(2,1)S(1)}, bf16[1,4,2,2,4,2,16,128]{7,6,5,4,3,2,1,0:T(8,128)(2,1)S(1)}, bf16[1,4,2,2,4,2,16,128]{...) fusion(bf16[8,4,2,2,4,2,16,128]{7,6,5,4,3,2,1,0:T(8,128)(2,1)} , ...), kind=kLoop, calls=%fused_computation.20 | loop fusion | bytes 8388608 | tf_op jit(solution)/shard_map/slice | solution.py:257
  29.7 1.6 %collective-permute-start = (bf16[1,4,2,2,4,2,16,128]{7,6,5,4,3,2,1,0:T(8,128)(2,1)}, bf16[1,4,2,2,4,2,16,128]{7,6,5,4,3,2,1,0:T(8,128)(2,1)}, u32[]{:S(2)}, u32[]{:S(2)}) collective-permute-start(bf16[1,4,2,2,4,2,16,128]{7,6,5,4,3,2,1,0:T(8,128)(2,1)} %get-tuple-element.11), channel_id=1, source_target_pairs={{0,16},{16,32},{32,48},{48,64},{64,80},{80,96},{96,112},{112,0},{1... | collective-permute-start | bytes 1572872 | tf_op jit(solution)/shard_map/ppermute | solution.py:257
  31.3 1.2 collective-permute-start.1
  32.5 1.6 %collective-permute-start.2 = (bf16[1,4,2,2,4,2,16,128]{7,6,5,4,3,2,1,0:T(8,128)(2,1)}, bf16[1,4,2,2,4,2,16,128]{7,6,5,4,3,2,1,0:T(8,128)(2,1)}, u32[]{:S(2)}, u32[]{:S(2)}) collective-permute-start(bf16[1,4,2,2,4,2,16,128]{7,6,5,4,3,2,1,0:T(8,128)(2,1)} %get-tuple-element.9), channel_id=1, source_target_pairs={{0,48},{16,64},{32,80},{48,96},{64,112},{80,0},{96,16},{112,32},{1... | collective-permute-start | bytes 1572872 | tf_op jit(solution)/shard_map/ppermute | solution.py:257
  34.2 0.6 collective-permute-start.3
  34.7 1.7 %collective-permute-start.4 = (bf16[1,4,2,2,4,2,16,128]{7,6,5,4,3,2,1,0:T(8,128)(2,1)S(1)}, bf16[1,4,2,2,4,2,16,128]{7,6,5,4,3,2,1,0:T(8,128)(2,1)}, u32[]{:S(2)}, u32[]{:S(2)}) collective-permute-start(bf16[1,4,2,2,4,2,16,128]{7,6,5,4,3,2,1,0:T(8,128)(2,1)S(1)} %get-tuple-element.7), channel_id=1, source_target_pairs={{0,80},{16,96},{32,112},{48,0},{64,16},{80,32},{96,48},{112,64},{1... | collective-permute-start | bytes 1572872 | tf_op jit(solution)/shard_map/ppermute | solution.py:257
  36.4 0.0 copy-done.2
  36.4 0.1 fusion.2
  36.5 0.0 copy-done.1
  36.5 3.7 %fusion.1.sel_ref.refs_9_ = bf16[1024,2048]{1,0:T(8,128)(2,1)} fusion(s32[2048]{0:T(1024)S(1)} %bitcast.31, pred[2048]{0:T(1024)(128)(4,1)S(1)} %fusion.2), kind=kLoop, calls=%fused_computation.3 | loop fusion | flops 6291456 | bytes 4204544 | tf_op jit(solution)/shard_map/convert_element_type | solution.py:244
  40.1 24.5 %all-to-all-done.cal_ref = bf16[8,4,2,2,4,2,16,128]{7,6,5,4,3,2,1,0:T(8,128)(2,1)} async-done(((bf16[8,4,2,2,4,2,16,128]{7,6,5,4,3,2,1,0:T(8,128)(2,1)}), bf16[8,4,2,2,4,2,16,128]{7,6,5,4,3,2,1,0:T(8,128)(2,1)}, u32[]{:S(2)}, u32[]{:S(2)}) %all-to-all-start) | async-done | bytes 4194336 | tf_op jit(solution)/shard_map/all_to_all | solution.py:252
  64.6 16.9 %shard_map.74 = bf16[16,16,16,128]{3,2,1,0:T(8,128)(2,1)} custom-call(bf16[8,4,2,2,4,2,16,128]{7,6,5,4,3,2,1,0:T(8,128)(2,1)} %all-to-all-done.cal_ref, bf16[2,1,1024,1024]{3,2,1,0:T(8,128)(2,1)} %w_ref.1, bf16[1024,2048]{1,0:T(8,128)(2,1)} %fusion.1.sel_ref.refs_9_), custom_call_target="tpu_custom_call" | custom-call | flops 9663676416 | bytes 13631488 | tf_op jit(solution)/shard_map/pallas_call | solution.py:218
  81.5 7.6 %all-to-all-start.1 = ((bf16[16,16,16,128]{3,2,1,0:T(8,128)(2,1)}), bf16[16,16,16,128]{3,2,1,0:T(8,128)(2,1)S(1)}, u32[]{:S(2)}, u32[]{:S(2)}) async-start(bf16[16,16,16,128]{3,2,1,0:T(8,128)(2,1)} %shard_map.74), calls=%async_computation.1 | async-start | bytes 2097152 | tf_op jit(solution)/shard_map/all_to_all | solution.py:260
  89.2 0.1 broadcast_bitcast_fusion
  89.2 0.0 collective-permute-done.refs_1_
  89.2 0.9 collective-permute-start.5
  90.1 0.0 collective-permute-done.1.refs_2_
  90.2 2.0 %collective-permute-start.6 = (bf16[1,4,2,2,4,2,16,128]{7,6,5,4,3,2,1,0:T(8,128)(2,1)S(1)}, bf16[1,4,2,2,4,2,16,128]{7,6,5,4,3,2,1,0:T(8,128)(2,1)}, u32[]{:S(2)}, u32[]{:S(2)}) collective-permute-start(bf16[1,4,2,2,4,2,16,128]{7,6,5,4,3,2,1,0:T(8,128)(2,1)S(1)} %get-tuple-element.5), channel_id=1, source_target_pairs={{0,112},{16,0},{32,16},{48,32},{64,48},{80,64},{96,80},{112,96},{1... | collective-permute-start | bytes 1572872 | tf_op jit(solution)/shard_map/ppermute | solution.py:257
  92.1 5.0 %gather_fusion = bf16[8,2,128,1024]{3,2,1,0:T(8,128)(2,1)} fusion(bf16[2,8,128,1024]{3,2,1,0:T(8,128)(2,1)} %bitcast.29, s32[1024]{0:T(1024)S(1)} %pad_clamp_fusion), kind=kCustom, calls=%fused_computation | custom fusion | bytes 8388640 | tf_op jit(solution)/shard_map/jit(_take)/gather | solution.py:250
  97.1 2.7 %copy.8 = bf16[2,8,128,1024]{3,2,1,0:T(8,128)(2,1)S(1)} copy(bf16[2,8,128,1024]{3,2,0,1:T(8,128)(2,1)} %bitcast.28) | data formatting | bytes 8388608 | tf_op jit(solution)/shard_map/jit(_take)/gather | solution.py:250
  99.8 2.4 %bitcast_select_fusion.refs_8_ = bf16[2,1,1024,1024]{3,2,1,0:T(8,128)(2,1)} fusion(pred[1024]{0:T(1024)(128)(4,1)S(1)} %broadcast_bitcast_fusion, bf16[2,1,1024,1024]{3,2,1,0:T(8,128)(2,1)S(1)} %bitcast.27), kind=kLoop, calls=%fused_computation.4 | loop fusion | flops 2097152 | bytes 8389632 | tf_op jit(solution)/shard_map/jit(_take)/select_n | solution.py:250
  102.2 0.0 collective-permute-done.2.refs_3_
  102.2 7.1 %collective-permute-done.3.refs_4_ = bf16[1,4,2,2,4,2,16,128]{7,6,5,4,3,2,1,0:T(8,128)(2,1)} collective-permute-done((bf16[1,4,2,2,4,2,16,128]{7,6,5,4,3,2,1,0:T(8,128)(2,1)S(1)}, bf16[1,4,2,2,4,2,16,128]{7,6,5,4,3,2,1,0:T(8,128)(2,1)}, u32[]{:S(2)}, u32[]{:S(2)}) %collective-permute-start.3) | collective-permute-done | bytes 524320 | tf_op jit(solution)/shard_map/ppermute | solution.py:257
  109.3 0.5 collective-permute-done.4.refs_5_
  109.7 0.0 collective-permute-done.5.refs_6_
  109.7 0.0 collective-permute-done.6.refs_7_
  109.7 0.0 all-to-all-done.1
  109.8 0.0 copy-start
  109.8 1.0 copy-done
  110.7 17.3 %shard_map.76 = bf16[16,16,16,128]{3,2,1,0:T(8,128)(2,1)} custom-call(bf16[1,4,2,2,4,2,16,128]{7,6,5,4,3,2,1,0:T(8,128)(2,1)} %get-tuple-element.12.refs_0_, bf16[1,4,2,2,4,2,16,128]{7,6,5,4,3,2,1,0:T(8,128)(2,1)} %collective-permute-done.refs_1_, bf16[1,4,2,2,4,2,16,128]{7,6,5,4,3,2,1,0:T(8,128)(2,1)} %collective-permute-done.1.refs_2_, ...), custom_call_target="tpu_custom_call" | custom-call | flops 9663676416 | bytes 13631488 | tf_op jit(solution)/shard_map/pallas_call | solution.py:193
  128.0 23.0 %all_to_all.15 = bf16[16,16,16,128]{3,2,1,0:T(8,128)(2,1)S(1)} all-to-all(bf16[16,16,16,128]{3,2,1,0:T(8,128)(2,1)} %shard_map.76), channel_id=1, replica_groups=mesh['feed'=8,'chan'=16] {'chan'}, dimensions={0} | all-to-all | bytes 2097152 | tf_op jit(solution)/shard_map/all_to_all | solution.py:262
  151.0 1.4 maximum_bitcast_fusion
  152.4 1.9 %copy.9 = bf16[32,16,16,128]{3,2,1,0:T(8,128)(2,1)} copy(bf16[32,16,16,128]{3,2,0,1:T(8,128)(2,1)S(1)} %maximum_bitcast_fusion) | data formatting | bytes 4194304 | tf_op jit(solution)/shard_map/transpose | solution.py:265
  (3 shorter events, 0.0 us)
Async XLA Ops:
  9.7 54.9 %all-to-all-start = ((bf16[8,4,2,2,4,2,16,128]{7,6,5,4,3,2,1,0:T(8,128)(2,1)}), bf16[8,4,2,2,4,2,16,128]{7,6,5,4,3,2,1,0:T(8,128)(2,1)}, u32[]{:S(2)}, u32[]{:S(2)}) async-start(bf16[8,4,2,2,4,2,16,128]{7,6,5,4,3,2,1,0:T(8,128)(2,1)} %shard_map.73), calls=%async_computation | async-start | bytes 8388608 | tf_op jit(solution)/shard_map/all_to_all | solution.py:252
  25.4 11.1 %copy-start.2 = (s32[16]{0:T(128)S(1)}, s32[16]{0:T(128)}, u32[]{:S(2)}) copy-start(s32[16]{0:T(128)} %param.12) | copy-start | bytes 196
  25.4 11.1 %copy-start.1 = (s32[16,128]{1,0:T(8,128)S(1)}, s32[16,128]{1,0:T(8,128)}, u32[]{:S(2)}) copy-start(s32[16,128]{1,0:T(8,128)} %param.11) | copy-start | bytes 24580
  29.7 59.5 %collective-permute-start = (bf16[1,4,2,2,4,2,16,128]{7,6,5,4,3,2,1,0:T(8,128)(2,1)}, bf16[1,4,2,2,4,2,16,128]{7,6,5,4,3,2,1,0:T(8,128)(2,1)}, u32[]{:S(2)}, u32[]{:S(2)}) collective-permute-start(bf16[1,4,2,2,4,2,16,128]{7,6,5,4,3,2,1,0:T(8,128)(2,1)} %get-tuple-element.11), channel_id=1, source_target_pairs={{0,16},{16,32},{32,48},{48,64},{64,80},{80,96},{96,112},{112,0},{1... | collective-permute-start | bytes 1572872 | tf_op jit(solution)/shard_map/ppermute | solution.py:257
  31.3 58.8 %collective-permute-start.1 = (bf16[1,4,2,2,4,2,16,128]{7,6,5,4,3,2,1,0:T(8,128)(2,1)}, bf16[1,4,2,2,4,2,16,128]{7,6,5,4,3,2,1,0:T(8,128)(2,1)}, u32[]{:S(2)}, u32[]{:S(2)}) collective-permute-start(bf16[1,4,2,2,4,2,16,128]{7,6,5,4,3,2,1,0:T(8,128)(2,1)} %get-tuple-element.10), channel_id=1, source_target_pairs={{0,32},{16,48},{32,64},{48,80},{64,96},{80,112},{96,0},{112,16},{1... | collective-permute-start | bytes 1572872 | tf_op jit(solution)/shard_map/ppermute | solution.py:257
  32.5 69.6 %collective-permute-start.2 = (bf16[1,4,2,2,4,2,16,128]{7,6,5,4,3,2,1,0:T(8,128)(2,1)}, bf16[1,4,2,2,4,2,16,128]{7,6,5,4,3,2,1,0:T(8,128)(2,1)}, u32[]{:S(2)}, u32[]{:S(2)}) collective-permute-start(bf16[1,4,2,2,4,2,16,128]{7,6,5,4,3,2,1,0:T(8,128)(2,1)} %get-tuple-element.9), channel_id=1, source_target_pairs={{0,48},{16,64},{32,80},{48,96},{64,112},{80,0},{96,16},{112,32},{1... | collective-permute-start | bytes 1572872 | tf_op jit(solution)/shard_map/ppermute | solution.py:257
  34.2 75.1 %collective-permute-start.3 = (bf16[1,4,2,2,4,2,16,128]{7,6,5,4,3,2,1,0:T(8,128)(2,1)S(1)}, bf16[1,4,2,2,4,2,16,128]{7,6,5,4,3,2,1,0:T(8,128)(2,1)}, u32[]{:S(2)}, u32[]{:S(2)}) collective-permute-start(bf16[1,4,2,2,4,2,16,128]{7,6,5,4,3,2,1,0:T(8,128)(2,1)S(1)} %get-tuple-element.8), channel_id=1, source_target_pairs={{0,64},{16,80},{32,96},{48,112},{64,0},{80,16},{96,32},{112,48},{1... | collective-permute-start | bytes 1572872 | tf_op jit(solution)/shard_map/ppermute | solution.py:257
  34.7 75.0 %collective-permute-start.4 = (bf16[1,4,2,2,4,2,16,128]{7,6,5,4,3,2,1,0:T(8,128)(2,1)S(1)}, bf16[1,4,2,2,4,2,16,128]{7,6,5,4,3,2,1,0:T(8,128)(2,1)}, u32[]{:S(2)}, u32[]{:S(2)}) collective-permute-start(bf16[1,4,2,2,4,2,16,128]{7,6,5,4,3,2,1,0:T(8,128)(2,1)S(1)} %get-tuple-element.7), channel_id=1, source_target_pairs={{0,80},{16,96},{32,112},{48,0},{64,16},{80,32},{96,48},{112,64},{1... | collective-permute-start | bytes 1572872 | tf_op jit(solution)/shard_map/ppermute | solution.py:257
  81.5 28.2 %all-to-all-start.1 = ((bf16[16,16,16,128]{3,2,1,0:T(8,128)(2,1)}), bf16[16,16,16,128]{3,2,1,0:T(8,128)(2,1)S(1)}, u32[]{:S(2)}, u32[]{:S(2)}) async-start(bf16[16,16,16,128]{3,2,1,0:T(8,128)(2,1)} %shard_map.74), calls=%async_computation.1 | async-start | bytes 2097152 | tf_op jit(solution)/shard_map/all_to_all | solution.py:260
  89.2 20.5 %collective-permute-start.5 = (bf16[1,4,2,2,4,2,16,128]{7,6,5,4,3,2,1,0:T(8,128)(2,1)S(1)}, bf16[1,4,2,2,4,2,16,128]{7,6,5,4,3,2,1,0:T(8,128)(2,1)}, u32[]{:S(2)}, u32[]{:S(2)}) collective-permute-start(bf16[1,4,2,2,4,2,16,128]{7,6,5,4,3,2,1,0:T(8,128)(2,1)S(1)} %get-tuple-element.6), channel_id=1, source_target_pairs={{0,96},{16,112},{32,0},{48,16},{64,32},{80,48},{96,64},{112,80},{1... | collective-permute-start | bytes 1572872 | tf_op jit(solution)/shard_map/ppermute | solution.py:257
  90.2 19.6 %collective-permute-start.6 = (bf16[1,4,2,2,4,2,16,128]{7,6,5,4,3,2,1,0:T(8,128)(2,1)S(1)}, bf16[1,4,2,2,4,2,16,128]{7,6,5,4,3,2,1,0:T(8,128)(2,1)}, u32[]{:S(2)}, u32[]{:S(2)}) collective-permute-start(bf16[1,4,2,2,4,2,16,128]{7,6,5,4,3,2,1,0:T(8,128)(2,1)S(1)} %get-tuple-element.5), channel_id=1, source_target_pairs={{0,112},{16,0},{32,16},{48,32},{64,48},{80,64},{96,80},{112,96},{1... | collective-permute-start | bytes 1572872 | tf_op jit(solution)/shard_map/ppermute | solution.py:257
  109.8 1.0 copy-start

commit v14 on v13

--- a/solution.py
+++ b/solution.py
@@ -260,9 +260,12 @@
     outs.append(lax.all_to_all(picked, "chan", split_axis=0, concat_axis=0, tiled=True))
     picked = beamform_pieces(pieces, wperm, select, outs[0].reshape(-1, 1, U, 128))
     outs.append(lax.all_to_all(picked, "chan", split_axis=0, concat_axis=0, tiled=True))
-    exchanged = jnp.concatenate(outs, axis=1)
-    nodes, bins, fine, width = exchanged.shape
-    return jnp.transpose(exchanged, (1, 0, 2, 3)).reshape(bins, nodes * fine, width)
+    nodes, part, fine, width = outs[0].shape
+    bins = part * len(outs)
+    first_part = jnp.transpose(outs[0], (1, 0, 2, 3)).reshape(part, nodes * fine, width)
+    result = lax.optimization_barrier(jnp.pad(first_part, ((0, bins - part), (0, 0), (0, 0))))
+    last_part = jnp.transpose(outs[1], (1, 0, 2, 3)).reshape(part, nodes * fine, width)
+    return lax.dynamic_update_slice_in_dim(result, last_part, part, axis=0)
 
 
 def solution(mesh):

time: 155 us -> 154 us (level)
  blocking collectives: 23 us -> 0 us
  waiting for transfers between devices: 32.1 us -> 44.5 us
  starting transfers between devices: 23.1 us -> 30.7 us
  local copies, waits for them, and re-layouts: 14.9 us -> 17.5 us
    all_to_all x1 -> x0, blocking collectives: 23 us -> none  [on_device(): lax.all_to_all(picked, 'chan', split_axis=0, concat_axis=0, tiled=True)]
    all_to_all x1 -> x2, waiting for transfers between devices: 0.01 us -> 12.5 us  [on_device(): lax.all_to_all(picked, 'chan', split_axis=0, concat_axis=0, tiled=True)]
    all_to_all x1 -> x2, starting transfers between devices: 7.6 us -> 15.2 us  [on_device(): lax.all_to_all(picked, 'chan', split_axis=0, concat_axis=0, tiled=True)]
    pad x0 -> x1, local copies, waits for them, and re-layouts: none -> 1.63 us  [on_device(): jnp.pad(first_part, ((0, bins - part), (0, 0), (0, 0)))]
  transfers between devices with their start and end apart: 9 -> 10, of which waited for: 3 -> 4; matrix products, arithmetic and copies ran while one was open for 12% -> 14% of each run, Pallas kernels for 17% -> 17%
where the time goes in v14:
time: 154 us; the launch traced here: 153 us
  Pallas kernels  53.6 us (35%)
  waiting for transfers between devices  44.5 us (29%)
  starting transfers between devices  30.7 us (20%)
  local copies, waits for them, and re-layouts  17.5 us (11%)
  other arithmetic  6.21 us (4%)
    all_to_all x1, waiting for transfers between devices, on_device(): lax.all_to_all(first, 'feed', split_axis=0, concat_axis=0, tiled=True)  24.5 us
    pallas_call x2, Pallas kernels, filterbank(): pl.pallas_call(lambda *refs: _filter_kernel(chunk, shifted, *refs), grid_...  19.4 us
    pallas_call x1, Pallas kernels, beamform_pieces(): pl.pallas_call(lambda *refs: _beam_pieces_kernel(len(pieces), *refs), gri...  17.3 us
    pallas_call x1, Pallas kernels, beamform(): pl.pallas_call(_beam_kernel, grid=(nb,), in_specs=[pl.BlockSpec((nsrc, 1,...  16.9 us
    all_to_all x2, starting transfers between devices, on_device(): lax.all_to_all(picked, 'chan', split_axis=0, concat_axis=0, tiled=True)  15.2 us
    all_to_all x2, waiting for transfers between devices, on_device(): lax.all_to_all(picked, 'chan', split_axis=0, concat_axis=0, tiled=True)  12.5 us
    ppermute x7, starting transfers between devices, on_device(): pieces.append(lax.ppermute(second[shift:shift + 1], 'feed', perm=pairs))  9.55 us
    gather x2, local copies, waits for them, and re-layouts, on_device(): jnp.take(weights.reshape(2, 1, nfeed, feeds_local, beams), order, axis=2)  7.64 us
  transfers between devices with their start and end apart: 10, of which 4 were waited for; matrix products, arithmetic and copies ran while one was open for 14% of the time, Pallas kernels for 17%

profile of v14, /device:TPU:1, one launch (start us, length us, event | category | flops | bytes accessed | tf_op | source)
XLA Modules:
  0.0 152.6 jit_solution(8781871588932966723)
XLA Ops:
  0.0 9.7 %shard_map.73 = bf16[8,4,2,2,4,2,16,128]{7,6,5,4,3,2,1,0:T(8,128)(2,1)} custom-call(bf16[2,2,8,2,512,128]{5,4,3,2,1,0:T(8,128)(2,1)} %bitcast.20, bf16[2,2,8,64,16,128]{5,4,3,2,1,0:T(8,128)(2,1)} %bitcast.21, bf16[2,2,8,64,16,128]{5,4,3,2,1,0:T(8,128)(2,1)} %bitcast.22, bf16[2,2,8,64,16,128]{5,4,3,2,1,0:T(8,128)(2,1)} %bitcast.23, ...), custom_call_target="tpu_custom_call" | custom-call | flops 2952790016 | bytes 8388608 | tf_op jit(solution)/shard_map/pallas_call | solution.py:138
  9.7 6.0 %all-to-all-start = ((bf16[8,4,2,2,4,2,16,128]{7,6,5,4,3,2,1,0:T(8,128)(2,1)}), bf16[8,4,2,2,4,2,16,128]{7,6,5,4,3,2,1,0:T(8,128)(2,1)}, u32[]{:S(2)}, u32[]{:S(2)}) async-start(bf16[8,4,2,2,4,2,16,128]{7,6,5,4,3,2,1,0:T(8,128)(2,1)} %shard_map.73), calls=%async_computation | async-start | bytes 8388608 | tf_op jit(solution)/shard_map/all_to_all | solution.py:252
  15.7 9.7 %shard_map.75 = bf16[8,4,2,2,4,2,16,128]{7,6,5,4,3,2,1,0:T(8,128)(2,1)} custom-call(s32[1]{0:T(128)} %bitcast.6.refs_0_, bf16[2,2,8,2,512,128]{5,4,3,2,1,0:T(8,128)(2,1)} %bitcast.24, bf16[2,2,8,64,16,128]{5,4,3,2,1,0:T(8,128)(2,1)} %bitcast.25, bf16[2,2,8,64,16,128]{5,4,3,2,1,0:T(8,128)(2,1)} %bitcast.26, bf16[2,2,8,64,16,128]{5,4,3,2,1,0:T(8,128)(2,1)} %bitcast.27, ...), custom_call_target="tpu_custom_call" | custom-call | flops 2952790016 | bytes 8388608 | tf_op jit(solution)/shard_map/pallas_call | solution.py:138
  25.3 0.0 copy-start.2
  25.4 0.0 copy-start.1
  25.4 4.4 %fusion.6 = (bf16[1,4,2,2,4,2,16,128]{7,6,5,4,3,2,1,0:T(8,128)(2,1)S(1)}, bf16[1,4,2,2,4,2,16,128]{7,6,5,4,3,2,1,0:T(8,128)(2,1)S(1)}, bf16[1,4,2,2,4,2,16,128]{...) fusion(bf16[8,4,2,2,4,2,16,128]{7,6,5,4,3,2,1,0:T(8,128)(2,1)} , ...), kind=kLoop, calls=%fused_computation.20 | loop fusion | bytes 8388608 | tf_op jit(solution)/shard_map/slice | solution.py:257
  29.7 1.6 %collective-permute-start = (bf16[1,4,2,2,4,2,16,128]{7,6,5,4,3,2,1,0:T(8,128)(2,1)}, bf16[1,4,2,2,4,2,16,128]{7,6,5,4,3,2,1,0:T(8,128)(2,1)}, u32[]{:S(2)}, u32[]{:S(2)}) collective-permute-start(bf16[1,4,2,2,4,2,16,128]{7,6,5,4,3,2,1,0:T(8,128)(2,1)} %get-tuple-element.11), channel_id=1, source_target_pairs={{0,16},{16,32},{32,48},{48,64},{64,80},{80,96},{96,112},{112,0},{1... | collective-permute-start | bytes 1572872 | tf_op jit(solution)/shard_map/ppermute | solution.py:257
  31.4 1.2 collective-permute-start.1
  32.6 1.6 %collective-permute-start.2 = (bf16[1,4,2,2,4,2,16,128]{7,6,5,4,3,2,1,0:T(8,128)(2,1)}, bf16[1,4,2,2,4,2,16,128]{7,6,5,4,3,2,1,0:T(8,128)(2,1)}, u32[]{:S(2)}, u32[]{:S(2)}) collective-permute-start(bf16[1,4,2,2,4,2,16,128]{7,6,5,4,3,2,1,0:T(8,128)(2,1)} %get-tuple-element.9), channel_id=1, source_target_pairs={{0,48},{16,64},{32,80},{48,96},{64,112},{80,0},{96,16},{112,32},{1... | collective-permute-start | bytes 1572872 | tf_op jit(solution)/shard_map/ppermute | solution.py:257
  34.2 0.6 collective-permute-start.3
  34.8 1.6 %collective-permute-start.4 = (bf16[1,4,2,2,4,2,16,128]{7,6,5,4,3,2,1,0:T(8,128)(2,1)S(1)}, bf16[1,4,2,2,4,2,16,128]{7,6,5,4,3,2,1,0:T(8,128)(2,1)}, u32[]{:S(2)}, u32[]{:S(2)}) collective-permute-start(bf16[1,4,2,2,4,2,16,128]{7,6,5,4,3,2,1,0:T(8,128)(2,1)S(1)} %get-tuple-element.7), channel_id=1, source_target_pairs={{0,80},{16,96},{32,112},{48,0},{64,16},{80,32},{96,48},{112,64},{1... | collective-permute-start | bytes 1572872 | tf_op jit(solution)/shard_map/ppermute | solution.py:257
  36.4 0.0 copy-done.2
  36.4 0.1 fusion.2
  36.5 0.0 copy-done.1
  36.5 3.7 %fusion.1.sel_ref.refs_9_ = bf16[1024,2048]{1,0:T(8,128)(2,1)} fusion(s32[2048]{0:T(1024)S(1)} %bitcast.36, pred[2048]{0:T(1024)(128)(4,1)S(1)} %fusion.2), kind=kLoop, calls=%fused_computation.3 | loop fusion | flops 6291456 | bytes 4204544 | tf_op jit(solution)/shard_map/convert_element_type | solution.py:244
  40.2 24.5 %all-to-all-done.cal_ref = bf16[8,4,2,2,4,2,16,128]{7,6,5,4,3,2,1,0:T(8,128)(2,1)} async-done(((bf16[8,4,2,2,4,2,16,128]{7,6,5,4,3,2,1,0:T(8,128)(2,1)}), bf16[8,4,2,2,4,2,16,128]{7,6,5,4,3,2,1,0:T(8,128)(2,1)}, u32[]{:S(2)}, u32[]{:S(2)}) %all-to-all-start) | async-done | bytes 4194336 | tf_op jit(solution)/shard_map/all_to_all | solution.py:252
  64.6 16.9 %shard_map.74 = bf16[16,16,16,128]{3,2,1,0:T(8,128)(2,1)} custom-call(bf16[8,4,2,2,4,2,16,128]{7,6,5,4,3,2,1,0:T(8,128)(2,1)} %all-to-all-done.cal_ref, bf16[2,1,1024,1024]{3,2,1,0:T(8,128)(2,1)} %w_ref.1, bf16[1024,2048]{1,0:T(8,128)(2,1)} %fusion.1.sel_ref.refs_9_), custom_call_target="tpu_custom_call" | custom-call | flops 9663676416 | bytes 13631488 | tf_op jit(solution)/shard_map/pallas_call | solution.py:218
  81.5 7.6 %all-to-all-start.1 = ((bf16[16,16,16,128]{3,2,1,0:T(8,128)(2,1)}), bf16[16,16,16,128]{3,2,1,0:T(8,128)(2,1)S(1)}, u32[]{:S(2)}, u32[]{:S(2)}) async-start(bf16[16,16,16,128]{3,2,1,0:T(8,128)(2,1)} %shard_map.74), calls=%async_computation.1 | async-start | bytes 2097152 | tf_op jit(solution)/shard_map/all_to_all | solution.py:260
  89.2 0.1 broadcast_bitcast_fusion
  89.3 0.0 collective-permute-done.refs_1_
  89.3 0.9 collective-permute-start.5
  90.1 0.0 collective-permute-done.1.refs_2_
  90.2 2.0 %collective-permute-start.6 = (bf16[1,4,2,2,4,2,16,128]{7,6,5,4,3,2,1,0:T(8,128)(2,1)S(1)}, bf16[1,4,2,2,4,2,16,128]{7,6,5,4,3,2,1,0:T(8,128)(2,1)}, u32[]{:S(2)}, u32[]{:S(2)}) collective-permute-start(bf16[1,4,2,2,4,2,16,128]{7,6,5,4,3,2,1,0:T(8,128)(2,1)S(1)} %get-tuple-element.5), channel_id=1, source_target_pairs={{0,112},{16,0},{32,16},{48,32},{64,48},{80,64},{96,80},{112,96},{1... | collective-permute-start | bytes 1572872 | tf_op jit(solution)/shard_map/ppermute | solution.py:257
  92.1 5.0 %gather_fusion = bf16[8,2,128,1024]{3,2,1,0:T(8,128)(2,1)} fusion(bf16[2,8,128,1024]{3,2,1,0:T(8,128)(2,1)} %bitcast.30, s32[1024]{0:T(1024)S(1)} %pad_clamp_fusion), kind=kCustom, calls=%fused_computation | custom fusion | bytes 8388640 | tf_op jit(solution)/shard_map/jit(_take)/gather | solution.py:250
  97.1 2.7 %copy.9 = bf16[2,8,128,1024]{3,2,1,0:T(8,128)(2,1)S(1)} copy(bf16[2,8,128,1024]{3,2,0,1:T(8,128)(2,1)} %bitcast.29) | data formatting | bytes 8388608 | tf_op jit(solution)/shard_map/jit(_take)/gather | solution.py:250
  99.8 2.4 %bitcast_select_fusion.refs_8_ = bf16[2,1,1024,1024]{3,2,1,0:T(8,128)(2,1)} fusion(pred[1024]{0:T(1024)(128)(4,1)S(1)} %broadcast_bitcast_fusion, bf16[2,1,1024,1024]{3,2,1,0:T(8,128)(2,1)S(1)} %bitcast.28), kind=kLoop, calls=%fused_computation.4 | loop fusion | flops 2097152 | bytes 8389632 | tf_op jit(solution)/shard_map/jit(_take)/select_n | solution.py:250
  102.2 0.0 collective-permute-done.2.refs_3_
  102.2 7.1 %collective-permute-done.3.refs_4_ = bf16[1,4,2,2,4,2,16,128]{7,6,5,4,3,2,1,0:T(8,128)(2,1)} collective-permute-done((bf16[1,4,2,2,4,2,16,128]{7,6,5,4,3,2,1,0:T(8,128)(2,1)S(1)}, bf16[1,4,2,2,4,2,16,128]{7,6,5,4,3,2,1,0:T(8,128)(2,1)}, u32[]{:S(2)}, u32[]{:S(2)}) %collective-permute-start.3) | collective-permute-done | bytes 524320 | tf_op jit(solution)/shard_map/ppermute | solution.py:257
  109.3 0.5 collective-permute-done.4.refs_5_
  109.7 0.0 collective-permute-done.5.refs_6_
  109.8 0.0 collective-permute-done.6.refs_7_
  109.8 0.0 all-to-all-done.1
  109.8 0.0 copy-start
  109.8 1.0 copy-done
  110.7 17.3 %shard_map.76 = bf16[16,16,16,128]{3,2,1,0:T(8,128)(2,1)} custom-call(bf16[1,4,2,2,4,2,16,128]{7,6,5,4,3,2,1,0:T(8,128)(2,1)} %get-tuple-element.12.refs_0_, bf16[1,4,2,2,4,2,16,128]{7,6,5,4,3,2,1,0:T(8,128)(2,1)} %collective-permute-done.refs_1_, bf16[1,4,2,2,4,2,16,128]{7,6,5,4,3,2,1,0:T(8,128)(2,1)} %collective-permute-done.1.refs_2_, ...), custom_call_target="tpu_custom_call" | custom-call | flops 9663676416 | bytes 13631488 | tf_op jit(solution)/shard_map/pallas_call | solution.py:193
  128.0 7.6 %all-to-all-start.2 = ((bf16[16,16,16,128]{3,2,1,0:T(8,128)(2,1)}), bf16[16,16,16,128]{3,2,1,0:T(8,128)(2,1)S(1)}, u32[]{:S(2)}, u32[]{:S(2)}) async-start(bf16[16,16,16,128]{3,2,1,0:T(8,128)(2,1)} %shard_map.76), calls=%async_computation.2 | async-start | bytes 2097152 | tf_op jit(solution)/shard_map/all_to_all | solution.py:262
  135.6 1.5 copy.8
  137.1 1.6 %pad.4 = bf16[32,256,128]{2,1,0:T(8,128)(2,1)} pad(bf16[16,256,128]{2,1,0:T(8,128)(2,1)S(1)} %bitcast.34, bf16[]{:T(256)} %constant.24.clone.1), padding=0_16x0_0x0_0 | pad | bytes 3145730 | tf_op jit(solution)/shard_map/jit(_pad)/pad | solution.py:266
  138.8 12.5 %all-to-all-done.2 = bf16[16,16,16,128]{3,2,1,0:T(8,128)(2,1)S(1)} async-done(((bf16[16,16,16,128]{3,2,1,0:T(8,128)(2,1)}), bf16[16,16,16,128]{3,2,1,0:T(8,128)(2,1)S(1)}, u32[]{:S(2)}, u32[]{:S(2)}) %all-to-all-start.2) | async-done | bytes 1048608 | tf_op jit(solution)/shard_map/all_to_all | solution.py:262
  151.3 0.3 copy.10
  151.5 1.0 constant_dynamic-update-slice_fusion
  (3 shorter events, 0.0 us)
Async XLA Ops:
  9.7 54.9 %all-to-all-start = ((bf16[8,4,2,2,4,2,16,128]{7,6,5,4,3,2,1,0:T(8,128)(2,1)}), bf16[8,4,2,2,4,2,16,128]{7,6,5,4,3,2,1,0:T(8,128)(2,1)}, u32[]{:S(2)}, u32[]{:S(2)}) async-start(bf16[8,4,2,2,4,2,16,128]{7,6,5,4,3,2,1,0:T(8,128)(2,1)} %shard_map.73), calls=%async_computation | async-start | bytes 8388608 | tf_op jit(solution)/shard_map/all_to_all | solution.py:252
  25.3 11.1 %copy-start.2 = (s32[16]{0:T(128)S(1)}, s32[16]{0:T(128)}, u32[]{:S(2)}) copy-start(s32[16]{0:T(128)} %param.12) | copy-start | bytes 196
  25.4 11.1 %copy-start.1 = (s32[16,128]{1,0:T(8,128)S(1)}, s32[16,128]{1,0:T(8,128)}, u32[]{:S(2)}) copy-start(s32[16,128]{1,0:T(8,128)} %param.11) | copy-start | bytes 24580
  29.7 59.5 %collective-permute-start = (bf16[1,4,2,2,4,2,16,128]{7,6,5,4,3,2,1,0:T(8,128)(2,1)}, bf16[1,4,2,2,4,2,16,128]{7,6,5,4,3,2,1,0:T(8,128)(2,1)}, u32[]{:S(2)}, u32[]{:S(2)}) collective-permute-start(bf16[1,4,2,2,4,2,16,128]{7,6,5,4,3,2,1,0:T(8,128)(2,1)} %get-tuple-element.11), channel_id=1, source_target_pairs={{0,16},{16,32},{32,48},{48,64},{64,80},{80,96},{96,112},{112,0},{1... | collective-permute-start | bytes 1572872 | tf_op jit(solution)/shard_map/ppermute | solution.py:257
  31.4 58.8 %collective-permute-start.1 = (bf16[1,4,2,2,4,2,16,128]{7,6,5,4,3,2,1,0:T(8,128)(2,1)}, bf16[1,4,2,2,4,2,16,128]{7,6,5,4,3,2,1,0:T(8,128)(2,1)}, u32[]{:S(2)}, u32[]{:S(2)}) collective-permute-start(bf16[1,4,2,2,4,2,16,128]{7,6,5,4,3,2,1,0:T(8,128)(2,1)} %get-tuple-element.10), channel_id=1, source_target_pairs={{0,32},{16,48},{32,64},{48,80},{64,96},{80,112},{96,0},{112,16},{1... | collective-permute-start | bytes 1572872 | tf_op jit(solution)/shard_map/ppermute | solution.py:257
  32.6 69.6 %collective-permute-start.2 = (bf16[1,4,2,2,4,2,16,128]{7,6,5,4,3,2,1,0:T(8,128)(2,1)}, bf16[1,4,2,2,4,2,16,128]{7,6,5,4,3,2,1,0:T(8,128)(2,1)}, u32[]{:S(2)}, u32[]{:S(2)}) collective-permute-start(bf16[1,4,2,2,4,2,16,128]{7,6,5,4,3,2,1,0:T(8,128)(2,1)} %get-tuple-element.9), channel_id=1, source_target_pairs={{0,48},{16,64},{32,80},{48,96},{64,112},{80,0},{96,16},{112,32},{1... | collective-permute-start | bytes 1572872 | tf_op jit(solution)/shard_map/ppermute | solution.py:257
  34.2 75.1 %collective-permute-start.3 = (bf16[1,4,2,2,4,2,16,128]{7,6,5,4,3,2,1,0:T(8,128)(2,1)S(1)}, bf16[1,4,2,2,4,2,16,128]{7,6,5,4,3,2,1,0:T(8,128)(2,1)}, u32[]{:S(2)}, u32[]{:S(2)}) collective-permute-start(bf16[1,4,2,2,4,2,16,128]{7,6,5,4,3,2,1,0:T(8,128)(2,1)S(1)} %get-tuple-element.8), channel_id=1, source_target_pairs={{0,64},{16,80},{32,96},{48,112},{64,0},{80,16},{96,32},{112,48},{1... | collective-permute-start | bytes 1572872 | tf_op jit(solution)/shard_map/ppermute | solution.py:257
  34.8 75.0 %collective-permute-start.4 = (bf16[1,4,2,2,4,2,16,128]{7,6,5,4,3,2,1,0:T(8,128)(2,1)S(1)}, bf16[1,4,2,2,4,2,16,128]{7,6,5,4,3,2,1,0:T(8,128)(2,1)}, u32[]{:S(2)}, u32[]{:S(2)}) collective-permute-start(bf16[1,4,2,2,4,2,16,128]{7,6,5,4,3,2,1,0:T(8,128)(2,1)S(1)} %get-tuple-element.7), channel_id=1, source_target_pairs={{0,80},{16,96},{32,112},{48,0},{64,16},{80,32},{96,48},{112,64},{1... | collective-permute-start | bytes 1572872 | tf_op jit(solution)/shard_map/ppermute | solution.py:257
  81.5 28.2 %all-to-all-start.1 = ((bf16[16,16,16,128]{3,2,1,0:T(8,128)(2,1)}), bf16[16,16,16,128]{3,2,1,0:T(8,128)(2,1)S(1)}, u32[]{:S(2)}, u32[]{:S(2)}) async-start(bf16[16,16,16,128]{3,2,1,0:T(8,128)(2,1)} %shard_map.74), calls=%async_computation.1 | async-start | bytes 2097152 | tf_op jit(solution)/shard_map/all_to_all | solution.py:260
  89.3 20.5 %collective-permute-start.5 = (bf16[1,4,2,2,4,2,16,128]{7,6,5,4,3,2,1,0:T(8,128)(2,1)S(1)}, bf16[1,4,2,2,4,2,16,128]{7,6,5,4,3,2,1,0:T(8,128)(2,1)}, u32[]{:S(2)}, u32[]{:S(2)}) collective-permute-start(bf16[1,4,2,2,4,2,16,128]{7,6,5,4,3,2,1,0:T(8,128)(2,1)S(1)} %get-tuple-element.6), channel_id=1, source_target_pairs={{0,96},{16,112},{32,0},{48,16},{64,32},{80,48},{96,64},{112,80},{1... | collective-permute-start | bytes 1572872 | tf_op jit(solution)/shard_map/ppermute | solution.py:257
  90.2 19.6 %collective-permute-start.6 = (bf16[1,4,2,2,4,2,16,128]{7,6,5,4,3,2,1,0:T(8,128)(2,1)S(1)}, bf16[1,4,2,2,4,2,16,128]{7,6,5,4,3,2,1,0:T(8,128)(2,1)}, u32[]{:S(2)}, u32[]{:S(2)}) collective-permute-start(bf16[1,4,2,2,4,2,16,128]{7,6,5,4,3,2,1,0:T(8,128)(2,1)S(1)} %get-tuple-element.5), channel_id=1, source_target_pairs={{0,112},{16,0},{32,16},{48,32},{64,48},{80,64},{96,80},{112,96},{1... | collective-permute-start | bytes 1572872 | tf_op jit(solution)/shard_map/ppermute | solution.py:257
  109.8 1.0 copy-start
  128.0 23.2 %all-to-all-start.2 = ((bf16[16,16,16,128]{3,2,1,0:T(8,128)(2,1)}), bf16[16,16,16,128]{3,2,1,0:T(8,128)(2,1)S(1)}, u32[]{:S(2)}, u32[]{:S(2)}) async-start(bf16[16,16,16,128]{3,2,1,0:T(8,128)(2,1)} %shard_map.76), calls=%async_computation.2 | async-start | bytes 2097152 | tf_op jit(solution)/shard_map/all_to_all | solution.py:262

commit v15 on v14

--- a/solution.py
+++ b/solution.py
@@ -210,19 +210,20 @@
     )(*pieces, weights, select, after)
 
 
-def beamform(cal, weights, select):
+def beamform(cal, weights, select, after=()):
     nsrc, nb = cal.shape[0], cal.shape[1]
     feeds, beams = weights.shape[2], weights.shape[3]
     slots = select.shape[1]
     nodes = slots // 128
     return pl.pallas_call(
-        _beam_kernel,
+        lambda *refs: _beam_kernel(*refs[:3], refs[-1]),
         grid=(nb,),
         in_specs=[
             pl.BlockSpec((nsrc, 1, 2, 2, IB, TINT, U, 128), lambda i: (0, i, 0, 0, 0, 0, 0, 0)),
             pl.BlockSpec((2, 1, feeds, beams), lambda i: (0, 0, 0, 0)),
             pl.BlockSpec((beams, slots), lambda i: (0, 0)),
-        ],
+        ]
+        + [pl.BlockSpec((1, 1, U, 128), lambda i: (0, 0, 0, 0)) for _ in after],
         out_specs=pl.BlockSpec((nodes, IB, U, 128), lambda i: (0, i, 0, 0)),
         out_shape=jax.ShapeDtypeStruct((nodes, nb * IB, U, 128), jnp.bfloat16),
         cost_estimate=pl.CostEstimate(
@@ -231,7 +232,7 @@
             transcendentals=0,
         ),
         compiler_params=pltpu.CompilerParams(vmem_limit_bytes=60 * 1024 * 1024),
-    )(cal, weights, select)
+    )(cal, weights, select, *after)
 
 
 def on_device(voltages, history, gains, weights, beam_lists, beam_counts):
@@ -256,7 +257,7 @@
         pairs = [(i, (i + shift) % nfeed) for i in range(nfeed)]
         pieces.append(lax.ppermute(second[shift : shift + 1], "feed", perm=pairs))
     outs = []
-    picked = beamform(gathered, weights, select)
+    picked = beamform(gathered, weights, select, [p.reshape(-1, 1, U, 128) for p in pieces[1:3]])
     outs.append(lax.all_to_all(picked, "chan", split_axis=0, concat_axis=0, tiled=True))
     picked = beamform_pieces(pieces, wperm, select, outs[0].reshape(-1, 1, U, 128))
     outs.append(lax.all_to_all(picked, "chan", split_axis=0, concat_axis=0, tiled=True))

time: 154 us -> 171 us (1.11); the launches traced: 153 us -> 168 us
  waiting for transfers between devices: 44.5 us -> 62.2 us
  starting transfers between devices: 30.7 us -> 27.2 us
    ppermute x7, waiting for transfers between devices: 7.55 us -> 43.9 us  [on_device(): pieces.append(lax.ppermute(second[shift:shift + 1], 'feed', perm=pairs))]
    all_to_all x1, waiting for transfers between devices: 24.5 us -> 0.01 us  [on_device(): lax.all_to_all(first, 'feed', split_axis=0, concat_axis=0, tiled=True)]
    all_to_all x2, waiting for transfers between devices: 12.5 us -> 18.3 us  [on_device(): lax.all_to_all(picked, 'chan', split_axis=0, concat_axis=0, tiled=True)]
    all_to_all x2, starting transfers between devices: 15.2 us -> 12.1 us  [on_device(): lax.all_to_all(picked, 'chan', split_axis=0, concat_axis=0, tiled=True)]
  transfers between devices with their start and end apart: 10 -> 10, of which waited for: 4 -> 4; matrix products, arithmetic and copies ran while one was open for 14% -> 13% of each run, Pallas kernels for 17% -> 16%
where the time goes in v15:
time: 171 us; the launch traced here: 168 us
  waiting for transfers between devices  62.2 us (36%)
  Pallas kernels  53.7 us (31%)
  starting transfers between devices  27.2 us (16%)
  local copies, waits for them, and re-layouts  18.3 us (11%)
  other arithmetic  6.21 us (4%)
    ppermute x7, waiting for transfers between devices, on_device(): pieces.append(lax.ppermute(second[shift:shift + 1], 'feed', perm=pairs))  43.9 us
    pallas_call x2, Pallas kernels, filterbank(): pl.pallas_call(lambda *refs: _filter_kernel(chunk, shifted, *refs), grid_...  19.4 us
    all_to_all x2, waiting for transfers between devices, on_device(): lax.all_to_all(picked, 'chan', split_axis=0, concat_axis=0, tiled=True)  18.3 us
    pallas_call x1, Pallas kernels, beamform_pieces(): pl.pallas_call(lambda *refs: _beam_pieces_kernel(len(pieces), *refs), gri...  17.3 us
    pallas_call x1, Pallas kernels, beamform(): pl.pallas_call(lambda *refs: _beam_kernel(*refs[:3], refs[-1]), grid=(nb,...  17 us
    all_to_all x2, starting transfers between devices, on_device(): lax.all_to_all(picked, 'chan', split_axis=0, concat_axis=0, tiled=True)  12.1 us
    ppermute x7, starting transfers between devices, on_device(): pieces.append(lax.ppermute(second[shift:shift + 1], 'feed', perm=pairs))  9.11 us
    gather x2, local copies, waits for them, and re-layouts, on_device(): jnp.take(weights.reshape(2, 1, nfeed, feeds_local, beams), order, axis=2)  7.65 us
  transfers between devices with their start and end apart: 10, of which 4 were waited for; matrix products, arithmetic and copies ran while one was open for 13% of the time, Pallas kernels for 16%

profile of v15, /device:TPU:1, one launch (start us, length us, event | category | flops | bytes accessed | tf_op | source)
XLA Modules:
  0.0 167.7 jit_solution(18026572273697501867)
XLA Ops:
  0.0 9.7 %shard_map.73 = bf16[8,4,2,2,4,2,16,128]{7,6,5,4,3,2,1,0:T(8,128)(2,1)} custom-call(bf16[2,2,8,2,512,128]{5,4,3,2,1,0:T(8,128)(2,1)} %bitcast.26, bf16[2,2,8,64,16,128]{5,4,3,2,1,0:T(8,128)(2,1)} %bitcast.27, bf16[2,2,8,64,16,128]{5,4,3,2,1,0:T(8,128)(2,1)} %bitcast.28, bf16[2,2,8,64,16,128]{5,4,3,2,1,0:T(8,128)(2,1)} %bitcast.29, ...), custom_call_target="tpu_custom_call" | custom-call | flops 2952790016 | bytes 8388608 | tf_op jit(solution)/shard_map/pallas_call | solution.py:138
  9.7 6.0 %all-to-all-start = ((bf16[8,4,2,2,4,2,16,128]{7,6,5,4,3,2,1,0:T(8,128)(2,1)}), bf16[8,4,2,2,4,2,16,128]{7,6,5,4,3,2,1,0:T(8,128)(2,1)}, u32[]{:S(2)}, u32[]{:S(2)}) async-start(bf16[8,4,2,2,4,2,16,128]{7,6,5,4,3,2,1,0:T(8,128)(2,1)} %shard_map.73), calls=%async_computation | async-start | bytes 8388608 | tf_op jit(solution)/shard_map/all_to_all | solution.py:253
  15.7 9.7 %shard_map.74 = bf16[8,4,2,2,4,2,16,128]{7,6,5,4,3,2,1,0:T(8,128)(2,1)} custom-call(s32[1]{0:T(128)} %bitcast.4.refs_0_, bf16[2,2,8,2,512,128]{5,4,3,2,1,0:T(8,128)(2,1)} %bitcast.30, bf16[2,2,8,64,16,128]{5,4,3,2,1,0:T(8,128)(2,1)} %bitcast.31, bf16[2,2,8,64,16,128]{5,4,3,2,1,0:T(8,128)(2,1)} %bitcast.32, bf16[2,2,8,64,16,128]{5,4,3,2,1,0:T(8,128)(2,1)} %bitcast.33, ...), custom_call_target="tpu_custom_call" | custom-call | flops 2952790016 | bytes 8388608 | tf_op jit(solution)/shard_map/pallas_call | solution.py:138
  25.4 0.0 copy-start.2
  25.4 0.0 copy-start.1
  25.4 4.4 %fusion.6 = (bf16[1,4,2,2,4,2,16,128]{7,6,5,4,3,2,1,0:T(8,128)(2,1)S(1)}, bf16[1,4,2,2,4,2,16,128]{7,6,5,4,3,2,1,0:T(8,128)(2,1)S(1)}, bf16[1,4,2,2,4,2,16,128]{...) fusion(bf16[8,4,2,2,4,2,16,128]{7,6,5,4,3,2,1,0:T(8,128)(2,1)} , ...), kind=kLoop, calls=%fused_computation.20 | loop fusion | bytes 8388608 | tf_op jit(solution)/shard_map/slice | solution.py:258
  29.8 1.6 collective-permute-start
  31.4 1.2 collective-permute-start.1
  32.6 1.6 collective-permute-start.2
  34.2 0.6 collective-permute-start.3
  34.8 1.7 collective-permute-start.4
  36.5 0.0 copy-done.2
  36.5 0.1 fusion.2
  36.5 0.0 copy-done.1
  36.6 3.7 %fusion.1.refs_2_.refs_9_ = bf16[1024,2048]{1,0:T(8,128)(2,1)} fusion(s32[2048]{0:T(1024)S(1)} %bitcast.42, pred[2048]{0:T(1024)(128)(4,1)S(1)} %fusion.2), kind=kLoop, calls=%fused_computation.3 | loop fusion | flops 6291456 | bytes 4204544 | tf_op jit(solution)/shard_map/convert_element_type | solution.py:245
  40.2 32.2 %collective-permute-done.refs_1_ = bf16[1,4,2,2,4,2,16,128]{7,6,5,4,3,2,1,0:T(8,128)(2,1)S(1)} collective-permute-done((bf16[1,4,2,2,4,2,16,128]{7,6,5,4,3,2,1,0:T(8,128)(2,1)S(1)}, bf16[1,4,2,2,4,2,16,128]{7,6,5,4,3,2,1,0:T(8,128)(2,1)S(1)}, u32[]{:S(2)}, u32[]{:S(2)}) %collective-permute-start) | collective-permute-done | bytes 524320 | tf_op jit(solution)/shard_map/ppermute | solution.py:258
  72.4 0.0 copy-start.3
  72.4 2.4 %collective-permute-start.5 = (bf16[1,4,2,2,4,2,16,128]{7,6,5,4,3,2,1,0:T(8,128)(2,1)S(1)}, bf16[1,4,2,2,4,2,16,128]{7,6,5,4,3,2,1,0:T(8,128)(2,1)}, u32[]{:S(2)}, u32[]{:S(2)}) collective-permute-start(bf16[1,4,2,2,4,2,16,128]{7,6,5,4,3,2,1,0:T(8,128)(2,1)S(1)} %get-tuple-element.6), channel_id=1, source_target_pairs={{0,96},{16,112},{32,0},{48,16},{64,32},{80,48},{96,64},{112,80},{1... | collective-permute-start | bytes 1572872 | tf_op jit(solution)/shard_map/ppermute | solution.py:258
  74.8 11.7 %collective-permute-done.1.refs_2_ = bf16[1,4,2,2,4,2,16,128]{7,6,5,4,3,2,1,0:T(8,128)(2,1)S(1)} collective-permute-done((bf16[1,4,2,2,4,2,16,128]{7,6,5,4,3,2,1,0:T(8,128)(2,1)S(1)}, bf16[1,4,2,2,4,2,16,128]{7,6,5,4,3,2,1,0:T(8,128)(2,1)S(1)}, u32[]{:S(2)}, u32[]{:S(2)}) %collective-permute-start.1) | collective-permute-done | bytes 524320 | tf_op jit(solution)/shard_map/ppermute | solution.py:258
  86.5 0.0 copy-start.4
  86.5 0.0 collective-permute-start.6
  86.5 0.0 all-to-all-done.refs_0_
  86.5 0.0 copy-done.3
  86.5 0.8 copy-done.4
  87.3 17.0 %shard_map.75 = bf16[16,16,16,128]{3,2,1,0:T(8,128)(2,1)} custom-call(bf16[8,4,2,2,4,2,16,128]{7,6,5,4,3,2,1,0:T(8,128)(2,1)} %all-to-all-done.refs_0_, bf16[2,1,1024,1024]{3,2,1,0:T(8,128)(2,1)} %refs_1_.1, bf16[1024,2048]{1,0:T(8,128)(2,1)} %fusion.1.refs_2_.refs_9_, bf16[128,1,16,128]{3,2,1,0:T(8,128)(2,1)} %bitcast.43, bf16[128,1,16,128]{3,2,1,0:T(8,128)(2,1)} %bitcast.44), custom_call_target="tpu_custom_call" | custom-call | flops 9663676416 | bytes 13631488 | tf_op jit(solution)/shard_map/pallas_call | solution.py:218
  104.3 7.6 %all-to-all-start.1 = ((bf16[16,16,16,128]{3,2,1,0:T(8,128)(2,1)}), bf16[16,16,16,128]{3,2,1,0:T(8,128)(2,1)S(1)}, u32[]{:S(2)}, u32[]{:S(2)}) async-start(bf16[16,16,16,128]{3,2,1,0:T(8,128)(2,1)} %shard_map.75), calls=%async_computation.1 | async-start | bytes 2097152 | tf_op jit(solution)/shard_map/all_to_all | solution.py:261
  111.9 0.1 broadcast_bitcast_fusion
  112.0 5.0 %gather_fusion = bf16[8,2,128,1024]{3,2,1,0:T(8,128)(2,1)} fusion(bf16[2,8,128,1024]{3,2,1,0:T(8,128)(2,1)} %bitcast.36, s32[1024]{0:T(1024)S(1)} %pad_clamp_fusion), kind=kCustom, calls=%fused_computation | custom fusion | bytes 8388640 | tf_op jit(solution)/shard_map/jit(_take)/gather | solution.py:251
  117.0 2.7 %copy.13 = bf16[2,8,128,1024]{3,2,1,0:T(8,128)(2,1)S(1)} copy(bf16[2,8,128,1024]{3,2,0,1:T(8,128)(2,1)} %bitcast.35) | data formatting | bytes 8388608 | tf_op jit(solution)/shard_map/jit(_take)/gather | solution.py:251
  119.7 2.4 %bitcast_select_fusion.refs_8_ = bf16[2,1,1024,1024]{3,2,1,0:T(8,128)(2,1)} fusion(pred[1024]{0:T(1024)(128)(4,1)S(1)} %broadcast_bitcast_fusion, bf16[2,1,1024,1024]{3,2,1,0:T(8,128)(2,1)S(1)} %bitcast.34), kind=kLoop, calls=%fused_computation.4 | loop fusion | flops 2097152 | bytes 8389632 | tf_op jit(solution)/shard_map/jit(_take)/select_n | solution.py:251
  122.1 0.0 collective-permute-done.2.refs_3_
  122.1 0.0 collective-permute-done.3.refs_4_
  122.1 0.0 collective-permute-done.4.refs_5_
  122.1 0.0 collective-permute-done.5.refs_6_
  122.1 0.0 collective-permute-done.6.refs_7_
  122.2 6.0 %all-to-all-done.1 = bf16[16,16,16,128]{3,2,1,0:T(8,128)(2,1)S(1)} async-done(((bf16[16,16,16,128]{3,2,1,0:T(8,128)(2,1)}), bf16[16,16,16,128]{3,2,1,0:T(8,128)(2,1)S(1)}, u32[]{:S(2)}, u32[]{:S(2)}) %all-to-all-start.1) | async-done | bytes 1048608 | tf_op jit(solution)/shard_map/all_to_all | solution.py:261
  128.1 0.0 copy-start
  128.1 1.0 copy-done
  129.1 17.3 %shard_map.76 = bf16[16,16,16,128]{3,2,1,0:T(8,128)(2,1)} custom-call(bf16[1,4,2,2,4,2,16,128]{7,6,5,4,3,2,1,0:T(8,128)(2,1)} %get-tuple-element.10.refs_0_, bf16[1,4,2,2,4,2,16,128]{7,6,5,4,3,2,1,0:T(8,128)(2,1)} %copy-done.3, bf16[1,4,2,2,4,2,16,128]{7,6,5,4,3,2,1,0:T(8,128)(2,1)} %copy-done.4, ...), custom_call_target="tpu_custom_call" | custom-call | flops 9663676416 | bytes 13631488 | tf_op jit(solution)/shard_map/pallas_call | solution.py:193
  146.4 4.5 %all-to-all-start.2 = ((bf16[16,16,16,128]{3,2,1,0:T(8,128)(2,1)}), bf16[16,16,16,128]{3,2,1,0:T(8,128)(2,1)S(1)}, u32[]{:S(2)}, u32[]{:S(2)}) async-start(bf16[16,16,16,128]{3,2,1,0:T(8,128)(2,1)} %shard_map.76), calls=%async_computation.2 | async-start | bytes 2097152 | tf_op jit(solution)/shard_map/all_to_all | solution.py:263
  150.9 1.5 copy.12
  152.4 1.6 pad.4
  154.0 12.3 %all-to-all-done.2 = bf16[16,16,16,128]{3,2,1,0:T(8,128)(2,1)S(1)} async-done(((bf16[16,16,16,128]{3,2,1,0:T(8,128)(2,1)}), bf16[16,16,16,128]{3,2,1,0:T(8,128)(2,1)S(1)}, u32[]{:S(2)}, u32[]{:S(2)}) %all-to-all-start.2) | async-done | bytes 1048608 | tf_op jit(solution)/shard_map/all_to_all | solution.py:263
  166.4 0.3 copy.14
  166.7 1.0 constant_dynamic-update-slice_fusion
  (3 shorter events, 0.0 us)
Async XLA Ops:
  9.7 76.8 %all-to-all-start = ((bf16[8,4,2,2,4,2,16,128]{7,6,5,4,3,2,1,0:T(8,128)(2,1)}), bf16[8,4,2,2,4,2,16,128]{7,6,5,4,3,2,1,0:T(8,128)(2,1)}, u32[]{:S(2)}, u32[]{:S(2)}) async-start(bf16[8,4,2,2,4,2,16,128]{7,6,5,4,3,2,1,0:T(8,128)(2,1)} %shard_map.73), calls=%async_computation | async-start | bytes 8388608 | tf_op jit(solution)/shard_map/all_to_all | solution.py:253
  25.4 11.1 %copy-start.2 = (s32[16]{0:T(128)S(1)}, s32[16]{0:T(128)}, u32[]{:S(2)}) copy-start(s32[16]{0:T(128)} %param.12) | copy-start | bytes 196
  25.4 11.2 %copy-start.1 = (s32[16,128]{1,0:T(8,128)S(1)}, s32[16,128]{1,0:T(8,128)}, u32[]{:S(2)}) copy-start(s32[16,128]{1,0:T(8,128)} %param.11) | copy-start | bytes 24580
  29.8 42.7 %collective-permute-start = (bf16[1,4,2,2,4,2,16,128]{7,6,5,4,3,2,1,0:T(8,128)(2,1)S(1)}, bf16[1,4,2,2,4,2,16,128]{7,6,5,4,3,2,1,0:T(8,128)(2,1)S(1)}, u32[]{:S(2)}, u32[]{:S(2)}) collective-permute-start(bf16[1,4,2,2,4,2,16,128]{7,6,5,4,3,2,1,0:T(8,128)(2,1)S(1)} %get-tuple-element.12), channel_id=1, source_target_pairs={{0,16},{16,32},{32,48},{48,64},{64,80},{80,96},{96,112},{112,0},{1... | collective-permute-start | bytes 1572872 | tf_op jit(solution)/shard_map/ppermute | solution.py:258
  31.4 55.1 %collective-permute-start.1 = (bf16[1,4,2,2,4,2,16,128]{7,6,5,4,3,2,1,0:T(8,128)(2,1)S(1)}, bf16[1,4,2,2,4,2,16,128]{7,6,5,4,3,2,1,0:T(8,128)(2,1)S(1)}, u32[]{:S(2)}, u32[]{:S(2)}) collective-permute-start(bf16[1,4,2,2,4,2,16,128]{7,6,5,4,3,2,1,0:T(8,128)(2,1)S(1)} %get-tuple-element.11), channel_id=1, source_target_pairs={{0,32},{16,48},{32,64},{48,80},{64,96},{80,112},{96,0},{112,16},{1... | collective-permute-start | bytes 1572872 | tf_op jit(solution)/shard_map/ppermute | solution.py:258
  32.6 89.5 %collective-permute-start.2 = (bf16[1,4,2,2,4,2,16,128]{7,6,5,4,3,2,1,0:T(8,128)(2,1)}, bf16[1,4,2,2,4,2,16,128]{7,6,5,4,3,2,1,0:T(8,128)(2,1)}, u32[]{:S(2)}, u32[]{:S(2)}) collective-permute-start(bf16[1,4,2,2,4,2,16,128]{7,6,5,4,3,2,1,0:T(8,128)(2,1)} %get-tuple-element.9), channel_id=1, source_target_pairs={{0,48},{16,64},{32,80},{48,96},{64,112},{80,0},{96,16},{112,32},{1... | collective-permute-start | bytes 1572872 | tf_op jit(solution)/shard_map/ppermute | solution.py:258
  34.2 87.9 %collective-permute-start.3 = (bf16[1,4,2,2,4,2,16,128]{7,6,5,4,3,2,1,0:T(8,128)(2,1)S(1)}, bf16[1,4,2,2,4,2,16,128]{7,6,5,4,3,2,1,0:T(8,128)(2,1)}, u32[]{:S(2)}, u32[]{:S(2)}) collective-permute-start(bf16[1,4,2,2,4,2,16,128]{7,6,5,4,3,2,1,0:T(8,128)(2,1)S(1)} %get-tuple-element.8), channel_id=1, source_target_pairs={{0,64},{16,80},{32,96},{48,112},{64,0},{80,16},{96,32},{112,48},{1... | collective-permute-start | bytes 1572872 | tf_op jit(solution)/shard_map/ppermute | solution.py:258
  34.8 87.3 %collective-permute-start.4 = (bf16[1,4,2,2,4,2,16,128]{7,6,5,4,3,2,1,0:T(8,128)(2,1)S(1)}, bf16[1,4,2,2,4,2,16,128]{7,6,5,4,3,2,1,0:T(8,128)(2,1)}, u32[]{:S(2)}, u32[]{:S(2)}) collective-permute-start(bf16[1,4,2,2,4,2,16,128]{7,6,5,4,3,2,1,0:T(8,128)(2,1)S(1)} %get-tuple-element.7), channel_id=1, source_target_pairs={{0,80},{16,96},{32,112},{48,0},{64,16},{80,32},{96,48},{112,64},{1... | collective-permute-start | bytes 1572872 | tf_op jit(solution)/shard_map/ppermute | solution.py:258
  72.4 14.1 %copy-start.3 = (bf16[1,4,2,2,4,2,16,128]{7,6,5,4,3,2,1,0:T(8,128)(2,1)}, bf16[1,4,2,2,4,2,16,128]{7,6,5,4,3,2,1,0:T(8,128)(2,1)S(1)}, u32[]{:S(2)}) copy-start(bf16[1,4,2,2,4,2,16,128]{7,6,5,4,3,2,1,0:T(8,128)(2,1)S(1)} %collective-permute-done.refs_1_) | copy-start | bytes 1572868
  72.4 49.7 %collective-permute-start.5 = (bf16[1,4,2,2,4,2,16,128]{7,6,5,4,3,2,1,0:T(8,128)(2,1)S(1)}, bf16[1,4,2,2,4,2,16,128]{7,6,5,4,3,2,1,0:T(8,128)(2,1)}, u32[]{:S(2)}, u32[]{:S(2)}) collective-permute-start(bf16[1,4,2,2,4,2,16,128]{7,6,5,4,3,2,1,0:T(8,128)(2,1)S(1)} %get-tuple-element.6), channel_id=1, source_target_pairs={{0,96},{16,112},{32,0},{48,16},{64,32},{80,48},{96,64},{112,80},{1... | collective-permute-start | bytes 1572872 | tf_op jit(solution)/shard_map/ppermute | solution.py:258
  86.5 0.8 copy-start.4
  86.5 35.6 %collective-permute-start.6 = (bf16[1,4,2,2,4,2,16,128]{7,6,5,4,3,2,1,0:T(8,128)(2,1)S(1)}, bf16[1,4,2,2,4,2,16,128]{7,6,5,4,3,2,1,0:T(8,128)(2,1)}, u32[]{:S(2)}, u32[]{:S(2)}) collective-permute-start(bf16[1,4,2,2,4,2,16,128]{7,6,5,4,3,2,1,0:T(8,128)(2,1)S(1)} %get-tuple-element.5), channel_id=1, source_target_pairs={{0,112},{16,0},{32,16},{48,32},{64,48},{80,64},{96,80},{112,96},{1... | collective-permute-start | bytes 1572872 | tf_op jit(solution)/shard_map/ppermute | solution.py:258
  104.3 23.8 %all-to-all-start.1 = ((bf16[16,16,16,128]{3,2,1,0:T(8,128)(2,1)}), bf16[16,16,16,128]{3,2,1,0:T(8,128)(2,1)S(1)}, u32[]{:S(2)}, u32[]{:S(2)}) async-start(bf16[16,16,16,128]{3,2,1,0:T(8,128)(2,1)} %shard_map.75), calls=%async_computation.1 | async-start | bytes 2097152 | tf_op jit(solution)/shard_map/all_to_all | solution.py:261
  128.1 1.0 copy-start
  146.4 20.0 %all-to-all-start.2 = ((bf16[16,16,16,128]{3,2,1,0:T(8,128)(2,1)}), bf16[16,16,16,128]{3,2,1,0:T(8,128)(2,1)S(1)}, u32[]{:S(2)}, u32[]{:S(2)}) async-start(bf16[16,16,16,128]{3,2,1,0:T(8,128)(2,1)} %shard_map.76), calls=%async_computation.2 | async-start | bytes 2097152 | tf_op jit(solution)/shard_map/all_to_all | solution.py:263

commit v16 on v14

--- a/solution.py
+++ b/solution.py
@@ -42,7 +42,7 @@
     band = band.reshape(2 * FRAMES * U, 2 * span).astype(np.float32)
     high = band.astype(jnp.bfloat16)
     low = (band - high.astype(np.float32)).astype(jnp.bfloat16)
-    return np.concatenate([high, low], axis=0)
+    return np.concatenate([high, low], axis=1)
 
 
 def _filter_kernel(chunk, shifted, *refs):
@@ -80,10 +80,8 @@
                 parts.append(jnp.concatenate([prefix_of(r), rows_of(r, 0, span - 48)], axis=0))
             else:
                 parts.append(rows_of(r, ib * half - 48, span))
-        rhs = jnp.concatenate(parts, axis=0)
-        both = jnp.dot(band_ref[...], rhs, preferred_element_type=jnp.float32)
-        rows = both.shape[0] // 2
-        spec = both[:rows] + both[rows:]
+        rhs = jnp.concatenate(parts + parts, axis=0)
+        spec = jnp.dot(band_ref[...], rhs, preferred_element_type=jnp.float32)
         s_re = spec[:half]
         s_im = spec[half:]
         c_re = (g_re * s_re - g_im * s_im).astype(jnp.bfloat16)

time: 154 us -> 154 us (level)
  no operation moved by 1% of the time
where the time goes in v16:
time: 154 us; the launch traced here: 152 us
  Pallas kernels  52.2 us (34%)
  waiting for transfers between devices  45.2 us (29%)
  starting transfers between devices  30.7 us (20%)
  local copies, waits for them, and re-layouts  17.5 us (11%)
  other arithmetic  6.21 us (4%)
    all_to_all x1, waiting for transfers between devices, on_device(): lax.all_to_all(first, 'feed', split_axis=0, concat_axis=0, tiled=True)  25.1 us
    pallas_call x2, Pallas kernels, filterbank(): pl.pallas_call(lambda *refs: _filter_kernel(chunk, shifted, *refs), grid_...  18 us
    pallas_call x1, Pallas kernels, beamform_pieces(): pl.pallas_call(lambda *refs: _beam_pieces_kernel(len(pieces), *refs), gri...  17.3 us
    pallas_call x1, Pallas kernels, beamform(): pl.pallas_call(_beam_kernel, grid=(nb,), in_specs=[pl.BlockSpec((nsrc, 1,...  16.9 us
    all_to_all x2, starting transfers between devices, on_device(): lax.all_to_all(picked, 'chan', split_axis=0, concat_axis=0, tiled=True)  15.2 us
    all_to_all x2, waiting for transfers between devices, on_device(): lax.all_to_all(picked, 'chan', split_axis=0, concat_axis=0, tiled=True)  12.5 us
    ppermute x7, starting transfers between devices, on_device(): pieces.append(lax.ppermute(second[shift:shift + 1], 'feed', perm=pairs))  9.55 us
    gather x2, local copies, waits for them, and re-layouts, on_device(): jnp.take(weights.reshape(2, 1, nfeed, feeds_local, beams), order, axis=2)  7.64 us
  transfers between devices with their start and end apart: 10, of which 4 were waited for; matrix products, arithmetic and copies ran while one was open for 14% of the time, Pallas kernels for 17%

profile of v16, /device:TPU:1, one launch (start us, length us, event | category | flops | bytes accessed | tf_op | source)
XLA Modules:
  0.0 151.9 jit_solution(11090538105515464926)
XLA Ops:
  0.0 9.0 %shard_map.73 = bf16[8,4,2,2,4,2,16,128]{7,6,5,4,3,2,1,0:T(8,128)(2,1)} custom-call(bf16[2,2,8,2,512,128]{5,4,3,2,1,0:T(8,128)(2,1)} %bitcast.20, bf16[2,2,8,64,16,128]{5,4,3,2,1,0:T(8,128)(2,1)} %bitcast.21, bf16[2,2,8,64,16,128]{5,4,3,2,1,0:T(8,128)(2,1)} %bitcast.22, bf16[2,2,8,64,16,128]{5,4,3,2,1,0:T(8,128)(2,1)} %bitcast.23, ...), custom_call_target="tpu_custom_call" | custom-call | flops 2952790016 | bytes 8388608 | tf_op jit(solution)/shard_map/pallas_call | solution.py:136
  9.0 6.0 %all-to-all-start = ((bf16[8,4,2,2,4,2,16,128]{7,6,5,4,3,2,1,0:T(8,128)(2,1)}), bf16[8,4,2,2,4,2,16,128]{7,6,5,4,3,2,1,0:T(8,128)(2,1)}, u32[]{:S(2)}, u32[]{:S(2)}) async-start(bf16[8,4,2,2,4,2,16,128]{7,6,5,4,3,2,1,0:T(8,128)(2,1)} %shard_map.73), calls=%async_computation | async-start | bytes 8388608 | tf_op jit(solution)/shard_map/all_to_all | solution.py:250
  15.0 9.0 %shard_map.75 = bf16[8,4,2,2,4,2,16,128]{7,6,5,4,3,2,1,0:T(8,128)(2,1)} custom-call(s32[1]{0:T(128)} %bitcast.6.refs_0_, bf16[2,2,8,2,512,128]{5,4,3,2,1,0:T(8,128)(2,1)} %bitcast.24, bf16[2,2,8,64,16,128]{5,4,3,2,1,0:T(8,128)(2,1)} %bitcast.25, bf16[2,2,8,64,16,128]{5,4,3,2,1,0:T(8,128)(2,1)} %bitcast.26, bf16[2,2,8,64,16,128]{5,4,3,2,1,0:T(8,128)(2,1)} %bitcast.27, ...), custom_call_target="tpu_custom_call" | custom-call | flops 2952790016 | bytes 8388608 | tf_op jit(solution)/shard_map/pallas_call | solution.py:136
  24.0 0.0 copy-start.2
  24.0 0.0 copy-start.1
  24.0 4.4 %fusion.6 = (bf16[1,4,2,2,4,2,16,128]{7,6,5,4,3,2,1,0:T(8,128)(2,1)S(1)}, bf16[1,4,2,2,4,2,16,128]{7,6,5,4,3,2,1,0:T(8,128)(2,1)S(1)}, bf16[1,4,2,2,4,2,16,128]{...) fusion(bf16[8,4,2,2,4,2,16,128]{7,6,5,4,3,2,1,0:T(8,128)(2,1)} , ...), kind=kLoop, calls=%fused_computation.20 | loop fusion | bytes 8388608 | tf_op jit(solution)/shard_map/slice | solution.py:255
  28.3 1.6 %collective-permute-start = (bf16[1,4,2,2,4,2,16,128]{7,6,5,4,3,2,1,0:T(8,128)(2,1)}, bf16[1,4,2,2,4,2,16,128]{7,6,5,4,3,2,1,0:T(8,128)(2,1)}, u32[]{:S(2)}, u32[]{:S(2)}) collective-permute-start(bf16[1,4,2,2,4,2,16,128]{7,6,5,4,3,2,1,0:T(8,128)(2,1)} %get-tuple-element.11), channel_id=1, source_target_pairs={{0,16},{16,32},{32,48},{48,64},{64,80},{80,96},{96,112},{112,0},{1... | collective-permute-start | bytes 1572872 | tf_op jit(solution)/shard_map/ppermute | solution.py:255
  30.0 1.2 collective-permute-start.1
  31.2 1.6 %collective-permute-start.2 = (bf16[1,4,2,2,4,2,16,128]{7,6,5,4,3,2,1,0:T(8,128)(2,1)}, bf16[1,4,2,2,4,2,16,128]{7,6,5,4,3,2,1,0:T(8,128)(2,1)}, u32[]{:S(2)}, u32[]{:S(2)}) collective-permute-start(bf16[1,4,2,2,4,2,16,128]{7,6,5,4,3,2,1,0:T(8,128)(2,1)} %get-tuple-element.9), channel_id=1, source_target_pairs={{0,48},{16,64},{32,80},{48,96},{64,112},{80,0},{96,16},{112,32},{1... | collective-permute-start | bytes 1572872 | tf_op jit(solution)/shard_map/ppermute | solution.py:255
  32.8 0.6 collective-permute-start.3
  33.4 1.6 %collective-permute-start.4 = (bf16[1,4,2,2,4,2,16,128]{7,6,5,4,3,2,1,0:T(8,128)(2,1)S(1)}, bf16[1,4,2,2,4,2,16,128]{7,6,5,4,3,2,1,0:T(8,128)(2,1)}, u32[]{:S(2)}, u32[]{:S(2)}) collective-permute-start(bf16[1,4,2,2,4,2,16,128]{7,6,5,4,3,2,1,0:T(8,128)(2,1)S(1)} %get-tuple-element.7), channel_id=1, source_target_pairs={{0,80},{16,96},{32,112},{48,0},{64,16},{80,32},{96,48},{112,64},{1... | collective-permute-start | bytes 1572872 | tf_op jit(solution)/shard_map/ppermute | solution.py:255
  35.0 0.0 copy-done.2
  35.0 0.1 fusion.2
  35.1 0.0 copy-done.1
  35.1 3.7 %fusion.1.sel_ref.refs_9_ = bf16[1024,2048]{1,0:T(8,128)(2,1)} fusion(s32[2048]{0:T(1024)S(1)} %bitcast.36, pred[2048]{0:T(1024)(128)(4,1)S(1)} %fusion.2), kind=kLoop, calls=%fused_computation.3 | loop fusion | flops 6291456 | bytes 4204544 | tf_op jit(solution)/shard_map/convert_element_type | solution.py:242
  38.8 25.1 %all-to-all-done.cal_ref = bf16[8,4,2,2,4,2,16,128]{7,6,5,4,3,2,1,0:T(8,128)(2,1)} async-done(((bf16[8,4,2,2,4,2,16,128]{7,6,5,4,3,2,1,0:T(8,128)(2,1)}), bf16[8,4,2,2,4,2,16,128]{7,6,5,4,3,2,1,0:T(8,128)(2,1)}, u32[]{:S(2)}, u32[]{:S(2)}) %all-to-all-start) | async-done | bytes 4194336 | tf_op jit(solution)/shard_map/all_to_all | solution.py:250
  63.9 16.9 %shard_map.74 = bf16[16,16,16,128]{3,2,1,0:T(8,128)(2,1)} custom-call(bf16[8,4,2,2,4,2,16,128]{7,6,5,4,3,2,1,0:T(8,128)(2,1)} %all-to-all-done.cal_ref, bf16[2,1,1024,1024]{3,2,1,0:T(8,128)(2,1)} %w_ref.1, bf16[1024,2048]{1,0:T(8,128)(2,1)} %fusion.1.sel_ref.refs_9_), custom_call_target="tpu_custom_call" | custom-call | flops 9663676416 | bytes 13631488 | tf_op jit(solution)/shard_map/pallas_call | solution.py:216
  80.8 7.6 %all-to-all-start.1 = ((bf16[16,16,16,128]{3,2,1,0:T(8,128)(2,1)}), bf16[16,16,16,128]{3,2,1,0:T(8,128)(2,1)S(1)}, u32[]{:S(2)}, u32[]{:S(2)}) async-start(bf16[16,16,16,128]{3,2,1,0:T(8,128)(2,1)} %shard_map.74), calls=%async_computation.1 | async-start | bytes 2097152 | tf_op jit(solution)/shard_map/all_to_all | solution.py:258
  88.5 0.1 broadcast_bitcast_fusion
  88.5 0.0 collective-permute-done.refs_1_
  88.6 0.9 collective-permute-start.5
  89.5 0.0 collective-permute-done.1.refs_2_
  89.5 2.0 %collective-permute-start.6 = (bf16[1,4,2,2,4,2,16,128]{7,6,5,4,3,2,1,0:T(8,128)(2,1)S(1)}, bf16[1,4,2,2,4,2,16,128]{7,6,5,4,3,2,1,0:T(8,128)(2,1)}, u32[]{:S(2)}, u32[]{:S(2)}) collective-permute-start(bf16[1,4,2,2,4,2,16,128]{7,6,5,4,3,2,1,0:T(8,128)(2,1)S(1)} %get-tuple-element.5), channel_id=1, source_target_pairs={{0,112},{16,0},{32,16},{48,32},{64,48},{80,64},{96,80},{112,96},{1... | collective-permute-start | bytes 1572872 | tf_op jit(solution)/shard_map/ppermute | solution.py:255
  91.4 5.0 %gather_fusion = bf16[8,2,128,1024]{3,2,1,0:T(8,128)(2,1)} fusion(bf16[2,8,128,1024]{3,2,1,0:T(8,128)(2,1)} %bitcast.30, s32[1024]{0:T(1024)S(1)} %pad_clamp_fusion), kind=kCustom, calls=%fused_computation | custom fusion | bytes 8388640 | tf_op jit(solution)/shard_map/jit(_take)/gather | solution.py:248
  96.4 2.7 %copy.9 = bf16[2,8,128,1024]{3,2,1,0:T(8,128)(2,1)S(1)} copy(bf16[2,8,128,1024]{3,2,0,1:T(8,128)(2,1)} %bitcast.29) | data formatting | bytes 8388608 | tf_op jit(solution)/shard_map/jit(_take)/gather | solution.py:248
  99.1 2.4 %bitcast_select_fusion.refs_8_ = bf16[2,1,1024,1024]{3,2,1,0:T(8,128)(2,1)} fusion(pred[1024]{0:T(1024)(128)(4,1)S(1)} %broadcast_bitcast_fusion, bf16[2,1,1024,1024]{3,2,1,0:T(8,128)(2,1)S(1)} %bitcast.28), kind=kLoop, calls=%fused_computation.4 | loop fusion | flops 2097152 | bytes 8389632 | tf_op jit(solution)/shard_map/jit(_take)/select_n | solution.py:248
  101.5 0.0 collective-permute-done.2.refs_3_
  101.5 7.1 %collective-permute-done.3.refs_4_ = bf16[1,4,2,2,4,2,16,128]{7,6,5,4,3,2,1,0:T(8,128)(2,1)} collective-permute-done((bf16[1,4,2,2,4,2,16,128]{7,6,5,4,3,2,1,0:T(8,128)(2,1)S(1)}, bf16[1,4,2,2,4,2,16,128]{7,6,5,4,3,2,1,0:T(8,128)(2,1)}, u32[]{:S(2)}, u32[]{:S(2)}) %collective-permute-start.3) | collective-permute-done | bytes 524320 | tf_op jit(solution)/shard_map/ppermute | solution.py:255
  108.6 0.5 collective-permute-done.4.refs_5_
  109.1 0.0 collective-permute-done.5.refs_6_
  109.1 0.0 collective-permute-done.6.refs_7_
  109.1 0.0 all-to-all-done.1
  109.1 0.0 copy-start
  109.1 1.0 copy-done
  110.0 17.3 %shard_map.76 = bf16[16,16,16,128]{3,2,1,0:T(8,128)(2,1)} custom-call(bf16[1,4,2,2,4,2,16,128]{7,6,5,4,3,2,1,0:T(8,128)(2,1)} %get-tuple-element.12.refs_0_, bf16[1,4,2,2,4,2,16,128]{7,6,5,4,3,2,1,0:T(8,128)(2,1)} %collective-permute-done.refs_1_, bf16[1,4,2,2,4,2,16,128]{7,6,5,4,3,2,1,0:T(8,128)(2,1)} %collective-permute-done.1.refs_2_, ...), custom_call_target="tpu_custom_call" | custom-call | flops 9663676416 | bytes 13631488 | tf_op jit(solution)/shard_map/pallas_call | solution.py:191
  127.3 7.6 %all-to-all-start.2 = ((bf16[16,16,16,128]{3,2,1,0:T(8,128)(2,1)}), bf16[16,16,16,128]{3,2,1,0:T(8,128)(2,1)S(1)}, u32[]{:S(2)}, u32[]{:S(2)}) async-start(bf16[16,16,16,128]{3,2,1,0:T(8,128)(2,1)} %shard_map.76), calls=%async_computation.2 | async-start | bytes 2097152 | tf_op jit(solution)/shard_map/all_to_all | solution.py:260
  134.9 1.5 copy.8
  136.4 1.6 %pad.4 = bf16[32,256,128]{2,1,0:T(8,128)(2,1)} pad(bf16[16,256,128]{2,1,0:T(8,128)(2,1)S(1)} %bitcast.34, bf16[]{:T(256)} %constant.24.clone.1), padding=0_16x0_0x0_0 | pad | bytes 3145730 | tf_op jit(solution)/shard_map/jit(_pad)/pad | solution.py:264
  138.1 12.5 %all-to-all-done.2 = bf16[16,16,16,128]{3,2,1,0:T(8,128)(2,1)S(1)} async-done(((bf16[16,16,16,128]{3,2,1,0:T(8,128)(2,1)}), bf16[16,16,16,128]{3,2,1,0:T(8,128)(2,1)S(1)}, u32[]{:S(2)}, u32[]{:S(2)}) %all-to-all-start.2) | async-done | bytes 1048608 | tf_op jit(solution)/shard_map/all_to_all | solution.py:260
  150.6 0.3 copy.10
  150.8 1.0 constant_dynamic-update-slice_fusion
  (3 shorter events, 0.0 us)
Async XLA Ops:
  9.0 54.9 %all-to-all-start = ((bf16[8,4,2,2,4,2,16,128]{7,6,5,4,3,2,1,0:T(8,128)(2,1)}), bf16[8,4,2,2,4,2,16,128]{7,6,5,4,3,2,1,0:T(8,128)(2,1)}, u32[]{:S(2)}, u32[]{:S(2)}) async-start(bf16[8,4,2,2,4,2,16,128]{7,6,5,4,3,2,1,0:T(8,128)(2,1)} %shard_map.73), calls=%async_computation | async-start | bytes 8388608 | tf_op jit(solution)/shard_map/all_to_all | solution.py:250
  24.0 11.1 %copy-start.2 = (s32[16]{0:T(128)S(1)}, s32[16]{0:T(128)}, u32[]{:S(2)}) copy-start(s32[16]{0:T(128)} %param.12) | copy-start | bytes 196
  24.0 11.1 %copy-start.1 = (s32[16,128]{1,0:T(8,128)S(1)}, s32[16,128]{1,0:T(8,128)}, u32[]{:S(2)}) copy-start(s32[16,128]{1,0:T(8,128)} %param.11) | copy-start | bytes 24580
  28.3 60.2 %collective-permute-start = (bf16[1,4,2,2,4,2,16,128]{7,6,5,4,3,2,1,0:T(8,128)(2,1)}, bf16[1,4,2,2,4,2,16,128]{7,6,5,4,3,2,1,0:T(8,128)(2,1)}, u32[]{:S(2)}, u32[]{:S(2)}) collective-permute-start(bf16[1,4,2,2,4,2,16,128]{7,6,5,4,3,2,1,0:T(8,128)(2,1)} %get-tuple-element.11), channel_id=1, source_target_pairs={{0,16},{16,32},{32,48},{48,64},{64,80},{80,96},{96,112},{112,0},{1... | collective-permute-start | bytes 1572872 | tf_op jit(solution)/shard_map/ppermute | solution.py:255
  30.0 59.5 %collective-permute-start.1 = (bf16[1,4,2,2,4,2,16,128]{7,6,5,4,3,2,1,0:T(8,128)(2,1)}, bf16[1,4,2,2,4,2,16,128]{7,6,5,4,3,2,1,0:T(8,128)(2,1)}, u32[]{:S(2)}, u32[]{:S(2)}) collective-permute-start(bf16[1,4,2,2,4,2,16,128]{7,6,5,4,3,2,1,0:T(8,128)(2,1)} %get-tuple-element.10), channel_id=1, source_target_pairs={{0,32},{16,48},{32,64},{48,80},{64,96},{80,112},{96,0},{112,16},{1... | collective-permute-start | bytes 1572872 | tf_op jit(solution)/shard_map/ppermute | solution.py:255
  31.2 70.3 %collective-permute-start.2 = (bf16[1,4,2,2,4,2,16,128]{7,6,5,4,3,2,1,0:T(8,128)(2,1)}, bf16[1,4,2,2,4,2,16,128]{7,6,5,4,3,2,1,0:T(8,128)(2,1)}, u32[]{:S(2)}, u32[]{:S(2)}) collective-permute-start(bf16[1,4,2,2,4,2,16,128]{7,6,5,4,3,2,1,0:T(8,128)(2,1)} %get-tuple-element.9), channel_id=1, source_target_pairs={{0,48},{16,64},{32,80},{48,96},{64,112},{80,0},{96,16},{112,32},{1... | collective-permute-start | bytes 1572872 | tf_op jit(solution)/shard_map/ppermute | solution.py:255
  32.8 75.8 %collective-permute-start.3 = (bf16[1,4,2,2,4,2,16,128]{7,6,5,4,3,2,1,0:T(8,128)(2,1)S(1)}, bf16[1,4,2,2,4,2,16,128]{7,6,5,4,3,2,1,0:T(8,128)(2,1)}, u32[]{:S(2)}, u32[]{:S(2)}) collective-permute-start(bf16[1,4,2,2,4,2,16,128]{7,6,5,4,3,2,1,0:T(8,128)(2,1)S(1)} %get-tuple-element.8), channel_id=1, source_target_pairs={{0,64},{16,80},{32,96},{48,112},{64,0},{80,16},{96,32},{112,48},{1... | collective-permute-start | bytes 1572872 | tf_op jit(solution)/shard_map/ppermute | solution.py:255
  33.4 75.7 %collective-permute-start.4 = (bf16[1,4,2,2,4,2,16,128]{7,6,5,4,3,2,1,0:T(8,128)(2,1)S(1)}, bf16[1,4,2,2,4,2,16,128]{7,6,5,4,3,2,1,0:T(8,128)(2,1)}, u32[]{:S(2)}, u32[]{:S(2)}) collective-permute-start(bf16[1,4,2,2,4,2,16,128]{7,6,5,4,3,2,1,0:T(8,128)(2,1)S(1)} %get-tuple-element.7), channel_id=1, source_target_pairs={{0,80},{16,96},{32,112},{48,0},{64,16},{80,32},{96,48},{112,64},{1... | collective-permute-start | bytes 1572872 | tf_op jit(solution)/shard_map/ppermute | solution.py:255
  80.8 28.2 %all-to-all-start.1 = ((bf16[16,16,16,128]{3,2,1,0:T(8,128)(2,1)}), bf16[16,16,16,128]{3,2,1,0:T(8,128)(2,1)S(1)}, u32[]{:S(2)}, u32[]{:S(2)}) async-start(bf16[16,16,16,128]{3,2,1,0:T(8,128)(2,1)} %shard_map.74), calls=%async_computation.1 | async-start | bytes 2097152 | tf_op jit(solution)/shard_map/all_to_all | solution.py:258
  88.6 20.5 %collective-permute-start.5 = (bf16[1,4,2,2,4,2,16,128]{7,6,5,4,3,2,1,0:T(8,128)(2,1)S(1)}, bf16[1,4,2,2,4,2,16,128]{7,6,5,4,3,2,1,0:T(8,128)(2,1)}, u32[]{:S(2)}, u32[]{:S(2)}) collective-permute-start(bf16[1,4,2,2,4,2,16,128]{7,6,5,4,3,2,1,0:T(8,128)(2,1)S(1)} %get-tuple-element.6), channel_id=1, source_target_pairs={{0,96},{16,112},{32,0},{48,16},{64,32},{80,48},{96,64},{112,80},{1... | collective-permute-start | bytes 1572872 | tf_op jit(solution)/shard_map/ppermute | solution.py:255
  89.5 19.6 %collective-permute-start.6 = (bf16[1,4,2,2,4,2,16,128]{7,6,5,4,3,2,1,0:T(8,128)(2,1)S(1)}, bf16[1,4,2,2,4,2,16,128]{7,6,5,4,3,2,1,0:T(8,128)(2,1)}, u32[]{:S(2)}, u32[]{:S(2)}) collective-permute-start(bf16[1,4,2,2,4,2,16,128]{7,6,5,4,3,2,1,0:T(8,128)(2,1)S(1)} %get-tuple-element.5), channel_id=1, source_target_pairs={{0,112},{16,0},{32,16},{48,32},{64,48},{80,64},{96,80},{112,96},{1... | collective-permute-start | bytes 1572872 | tf_op jit(solution)/shard_map/ppermute | solution.py:255
  109.1 1.0 copy-start
  127.3 23.2 %all-to-all-start.2 = ((bf16[16,16,16,128]{3,2,1,0:T(8,128)(2,1)}), bf16[16,16,16,128]{3,2,1,0:T(8,128)(2,1)S(1)}, u32[]{:S(2)}, u32[]{:S(2)}) async-start(bf16[16,16,16,128]{3,2,1,0:T(8,128)(2,1)} %shard_map.76), calls=%async_computation.2 | async-start | bytes 2097152 | tf_op jit(solution)/shard_map/all_to_all | solution.py:260

commit v17 on v16

--- a/solution.py
+++ b/solution.py
@@ -204,7 +204,7 @@
             bytes_accessed=sum(p.size for p in pieces) * 2 + weights.size * 2 + select.size * 2 + nb * IB * U * slots * 2,
             transcendentals=0,
         ),
-        compiler_params=pltpu.CompilerParams(vmem_limit_bytes=60 * 1024 * 1024),
+        compiler_params=pltpu.CompilerParams(vmem_limit_bytes=36 * 1024 * 1024),
     )(*pieces, weights, select, after)
 
 
@@ -228,7 +228,7 @@
             bytes_accessed=cal.size * 2 + weights.size * 2 + select.size * 2 + nb * IB * U * slots * 2,
             transcendentals=0,
         ),
-        compiler_params=pltpu.CompilerParams(vmem_limit_bytes=60 * 1024 * 1024),
+        compiler_params=pltpu.CompilerParams(vmem_limit_bytes=36 * 1024 * 1024),
     )(cal, weights, select)
 
 

time: 154 us -> 158 us (1.026)
  local copies, waits for them, and re-layouts: 17.5 us -> 24.2 us
  Pallas kernels: 52.2 us -> 46.7 us
  waiting for transfers between devices: 45.2 us -> 49.7 us
    unnamed x6 -> x12, local copies, waits for them, and re-layouts: 0.97 us -> 8.76 us
    all_to_all x2, waiting for transfers between devices: 12.5 us -> 18.1 us  [on_device(): lax.all_to_all(picked, 'chan', split_axis=0, concat_axis=0, tiled=True)]
    pallas_call x1, Pallas kernels: 17.3 us -> 14.3 us  [beamform_pieces(): pl.pallas_call(lambda *refs: _beam_pieces_kernel(len(pieces), *refs), gri...]
    pallas_call x1, Pallas kernels: 16.9 us -> 14.4 us  [beamform(): pl.pallas_call(_beam_kernel, grid=(nb,), in_specs=[pl.BlockSpec((nsrc, 1,...]
  transfers between devices with their start and end apart: 10 -> 10, of which waited for: 4 -> 5; matrix products, arithmetic and copies ran while one was open for 14% -> 13% of each run, Pallas kernels for 17% -> 15%
where the time goes in v17:
time: 158 us; the launch traced here: 157 us
  waiting for transfers between devices  49.7 us (31%)
  Pallas kernels  46.7 us (30%)
  starting transfers between devices  29.8 us (19%)
  local copies, waits for them, and re-layouts  24.2 us (15%)
  other arithmetic  6.2 us (4%)
    all_to_all x1, waiting for transfers between devices, on_device(): lax.all_to_all(first, 'feed', split_axis=0, concat_axis=0, tiled=True)  25 us
    all_to_all x2, waiting for transfers between devices, on_device(): lax.all_to_all(picked, 'chan', split_axis=0, concat_axis=0, tiled=True)  18.1 us
    pallas_call x2, Pallas kernels, filterbank(): pl.pallas_call(lambda *refs: _filter_kernel(chunk, shifted, *refs), grid_...  18 us
    pallas_call x1, Pallas kernels, beamform(): pl.pallas_call(_beam_kernel, grid=(nb,), in_specs=[pl.BlockSpec((nsrc, 1,...  14.4 us
    pallas_call x1, Pallas kernels, beamform_pieces(): pl.pallas_call(lambda *refs: _beam_pieces_kernel(len(pieces), *refs), gri...  14.3 us
    all_to_all x2, starting transfers between devices, on_device(): lax.all_to_all(picked, 'chan', split_axis=0, concat_axis=0, tiled=True)  14.2 us
    ppermute x7, starting transfers between devices, on_device(): pieces.append(lax.ppermute(second[shift:shift + 1], 'feed', perm=pairs))  9.55 us
    unnamed x12, local copies, waits for them, and re-layouts  8.76 us
  transfers between devices with their start and end apart: 10, of which 5 were waited for; matrix products, arithmetic and copies ran while one was open for 13% of the time, Pallas kernels for 15%

profile of v17, /device:TPU:1, one launch (start us, length us, event | category | flops | bytes accessed | tf_op | source)
XLA Modules:
  0.0 156.7 jit_solution(6339410891806201386)
XLA Ops:
  0.0 9.0 %shard_map.73 = bf16[8,4,2,2,4,2,16,128]{7,6,5,4,3,2,1,0:T(8,128)(2,1)} custom-call(bf16[2,2,8,2,512,128]{5,4,3,2,1,0:T(8,128)(2,1)} %bitcast.23, bf16[2,2,8,64,16,128]{5,4,3,2,1,0:T(8,128)(2,1)} %bitcast.24, bf16[2,2,8,64,16,128]{5,4,3,2,1,0:T(8,128)(2,1)} %bitcast.25, bf16[2,2,8,64,16,128]{5,4,3,2,1,0:T(8,128)(2,1)} %bitcast.26, ...), custom_call_target="tpu_custom_call" | custom-call | flops 2952790016 | bytes 8388608 | tf_op jit(solution)/shard_map/pallas_call | solution.py:136
  9.0 6.0 %all-to-all-start = ((bf16[8,4,2,2,4,2,16,128]{7,6,5,4,3,2,1,0:T(8,128)(2,1)}), bf16[8,4,2,2,4,2,16,128]{7,6,5,4,3,2,1,0:T(8,128)(2,1)}, u32[]{:S(2)}, u32[]{:S(2)}) async-start(bf16[8,4,2,2,4,2,16,128]{7,6,5,4,3,2,1,0:T(8,128)(2,1)} %shard_map.73), calls=%async_computation | async-start | bytes 8388608 | tf_op jit(solution)/shard_map/all_to_all | solution.py:250
  15.0 9.0 %shard_map.75 = bf16[8,4,2,2,4,2,16,128]{7,6,5,4,3,2,1,0:T(8,128)(2,1)} custom-call(s32[1]{0:T(128)} %bitcast.6.refs_0_, bf16[2,2,8,2,512,128]{5,4,3,2,1,0:T(8,128)(2,1)} %bitcast.27, bf16[2,2,8,64,16,128]{5,4,3,2,1,0:T(8,128)(2,1)} %bitcast.28, bf16[2,2,8,64,16,128]{5,4,3,2,1,0:T(8,128)(2,1)} %bitcast.29, bf16[2,2,8,64,16,128]{5,4,3,2,1,0:T(8,128)(2,1)} %bitcast.30, ...), custom_call_target="tpu_custom_call" | custom-call | flops 2952790016 | bytes 8388608 | tf_op jit(solution)/shard_map/pallas_call | solution.py:136
  24.0 0.0 copy-start.5
  24.0 0.0 copy-start.4
  24.0 4.5 %fusion.6 = (bf16[1,4,2,2,4,2,16,128]{7,6,5,4,3,2,1,0:T(8,128)(2,1)}, bf16[1,4,2,2,4,2,16,128]{7,6,5,4,3,2,1,0:T(8,128)(2,1)}, bf16[1,4,2,2,4,2,16,128]{7,6,5,4,...) fusion(bf16[8,4,2,2,4,2,16,128]{7,6,5,4,3,2,1,0:T(8,128)(2,1)} , ...), kind=kLoop, calls=%fused_computation.20 | loop fusion | bytes 8388608 | tf_op jit(solution)/shard_map/slice | solution.py:255
  28.5 1.6 %collective-permute-start = (bf16[1,4,2,2,4,2,16,128]{7,6,5,4,3,2,1,0:T(8,128)(2,1)}, bf16[1,4,2,2,4,2,16,128]{7,6,5,4,3,2,1,0:T(8,128)(2,1)S(1)}, u32[]{:S(2)}, u32[]{:S(2)}) collective-permute-start(bf16[1,4,2,2,4,2,16,128]{7,6,5,4,3,2,1,0:T(8,128)(2,1)} %get-tuple-element.11), channel_id=1, source_target_pairs={{0,16},{16,32},{32,48},{48,64},{64,80},{80,96},{96,112},{112,0},{1... | collective-permute-start | bytes 1572872 | tf_op jit(solution)/shard_map/ppermute | solution.py:255
  30.2 1.2 collective-permute-start.1
  31.4 1.6 %collective-permute-start.2 = (bf16[1,4,2,2,4,2,16,128]{7,6,5,4,3,2,1,0:T(8,128)(2,1)}, bf16[1,4,2,2,4,2,16,128]{7,6,5,4,3,2,1,0:T(8,128)(2,1)S(1)}, u32[]{:S(2)}, u32[]{:S(2)}) collective-permute-start(bf16[1,4,2,2,4,2,16,128]{7,6,5,4,3,2,1,0:T(8,128)(2,1)} %get-tuple-element.9), channel_id=1, source_target_pairs={{0,48},{16,64},{32,80},{48,96},{64,112},{80,0},{96,16},{112,32},{1... | collective-permute-start | bytes 1572872 | tf_op jit(solution)/shard_map/ppermute | solution.py:255
  33.0 0.6 collective-permute-start.3
  33.6 1.7 %collective-permute-start.4 = (bf16[1,4,2,2,4,2,16,128]{7,6,5,4,3,2,1,0:T(8,128)(2,1)}, bf16[1,4,2,2,4,2,16,128]{7,6,5,4,3,2,1,0:T(8,128)(2,1)}, u32[]{:S(2)}, u32[]{:S(2)}) collective-permute-start(bf16[1,4,2,2,4,2,16,128]{7,6,5,4,3,2,1,0:T(8,128)(2,1)} %get-tuple-element.7), channel_id=1, source_target_pairs={{0,80},{16,96},{32,112},{48,0},{64,16},{80,32},{96,48},{112,64},{1... | collective-permute-start | bytes 1572872 | tf_op jit(solution)/shard_map/ppermute | solution.py:255
  35.2 0.0 copy-done.5
  35.2 0.1 fusion.2
  35.3 0.0 copy-done.4
  35.3 3.7 %fusion.1.sel_ref.refs_9_ = bf16[1024,2048]{1,0:T(8,128)(2,1)} fusion(s32[2048]{0:T(1024)S(1)} %bitcast.36, pred[2048]{0:T(1024)(128)(4,1)S(1)} %fusion.2), kind=kLoop, calls=%fused_computation.3 | loop fusion | flops 6291456 | bytes 4204544 | tf_op jit(solution)/shard_map/convert_element_type | solution.py:242
  39.0 25.0 %all-to-all-done.cal_ref = bf16[8,4,2,2,4,2,16,128]{7,6,5,4,3,2,1,0:T(8,128)(2,1)} async-done(((bf16[8,4,2,2,4,2,16,128]{7,6,5,4,3,2,1,0:T(8,128)(2,1)}), bf16[8,4,2,2,4,2,16,128]{7,6,5,4,3,2,1,0:T(8,128)(2,1)}, u32[]{:S(2)}, u32[]{:S(2)}) %all-to-all-start) | async-done | bytes 4194336 | tf_op jit(solution)/shard_map/all_to_all | solution.py:250
  63.9 0.0 copy-start
  63.9 2.2 %copy-done = bf16[2,1,1024,1024]{3,2,1,0:T(8,128)(2,1)S(1)} copy-done((bf16[2,1,1024,1024]{3,2,1,0:T(8,128)(2,1)S(1)}, bf16[2,1,1024,1024]{3,2,1,0:T(8,128)(2,1)}, u32[]{:S(2)}) %copy-start) | copy-done | bytes 4194328
  66.1 0.0 copy-start.1
  66.1 2.2 %copy-done.1 = bf16[1024,2048]{1,0:T(8,128)(2,1)S(1)} copy-done((bf16[1024,2048]{1,0:T(8,128)(2,1)S(1)}, bf16[1024,2048]{1,0:T(8,128)(2,1)}, u32[]{:S(2)}) %copy-start.1) | copy-done | bytes 4194328
  68.3 14.4 %shard_map.74 = bf16[16,16,16,128]{3,2,1,0:T(8,128)(2,1)} custom-call(bf16[8,4,2,2,4,2,16,128]{7,6,5,4,3,2,1,0:T(8,128)(2,1)} %all-to-all-done.cal_ref, bf16[2,1,1024,1024]{3,2,1,0:T(8,128)(2,1)S(1)} %copy-done, bf16[1024,2048]{1,0:T(8,128)(2,1)S(1)} %copy-done.1), custom_call_target="tpu_custom_call" | custom-call | flops 9663676416 | bytes 13631488 | tf_op jit(solution)/shard_map/pallas_call | solution.py:216
  82.7 7.6 %all-to-all-start.1 = ((bf16[16,16,16,128]{3,2,1,0:T(8,128)(2,1)}), bf16[16,16,16,128]{3,2,1,0:T(8,128)(2,1)S(1)}, u32[]{:S(2)}, u32[]{:S(2)}) async-start(bf16[16,16,16,128]{3,2,1,0:T(8,128)(2,1)} %shard_map.74), calls=%async_computation.1 | async-start | bytes 2097152 | tf_op jit(solution)/shard_map/all_to_all | solution.py:258
  90.3 0.1 broadcast_bitcast_fusion
  90.4 0.0 collective-permute-done.refs_1_
  90.4 0.9 collective-permute-start.5
  91.3 0.0 collective-permute-done.1.refs_2_
  91.3 2.0 %collective-permute-start.6 = (bf16[1,4,2,2,4,2,16,128]{7,6,5,4,3,2,1,0:T(8,128)(2,1)}, bf16[1,4,2,2,4,2,16,128]{7,6,5,4,3,2,1,0:T(8,128)(2,1)}, u32[]{:S(2)}, u32[]{:S(2)}) collective-permute-start(bf16[1,4,2,2,4,2,16,128]{7,6,5,4,3,2,1,0:T(8,128)(2,1)} %get-tuple-element.5), channel_id=1, source_target_pairs={{0,112},{16,0},{32,16},{48,32},{64,48},{80,64},{96,80},{112,96},{1... | collective-permute-start | bytes 1572872 | tf_op jit(solution)/shard_map/ppermute | solution.py:255
  93.3 5.0 %gather_fusion = bf16[8,2,128,1024]{3,2,1,0:T(8,128)(2,1)} fusion(bf16[2,8,128,1024]{3,2,1,0:T(8,128)(2,1)} %bitcast.20, s32[1024]{0:T(1024)S(1)} %pad_clamp_fusion), kind=kCustom, calls=%fused_computation | custom fusion | bytes 8388640 | tf_op jit(solution)/shard_map/jit(_take)/gather | solution.py:248
  98.3 2.7 %copy.9 = bf16[2,8,128,1024]{3,2,1,0:T(8,128)(2,1)S(1)} copy(bf16[2,8,128,1024]{3,2,0,1:T(8,128)(2,1)} %bitcast.32) | data formatting | bytes 8388608 | tf_op jit(solution)/shard_map/jit(_take)/gather | solution.py:248
  100.9 2.4 %bitcast_select_fusion.refs_8_ = bf16[2,1,1024,1024]{3,2,1,0:T(8,128)(2,1)} fusion(pred[1024]{0:T(1024)(128)(4,1)S(1)} %broadcast_bitcast_fusion, bf16[2,1,1024,1024]{3,2,1,0:T(8,128)(2,1)S(1)} %bitcast.31), kind=kLoop, calls=%fused_computation.4 | loop fusion | flops 2097152 | bytes 8389632 | tf_op jit(solution)/shard_map/jit(_take)/select_n | solution.py:248
  103.4 0.0 collective-permute-done.2.refs_3_
  103.4 5.2 %collective-permute-done.3.refs_4_ = bf16[1,4,2,2,4,2,16,128]{7,6,5,4,3,2,1,0:T(8,128)(2,1)} collective-permute-done((bf16[1,4,2,2,4,2,16,128]{7,6,5,4,3,2,1,0:T(8,128)(2,1)}, bf16[1,4,2,2,4,2,16,128]{7,6,5,4,3,2,1,0:T(8,128)(2,1)}, u32[]{:S(2)}, u32[]{:S(2)}) %collective-permute-start.3) | collective-permute-done | bytes 524320 | tf_op jit(solution)/shard_map/ppermute | solution.py:255
  108.6 0.5 collective-permute-done.4.refs_5_
  109.1 0.0 collective-permute-done.5.refs_6_
  109.1 1.0 collective-permute-done.6.refs_7_
  110.0 0.0 all-to-all-done.1
  110.0 0.0 copy-start.2
  110.0 2.2 %copy-done.2 = bf16[1024,2048]{1,0:T(8,128)(2,1)S(1)} copy-done((bf16[1024,2048]{1,0:T(8,128)(2,1)S(1)}, bf16[1024,2048]{1,0:T(8,128)(2,1)}, u32[]{:S(2)}) %copy-start.2) | copy-done | bytes 4194328
  112.2 0.0 copy-start.3
  112.2 2.2 %copy-done.3 = bf16[2,1,1024,1024]{3,2,1,0:T(8,128)(2,1)S(1)} copy-done((bf16[2,1,1024,1024]{3,2,1,0:T(8,128)(2,1)S(1)}, bf16[2,1,1024,1024]{3,2,1,0:T(8,128)(2,1)}, u32[]{:S(2)}) %copy-start.3) | copy-done | bytes 4194328
  114.4 14.3 %shard_map.76 = bf16[16,16,16,128]{3,2,1,0:T(8,128)(2,1)} custom-call(bf16[1,4,2,2,4,2,16,128]{7,6,5,4,3,2,1,0:T(8,128)(2,1)S(1)} %get-tuple-element.12.refs_0_, bf16[1,4,2,2,4,2,16,128]{7,6,5,4,3,2,1,0:T(8,128)(2,1)S(1)} %collective-permute-done.refs_1_, bf16[1,4,2,2,4,2,16,128]{7,6,5,4,3,2,1,0:T(8,128)(2,1)S(1)} %collective-permute-done.1.refs_2_, ...), custom_call_target="tpu_custom_call" | custom-call | flops 9663676416 | bytes 13631488 | tf_op jit(solution)/shard_map/pallas_call | solution.py:191
  128.7 6.7 %all-to-all-start.2 = ((bf16[16,16,16,128]{3,2,1,0:T(8,128)(2,1)}), bf16[16,16,16,128]{3,2,1,0:T(8,128)(2,1)S(1)}, u32[]{:S(2)}, u32[]{:S(2)}) async-start(bf16[16,16,16,128]{3,2,1,0:T(8,128)(2,1)} %shard_map.76), calls=%async_computation.2 | async-start | bytes 2097152 | tf_op jit(solution)/shard_map/all_to_all | solution.py:260
  135.4 0.3 copy.8
  135.7 1.6 %pad.4 = bf16[32,256,128]{2,1,0:T(8,128)(2,1)} pad(bf16[16,256,128]{2,1,0:T(8,128)(2,1)S(1)} %bitcast.34, bf16[]{:T(256)} %constant.24.clone.1), padding=0_16x0_0x0_0 | pad | bytes 3145730 | tf_op jit(solution)/shard_map/jit(_pad)/pad | solution.py:264
  137.3 18.1 %all-to-all-done.2 = bf16[16,16,16,128]{3,2,1,0:T(8,128)(2,1)S(1)} async-done(((bf16[16,16,16,128]{3,2,1,0:T(8,128)(2,1)}), bf16[16,16,16,128]{3,2,1,0:T(8,128)(2,1)S(1)}, u32[]{:S(2)}, u32[]{:S(2)}) %all-to-all-start.2) | async-done | bytes 1048608 | tf_op jit(solution)/shard_map/all_to_all | solution.py:260
  155.4 0.3 copy.10
  155.7 1.0 constant_dynamic-update-slice_fusion
  (3 shorter events, 0.0 us)
Async XLA Ops:
  9.0 54.9 %all-to-all-start = ((bf16[8,4,2,2,4,2,16,128]{7,6,5,4,3,2,1,0:T(8,128)(2,1)}), bf16[8,4,2,2,4,2,16,128]{7,6,5,4,3,2,1,0:T(8,128)(2,1)}, u32[]{:S(2)}, u32[]{:S(2)}) async-start(bf16[8,4,2,2,4,2,16,128]{7,6,5,4,3,2,1,0:T(8,128)(2,1)} %shard_map.73), calls=%async_computation | async-start | bytes 8388608 | tf_op jit(solution)/shard_map/all_to_all | solution.py:250
  24.0 11.2 %copy-start.5 = (s32[16]{0:T(128)S(1)}, s32[16]{0:T(128)}, u32[]{:S(2)}) copy-start(s32[16]{0:T(128)} %param.12) | copy-start | bytes 196
  24.0 11.3 %copy-start.4 = (s32[16,128]{1,0:T(8,128)S(1)}, s32[16,128]{1,0:T(8,128)}, u32[]{:S(2)}) copy-start(s32[16,128]{1,0:T(8,128)} %param.11) | copy-start | bytes 24580
  28.5 61.9 %collective-permute-start = (bf16[1,4,2,2,4,2,16,128]{7,6,5,4,3,2,1,0:T(8,128)(2,1)}, bf16[1,4,2,2,4,2,16,128]{7,6,5,4,3,2,1,0:T(8,128)(2,1)S(1)}, u32[]{:S(2)}, u32[]{:S(2)}) collective-permute-start(bf16[1,4,2,2,4,2,16,128]{7,6,5,4,3,2,1,0:T(8,128)(2,1)} %get-tuple-element.11), channel_id=1, source_target_pairs={{0,16},{16,32},{32,48},{48,64},{64,80},{80,96},{96,112},{112,0},{1... | collective-permute-start | bytes 1572872 | tf_op jit(solution)/shard_map/ppermute | solution.py:255
  30.2 61.2 %collective-permute-start.1 = (bf16[1,4,2,2,4,2,16,128]{7,6,5,4,3,2,1,0:T(8,128)(2,1)}, bf16[1,4,2,2,4,2,16,128]{7,6,5,4,3,2,1,0:T(8,128)(2,1)S(1)}, u32[]{:S(2)}, u32[]{:S(2)}) collective-permute-start(bf16[1,4,2,2,4,2,16,128]{7,6,5,4,3,2,1,0:T(8,128)(2,1)} %get-tuple-element.10), channel_id=1, source_target_pairs={{0,32},{16,48},{32,64},{48,80},{64,96},{80,112},{96,0},{112,16},{1... | collective-permute-start | bytes 1572872 | tf_op jit(solution)/shard_map/ppermute | solution.py:255
  31.4 72.0 %collective-permute-start.2 = (bf16[1,4,2,2,4,2,16,128]{7,6,5,4,3,2,1,0:T(8,128)(2,1)}, bf16[1,4,2,2,4,2,16,128]{7,6,5,4,3,2,1,0:T(8,128)(2,1)S(1)}, u32[]{:S(2)}, u32[]{:S(2)}) collective-permute-start(bf16[1,4,2,2,4,2,16,128]{7,6,5,4,3,2,1,0:T(8,128)(2,1)} %get-tuple-element.9), channel_id=1, source_target_pairs={{0,48},{16,64},{32,80},{48,96},{64,112},{80,0},{96,16},{112,32},{1... | collective-permute-start | bytes 1572872 | tf_op jit(solution)/shard_map/ppermute | solution.py:255
  33.0 75.6 %collective-permute-start.3 = (bf16[1,4,2,2,4,2,16,128]{7,6,5,4,3,2,1,0:T(8,128)(2,1)}, bf16[1,4,2,2,4,2,16,128]{7,6,5,4,3,2,1,0:T(8,128)(2,1)}, u32[]{:S(2)}, u32[]{:S(2)}) collective-permute-start(bf16[1,4,2,2,4,2,16,128]{7,6,5,4,3,2,1,0:T(8,128)(2,1)} %get-tuple-element.8), channel_id=1, source_target_pairs={{0,64},{16,80},{32,96},{48,112},{64,0},{80,16},{96,32},{112,48},{1... | collective-permute-start | bytes 1572872 | tf_op jit(solution)/shard_map/ppermute | solution.py:255
  33.6 75.5 %collective-permute-start.4 = (bf16[1,4,2,2,4,2,16,128]{7,6,5,4,3,2,1,0:T(8,128)(2,1)}, bf16[1,4,2,2,4,2,16,128]{7,6,5,4,3,2,1,0:T(8,128)(2,1)}, u32[]{:S(2)}, u32[]{:S(2)}) collective-permute-start(bf16[1,4,2,2,4,2,16,128]{7,6,5,4,3,2,1,0:T(8,128)(2,1)} %get-tuple-element.7), channel_id=1, source_target_pairs={{0,80},{16,96},{32,112},{48,0},{64,16},{80,32},{96,48},{112,64},{1... | collective-permute-start | bytes 1572872 | tf_op jit(solution)/shard_map/ppermute | solution.py:255
  63.9 2.2 %copy-start = (bf16[2,1,1024,1024]{3,2,1,0:T(8,128)(2,1)S(1)}, bf16[2,1,1024,1024]{3,2,1,0:T(8,128)(2,1)}, u32[]{:S(2)}) copy-start(bf16[2,1,1024,1024]{3,2,1,0:T(8,128)(2,1)} %w_ref.1) | copy-start | bytes 12582916
  66.1 2.2 %copy-start.1 = (bf16[1024,2048]{1,0:T(8,128)(2,1)S(1)}, bf16[1024,2048]{1,0:T(8,128)(2,1)}, u32[]{:S(2)}) copy-start(bf16[1024,2048]{1,0:T(8,128)(2,1)} %fusion.1.sel_ref.refs_9_) | copy-start | bytes 12582916
  82.7 27.3 %all-to-all-start.1 = ((bf16[16,16,16,128]{3,2,1,0:T(8,128)(2,1)}), bf16[16,16,16,128]{3,2,1,0:T(8,128)(2,1)S(1)}, u32[]{:S(2)}, u32[]{:S(2)}) async-start(bf16[16,16,16,128]{3,2,1,0:T(8,128)(2,1)} %shard_map.74), calls=%async_computation.1 | async-start | bytes 2097152 | tf_op jit(solution)/shard_map/all_to_all | solution.py:258
  90.4 18.6 %collective-permute-start.5 = (bf16[1,4,2,2,4,2,16,128]{7,6,5,4,3,2,1,0:T(8,128)(2,1)}, bf16[1,4,2,2,4,2,16,128]{7,6,5,4,3,2,1,0:T(8,128)(2,1)}, u32[]{:S(2)}, u32[]{:S(2)}) collective-permute-start(bf16[1,4,2,2,4,2,16,128]{7,6,5,4,3,2,1,0:T(8,128)(2,1)} %get-tuple-element.6), channel_id=1, source_target_pairs={{0,96},{16,112},{32,0},{48,16},{64,32},{80,48},{96,64},{112,80},{1... | collective-permute-start | bytes 1572872 | tf_op jit(solution)/shard_map/ppermute | solution.py:255
  91.3 18.7 %collective-permute-start.6 = (bf16[1,4,2,2,4,2,16,128]{7,6,5,4,3,2,1,0:T(8,128)(2,1)}, bf16[1,4,2,2,4,2,16,128]{7,6,5,4,3,2,1,0:T(8,128)(2,1)}, u32[]{:S(2)}, u32[]{:S(2)}) collective-permute-start(bf16[1,4,2,2,4,2,16,128]{7,6,5,4,3,2,1,0:T(8,128)(2,1)} %get-tuple-element.5), channel_id=1, source_target_pairs={{0,112},{16,0},{32,16},{48,32},{64,48},{80,64},{96,80},{112,96},{1... | collective-permute-start | bytes 1572872 | tf_op jit(solution)/shard_map/ppermute | solution.py:255
  110.0 2.2 %copy-start.2 = (bf16[1024,2048]{1,0:T(8,128)(2,1)S(1)}, bf16[1024,2048]{1,0:T(8,128)(2,1)}, u32[]{:S(2)}) copy-start(bf16[1024,2048]{1,0:T(8,128)(2,1)} %fusion.1.sel_ref.refs_9_) | copy-start | bytes 12582916
  112.2 2.2 %copy-start.3 = (bf16[2,1,1024,1024]{3,2,1,0:T(8,128)(2,1)S(1)}, bf16[2,1,1024,1024]{3,2,1,0:T(8,128)(2,1)}, u32[]{:S(2)}) copy-start(bf16[2,1,1024,1024]{3,2,1,0:T(8,128)(2,1)} %bitcast_select_fusion.refs_8_) | copy-start | bytes 12582916
  128.7 26.7 %all-to-all-start.2 = ((bf16[16,16,16,128]{3,2,1,0:T(8,128)(2,1)}), bf16[16,16,16,128]{3,2,1,0:T(8,128)(2,1)S(1)}, u32[]{:S(2)}, u32[]{:S(2)}) async-start(bf16[16,16,16,128]{3,2,1,0:T(8,128)(2,1)} %shard_map.76), calls=%async_computation.2 | async-start | bytes 2097152 | tf_op jit(solution)/shard_map/all_to_all | solution.py:260
